TPU v7x, 256 devices: a whole 4x4x8 slice. The times are simulated.
256 devices in a mesh: row: 16 (over y_hi, x, core), col: 16 (over z, y_lo).
Axes of the slice: x: 4, y: 4 (y_hi: 2, y_lo: 2; y = y_hi * 2 + y_lo), z: 8, core: 2. Of those that a mesh axis runs over, the one named last changes fastest.
Arguments:
- data_rows: bfloat16 [393216, 256], P(('row', 'col')), may hold values from -7 to 7
- data_mass: float32 [393216], P(('row', 'col')), may hold values from 0.3 to 3
- block_links: int32 [3072, 16], P(('row', 'col')), may hold values from 0 to 31, all different within a row
- cand_rows: bfloat16 [4096, 256], P('col'), may hold values from -7 to 7
- cand_mass: float32 [4096], replicated, may hold values from 0.3 to 3
Outputs:
- data_scale: float32 [393216], P(('row', 'col'))
- cand_scale: float32 [4096], P('col')
- new_support: float32 [4096, 256], P('col')
Inputs may be any that keep to these rules, and one draw needn't show every extreme that they name: `block_links`: each row names 16 different candidate blocks; every candidate block is named by some row.
All inputs are finite; a program needn't handle non-finite values.
Results may differ from a plain program's by a relative error of at most 0.0014.
Values may be sent and summed in bfloat16 or wider, within the bound.
No kernel may reach another device: no remote copies, remote signals or barrier semaphores. Data moves between devices by JAX's collectives and lax.ppermute only.
A program may use at most 64 MiB of HBM per device.

v0:
```python
import jax
import jax.numpy as jnp
from jax import lax
from jax.sharding import PartitionSpec as P

BLOCK = 128
ITERS = 3


EPS = 0.05
OFFSET = 1.0


def normalize(matrix):
    values = matrix.astype(jnp.float32)
    return (values * lax.rsqrt(jnp.mean(values * values, axis=1, keepdims=True) + 1e-06)).astype(
        jnp.bfloat16
    )


def kernel_tiles(data_group, cand_blocks, link_group):
    feature_count = data_group.shape[-1]
    chosen = cand_blocks[link_group].reshape(link_group.shape[0], -1, feature_count)
    scores = jnp.einsum("gid,gjd->gij", data_group, chosen, preferred_element_type=jnp.float32)
    return jnp.exp(scores * (1.0 / (feature_count * EPS)) - OFFSET) * (1.0 / chosen.shape[1])


def row_update(kernel_tile, link_group, scale_blocks, mass_group):
    linked_scale = scale_blocks[link_group].reshape(link_group.shape[0], -1)
    row_total = jnp.sum(kernel_tile * linked_scale[:, None, :], axis=2)
    return mass_group / row_total


def column_part(kernel_tile, link_group, scale_rows, block_count):
    slot_mass = jnp.sum(kernel_tile * scale_rows[:, :, None], axis=1).reshape(-1, BLOCK)
    return jax.ops.segment_sum(slot_mass, link_group.reshape(-1), num_segments=block_count)


def weighted_part(kernel_tile, link_group, scale_rows, rows_group, block_count):
    plan_weights = (kernel_tile * scale_rows[:, :, None]).astype(jnp.bfloat16)
    slot_sums = jnp.einsum(
        "gij,gid->gjd", plan_weights, rows_group, preferred_element_type=jnp.float32
    )
    slot_sums = slot_sums.reshape(-1, BLOCK, rows_group.shape[-1])
    return jax.ops.segment_sum(slot_sums, link_group.reshape(-1), num_segments=block_count)


def on_device(data_rows, data_mass, block_links, cand_rows, cand_mass):
    local_rows, feature_count = data_rows.shape
    local_cands = cand_rows.shape[0]
    row_devices = lax.axis_size("row")
    col_devices = lax.axis_size("col")
    cand_total = local_cands * col_devices
    block_count = cand_total // BLOCK
    local_blocks = local_rows // BLOCK
    group_size = min(4, local_blocks)
    group_count = local_blocks // group_size
    mass_ratio = local_rows * row_devices / local_cands
    own_start = lax.axis_index("col") * local_cands
    gathered = lax.all_gather(normalize(cand_rows), "col", axis=0, tiled=True)
    cand_blocks = gathered.reshape(block_count, BLOCK, feature_count)
    data_groups = normalize(data_rows).reshape(group_count, group_size, BLOCK, feature_count)
    rows_groups = data_rows.reshape(group_count, group_size, BLOCK, feature_count)
    mass_groups = data_mass.reshape(group_count, group_size, BLOCK)
    link_groups = block_links.reshape(group_count, group_size, -1)
    scale_blocks = jnp.ones((block_count, BLOCK), jnp.float32)
    own_total = jnp.zeros((local_cands,), jnp.float32)
    scale_rows = jnp.zeros((group_count, group_size, BLOCK), jnp.float32)
    for sweep_index in range(ITERS):

        def sweep_step(running, inputs):
            data_group, rows_group, mass_group, link_group = inputs
            kernel_tile = kernel_tiles(data_group, cand_blocks, link_group)
            new_scale = row_update(kernel_tile, link_group, scale_blocks, mass_group)
            mass_sum = running[0] + column_part(kernel_tile, link_group, new_scale, block_count)
            return ((mass_sum,), new_scale)

        empty_mass = jnp.zeros((block_count, BLOCK), jnp.float32)
        start_carry = (empty_mass,)
        running, scale_rows = lax.scan(
            sweep_step, start_carry, (data_groups, rows_groups, mass_groups, link_groups)
        )
        whole_total = lax.psum(running[0], ("row", "col")).reshape(-1)
        combine_own_total = lax.dynamic_slice_in_dim(whole_total, own_start, local_cands)
        new_blocks = (mass_ratio * cand_mass / whole_total).reshape(block_count, BLOCK)
        scale_blocks = new_blocks
        own_total = combine_own_total

    def bary_step(running_sums, inputs):
        data_group, rows_group, link_group, scale_group = inputs
        kernel_tile = kernel_tiles(data_group, cand_blocks, link_group)
        return (
            running_sums
            + weighted_part(kernel_tile, link_group, scale_group, rows_group, block_count),
            None,
        )

    partial_sums, unused = lax.scan(
        bary_step,
        jnp.zeros((block_count, BLOCK, feature_count), jnp.float32),
        (data_groups, rows_groups, link_groups, scale_rows),
    )
    flat_sums = partial_sums.reshape(cand_total, feature_count)
    share_rows = lax.psum_scatter(flat_sums, "col", scatter_dimension=0, tiled=True)
    own_sums = lax.psum(share_rows, "row")
    new_support = own_sums / own_total[:, None]
    own_scale = lax.dynamic_slice_in_dim(scale_blocks.reshape(-1), own_start, local_cands)
    return (scale_rows.reshape(local_rows), own_scale, new_support)


def solution(mesh):
    placed = (
        P(("row", "col"), None),
        P(("row", "col")),
        P(("row", "col"), None),
        P("col", None),
        P(),
    )
    return jax.shard_map(
        on_device,
        mesh=mesh,
        in_specs=placed,
        out_specs=(P(("row", "col")), P("col"), P("col", None)),
        check_vma=False,
    )
```

profile of v0, /device:TPU:4, one launch (start us, length us, event | category | flops | bytes accessed | tf_op | source)
XLA Modules:
  0.0 669.9 jit_solution(7171661123215345616)
XLA Ops:
  7.2 1.0 fusion.29
  8.2 1.7 fusion.30
  10.0 0.7 reshape.328
  10.7 0.7 reshape.331
  11.4 1.4 fusion.27
  12.8 1.4 fusion.28
  14.2 72.3 %all-gather.2.cloned.1.call-done = bf16[4096,256]{1,0:T(8,128)(2,1)} async-done(((bf16[256,256]{1,0:T(8,128)(2,1)}), bf16[4096,256]{1,0:T(8,128)(2,1)}) %all-gather.2.cloned.1.call-update) | async-done | bytes 2097168 | tf_op jit(solution)/shard_map/all_gather | solution.py:60
  86.5 32.6 %while.50 = (s32[]{:T(128)}, f32[32,128]{1,0:T(8,128)S(1)}, s32[3,4,16]{2,1,0:T(4,128)S(1)}, bf16[3,4,128,256]{3,2,1,0:T(8,128)(2,1)S(1)}, bf16[32,128,256]{2,1,...) while((s32[]{:T(128)}, f32[32,128]{1,0:T(8,128)S(1)}, s32[3,4,16]{2,1,0:T(4,128)S(1)}, ...), condition=%wide.region_6.7_spmd, body=%wide.region_2.6_spmd.sunk | while | flops 545269440 | bytes 21693284 | solution.py:80
  86.6 4.3 gather_fusion.1
  91.6 3.8 multiply_reduce_fusion.12
  95.4 0.9 multiply_reduce_fusion.13
  96.5 0.9 scatter_fusion
  97.5 4.3 gather_fusion.1
  102.4 3.8 multiply_reduce_fusion.12
  106.3 0.9 multiply_reduce_fusion.13
  107.3 0.9 scatter_fusion
  108.4 4.3 gather_fusion.1
  113.3 3.8 multiply_reduce_fusion.12
  117.2 0.9 multiply_reduce_fusion.13
  118.2 0.9 scatter_fusion
  119.1 72.8 %psum.28 = f32[4096]{0:T(1024)S(1)} all-reduce(f32[4096]{0:T(1024)S(1)} %bitcast.132), channel_id=1, replica_groups=mesh['row'=16,'col'=16] {'row','col'}, use_global_device_ids=true, to_apply=%region_7.8 | all-reduce | flops 4096 | bytes 32768 | tf_op jit(solution)/shard_map/psum | solution.py:83
  192.0 32.6 %while.51 = (s32[]{:T(128)}, f32[32,128]{1,0:T(8,128)S(1)}, s32[3,4,16]{2,1,0:T(4,128)S(1)}, bf16[3,4,128,256]{3,2,1,0:T(8,128)(2,1)S(1)}, bf16[32,128,256]{2,1,...) while((s32[]{:T(128)}, f32[32,128]{1,0:T(8,128)S(1)}, ...), condition=%wide.region_12.13_spmd, body=%wide.region_8.12_spmd.sunk | while | flops 545269440 | bytes 21676896 | solution.py:80
  192.1 4.3 gather_fusion.3
  197.1 3.8 multiply_reduce_fusion.14
  200.9 0.9 multiply_reduce_fusion.15
  202.0 0.9 scatter_fusion.1
  203.0 4.3 gather_fusion.3
  207.9 3.8 multiply_reduce_fusion.14
  211.8 0.9 multiply_reduce_fusion.15
  212.8 0.9 scatter_fusion.1
  213.8 4.3 gather_fusion.3
  218.8 3.8 multiply_reduce_fusion.14
  222.6 0.9 multiply_reduce_fusion.15
  223.7 0.9 scatter_fusion.1
  224.6 73.5 %psum.29 = f32[4096]{0:T(1024)S(1)} all-reduce(f32[4096]{0:T(1024)S(1)} %bitcast.133), channel_id=1, replica_groups=mesh['row'=16,'col'=16] {'row','col'}, use_global_device_ids=true, to_apply=%region_13.14 | all-reduce | flops 4096 | bytes 32768 | tf_op jit(solution)/shard_map/psum | solution.py:83
  298.1 32.7 %while.52 = (s32[]{:T(128)}, f32[32,128]{1,0:T(8,128)S(1)}, f32[3,4,128]{2,1,0:T(4,128)S(1)}, s32[3,4,16]{2,1,0:T(4,128)S(1)}, bf16[3,4,128,256]{3,2,1,0:T(8,128...) while((s32[]{:T(128)}, f32[32,128]{1,0:T(8,128)S(1)}, ...), condition=%wide.region_18.19_spmd, body=%wide.region_14.18_spmd.sunk | while | flops 545269952 | bytes 21683052 | solution.py:80
  298.3 4.3 gather_fusion.5
  303.2 3.8 multiply_reduce_fusion.16
  307.0 0.9 multiply_reduce_fusion.17
  308.1 0.9 scatter_fusion.2
  309.1 4.3 gather_fusion.5
  314.1 3.8 multiply_reduce_fusion.16
  317.9 0.9 multiply_reduce_fusion.17
  319.0 0.9 scatter_fusion.2
  320.0 4.3 gather_fusion.5
  325.0 3.8 multiply_reduce_fusion.16
  328.8 0.9 multiply_reduce_fusion.17
  329.9 0.9 scatter_fusion.2
  330.8 2.5 broadcast.262
  333.3 91.5 %while.53 = (s32[]{:T(128)}, f32[32,128,256]{2,1,0:T(8,128)}, s32[3,4,16]{2,1,0:T(4,128)S(1)}, bf16[3,4,128,256]{3,2,1,0:T(8,128)(2,1)S(1)}, bf16[32,128,256]{2,...) while((s32[]{:T(128)}, f32[32,128,256]{2,1,0:T(8,128)}, ...), condition=%wide.region_22.23_spmd, body=%wide.region_20.22_spmd.sunk | while | flops 1080035072 | bytes 46675548 | solution.py:98
  333.4 2.8 gather_fusion.6
  336.2 7.8 %fusion.56 = f32[4,2048,256]{2,1,0:T(8,128)} fusion(bf16[4,2048,256]{2,1,0:T(8,128)(2,1)} %bitcast.130, f32[4,128]{1,0:T(4,128)S(1)} %multiply_bitcast_fusion.2, bf16[3,4,128,256]{3,2,1,0:T(8,128)(2,1)} %get-tuple-element.736, s32[]{:T(128)} %get-tuple-element.722, bf16[3,4,128,256]{3,2,1,0:T(8,128)(2,1)S(1)} %get-tuple-element.733), kind=kOutput, calls=%fused_computation.53.clone.1 | convolution fusion | flops 1077936128 | bytes 13110272 | tf_op jit(solution)/shard_map/while/body/eval_jaxpr/gij,gid->gjd/dot_general | solution.py:41
  344.0 19.8 %scatter_fusion.3 = f32[32,128,256]{2,1,0:T(8,128)} fusion(f32[32,128,256]{2,1,0:T(8,128)} %get-tuple-element.723, s32[64]{0:T(128)S(1)} %reshape.516, f32[64,128,256]{2,1,0:T(8,128)} %bitcast.125), kind=kCustom, calls=%fused_computation.10.clone.1 | custom fusion | flops 2097152 | bytes 25166080 | tf_op jit(solution)/shard_map/while/body/eval_jaxpr/scatter-add | solution.py:45
  363.9 2.8 gather_fusion.6
  366.6 7.8 %fusion.56 = f32[4,2048,256]{2,1,0:T(8,128)} fusion(bf16[4,2048,256]{2,1,0:T(8,128)(2,1)} %bitcast.130, f32[4,128]{1,0:T(4,128)S(1)} %multiply_bitcast_fusion.2, bf16[3,4,128,256]{3,2,1,0:T(8,128)(2,1)} %get-tuple-element.736, s32[]{:T(128)} %get-tuple-element.722, bf16[3,4,128,256]{3,2,1,0:T(8,128)(2,1)S(1)} %get-tuple-element.733), kind=kOutput, calls=%fused_computation.53.clone.1 | convolution fusion | flops 1077936128 | bytes 13110272 | tf_op jit(solution)/shard_map/while/body/eval_jaxpr/gij,gid->gjd/dot_general | solution.py:41
  374.5 19.7 %scatter_fusion.3 = f32[32,128,256]{2,1,0:T(8,128)} fusion(f32[32,128,256]{2,1,0:T(8,128)} %get-tuple-element.723, s32[64]{0:T(128)S(1)} %reshape.516, f32[64,128,256]{2,1,0:T(8,128)} %bitcast.125), kind=kCustom, calls=%fused_computation.10.clone.1 | custom fusion | flops 2097152 | bytes 25166080 | tf_op jit(solution)/shard_map/while/body/eval_jaxpr/scatter-add | solution.py:45
  394.3 2.8 gather_fusion.6
  397.1 7.8 %fusion.56 = f32[4,2048,256]{2,1,0:T(8,128)} fusion(bf16[4,2048,256]{2,1,0:T(8,128)(2,1)} %bitcast.130, f32[4,128]{1,0:T(4,128)S(1)} %multiply_bitcast_fusion.2, bf16[3,4,128,256]{3,2,1,0:T(8,128)(2,1)} %get-tuple-element.736, s32[]{:T(128)} %get-tuple-element.722, bf16[3,4,128,256]{3,2,1,0:T(8,128)(2,1)S(1)} %get-tuple-element.733), kind=kOutput, calls=%fused_computation.53.clone.1 | convolution fusion | flops 1077936128 | bytes 13110272 | tf_op jit(solution)/shard_map/while/body/eval_jaxpr/gij,gid->gjd/dot_general | solution.py:41
  405.0 19.8 %scatter_fusion.3 = f32[32,128,256]{2,1,0:T(8,128)} fusion(f32[32,128,256]{2,1,0:T(8,128)} %get-tuple-element.723, s32[64]{0:T(128)S(1)} %reshape.516, f32[64,128,256]{2,1,0:T(8,128)} %bitcast.125), kind=kCustom, calls=%fused_computation.10.clone.1 | custom fusion | flops 2097152 | bytes 25166080 | tf_op jit(solution)/shard_map/while/body/eval_jaxpr/scatter-add | solution.py:45
  424.8 98.7 %reduce-scatter.2.cloned.1.call-done = f32[256,256]{1,0:T(8,128)} async-done(((f32[4096,256]{1,0:T(8,128)}), f32[256,256]{1,0:T(8,128)}) %reduce-scatter.2.cloned.1.call-update) | async-done | bytes 262160 | tf_op jit(solution)/shard_map/reduce_scatter | solution.py:104
  524.2 73.8 %psum.30 = f32[4096]{0:T(1024)S(1)} all-reduce(f32[4096]{0:T(1024)S(1)} %bitcast.131), channel_id=1, replica_groups=mesh['row'=16,'col'=16] {'row','col'}, use_global_device_ids=true, to_apply=%region_19.20 | all-reduce | flops 4096 | bytes 32768 | tf_op jit(solution)/shard_map/psum | solution.py:83
  598.0 0.6 dynamic-slice_divide_fusion
  598.7 63.0 %all-reduce.2.cloned.1.call-done = f32[256,256]{1,0:T(8,128)} async-done(((f32[256,256]{1,0:T(8,128)}), f32[256,256]{1,0:T(8,128)}) %all-reduce.2.cloned.1.call-update) | async-done | bytes 262160 | tf_op jit(solution)/shard_map/psum | solution.py:105
  661.6 1.8 broadcast_divide_fusion
  (121 shorter events, 8.9 us)
Async XLA Ops:
  7.2 79.4 %all-gather.2.cloned.1.call-start = ((), (), s32[]{:S(2)}) async-start(), calls=%async_computation.1 | async-start | bytes 2228224 | tf_op jit(solution)/shard_map/all_gather | solution.py:60
  9.9 513.6 %reduce-scatter.2.cloned.1.call-start = ((), (), s32[]{:S(2)}) async-start(), calls=%async_computation.2 | async-start | bytes 4456448 | tf_op jit(solution)/shard_map/reduce_scatter | solution.py:104
  86.5 105.4 %copy-start.1 = (f32[4096]{0:T(1024)S(1)}, f32[4096]{0:T(1024)}, u32[]{:S(2)}) copy-start(f32[4096]{0:T(1024)} %param.17) | copy-start | bytes 49156
  330.8 2.5 copy-start
  424.8 236.8 %all-reduce.2.cloned.1.call-start = ((), (), s32[]{:S(2)}) async-start(), calls=%async_computation.3 | async-start | bytes 524288 | tf_op jit(solution)/shard_map/psum | solution.py:105
Sparse Core Ops, SparseCore 0:
  10.4 76.1 all-gather.1
  424.9 98.6 reduce-scatter.1
  526.2 135.4 all-reduce.1
where the time goes:
time: 679 us; the launch traced here: 670 us
  waiting for transfers between devices  234 us (34%)
  blocking collectives  220 us (32%)
  other arithmetic  84 us (12%)
  local copies, waits for them, and re-layouts  59.5 us (9%)
  matrix products  57.7 us (8%)
  between operations  13.8 us (2%)
    psum x3, blocking collectives, on_device(): whole_total = lax.psum(running[0], ('row', 'col')).reshape(-1)  220 us
    reduce_scatter x1, waiting for transfers between devices, on_device(): lax.psum_scatter(flat_sums, 'col', scatter_dimension=0, tiled=True)  98.7 us
    all_gather x1, waiting for transfers between devices, on_device(): gathered = lax.all_gather(normalize(cand_rows), 'col', axis=0, tiled=True)  72.3 us
    psum x1, waiting for transfers between devices, on_device(): own_sums = lax.psum(share_rows, 'row')  63 us
    scatter-add x3, other arithmetic, weighted_part(): jax.ops.segment_sum(slot_sums, link_group.reshape(-1), num_segments=block...  59.3 us
    gather x12, local copies, waits for them, and re-layouts, kernel_tiles(): cand_blocks[link_group].reshape(link_group.shape[0], -1, feature_count)  47.3 us
    dot_general x9, matrix products, kernel_tiles(): jnp.einsum('gid,gjd->gij', data_group, chosen, preferred_element_type=jnp...  34.4 us
    dot_general x3, matrix products, weighted_part(): jnp.einsum('gij,gid->gjd', plan_weights, rows_group, preferred_element_ty...  23.3 us
  transfers between devices with their start and end apart: 3, of which 3 were waited for; matrix products, arithmetic and copies ran while one was open for 1% of the time, Pallas kernels for 0%

commit v1 on v0

v1 whole, which is shorter than its diff:
```python
import functools

import jax
import jax.numpy as jnp
from jax import lax
from jax.experimental import pallas as pl
from jax.experimental.pallas import tpu as pltpu
from jax.sharding import Mesh
from jax.sharding import PartitionSpec as P

BLOCK = 128
ITERS = 3


EPS = 0.05
OFFSET = 1.0

ROW_AXES = ("yh", "x", "c")
COL_AXES = ("z", "yl")
ALL_AXES = ROW_AXES + COL_AXES


def normalize(matrix):
    values = matrix.astype(jnp.float32)
    return (values * lax.rsqrt(jnp.mean(values * values, axis=1, keepdims=True) + 1e-06)).astype(
        jnp.bfloat16
    )


def butterfly_sum(x, sizes):
    for axis in ALL_AXES:
        n = sizes[axis]
        k = 1
        while k < n:
            x = x + lax.ppermute(x, axis, [(j, j ^ k) for j in range(n)])
            k *= 2
    return x


def _kernel_slot(xn, cn_ref, blk, inv_width, inv_count):
    cand = cn_ref[blk]
    scores = lax.dot_general(
        xn, cand, (((1,), (1,)), ((), ())), preferred_element_type=jnp.float32
    )
    return jnp.exp(scores * inv_width - OFFSET) * inv_count


def sweep_body(nbr, inv_width, inv_count, bary, links_ref, xn_ref, cn_ref, scale_ref, mass_ref,
               *rest):
    if bary:
        rows_ref, ds_ref, ct_ref, ws_ref, kbuf = rest
    else:
        ds_ref, ct_ref, kbuf = rest
    b = pl.program_id(0)

    @pl.when(b == 0)
    def _():
        ct_ref[...] = jnp.zeros_like(ct_ref)
        if bary:
            ws_ref[...] = jnp.zeros_like(ws_ref)

    xn = xn_ref[...]
    acc = jnp.zeros((BLOCK, BLOCK), jnp.float32)
    for s in range(nbr):
        blk = links_ref[b, s]
        k = _kernel_slot(xn, cn_ref, blk, inv_width, inv_count)
        kbuf[s] = k
        acc = acc + k * scale_ref[pl.ds(blk, 1), :]
    row_total = jnp.sum(acc, axis=1, keepdims=True)
    ds = mass_ref[...] / row_total
    ds_ref[...] = ds
    if bary:
        rows = rows_ref[...]
    for s in range(nbr):
        blk = links_ref[b, s]
        k = kbuf[s]
        part = jnp.sum(k * ds, axis=0, keepdims=True)
        ct_ref[pl.ds(blk, 1), :] += part
        if bary:
            w = (k * ds).astype(jnp.bfloat16)
            ws_ref[blk] += lax.dot_general(
                w, rows, (((0,), (0,)), ((), ())), preferred_element_type=jnp.float32
            )


def sweep(xn, cn_blocks, scale_blocks, mass_col, links, rows=None):
    local_rows, feature_count = xn.shape
    block_count = cn_blocks.shape[0]
    local_blocks, nbr = links.shape
    bary = rows is not None
    inv_width = 1.0 / (feature_count * EPS)
    inv_count = 1.0 / (nbr * BLOCK)
    in_specs = [
        pl.BlockSpec((BLOCK, feature_count), lambda b, L: (b, 0)),
        pl.BlockSpec((block_count, BLOCK, feature_count), lambda b, L: (0, 0, 0)),
        pl.BlockSpec((block_count, BLOCK), lambda b, L: (0, 0)),
        pl.BlockSpec((BLOCK, 1), lambda b, L: (b, 0)),
    ]
    out_specs = [
        pl.BlockSpec((BLOCK, 1), lambda b, L: (b, 0)),
        pl.BlockSpec((block_count, BLOCK), lambda b, L: (0, 0)),
    ]
    out_shape = [
        jax.ShapeDtypeStruct((local_rows, 1), jnp.float32),
        jax.ShapeDtypeStruct((block_count, BLOCK), jnp.float32),
    ]
    args = [links, xn, cn_blocks, scale_blocks, mass_col]
    if bary:
        in_specs.append(pl.BlockSpec((BLOCK, feature_count), lambda b, L: (b, 0)))
        out_specs.append(
            pl.BlockSpec((block_count, BLOCK, feature_count), lambda b, L: (0, 0, 0))
        )
        out_shape.append(jax.ShapeDtypeStruct((block_count, BLOCK, feature_count), jnp.float32))
        args.append(rows)
    flops = 2 * local_rows * nbr * BLOCK * feature_count * (2 if bary else 1)
    return pl.pallas_call(
        functools.partial(sweep_body, nbr, inv_width, inv_count, bary),
        grid_spec=pltpu.PrefetchScalarGridSpec(
            num_scalar_prefetch=1,
            grid=(local_blocks,),
            in_specs=in_specs,
            out_specs=out_specs,
            scratch_shapes=[pltpu.VMEM((nbr, BLOCK, BLOCK), jnp.float32)],
        ),
        out_shape=out_shape,
        compiler_params=pltpu.CompilerParams(
            dimension_semantics=("arbitrary",), vmem_limit_bytes=48 * 1024 * 1024
        ),
        cost_estimate=pl.CostEstimate(
            flops=flops,
            transcendentals=local_rows * nbr * BLOCK,
            bytes_accessed=block_count * BLOCK * feature_count * (2 + (4 if bary else 0))
            + local_rows * feature_count * (4 if bary else 2),
        ),
    )(*args)


def on_device(sizes, data_rows, data_mass, block_links, cand_rows, cand_mass):
    local_rows, feature_count = data_rows.shape
    local_cands = cand_rows.shape[0]
    row_devices = sizes["yh"] * sizes["x"] * sizes["c"]
    col_devices = sizes["z"] * sizes["yl"]
    cand_total = local_cands * col_devices
    block_count = cand_total // BLOCK
    mass_ratio = local_rows * row_devices / local_cands
    col_index = lax.axis_index("z") * sizes["yl"] + lax.axis_index("yl")
    own_start = col_index * local_cands
    gathered = lax.all_gather(normalize(cand_rows), COL_AXES, axis=0, tiled=True)
    cn_blocks = gathered.reshape(block_count, BLOCK, feature_count)
    xn = normalize(data_rows)
    mass_col = data_mass.reshape(local_rows, 1)
    links = block_links.astype(jnp.int32)
    scale_blocks = jnp.ones((block_count, BLOCK), jnp.float32)
    for sweep_index in range(ITERS - 1):
        _, part_total = sweep(xn, cn_blocks, scale_blocks, mass_col, links)
        whole_total = butterfly_sum(part_total, sizes)
        scale_blocks = mass_ratio * cand_mass.reshape(block_count, BLOCK) / whole_total
    ds_col, part_total, partial_sums = sweep(
        xn, cn_blocks, scale_blocks, mass_col, links, rows=data_rows
    )
    whole_total = butterfly_sum(part_total, sizes).reshape(-1)
    own_total = lax.dynamic_slice_in_dim(whole_total, own_start, local_cands)
    own_scale = mass_ratio * lax.dynamic_slice_in_dim(cand_mass, own_start, local_cands) / own_total
    flat_sums = partial_sums.reshape(cand_total, feature_count)
    share_rows = lax.psum_scatter(flat_sums, COL_AXES, scatter_dimension=0, tiled=True)
    own_sums = lax.psum(share_rows, ROW_AXES)
    new_support = own_sums / own_total[:, None]
    return (ds_col.reshape(local_rows), own_scale, new_support)


def solution(mesh):
    row_size, col_size = mesh.devices.shape
    fine = Mesh(mesh.devices.reshape(2, row_size // 4, 2, col_size // 2, 2), ALL_AXES)
    sizes = dict(fine.shape)
    placed = (
        P(ALL_AXES, None),
        P(ALL_AXES),
        P(ALL_AXES, None),
        P(COL_AXES, None),
        P(),
    )
    return jax.shard_map(
        functools.partial(on_device, sizes),
        mesh=fine,
        in_specs=placed,
        out_specs=(P(ALL_AXES), P(COL_AXES), P(COL_AXES, None)),
        check_vma=False,
    )
```

time: 679 us -> 448 us (0.66)
  blocking collectives: 220 us -> 0 us
  waiting for transfers between devices: 234 us -> 355 us
  other arithmetic: 84 us -> 6.7 us
  matrix products: 57.7 us -> 0 us
  local copies, waits for them, and re-layouts: 59.5 us -> 2.56 us
  Pallas kernels: 0 us -> 37.3 us
  starting transfers between devices: 0.12 us -> 25.1 us
    psum x3 -> x0, blocking collectives: 220 us -> none  [on_device(): whole_total = lax.psum(running[0], ('row', 'col')).reshape(-1)]
    ppermute x0 -> x24, waiting for transfers between devices: none -> 77.5 us  [butterfly_sum(): x = x + lax.ppermute(x, axis, [(j, j ^ k) for j in range(n)])]
    psum x1, waiting for transfers between devices: 63 us -> 137 us  [on_device(): own_sums = lax.psum(share_rows, ROW_AXES)]
    scatter-add x12 -> x0, other arithmetic: 67.4 us -> none  [the longest x3 59.3 us: weighted_part(): jax.ops.segment_sum(slot_sums, link_group.reshape(-1), num_segments=block...]
    dot_general x12 -> x0, matrix products: 57.7 us -> none  [the longest x9 34.4 us: kernel_tiles(): jnp.einsum('gid,gjd->gij', data_group, chosen, preferred_element_type=jnp...]
    gather x21 -> x0, local copies, waits for them, and re-layouts: 52.7 us -> none  [the longest x12 47.3 us: kernel_tiles(): cand_blocks[link_group].reshape(link_group.shape[0], -1, feature_count)]
    pallas_call x0 -> x3, Pallas kernels: none -> 37.3 us  [sweep(): pl.pallas_call(functools.partial(sweep_body, nbr, inv_width, inv_count, b...]
    reduce_scatter x1, waiting for transfers between devices: 98.7 us -> 64.9 us  [on_device(): lax.psum_scatter(flat_sums, COL_AXES, scatter_dimension=0, tiled=True)]
  transfers between devices with their start and end apart: 3 -> 27, of which waited for: 3 -> 26; matrix products, arithmetic and copies ran while one was open for 1% -> 1% of each run, Pallas kernels for 0% -> 0%
where the time goes in v1:
time: 448 us; the launch traced here: 440 us
  waiting for transfers between devices  355 us (79%)
  Pallas kernels  37.3 us (8%)
  starting transfers between devices  25.1 us (6%)
  between operations  13.9 us (3%)
  other arithmetic  6.7 us (1%)
    psum x1, waiting for transfers between devices, on_device(): own_sums = lax.psum(share_rows, ROW_AXES)  137 us
    ppermute x24, waiting for transfers between devices, butterfly_sum(): x = x + lax.ppermute(x, axis, [(j, j ^ k) for j in range(n)])  77.5 us
    all_gather x1, waiting for transfers between devices, on_device(): lax.all_gather(normalize(cand_rows), COL_AXES, axis=0, tiled=True)  74.9 us
    reduce_scatter x1, waiting for transfers between devices, on_device(): lax.psum_scatter(flat_sums, COL_AXES, scatter_dimension=0, tiled=True)  64.9 us
    pallas_call x3, Pallas kernels, sweep(): pl.pallas_call(functools.partial(sweep_body, nbr, inv_width, inv_count, b...  37.3 us
    ppermute x24, starting transfers between devices, butterfly_sum(): x = x + lax.ppermute(x, axis, [(j, j ^ k) for j in range(n)])  25 us
  transfers between devices with their start and end apart: 27, of which 26 were waited for; matrix products, arithmetic and copies ran while one was open for 1% of the time, Pallas kernels for 0%

profile of v1, /device:TPU:4, one launch (start us, length us, event | category | flops | bytes accessed | tf_op | source)
XLA Modules:
  0.0 440.3 jit_solution(3824275891507241172)
XLA Ops:
  7.2 0.0 all-gather.2.cloned.1.call-start
  7.2 1.1 fusion.2
  8.3 1.7 fusion.3
  10.0 0.0 all-gather.2.cloned.1.call-update
  10.0 0.0 reduce-scatter.2.cloned.1.call-start
  10.1 1.0 reshape.47.mass_ref
  11.0 0.3 fusion
  11.3 0.3 fusion.1.xn_ref
  11.6 74.9 %all-gather.2.cloned.1.call-done = bf16[4096,256]{1,0:T(8,128)(2,1)} async-done(((bf16[256,256]{1,0:T(8,128)(2,1)}), bf16[4096,256]{1,0:T(8,128)(2,1)}) %all-gather.2.cloned.1.call-update) | async-done | bytes 2097168 | tf_op jit(solution)/shard_map/all_gather | solution.py:148
  86.5 1.6 copy-done.1
  88.1 10.4 %shard_map.76 = (f32[1536,1]{1,0:T(8,128)}, f32[32,128]{1,0:T(8,128)S(1)}) custom-call(s32[12,16]{1,0:T(8,128)S(1)} %copy-done.2, bf16[1536,256]{1,0:T(8,128)(2,1)S(1)} %fusion.1.xn_ref, bf16[32,128,256]{2,1,0:T(8,128)(2,1)S(1)} %bitcast.7, f32[32,128]{1,0:T(8,128)S(1)} %broadcast_in_dim.2.scale_ref, f32[1536,1]{1,0:T(8,128)S(1)} %reshape.47.mass_ref), custom_call_target="tpu_custom_call" | custom-call | flops 1610612736 | bytes 2883584 | tf_op jit(solution)/shard_map/pallas_call | solution.py:116
  98.5 2.9 collective-permute-start
  101.5 2.3 collective-permute-done
  103.8 1.2 collective-permute-start.1
  105.0 2.5 collective-permute-done.1
  107.5 0.3 collective-permute-start.2
  107.8 5.0 %collective-permute-done.2 = f32[32,128]{1,0:T(8,128)S(1)} collective-permute-done((f32[32,128]{1,0:T(8,128)S(1)}, f32[32,128]{1,0:T(8,128)S(1)}, u32[]{:S(2)}, u32[]{:S(2)}) %collective-permute-start.2) | collective-permute-done | bytes 16416 | tf_op jit(solution)/shard_map/ppermute | solution.py:35
  112.8 1.2 collective-permute-done.3
  114.0 0.4 collective-permute-start.4
  114.3 3.4 collective-permute-done.4
  117.7 0.7 collective-permute-start.5
  118.4 3.9 collective-permute-done.5
  122.4 2.7 collective-permute-start.6
  125.1 4.9 %collective-permute-done.6 = f32[32,128]{1,0:T(8,128)S(1)} collective-permute-done((f32[32,128]{1,0:T(8,128)S(1)}, f32[32,128]{1,0:T(8,128)S(1)}, u32[]{:S(2)}, u32[]{:S(2)}) %collective-permute-start.6) | collective-permute-done | bytes 16416 | tf_op jit(solution)/shard_map/ppermute | solution.py:35
  130.0 0.2 collective-permute-start.7
  130.3 3.5 collective-permute-done.7
  133.8 10.4 %shard_map.77 = (f32[1536,1]{1,0:T(8,128)}, f32[32,128]{1,0:T(8,128)S(1)}) custom-call(s32[12,16]{1,0:T(8,128)S(1)} %copy-done.2, bf16[1536,256]{1,0:T(8,128)(2,1)S(1)} %fusion.1.xn_ref, bf16[32,128,256]{2,1,0:T(8,128)(2,1)S(1)} %bitcast.8, f32[32,128]{1,0:T(8,128)S(1)} %bitcast_divide_fusion.1.scale_ref, f32[1536,1]{1,0:T(8,128)S(1)} %reshape.47.mass_ref), custom_call_target="tpu_custom_call" | custom-call | flops 1610612736 | bytes 2883584 | tf_op jit(solution)/shard_map/pallas_call | solution.py:116
  144.2 3.1 collective-permute-start.8
  147.2 2.2 collective-permute-done.8
  149.4 1.2 collective-permute-start.9
  150.6 2.5 collective-permute-done.9
  153.2 0.3 collective-permute-start.10
  153.4 5.0 %collective-permute-done.10 = f32[32,128]{1,0:T(8,128)S(1)} collective-permute-done((f32[32,128]{1,0:T(8,128)S(1)}, f32[32,128]{1,0:T(8,128)S(1)}, u32[]{:S(2)}, u32[]{:S(2)}) %collective-permute-start.10) | collective-permute-done | bytes 16416 | tf_op jit(solution)/shard_map/ppermute | solution.py:35
  158.4 1.2 collective-permute-done.11
  159.6 0.4 collective-permute-start.12
  160.0 3.4 collective-permute-done.12
  163.4 0.8 collective-permute-start.13
  164.1 3.8 collective-permute-done.13
  168.0 2.7 collective-permute-start.14
  170.7 4.9 %collective-permute-done.14 = f32[32,128]{1,0:T(8,128)S(1)} collective-permute-done((f32[32,128]{1,0:T(8,128)S(1)}, f32[32,128]{1,0:T(8,128)S(1)}, u32[]{:S(2)}, u32[]{:S(2)}) %collective-permute-start.14) | collective-permute-done | bytes 16416 | tf_op jit(solution)/shard_map/ppermute | solution.py:35
  175.6 0.3 collective-permute-start.15
  175.9 3.5 collective-permute-done.15
  179.4 16.5 %shard_map.78 = (f32[1536,1]{1,0:T(8,128)S(1)}, f32[32,128]{1,0:T(8,128)S(1)}, f32[32,128,256]{2,1,0:T(8,128)}) custom-call(s32[12,16]{1,0:T(8,128)S(1)} %copy-done.2, bf16[1536,256]{1,0:T(8,128)(2,1)S(1)} %fusion.1.xn_ref, bf16[32,128,256]{2,1,0:T(8,128)(2,1)S(1)} %bitcast.9, f32[32,128]{1,0:T(8,128)S(1)} %bitcast_divide_fusion.scale_ref, ...), custom_call_target="tpu_custom_call" | custom-call | flops 3221225472 | bytes 7864320 | tf_op jit(solution)/shard_map/pallas_call | solution.py:116
  195.9 0.0 reduce-scatter.2.cloned.1.call-update
  195.9 0.0 all-reduce.2.cloned.1.call-start
  196.0 3.2 collective-permute-start.16
  199.2 2.1 collective-permute-done.16
  201.3 1.2 collective-permute-start.17
  202.5 2.5 collective-permute-done.17
  205.0 0.3 collective-permute-start.18
  205.3 5.0 %collective-permute-done.18 = f32[32,128]{1,0:T(8,128)S(1)} collective-permute-done((f32[32,128]{1,0:T(8,128)S(1)}, f32[32,128]{1,0:T(8,128)S(1)}, u32[]{:S(2)}, u32[]{:S(2)}) %collective-permute-start.18) | collective-permute-done | bytes 16416 | tf_op jit(solution)/shard_map/ppermute | solution.py:35
  210.3 1.2 collective-permute-done.19
  211.5 0.4 collective-permute-start.20
  211.8 3.7 collective-permute-done.20
  215.5 0.6 collective-permute-start.21
  216.2 4.2 collective-permute-done.21
  220.4 2.2 collective-permute-start.22
  222.6 5.6 %collective-permute-done.22 = f32[32,128]{1,0:T(8,128)S(1)} collective-permute-done((f32[32,128]{1,0:T(8,128)S(1)}, f32[32,128]{1,0:T(8,128)S(1)}, u32[]{:S(2)}, u32[]{:S(2)}) %collective-permute-start.22) | collective-permute-done | bytes 16416 | tf_op jit(solution)/shard_map/ppermute | solution.py:35
  228.2 0.9 reduce
  229.1 64.9 %reduce-scatter.2.cloned.1.call-done = f32[256,256]{1,0:T(8,128)} async-done(((f32[4096,256]{1,0:T(8,128)}), f32[256,256]{1,0:T(8,128)}) %reduce-scatter.2.cloned.1.call-update) | async-done | bytes 262160 | tf_op jit(solution)/shard_map/reduce_scatter | solution.py:165
  293.9 0.0 all-reduce.2.cloned.1.call-update
  294.0 0.6 multiply_divide_fusion
  294.6 137.4 %all-reduce.2.cloned.1.call-done = f32[256,256]{1,0:T(8,128)} async-done(((f32[256,256]{1,0:T(8,128)}), f32[256,256]{1,0:T(8,128)}) %all-reduce.2.cloned.1.call-update) | async-done | bytes 262160 | tf_op jit(solution)/shard_map/psum | solution.py:166
  432.0 1.8 broadcast_divide_fusion
  (39 shorter events, 0.2 us)
Async XLA Ops:
  7.2 3.9 copy-start
  7.2 79.4 %all-gather.2.cloned.1.call-start = ((), (), s32[]{:S(2)}) async-start(), calls=%async_computation.1 | async-start | bytes 2228224 | tf_op jit(solution)/shard_map/all_gather | solution.py:148
  10.0 76.5 %copy-start.2 = (s32[12,16]{1,0:T(8,128)S(1)}, s32[12,16]{1,0:T(8,128)}, u32[]{:S(2)}) copy-start(s32[12,16]{1,0:T(8,128)} %links_ref.5) | copy-start | bytes 2308
  10.0 283.9 %reduce-scatter.2.cloned.1.call-start = ((), (), s32[]{:S(2)}) async-start(), calls=%async_computation.2 | async-start | bytes 4456448 | tf_op jit(solution)/shard_map/reduce_scatter | solution.py:165
  86.5 1.6 copy-start.1
  88.1 45.6 %copy-start.3 = (f32[4096]{0:T(1024)S(1)}, f32[4096]{0:T(1024)}, u32[]{:S(2)}) copy-start(f32[4096]{0:T(1024)} %param.9) | copy-start | bytes 49156
  98.5 5.2 %collective-permute-start = (f32[32,128]{1,0:T(8,128)S(1)}, f32[32,128]{1,0:T(8,128)S(1)}, u32[]{:S(2)}, u32[]{:S(2)}) collective-permute-start(f32[32,128]{1,0:T(8,128)S(1)} %get-tuple-element.8), channel_id=1, source_target_pairs={{0,128},{128,0},{1,129},{129,1},{2,130},{130,2},{3,131},{131,3},{4... | collective-permute-start | bytes 49160 | tf_op jit(solution)/shard_map/ppermute | solution.py:35
  103.8 3.7 collective-permute-start.1
  107.5 5.2 %collective-permute-start.2 = (f32[32,128]{1,0:T(8,128)S(1)}, f32[32,128]{1,0:T(8,128)S(1)}, u32[]{:S(2)}, u32[]{:S(2)}) collective-permute-start(f32[32,128]{1,0:T(8,128)S(1)} %add.110), channel_id=1, source_target_pairs={{0,64},{32,96},{64,0},{96,32},{1,65},{33,97},{65,1},{97,33},{2,66}... | collective-permute-start | bytes 49160 | tf_op jit(solution)/shard_map/ppermute | solution.py:35
  112.8 1.2 collective-permute-start.3
  114.0 3.7 collective-permute-start.4
  117.7 4.6 %collective-permute-start.5 = (f32[32,128]{1,0:T(8,128)S(1)}, f32[32,128]{1,0:T(8,128)S(1)}, u32[]{:S(2)}, u32[]{:S(2)}) collective-permute-start(f32[32,128]{1,0:T(8,128)S(1)} %add.113), channel_id=1, source_target_pairs={{0,4},{2,6},{4,0},{6,2},{8,12},{10,14},{12,8},{14,10},{1,5},{3,7},... | collective-permute-start | bytes 49160 | tf_op jit(solution)/shard_map/ppermute | solution.py:35
  122.4 7.6 %collective-permute-start.6 = (f32[32,128]{1,0:T(8,128)S(1)}, f32[32,128]{1,0:T(8,128)S(1)}, u32[]{:S(2)}, u32[]{:S(2)}) collective-permute-start(f32[32,128]{1,0:T(8,128)S(1)} %add.114), channel_id=1, source_target_pairs={{0,8},{2,10},{4,12},{6,14},{8,0},{10,2},{12,4},{14,6},{1,9},{3,11}... | collective-permute-start | bytes 49160 | tf_op jit(solution)/shard_map/ppermute | solution.py:35
  130.0 3.7 collective-permute-start.7
  144.2 5.2 %collective-permute-start.8 = (f32[32,128]{1,0:T(8,128)S(1)}, f32[32,128]{1,0:T(8,128)S(1)}, u32[]{:S(2)}, u32[]{:S(2)}) collective-permute-start(f32[32,128]{1,0:T(8,128)S(1)} %get-tuple-element.9), channel_id=1, source_target_pairs={{0,128},{128,0},{1,129},{129,1},{2,130},{130,2},{3,131},{131,3},{4... | collective-permute-start | bytes 49160 | tf_op jit(solution)/shard_map/ppermute | solution.py:35
  149.4 3.7 collective-permute-start.9
  153.2 5.2 %collective-permute-start.10 = (f32[32,128]{1,0:T(8,128)S(1)}, f32[32,128]{1,0:T(8,128)S(1)}, u32[]{:S(2)}, u32[]{:S(2)}) collective-permute-start(f32[32,128]{1,0:T(8,128)S(1)} %add.118), channel_id=1, source_target_pairs={{0,64},{32,96},{64,0},{96,32},{1,65},{33,97},{65,1},{97,33},{2,66}... | collective-permute-start | bytes 49160 | tf_op jit(solution)/shard_map/ppermute | solution.py:35
  158.4 1.2 collective-permute-start.11
  159.6 3.7 collective-permute-start.12
  163.4 4.6 %collective-permute-start.13 = (f32[32,128]{1,0:T(8,128)S(1)}, f32[32,128]{1,0:T(8,128)S(1)}, u32[]{:S(2)}, u32[]{:S(2)}) collective-permute-start(f32[32,128]{1,0:T(8,128)S(1)} %add.121), channel_id=1, source_target_pairs={{0,4},{2,6},{4,0},{6,2},{8,12},{10,14},{12,8},{14,10},{1,5},{3,7},... | collective-permute-start | bytes 49160 | tf_op jit(solution)/shard_map/ppermute | solution.py:35
  168.0 7.6 %collective-permute-start.14 = (f32[32,128]{1,0:T(8,128)S(1)}, f32[32,128]{1,0:T(8,128)S(1)}, u32[]{:S(2)}, u32[]{:S(2)}) collective-permute-start(f32[32,128]{1,0:T(8,128)S(1)} %add.122), channel_id=1, source_target_pairs={{0,8},{2,10},{4,12},{6,14},{8,0},{10,2},{12,4},{14,6},{1,9},{3,11}... | collective-permute-start | bytes 49160 | tf_op jit(solution)/shard_map/ppermute | solution.py:35
  175.6 3.7 collective-permute-start.15
  195.9 236.1 %all-reduce.2.cloned.1.call-start = ((), (), s32[]{:S(2)}) async-start(), calls=%async_computation.3 | async-start | bytes 524288 | tf_op jit(solution)/shard_map/psum | solution.py:166
  196.0 5.3 %collective-permute-start.16 = (f32[32,128]{1,0:T(8,128)S(1)}, f32[32,128]{1,0:T(8,128)S(1)}, u32[]{:S(2)}, u32[]{:S(2)}) collective-permute-start(f32[32,128]{1,0:T(8,128)S(1)} %get-tuple-element.11), channel_id=1, source_target_pairs={{0,128},{128,0},{1,129},{129,1},{2,130},{130,2},{3,131},{131,3},{4... | collective-permute-start | bytes 49160 | tf_op jit(solution)/shard_map/ppermute | solution.py:35
  201.3 3.7 collective-permute-start.17
  205.0 5.2 %collective-permute-start.18 = (f32[32,128]{1,0:T(8,128)S(1)}, f32[32,128]{1,0:T(8,128)S(1)}, u32[]{:S(2)}, u32[]{:S(2)}) collective-permute-start(f32[32,128]{1,0:T(8,128)S(1)} %add.128), channel_id=1, source_target_pairs={{0,64},{32,96},{64,0},{96,32},{1,65},{33,97},{65,1},{97,33},{2,66}... | collective-permute-start | bytes 49160 | tf_op jit(solution)/shard_map/ppermute | solution.py:35
  210.3 1.2 collective-permute-start.19
  211.5 4.1 collective-permute-start.20
  215.5 4.8 %collective-permute-start.21 = (f32[32,128]{1,0:T(8,128)S(1)}, f32[32,128]{1,0:T(8,128)S(1)}, u32[]{:S(2)}, u32[]{:S(2)}) collective-permute-start(f32[32,128]{1,0:T(8,128)S(1)} %add.131), channel_id=1, source_target_pairs={{0,4},{2,6},{4,0},{6,2},{8,12},{10,14},{12,8},{14,10},{1,5},{3,7},... | collective-permute-start | bytes 49160 | tf_op jit(solution)/shard_map/ppermute | solution.py:35
  220.4 7.8 %collective-permute-start.22 = (f32[32,128]{1,0:T(8,128)S(1)}, f32[32,128]{1,0:T(8,128)S(1)}, u32[]{:S(2)}, u32[]{:S(2)}) collective-permute-start(f32[32,128]{1,0:T(8,128)S(1)} %add.132), channel_id=1, source_target_pairs={{0,8},{2,10},{4,12},{6,14},{8,0},{10,2},{12,4},{14,6},{1,9},{3,11}... | collective-permute-start | bytes 49160 | tf_op jit(solution)/shard_map/ppermute | solution.py:35
  228.2 65.8 %collective-permute-start.23 = (f32[32,128]{1,0:T(8,128)S(1)}, f32[32,128]{1,0:T(8,128)S(1)}, u32[]{:S(2)}, u32[]{:S(2)}) collective-permute-start(f32[32,128]{1,0:T(8,128)S(1)} %add.133), channel_id=1, source_target_pairs={{0,1},{1,0},{2,3},{3,2},{4,5},{5,4},{6,7},{7,6},{8,9},{9,8},{10,11... | collective-permute-start | bytes 49160 | tf_op jit(solution)/shard_map/ppermute | solution.py:35
Sparse Core Ops, SparseCore 0:
  10.4 76.1 all-gather.1
  196.0 97.8 reduce-scatter.1
  296.5 135.4 all-reduce.1

commit v2 on v1

--- a/solution.py
+++ b/solution.py
@@ -18,6 +18,7 @@
 ROW_AXES = ("yh", "x", "c")
 COL_AXES = ("z", "yl")
 ALL_AXES = ROW_AXES + COL_AXES
+TOTAL_GROUPS = (("yh", "c", "yl"), ("x",), ("z",))
 
 
 def normalize(matrix):
@@ -27,13 +28,30 @@
     )
 
 
-def butterfly_sum(x, sizes):
-    for axis in ALL_AXES:
+def butterfly_sum(x, axes, sizes):
+    for axis in axes:
         n = sizes[axis]
         k = 1
         while k < n:
             x = x + lax.ppermute(x, axis, [(j, j ^ k) for j in range(n)])
             k *= 2
+    return x
+
+
+def group_sum(x, groups, sizes):
+    for group in groups:
+        n = 1
+        for axis in group:
+            n *= sizes[axis]
+        me = lax.axis_index(group)
+        held = [x] + [
+            lax.ppermute(x, group, [(j, (j + k) % n) for j in range(n)]) for k in range(1, n)
+        ]
+        stacked = jnp.stack(held)
+        ordered = jnp.take(stacked, (me - jnp.arange(n)) % n, axis=0)
+        x = ordered[0]
+        for i in range(1, n):
+            x = x + ordered[i]
     return x
 
 
@@ -145,7 +163,9 @@
     mass_ratio = local_rows * row_devices / local_cands
     col_index = lax.axis_index("z") * sizes["yl"] + lax.axis_index("yl")
     own_start = col_index * local_cands
-    gathered = lax.all_gather(normalize(cand_rows), COL_AXES, axis=0, tiled=True)
+    gathered = lax.all_gather(
+        lax.all_gather(normalize(cand_rows), "yl", axis=0, tiled=True), "z", axis=0, tiled=True
+    )
     cn_blocks = gathered.reshape(block_count, BLOCK, feature_count)
     xn = normalize(data_rows)
     mass_col = data_mass.reshape(local_rows, 1)
@@ -153,17 +173,17 @@
     scale_blocks = jnp.ones((block_count, BLOCK), jnp.float32)
     for sweep_index in range(ITERS - 1):
         _, part_total = sweep(xn, cn_blocks, scale_blocks, mass_col, links)
-        whole_total = butterfly_sum(part_total, sizes)
+        whole_total = group_sum(part_total, TOTAL_GROUPS, sizes)
         scale_blocks = mass_ratio * cand_mass.reshape(block_count, BLOCK) / whole_total
     ds_col, part_total, partial_sums = sweep(
         xn, cn_blocks, scale_blocks, mass_col, links, rows=data_rows
     )
-    whole_total = butterfly_sum(part_total, sizes).reshape(-1)
+    whole_total = group_sum(part_total, TOTAL_GROUPS, sizes).reshape(-1)
     own_total = lax.dynamic_slice_in_dim(whole_total, own_start, local_cands)
     own_scale = mass_ratio * lax.dynamic_slice_in_dim(cand_mass, own_start, local_cands) / own_total
     flat_sums = partial_sums.reshape(cand_total, feature_count)
     share_rows = lax.psum_scatter(flat_sums, COL_AXES, scatter_dimension=0, tiled=True)
-    own_sums = lax.psum(share_rows, ROW_AXES)
+    own_sums = butterfly_sum(share_rows, ("c", "x", "yh"), sizes)
     new_support = own_sums / own_total[:, None]
     return (ds_col.reshape(local_rows), own_scale, new_support)
 

time: 448 us -> 349 us (0.78)
  waiting for transfers between devices: 355 us -> 192 us
  starting transfers between devices: 25.1 us -> 76.4 us
  local copies, waits for them, and re-layouts: 2.56 us -> 10.8 us
  blocking collectives: 0 us -> 6.02 us
    psum x1 -> x0, waiting for transfers between devices: 137 us -> none  [on_device(): own_sums = lax.psum(share_rows, ROW_AXES)]
    ppermute x0 -> x51, waiting for transfers between devices: none -> 82.8 us  [group_sum(): lax.ppermute(x, group, [(j, (j + k) % n) for j in range(n)])]
    ppermute x0 -> x51, starting transfers between devices: none -> 72.3 us  [group_sum(): lax.ppermute(x, group, [(j, (j + k) % n) for j in range(n)])]
    ppermute x24 -> x4, waiting for transfers between devices: 77.5 us -> 22.1 us  [butterfly_sum(): x = x + lax.ppermute(x, axis, [(j, j ^ k) for j in range(n)])]
    all_gather x1, waiting for transfers between devices: 74.9 us -> 42.4 us  [on_device(): lax.all_gather(lax.all_gather(normalize(cand_rows), 'yl', axis=0, tiled=T...]
    ppermute x24 -> x4, starting transfers between devices: 25 us -> 4.03 us  [butterfly_sum(): x = x + lax.ppermute(x, axis, [(j, j ^ k) for j in range(n)])]
    reduce_scatter x1, waiting for transfers between devices: 64.9 us -> 44.8 us  [on_device(): lax.psum_scatter(flat_sums, COL_AXES, scatter_dimension=0, tiled=True)]
    all_gather x0 -> x1, blocking collectives: none -> 6.02 us  [on_device(): lax.all_gather(normalize(cand_rows), 'yl', axis=0, tiled=True)]
  transfers between devices with their start and end apart: 27 -> 57, of which waited for: 26 -> 28; matrix products, arithmetic and copies ran while one was open for 1% -> 2% of each run, Pallas kernels for 0% -> 0%
where the time goes in v2:
time: 349 us; the launch traced here: 345 us
  waiting for transfers between devices  192 us (55%)
  starting transfers between devices  76.4 us (22%)
  Pallas kernels  37.3 us (11%)
  between operations  14.9 us (4%)
  local copies, waits for them, and re-layouts  10.8 us (3%)
  other arithmetic  7.01 us (2%)
  blocking collectives  6.02 us (2%)
    ppermute x51, waiting for transfers between devices, group_sum(): lax.ppermute(x, group, [(j, (j + k) % n) for j in range(n)])  82.8 us
    ppermute x51, starting transfers between devices, group_sum(): lax.ppermute(x, group, [(j, (j + k) % n) for j in range(n)])  72.3 us
    reduce_scatter x1, waiting for transfers between devices, on_device(): lax.psum_scatter(flat_sums, COL_AXES, scatter_dimension=0, tiled=True)  44.8 us
    all_gather x1, waiting for transfers between devices, on_device(): lax.all_gather(lax.all_gather(normalize(cand_rows), 'yl', axis=0, tiled=T...  42.4 us
    pallas_call x3, Pallas kernels, sweep(): pl.pallas_call(functools.partial(sweep_body, nbr, inv_width, inv_count, b...  37.3 us
    ppermute x4, waiting for transfers between devices, butterfly_sum(): x = x + lax.ppermute(x, axis, [(j, j ^ k) for j in range(n)])  22.1 us
  transfers between devices with their start and end apart: 57, of which 28 were waited for; matrix products, arithmetic and copies ran while one was open for 2% of the time, Pallas kernels for 0%

profile of v2, /device:TPU:4, one launch (start us, length us, event | category | flops | bytes accessed | tf_op | source)
XLA Modules:
  0.0 344.7 jit_solution(17068322200852350486)
XLA Ops:
  7.2 1.1 fusion.2
  8.3 1.0 fusion.3
  9.3 6.0 %all_gather.6 = bf16[512,256]{1,0:T(8,128)(2,1)} all-gather(bf16[256,256]{1,0:T(8,128)(2,1)S(1)} %fusion.3), channel_id=1, replica_groups=mesh['yh'=2,'x'=4,'c'=2,'z'=8,'yl'=2] {'yl'}, dimensions={0}, use_global_device_ids=true | all-gather | bytes 393216 | tf_op jit(solution)/shard_map/all_gather | solution.py:167
  15.4 1.0 reshape.212.mass_ref
  17.1 42.4 %all-gather.2.cloned.1.call-done = bf16[4096,256]{1,0:T(8,128)(2,1)} async-done(((bf16[512,256]{1,0:T(8,128)(2,1)}), bf16[4096,256]{1,0:T(8,128)(2,1)}) %all-gather.2.cloned.1.call-update) | async-done | bytes 2097168 | tf_op jit(solution)/shard_map/all_gather | solution.py:166
  59.6 1.6 copy-done.1
  61.2 10.4 %shard_map.76 = (f32[1536,1]{1,0:T(8,128)}, f32[32,128]{1,0:T(8,128)S(1)}) custom-call(s32[12,16]{1,0:T(8,128)S(1)} %copy-done.4, bf16[1536,256]{1,0:T(8,128)(2,1)S(1)} %fusion.1.xn_ref, bf16[32,128,256]{2,1,0:T(8,128)(2,1)S(1)} %bitcast.123, f32[32,128]{1,0:T(8,128)S(1)} %broadcast_in_dim.24.scale_ref, f32[1536,1]{1,0:T(8,128)S(1)} %reshape.212.mass_ref), custom_call_target="tpu_custom_call" | custom-call | flops 1610612736 | bytes 2883584 | tf_op jit(solution)/shard_map/pallas_call | solution.py:134
  71.5 3.9 %collective-permute-start.5 = (f32[32,128]{1,0:T(8,128)S(1)}, f32[32,128]{1,0:T(8,128)S(1)}, u32[]{:S(2)}, u32[]{:S(2)}) collective-permute-start(f32[32,128]{1,0:T(8,128)S(1)} %get-tuple-element.10), channel_id=1, source_target_pairs={{0,144},{1,145},{16,0},{17,1},{128,16},{129,17},{144,128},{145,129... | collective-permute-start | bytes 49160 | tf_op jit(solution)/shard_map/ppermute | solution.py:48
  76.9 4.2 %collective-permute-done = f32[32,128]{1,0:T(8,128)S(1)} collective-permute-done((f32[32,128]{1,0:T(8,128)S(1)}, f32[32,128]{1,0:T(8,128)S(1)}, u32[]{:S(2)}, u32[]{:S(2)}) %collective-permute-start) | collective-permute-done | bytes 16416 | tf_op jit(solution)/shard_map/ppermute | solution.py:48
  81.0 4.7 %collective-permute-done.1 = f32[32,128]{1,0:T(8,128)S(1)} collective-permute-done((f32[32,128]{1,0:T(8,128)S(1)}, f32[32,128]{1,0:T(8,128)S(1)}, u32[]{:S(2)}, u32[]{:S(2)}) %collective-permute-start.1) | collective-permute-done | bytes 16416 | tf_op jit(solution)/shard_map/ppermute | solution.py:48
  85.7 4.9 %collective-permute-done.2 = f32[32,128]{1,0:T(8,128)S(1)} collective-permute-done((f32[32,128]{1,0:T(8,128)S(1)}, f32[32,128]{1,0:T(8,128)S(1)}, u32[]{:S(2)}, u32[]{:S(2)}) %collective-permute-start.2) | collective-permute-done | bytes 16416 | tf_op jit(solution)/shard_map/ppermute | solution.py:48
  92.0 2.7 collective-permute-start.8
  95.2 2.1 collective-permute-done.8
  97.3 1.2 collective-permute-done.7
  99.1 1.3 collective-permute-start.10
  100.4 2.1 collective-permute-start.16
  102.5 1.1 collective-permute-start.15
  103.6 3.3 collective-permute-start.14
  106.9 2.5 collective-permute-start.13
  110.2 5.1 %collective-permute-done.11 = f32[32,128]{1,0:T(8,128)S(1)} collective-permute-done((f32[32,128]{1,0:T(8,128)S(1)}, f32[32,128]{1,0:T(8,128)S(1)}, u32[]{:S(2)}, u32[]{:S(2)}) %collective-permute-start.11) | collective-permute-done | bytes 16416 | tf_op jit(solution)/shard_map/ppermute | solution.py:48
  115.3 6.7 %collective-permute-done.12 = f32[32,128]{1,0:T(8,128)S(1)} collective-permute-done((f32[32,128]{1,0:T(8,128)S(1)}, f32[32,128]{1,0:T(8,128)S(1)}, u32[]{:S(2)}, u32[]{:S(2)}) %collective-permute-start.12) | collective-permute-done | bytes 16416 | tf_op jit(solution)/shard_map/ppermute | solution.py:48
  122.8 1.6 copy-done.2
  124.4 10.4 %shard_map.77 = (f32[1536,1]{1,0:T(8,128)}, f32[32,128]{1,0:T(8,128)S(1)}) custom-call(s32[12,16]{1,0:T(8,128)S(1)} %copy-done.4, bf16[1536,256]{1,0:T(8,128)(2,1)S(1)} %fusion.1.xn_ref, bf16[32,128,256]{2,1,0:T(8,128)(2,1)S(1)} %bitcast.124, f32[32,128]{1,0:T(8,128)S(1)} %fusion.8.scale_ref, f32[1536,1]{1,0:T(8,128)S(1)} %reshape.212.mass_ref), custom_call_target="tpu_custom_call" | custom-call | flops 1610612736 | bytes 2883584 | tf_op jit(solution)/shard_map/pallas_call | solution.py:134
  134.8 1.6 collective-permute-start.22
  136.3 2.5 collective-permute-start.20
  139.0 4.3 %collective-permute-done.17 = f32[32,128]{1,0:T(8,128)S(1)} collective-permute-done((f32[32,128]{1,0:T(8,128)S(1)}, f32[32,128]{1,0:T(8,128)S(1)}, u32[]{:S(2)}, u32[]{:S(2)}) %collective-permute-start.17) | collective-permute-done | bytes 16416 | tf_op jit(solution)/shard_map/ppermute | solution.py:48
  143.2 4.7 %collective-permute-done.18 = f32[32,128]{1,0:T(8,128)S(1)} collective-permute-done((f32[32,128]{1,0:T(8,128)S(1)}, f32[32,128]{1,0:T(8,128)S(1)}, u32[]{:S(2)}, u32[]{:S(2)}) %collective-permute-start.18) | collective-permute-done | bytes 16416 | tf_op jit(solution)/shard_map/ppermute | solution.py:48
  147.9 4.9 %collective-permute-done.19 = f32[32,128]{1,0:T(8,128)S(1)} collective-permute-done((f32[32,128]{1,0:T(8,128)S(1)}, f32[32,128]{1,0:T(8,128)S(1)}, u32[]{:S(2)}, u32[]{:S(2)}) %collective-permute-start.19) | collective-permute-done | bytes 16416 | tf_op jit(solution)/shard_map/ppermute | solution.py:48
  153.9 2.1 collective-permute-start.25
  156.0 2.3 collective-permute-start.24
  160.5 10.2 %collective-permute-start.27 = (f32[32,128]{1,0:T(8,128)S(1)}, f32[32,128]{1,0:T(8,128)S(1)}, u32[]{:S(2)}, u32[]{:S(2)}) collective-permute-start(f32[32,128]{1,0:T(8,128)S(1)} %bitcast.141), channel_id=1, source_target_pairs={{0,2},{2,4},{4,6},{6,8},{8,10},{10,12},{12,14},{14,0},{1,3},{3,5},... | collective-permute-start | bytes 49160 | tf_op jit(solution)/shard_map/ppermute | solution.py:48
  170.6 2.0 collective-permute-start.33
  172.8 3.2 collective-permute-start.31
  176.0 2.5 collective-permute-start.30
  178.5 1.5 collective-permute-start.28
  180.0 4.3 %collective-permute-done.28 = f32[32,128]{1,0:T(8,128)S(1)} collective-permute-done((f32[32,128]{1,0:T(8,128)S(1)}, f32[32,128]{1,0:T(8,128)S(1)}, u32[]{:S(2)}, u32[]{:S(2)}) %collective-permute-start.28) | collective-permute-done | bytes 16416 | tf_op jit(solution)/shard_map/ppermute | solution.py:48
  184.4 1.0 collective-permute-start.29
  185.4 5.7 %collective-permute-done.29 = f32[32,128]{1,0:T(8,128)S(1)} collective-permute-done((f32[32,128]{1,0:T(8,128)S(1)}, f32[32,128]{1,0:T(8,128)S(1)}, u32[]{:S(2)}, u32[]{:S(2)}) %collective-permute-start.29) | collective-permute-done | bytes 16416 | tf_op jit(solution)/shard_map/ppermute | solution.py:48
  191.9 1.6 copy-done.3
  193.5 16.6 %shard_map.78 = (f32[1536,1]{1,0:T(8,128)S(1)}, f32[32,128]{1,0:T(8,128)S(1)}, f32[32,128,256]{2,1,0:T(8,128)}) custom-call(s32[12,16]{1,0:T(8,128)S(1)} %copy-done.4, bf16[1536,256]{1,0:T(8,128)(2,1)S(1)} %fusion.1.xn_ref, bf16[32,128,256]{2,1,0:T(8,128)(2,1)S(1)} %bitcast.125, f32[32,128]{1,0:T(8,128)S(1)} %fusion.6.scale_ref, ...), custom_call_target="tpu_custom_call" | custom-call | flops 3221225472 | bytes 7864320 | tf_op jit(solution)/shard_map/pallas_call | solution.py:134
  211.1 3.2 collective-permute-start.37
  214.4 4.2 %collective-permute-done.34 = f32[32,128]{1,0:T(8,128)S(1)} collective-permute-done((f32[32,128]{1,0:T(8,128)S(1)}, f32[32,128]{1,0:T(8,128)S(1)}, u32[]{:S(2)}, u32[]{:S(2)}) %collective-permute-start.34) | collective-permute-done | bytes 16416 | tf_op jit(solution)/shard_map/ppermute | solution.py:48
  218.6 4.8 %collective-permute-done.35 = f32[32,128]{1,0:T(8,128)S(1)} collective-permute-done((f32[32,128]{1,0:T(8,128)S(1)}, f32[32,128]{1,0:T(8,128)S(1)}, u32[]{:S(2)}, u32[]{:S(2)}) %collective-permute-start.35) | collective-permute-done | bytes 16416 | tf_op jit(solution)/shard_map/ppermute | solution.py:48
  223.5 4.9 %collective-permute-done.36 = f32[32,128]{1,0:T(8,128)S(1)} collective-permute-done((f32[32,128]{1,0:T(8,128)S(1)}, f32[32,128]{1,0:T(8,128)S(1)}, u32[]{:S(2)}, u32[]{:S(2)}) %collective-permute-start.36) | collective-permute-done | bytes 16416 | tf_op jit(solution)/shard_map/ppermute | solution.py:48
  229.2 4.6 %collective-permute-start.43 = (f32[32,128]{1,0:T(8,128)S(1)}, f32[32,128]{1,0:T(8,128)S(1)}, u32[]{:S(2)}, u32[]{:S(2)}) collective-permute-start(f32[32,128]{1,0:T(8,128)S(1)} %fusion.12), channel_id=1, source_target_pairs={{0,96},{32,0},{64,32},{96,64},{1,97},{33,1},{65,33},{97,65},{2,98}... | collective-permute-start | bytes 49160 | tf_op jit(solution)/shard_map/ppermute | solution.py:48
  233.7 2.7 collective-permute-start.42
  236.4 2.5 collective-permute-done.42
  239.0 1.2 collective-permute-done.41
  240.8 1.8 collective-permute-start.44
  243.4 1.6 collective-permute-start.50
  245.0 1.7 collective-permute-start.49
  246.7 1.4 collective-permute-start.48
  248.1 2.8 collective-permute-start.47
  250.9 1.9 collective-permute-start.45
  252.8 3.9 %collective-permute-done.45 = f32[32,128]{1,0:T(8,128)S(1)} collective-permute-done((f32[32,128]{1,0:T(8,128)S(1)}, f32[32,128]{1,0:T(8,128)S(1)}, u32[]{:S(2)}, u32[]{:S(2)}) %collective-permute-start.45) | collective-permute-done | bytes 16416 | tf_op jit(solution)/shard_map/ppermute | solution.py:48
  257.1 6.4 %collective-permute-done.46 = f32[32,128]{1,0:T(8,128)S(1)} collective-permute-done((f32[32,128]{1,0:T(8,128)S(1)}, f32[32,128]{1,0:T(8,128)S(1)}, u32[]{:S(2)}, u32[]{:S(2)}) %collective-permute-start.46) | collective-permute-done | bytes 16416 | tf_op jit(solution)/shard_map/ppermute | solution.py:48
  263.5 44.8 %reduce-scatter.2.cloned.1.call-done = f32[256,256]{1,0:T(8,128)} async-done(((f32[4096,256]{1,0:T(8,128)}), f32[256,256]{1,0:T(8,128)}) %reduce-scatter.2.cloned.1.call-update) | async-done | bytes 262160 | tf_op jit(solution)/shard_map/reduce_scatter | solution.py:185
  308.3 1.7 collective-permute-done.51
  310.0 1.0 add.426
  311.0 1.3 collective-permute-start.52
  312.3 7.1 %collective-permute-done.52 = f32[256,256]{1,0:T(8,128)S(1)} collective-permute-done((f32[256,256]{1,0:T(8,128)S(1)}, f32[256,256]{1,0:T(8,128)S(1)}, u32[]{:S(2)}, u32[]{:S(2)}) %collective-permute-start.52) | collective-permute-done | bytes 262176 | tf_op jit(solution)/shard_map/ppermute | solution.py:36
  320.8 7.8 %collective-permute-done.53 = f32[256,256]{1,0:T(8,128)S(1)} collective-permute-done((f32[256,256]{1,0:T(8,128)S(1)}, f32[256,256]{1,0:T(8,128)S(1)}, u32[]{:S(2)}, u32[]{:S(2)}) %collective-permute-start.53) | collective-permute-done | bytes 262176 | tf_op jit(solution)/shard_map/ppermute | solution.py:36
  328.6 2.1 collective-permute-start.54
  331.4 5.4 %collective-permute-done.54 = f32[256,256]{1,0:T(8,128)S(1)} collective-permute-done((f32[256,256]{1,0:T(8,128)S(1)}, f32[256,256]{1,0:T(8,128)S(1)}, u32[]{:S(2)}, u32[]{:S(2)}) %collective-permute-start.54) | collective-permute-done | bytes 262176 | tf_op jit(solution)/shard_map/ppermute | solution.py:36
  (169 shorter events, 16.7 us)
Async XLA Ops:
  7.2 9.4 %copy-start = (bf16[1536,256]{1,0:T(8,128)(2,1)S(1)}, bf16[1536,256]{1,0:T(8,128)(2,1)}, u32[]{:S(2)}) copy-start(bf16[1536,256]{1,0:T(8,128)(2,1)} %rest_0_.1) | copy-start | bytes 2359300
  7.2 52.4 %all-gather.2.cloned.1.call-start = ((), (), s32[]{:S(2)}) async-start(), calls=%async_computation.1 | async-start | bytes 2359296 | tf_op jit(solution)/shard_map/all_gather | solution.py:166
  15.4 292.9 %reduce-scatter.2.cloned.1.call-start = ((), (), s32[]{:S(2)}) async-start(), calls=%async_computation.2 | async-start | bytes 4456448 | tf_op jit(solution)/shard_map/reduce_scatter | solution.py:185
  15.4 44.1 %copy-start.4 = (s32[12,16]{1,0:T(8,128)S(1)}, s32[12,16]{1,0:T(8,128)}, u32[]{:S(2)}) copy-start(s32[12,16]{1,0:T(8,128)} %links_ref.5) | copy-start | bytes 2308
  59.6 1.6 copy-start.1
  71.5 51.2 %copy-start.5 = (f32[4096]{0:T(1024)S(1)}, f32[4096]{0:T(1024)}, u32[]{:S(2)}) copy-start(f32[4096]{0:T(1024)} %param.13) | copy-start | bytes 49156
  71.5 19.2 %collective-permute-start.6 = (f32[32,128]{1,0:T(8,128)S(1)}, f32[32,128]{1,0:T(8,128)S(1)}, u32[]{:S(2)}, u32[]{:S(2)}) collective-permute-start(f32[32,128]{1,0:T(8,128)S(1)} %get-tuple-element.10), channel_id=1, source_target_pairs={{0,145},{1,0},{16,1},{17,16},{128,17},{129,128},{144,129},{145,144... | collective-permute-start | bytes 49160 | tf_op jit(solution)/shard_map/ppermute | solution.py:48
  71.5 19.1 %collective-permute-start.5 = (f32[32,128]{1,0:T(8,128)S(1)}, f32[32,128]{1,0:T(8,128)S(1)}, u32[]{:S(2)}, u32[]{:S(2)}) collective-permute-start(f32[32,128]{1,0:T(8,128)S(1)} %get-tuple-element.10), channel_id=1, source_target_pairs={{0,144},{1,145},{16,0},{17,1},{128,16},{129,17},{144,128},{145,129... | collective-permute-start | bytes 49160 | tf_op jit(solution)/shard_map/ppermute | solution.py:48
  75.5 15.2 %collective-permute-start.4 = (f32[32,128]{1,0:T(8,128)S(1)}, f32[32,128]{1,0:T(8,128)S(1)}, u32[]{:S(2)}, u32[]{:S(2)}) collective-permute-start(f32[32,128]{1,0:T(8,128)S(1)} %get-tuple-element.10), channel_id=1, source_target_pairs={{0,129},{1,144},{16,145},{17,0},{128,1},{129,16},{144,17},{145,128... | collective-permute-start | bytes 49160 | tf_op jit(solution)/shard_map/ppermute | solution.py:48
  75.5 15.2 %collective-permute-start.3 = (f32[32,128]{1,0:T(8,128)S(1)}, f32[32,128]{1,0:T(8,128)S(1)}, u32[]{:S(2)}, u32[]{:S(2)}) collective-permute-start(f32[32,128]{1,0:T(8,128)S(1)} %get-tuple-element.10), channel_id=1, source_target_pairs={{0,128},{1,129},{16,144},{17,145},{128,0},{129,1},{144,16},{145,17... | collective-permute-start | bytes 49160 | tf_op jit(solution)/shard_map/ppermute | solution.py:48
  76.3 4.8 %collective-permute-start = (f32[32,128]{1,0:T(8,128)S(1)}, f32[32,128]{1,0:T(8,128)S(1)}, u32[]{:S(2)}, u32[]{:S(2)}) collective-permute-start(f32[32,128]{1,0:T(8,128)S(1)} %get-tuple-element.10), channel_id=1, source_target_pairs={{0,1},{1,16},{16,17},{17,128},{128,129},{129,144},{144,145},{145,0... | collective-permute-start | bytes 49160 | tf_op jit(solution)/shard_map/ppermute | solution.py:48
  81.0 4.7 %collective-permute-start.1 = (f32[32,128]{1,0:T(8,128)S(1)}, f32[32,128]{1,0:T(8,128)S(1)}, u32[]{:S(2)}, u32[]{:S(2)}) collective-permute-start(f32[32,128]{1,0:T(8,128)S(1)} %get-tuple-element.10), channel_id=1, source_target_pairs={{0,16},{1,17},{16,128},{17,129},{128,144},{129,145},{144,0},{145,1... | collective-permute-start | bytes 49160 | tf_op jit(solution)/shard_map/ppermute | solution.py:48
  85.7 4.9 %collective-permute-start.2 = (f32[32,128]{1,0:T(8,128)S(1)}, f32[32,128]{1,0:T(8,128)S(1)}, u32[]{:S(2)}, u32[]{:S(2)}) collective-permute-start(f32[32,128]{1,0:T(8,128)S(1)} %get-tuple-element.10), channel_id=1, source_target_pairs={{0,17},{1,128},{16,129},{17,144},{128,145},{129,0},{144,1},{145,16... | collective-permute-start | bytes 49160 | tf_op jit(solution)/shard_map/ppermute | solution.py:48
  91.4 3.8 %collective-permute-start.9 = (f32[32,128]{1,0:T(8,128)S(1)}, f32[32,128]{1,0:T(8,128)S(1)}, u32[]{:S(2)}, u32[]{:S(2)}) collective-permute-start(f32[32,128]{1,0:T(8,128)S(1)} %fusion.14), channel_id=1, source_target_pairs={{0,96},{32,0},{64,32},{96,64},{1,97},{33,1},{65,33},{97,65},{2,98}... | collective-permute-start | bytes 49160 | tf_op jit(solution)/shard_map/ppermute | solution.py:48
  92.0 5.2 %collective-permute-start.8 = (f32[32,128]{1,0:T(8,128)S(1)}, f32[32,128]{1,0:T(8,128)S(1)}, u32[]{:S(2)}, u32[]{:S(2)}) collective-permute-start(f32[32,128]{1,0:T(8,128)S(1)} %fusion.14), channel_id=1, source_target_pairs={{0,64},{32,96},{64,0},{96,32},{1,65},{33,97},{65,1},{97,33},{2,66}... | collective-permute-start | bytes 49160 | tf_op jit(solution)/shard_map/ppermute | solution.py:48
  94.7 3.7 %collective-permute-start.7 = (f32[32,128]{1,0:T(8,128)S(1)}, f32[32,128]{1,0:T(8,128)S(1)}, u32[]{:S(2)}, u32[]{:S(2)}) collective-permute-start(f32[32,128]{1,0:T(8,128)S(1)} %fusion.14), channel_id=1, source_target_pairs={{0,32},{32,64},{64,96},{96,0},{1,33},{33,65},{65,97},{97,1},{2,34}... | collective-permute-start | bytes 49160 | tf_op jit(solution)/shard_map/ppermute | solution.py:48
  99.1 10.3 %collective-permute-start.10 = (f32[32,128]{1,0:T(8,128)S(1)}, f32[32,128]{1,0:T(8,128)S(1)}, u32[]{:S(2)}, u32[]{:S(2)}) collective-permute-start(f32[32,128]{1,0:T(8,128)S(1)} %bitcast.134), channel_id=1, source_target_pairs={{0,2},{2,4},{4,6},{6,8},{8,10},{10,12},{12,14},{14,0},{1,3},{3,5},... | collective-permute-start | bytes 49160 | tf_op jit(solution)/shard_map/ppermute | solution.py:48
  100.4 21.7 %collective-permute-start.16 = (f32[32,128]{1,0:T(8,128)S(1)}, f32[32,128]{1,0:T(8,128)S(1)}, u32[]{:S(2)}, u32[]{:S(2)}) collective-permute-start(f32[32,128]{1,0:T(8,128)S(1)} %bitcast.135), channel_id=1, source_target_pairs={{0,14},{2,0},{4,2},{6,4},{8,6},{10,8},{12,10},{14,12},{1,15},{3,1}... | collective-permute-start | bytes 49160 | tf_op jit(solution)/shard_map/ppermute | solution.py:48
  102.5 19.6 %collective-permute-start.15 = (f32[32,128]{1,0:T(8,128)S(1)}, f32[32,128]{1,0:T(8,128)S(1)}, u32[]{:S(2)}, u32[]{:S(2)}) collective-permute-start(f32[32,128]{1,0:T(8,128)S(1)} %bitcast.136), channel_id=1, source_target_pairs={{0,12},{2,14},{4,0},{6,2},{8,4},{10,6},{12,8},{14,10},{1,13},{3,15... | collective-permute-start | bytes 49160 | tf_op jit(solution)/shard_map/ppermute | solution.py:48
  103.6 18.5 %collective-permute-start.14 = (f32[32,128]{1,0:T(8,128)S(1)}, f32[32,128]{1,0:T(8,128)S(1)}, u32[]{:S(2)}, u32[]{:S(2)}) collective-permute-start(f32[32,128]{1,0:T(8,128)S(1)} %bitcast.137), channel_id=1, source_target_pairs={{0,10},{2,12},{4,14},{6,0},{8,2},{10,4},{12,6},{14,8},{1,11},{3,13... | collective-permute-start | bytes 49160 | tf_op jit(solution)/shard_map/ppermute | solution.py:48
  106.9 15.1 %collective-permute-start.13 = (f32[32,128]{1,0:T(8,128)S(1)}, f32[32,128]{1,0:T(8,128)S(1)}, u32[]{:S(2)}, u32[]{:S(2)}) collective-permute-start(f32[32,128]{1,0:T(8,128)S(1)} %bitcast.138), channel_id=1, source_target_pairs={{0,8},{2,10},{4,12},{6,14},{8,0},{10,2},{12,4},{14,6},{1,9},{3,11}... | collective-permute-start | bytes 49160 | tf_op jit(solution)/shard_map/ppermute | solution.py:48
  109.4 5.8 %collective-permute-start.11 = (f32[32,128]{1,0:T(8,128)S(1)}, f32[32,128]{1,0:T(8,128)S(1)}, u32[]{:S(2)}, u32[]{:S(2)}) collective-permute-start(f32[32,128]{1,0:T(8,128)S(1)} %bitcast.139), channel_id=1, source_target_pairs={{0,4},{2,6},{4,8},{6,10},{8,12},{10,14},{12,0},{14,2},{1,5},{3,7},... | collective-permute-start | bytes 49160 | tf_op jit(solution)/shard_map/ppermute | solution.py:48
  115.3 6.7 %collective-permute-start.12 = (f32[32,128]{1,0:T(8,128)S(1)}, f32[32,128]{1,0:T(8,128)S(1)}, u32[]{:S(2)}, u32[]{:S(2)}) collective-permute-start(f32[32,128]{1,0:T(8,128)S(1)} %bitcast.140), channel_id=1, source_target_pairs={{0,6},{2,8},{4,10},{6,12},{8,14},{10,0},{12,2},{14,4},{1,7},{3,9},... | collective-permute-start | bytes 49160 | tf_op jit(solution)/shard_map/ppermute | solution.py:48
  122.8 1.6 copy-start.2
  134.8 18.1 %collective-permute-start.23 = (f32[32,128]{1,0:T(8,128)S(1)}, f32[32,128]{1,0:T(8,128)S(1)}, u32[]{:S(2)}, u32[]{:S(2)}) collective-permute-start(f32[32,128]{1,0:T(8,128)S(1)} %get-tuple-element.11), channel_id=1, source_target_pairs={{0,145},{1,0},{16,1},{17,16},{128,17},{129,128},{144,129},{145,144... | collective-permute-start | bytes 49160 | tf_op jit(solution)/shard_map/ppermute | solution.py:48
  134.8 18.1 %collective-permute-start.22 = (f32[32,128]{1,0:T(8,128)S(1)}, f32[32,128]{1,0:T(8,128)S(1)}, u32[]{:S(2)}, u32[]{:S(2)}) collective-permute-start(f32[32,128]{1,0:T(8,128)S(1)} %get-tuple-element.11), channel_id=1, source_target_pairs={{0,144},{1,145},{16,0},{17,1},{128,16},{129,17},{144,128},{145,129... | collective-permute-start | bytes 49160 | tf_op jit(solution)/shard_map/ppermute | solution.py:48
  136.3 16.5 %collective-permute-start.21 = (f32[32,128]{1,0:T(8,128)S(1)}, f32[32,128]{1,0:T(8,128)S(1)}, u32[]{:S(2)}, u32[]{:S(2)}) collective-permute-start(f32[32,128]{1,0:T(8,128)S(1)} %get-tuple-element.11), channel_id=1, source_target_pairs={{0,129},{1,144},{16,145},{17,0},{128,1},{129,16},{144,17},{145,128... | collective-permute-start | bytes 49160 | tf_op jit(solution)/shard_map/ppermute | solution.py:48
  136.3 16.5 %collective-permute-start.20 = (f32[32,128]{1,0:T(8,128)S(1)}, f32[32,128]{1,0:T(8,128)S(1)}, u32[]{:S(2)}, u32[]{:S(2)}) collective-permute-start(f32[32,128]{1,0:T(8,128)S(1)} %get-tuple-element.11), channel_id=1, source_target_pairs={{0,128},{1,129},{16,144},{17,145},{128,0},{129,1},{144,16},{145,17... | collective-permute-start | bytes 49160 | tf_op jit(solution)/shard_map/ppermute | solution.py:48
  138.9 4.4 %collective-permute-start.17 = (f32[32,128]{1,0:T(8,128)S(1)}, f32[32,128]{1,0:T(8,128)S(1)}, u32[]{:S(2)}, u32[]{:S(2)}) collective-permute-start(f32[32,128]{1,0:T(8,128)S(1)} %get-tuple-element.11), channel_id=1, source_target_pairs={{0,1},{1,16},{16,17},{17,128},{128,129},{129,144},{144,145},{145,0... | collective-permute-start | bytes 49160 | tf_op jit(solution)/shard_map/ppermute | solution.py:48
  143.2 4.7 %collective-permute-start.18 = (f32[32,128]{1,0:T(8,128)S(1)}, f32[32,128]{1,0:T(8,128)S(1)}, u32[]{:S(2)}, u32[]{:S(2)}) collective-permute-start(f32[32,128]{1,0:T(8,128)S(1)} %get-tuple-element.11), channel_id=1, source_target_pairs={{0,16},{1,17},{16,128},{17,129},{128,144},{129,145},{144,0},{145,1... | collective-permute-start | bytes 49160 | tf_op jit(solution)/shard_map/ppermute | solution.py:48
  147.9 4.9 %collective-permute-start.19 = (f32[32,128]{1,0:T(8,128)S(1)}, f32[32,128]{1,0:T(8,128)S(1)}, u32[]{:S(2)}, u32[]{:S(2)}) collective-permute-start(f32[32,128]{1,0:T(8,128)S(1)} %get-tuple-element.11), channel_id=1, source_target_pairs={{0,17},{1,128},{16,129},{17,144},{128,145},{129,0},{144,1},{145,16... | collective-permute-start | bytes 49160 | tf_op jit(solution)/shard_map/ppermute | solution.py:48
  153.6 4.8 %collective-permute-start.26 = (f32[32,128]{1,0:T(8,128)S(1)}, f32[32,128]{1,0:T(8,128)S(1)}, u32[]{:S(2)}, u32[]{:S(2)}) collective-permute-start(f32[32,128]{1,0:T(8,128)S(1)} %fusion.13), channel_id=1, source_target_pairs={{0,96},{32,0},{64,32},{96,64},{1,97},{33,1},{65,33},{97,65},{2,98}... | collective-permute-start | bytes 49160 | tf_op jit(solution)/shard_map/ppermute | solution.py:48
  153.9 5.2 %collective-permute-start.25 = (f32[32,128]{1,0:T(8,128)S(1)}, f32[32,128]{1,0:T(8,128)S(1)}, u32[]{:S(2)}, u32[]{:S(2)}) collective-permute-start(f32[32,128]{1,0:T(8,128)S(1)} %fusion.13), channel_id=1, source_target_pairs={{0,64},{32,96},{64,0},{96,32},{1,65},{33,97},{65,1},{97,33},{2,66}... | collective-permute-start | bytes 49160 | tf_op jit(solution)/shard_map/ppermute | solution.py:48
  156.0 3.8 %collective-permute-start.24 = (f32[32,128]{1,0:T(8,128)S(1)}, f32[32,128]{1,0:T(8,128)S(1)}, u32[]{:S(2)}, u32[]{:S(2)}) collective-permute-start(f32[32,128]{1,0:T(8,128)S(1)} %fusion.13), channel_id=1, source_target_pairs={{0,32},{32,64},{64,96},{96,0},{1,33},{33,65},{65,97},{97,1},{2,34}... | collective-permute-start | bytes 49160 | tf_op jit(solution)/shard_map/ppermute | solution.py:48
  160.5 18.0 %collective-permute-start.27 = (f32[32,128]{1,0:T(8,128)S(1)}, f32[32,128]{1,0:T(8,128)S(1)}, u32[]{:S(2)}, u32[]{:S(2)}) collective-permute-start(f32[32,128]{1,0:T(8,128)S(1)} %bitcast.141), channel_id=1, source_target_pairs={{0,2},{2,4},{4,6},{6,8},{8,10},{10,12},{12,14},{14,0},{1,3},{3,5},... | collective-permute-start | bytes 49160 | tf_op jit(solution)/shard_map/ppermute | solution.py:48
  170.6 20.6 %collective-permute-start.33 = (f32[32,128]{1,0:T(8,128)S(1)}, f32[32,128]{1,0:T(8,128)S(1)}, u32[]{:S(2)}, u32[]{:S(2)}) collective-permute-start(f32[32,128]{1,0:T(8,128)S(1)} %bitcast.142), channel_id=1, source_target_pairs={{0,14},{2,0},{4,2},{6,4},{8,6},{10,8},{12,10},{14,12},{1,15},{3,1}... | collective-permute-start | bytes 49160 | tf_op jit(solution)/shard_map/ppermute | solution.py:48
  172.6 18.6 %collective-permute-start.32 = (f32[32,128]{1,0:T(8,128)S(1)}, f32[32,128]{1,0:T(8,128)S(1)}, u32[]{:S(2)}, u32[]{:S(2)}) collective-permute-start(f32[32,128]{1,0:T(8,128)S(1)} %bitcast.143), channel_id=1, source_target_pairs={{0,12},{2,14},{4,0},{6,2},{8,4},{10,6},{12,8},{14,10},{1,13},{3,15... | collective-permute-start | bytes 49160 | tf_op jit(solution)/shard_map/ppermute | solution.py:48
  172.8 18.4 %collective-permute-start.31 = (f32[32,128]{1,0:T(8,128)S(1)}, f32[32,128]{1,0:T(8,128)S(1)}, u32[]{:S(2)}, u32[]{:S(2)}) collective-permute-start(f32[32,128]{1,0:T(8,128)S(1)} %bitcast.144), channel_id=1, source_target_pairs={{0,10},{2,12},{4,14},{6,0},{8,2},{10,4},{12,6},{14,8},{1,11},{3,13... | collective-permute-start | bytes 49160 | tf_op jit(solution)/shard_map/ppermute | solution.py:48
  176.0 15.1 %collective-permute-start.30 = (f32[32,128]{1,0:T(8,128)S(1)}, f32[32,128]{1,0:T(8,128)S(1)}, u32[]{:S(2)}, u32[]{:S(2)}) collective-permute-start(f32[32,128]{1,0:T(8,128)S(1)} %bitcast.145), channel_id=1, source_target_pairs={{0,8},{2,10},{4,12},{6,14},{8,0},{10,2},{12,4},{14,6},{1,9},{3,11}... | collective-permute-start | bytes 49160 | tf_op jit(solution)/shard_map/ppermute | solution.py:48
  178.5 5.9 %collective-permute-start.28 = (f32[32,128]{1,0:T(8,128)S(1)}, f32[32,128]{1,0:T(8,128)S(1)}, u32[]{:S(2)}, u32[]{:S(2)}) collective-permute-start(f32[32,128]{1,0:T(8,128)S(1)} %bitcast.146), channel_id=1, source_target_pairs={{0,4},{2,6},{4,8},{6,10},{8,12},{10,14},{12,0},{14,2},{1,5},{3,7},... | collective-permute-start | bytes 49160 | tf_op jit(solution)/shard_map/ppermute | solution.py:48
  184.4 6.7 %collective-permute-start.29 = (f32[32,128]{1,0:T(8,128)S(1)}, f32[32,128]{1,0:T(8,128)S(1)}, u32[]{:S(2)}, u32[]{:S(2)}) collective-permute-start(f32[32,128]{1,0:T(8,128)S(1)} %bitcast.147), channel_id=1, source_target_pairs={{0,6},{2,8},{4,10},{6,12},{8,14},{10,0},{12,2},{14,4},{1,7},{3,9},... | collective-permute-start | bytes 49160 | tf_op jit(solution)/shard_map/ppermute | solution.py:48
  191.9 1.6 copy-start.3
  210.1 18.4 %collective-permute-start.40 = (f32[32,128]{1,0:T(8,128)S(1)}, f32[32,128]{1,0:T(8,128)S(1)}, u32[]{:S(2)}, u32[]{:S(2)}) collective-permute-start(f32[32,128]{1,0:T(8,128)S(1)} %get-tuple-element.13), channel_id=1, source_target_pairs={{0,145},{1,0},{16,1},{17,16},{128,17},{129,128},{144,129},{145,144... | collective-permute-start | bytes 49160 | tf_op jit(solution)/shard_map/ppermute | solution.py:48
  210.2 18.3 %collective-permute-start.39 = (f32[32,128]{1,0:T(8,128)S(1)}, f32[32,128]{1,0:T(8,128)S(1)}, u32[]{:S(2)}, u32[]{:S(2)}) collective-permute-start(f32[32,128]{1,0:T(8,128)S(1)} %get-tuple-element.13), channel_id=1, source_target_pairs={{0,144},{1,145},{16,0},{17,1},{128,16},{129,17},{144,128},{145,129... | collective-permute-start | bytes 49160 | tf_op jit(solution)/shard_map/ppermute | solution.py:48
  211.1 17.4 %collective-permute-start.38 = (f32[32,128]{1,0:T(8,128)S(1)}, f32[32,128]{1,0:T(8,128)S(1)}, u32[]{:S(2)}, u32[]{:S(2)}) collective-permute-start(f32[32,128]{1,0:T(8,128)S(1)} %get-tuple-element.13), channel_id=1, source_target_pairs={{0,129},{1,144},{16,145},{17,0},{128,1},{129,16},{144,17},{145,128... | collective-permute-start | bytes 49160 | tf_op jit(solution)/shard_map/ppermute | solution.py:48
  211.1 17.3 %collective-permute-start.37 = (f32[32,128]{1,0:T(8,128)S(1)}, f32[32,128]{1,0:T(8,128)S(1)}, u32[]{:S(2)}, u32[]{:S(2)}) collective-permute-start(f32[32,128]{1,0:T(8,128)S(1)} %get-tuple-element.13), channel_id=1, source_target_pairs={{0,128},{1,129},{16,144},{17,145},{128,0},{129,1},{144,16},{145,17... | collective-permute-start | bytes 49160 | tf_op jit(solution)/shard_map/ppermute | solution.py:48
  214.2 4.4 %collective-permute-start.34 = (f32[32,128]{1,0:T(8,128)S(1)}, f32[32,128]{1,0:T(8,128)S(1)}, u32[]{:S(2)}, u32[]{:S(2)}) collective-permute-start(f32[32,128]{1,0:T(8,128)S(1)} %get-tuple-element.13), channel_id=1, source_target_pairs={{0,1},{1,16},{16,17},{17,128},{128,129},{129,144},{144,145},{145,0... | collective-permute-start | bytes 49160 | tf_op jit(solution)/shard_map/ppermute | solution.py:48
  218.6 4.8 %collective-permute-start.35 = (f32[32,128]{1,0:T(8,128)S(1)}, f32[32,128]{1,0:T(8,128)S(1)}, u32[]{:S(2)}, u32[]{:S(2)}) collective-permute-start(f32[32,128]{1,0:T(8,128)S(1)} %get-tuple-element.13), channel_id=1, source_target_pairs={{0,16},{1,17},{16,128},{17,129},{128,144},{129,145},{144,0},{145,1... | collective-permute-start | bytes 49160 | tf_op jit(solution)/shard_map/ppermute | solution.py:48
  223.5 4.9 %collective-permute-start.36 = (f32[32,128]{1,0:T(8,128)S(1)}, f32[32,128]{1,0:T(8,128)S(1)}, u32[]{:S(2)}, u32[]{:S(2)}) collective-permute-start(f32[32,128]{1,0:T(8,128)S(1)} %get-tuple-element.13), channel_id=1, source_target_pairs={{0,17},{1,128},{16,129},{17,144},{128,145},{129,0},{144,1},{145,16... | collective-permute-start | bytes 49160 | tf_op jit(solution)/shard_map/ppermute | solution.py:48
  229.2 7.2 %collective-permute-start.43 = (f32[32,128]{1,0:T(8,128)S(1)}, f32[32,128]{1,0:T(8,128)S(1)}, u32[]{:S(2)}, u32[]{:S(2)}) collective-permute-start(f32[32,128]{1,0:T(8,128)S(1)} %fusion.12), channel_id=1, source_target_pairs={{0,96},{32,0},{64,32},{96,64},{1,97},{33,1},{65,33},{97,65},{2,98}... | collective-permute-start | bytes 49160 | tf_op jit(solution)/shard_map/ppermute | solution.py:48
  233.7 5.2 %collective-permute-start.42 = (f32[32,128]{1,0:T(8,128)S(1)}, f32[32,128]{1,0:T(8,128)S(1)}, u32[]{:S(2)}, u32[]{:S(2)}) collective-permute-start(f32[32,128]{1,0:T(8,128)S(1)} %fusion.12), channel_id=1, source_target_pairs={{0,64},{32,96},{64,0},{96,32},{1,65},{33,97},{65,1},{97,33},{2,66}... | collective-permute-start | bytes 49160 | tf_op jit(solution)/shard_map/ppermute | solution.py:48
  236.4 3.7 %collective-permute-start.41 = (f32[32,128]{1,0:T(8,128)S(1)}, f32[32,128]{1,0:T(8,128)S(1)}, u32[]{:S(2)}, u32[]{:S(2)}) collective-permute-start(f32[32,128]{1,0:T(8,128)S(1)} %fusion.12), channel_id=1, source_target_pairs={{0,32},{32,64},{64,96},{96,0},{1,33},{33,65},{65,97},{97,1},{2,34}... | collective-permute-start | bytes 49160 | tf_op jit(solution)/shard_map/ppermute | solution.py:48
  240.8 10.1 %collective-permute-start.44 = (f32[32,128]{1,0:T(8,128)S(1)}, f32[32,128]{1,0:T(8,128)S(1)}, u32[]{:S(2)}, u32[]{:S(2)}) collective-permute-start(f32[32,128]{1,0:T(8,128)S(1)} %bitcast.127), channel_id=1, source_target_pairs={{0,2},{2,4},{4,6},{6,8},{8,10},{10,12},{12,14},{14,0},{1,3},{3,5},... | collective-permute-start | bytes 49160 | tf_op jit(solution)/shard_map/ppermute | solution.py:48
  243.4 76.7 %collective-permute-start.50 = (f32[32,128]{1,0:T(8,128)S(1)}, f32[32,128]{1,0:T(8,128)S(1)}, u32[]{:S(2)}, u32[]{:S(2)}) collective-permute-start(f32[32,128]{1,0:T(8,128)S(1)} %bitcast.128), channel_id=1, source_target_pairs={{0,14},{2,0},{4,2},{6,4},{8,6},{10,8},{12,10},{14,12},{1,15},{3,1}... | collective-permute-start | bytes 49160 | tf_op jit(solution)/shard_map/ppermute | solution.py:48
  245.0 67.3 %collective-permute-start.49 = (f32[32,128]{1,0:T(8,128)S(1)}, f32[32,128]{1,0:T(8,128)S(1)}, u32[]{:S(2)}, u32[]{:S(2)}) collective-permute-start(f32[32,128]{1,0:T(8,128)S(1)} %bitcast.129), channel_id=1, source_target_pairs={{0,12},{2,14},{4,0},{6,2},{8,4},{10,6},{12,8},{14,10},{1,13},{3,15... | collective-permute-start | bytes 49160 | tf_op jit(solution)/shard_map/ppermute | solution.py:48
  246.7 65.6 %collective-permute-start.48 = (f32[32,128]{1,0:T(8,128)S(1)}, f32[32,128]{1,0:T(8,128)S(1)}, u32[]{:S(2)}, u32[]{:S(2)}) collective-permute-start(f32[32,128]{1,0:T(8,128)S(1)} %bitcast.130), channel_id=1, source_target_pairs={{0,10},{2,12},{4,14},{6,0},{8,2},{10,4},{12,6},{14,8},{1,11},{3,13... | collective-permute-start | bytes 49160 | tf_op jit(solution)/shard_map/ppermute | solution.py:48
  248.1 60.2 %collective-permute-start.47 = (f32[32,128]{1,0:T(8,128)S(1)}, f32[32,128]{1,0:T(8,128)S(1)}, u32[]{:S(2)}, u32[]{:S(2)}) collective-permute-start(f32[32,128]{1,0:T(8,128)S(1)} %bitcast.131), channel_id=1, source_target_pairs={{0,8},{2,10},{4,12},{6,14},{8,0},{10,2},{12,4},{14,6},{1,9},{3,11}... | collective-permute-start | bytes 49160 | tf_op jit(solution)/shard_map/ppermute | solution.py:48
  250.9 5.8 %collective-permute-start.45 = (f32[32,128]{1,0:T(8,128)S(1)}, f32[32,128]{1,0:T(8,128)S(1)}, u32[]{:S(2)}, u32[]{:S(2)}) collective-permute-start(f32[32,128]{1,0:T(8,128)S(1)} %bitcast.132), channel_id=1, source_target_pairs={{0,4},{2,6},{4,8},{6,10},{8,12},{10,14},{12,0},{14,2},{1,5},{3,7},... | collective-permute-start | bytes 49160 | tf_op jit(solution)/shard_map/ppermute | solution.py:48
  256.8 6.7 %collective-permute-start.46 = (f32[32,128]{1,0:T(8,128)S(1)}, f32[32,128]{1,0:T(8,128)S(1)}, u32[]{:S(2)}, u32[]{:S(2)}) collective-permute-start(f32[32,128]{1,0:T(8,128)S(1)} %bitcast.133), channel_id=1, source_target_pairs={{0,6},{2,8},{4,10},{6,12},{8,14},{10,0},{12,2},{14,4},{1,7},{3,9},... | collective-permute-start | bytes 49160 | tf_op jit(solution)/shard_map/ppermute | solution.py:48
  308.3 1.7 collective-permute-start.51
  311.0 8.4 %collective-permute-start.52 = (f32[256,256]{1,0:T(8,128)S(1)}, f32[256,256]{1,0:T(8,128)S(1)}, u32[]{:S(2)}, u32[]{:S(2)}) collective-permute-start(f32[256,256]{1,0:T(8,128)S(1)} %add.426), channel_id=1, source_target_pairs={{0,32},{32,0},{64,96},{96,64},{1,33},{33,1},{65,97},{97,65},{2,34}... | collective-permute-start | bytes 786440 | tf_op jit(solution)/shard_map/ppermute | solution.py:36
  319.5 9.1 %collective-permute-start.53 = (f32[256,256]{1,0:T(8,128)S(1)}, f32[256,256]{1,0:T(8,128)S(1)}, u32[]{:S(2)}, u32[]{:S(2)}) collective-permute-start(f32[256,256]{1,0:T(8,128)S(1)} %add.427), channel_id=1, source_target_pairs={{0,64},{32,96},{64,0},{96,32},{1,65},{33,97},{65,1},{97,33},{2,66}... | collective-permute-start | bytes 786440 | tf_op jit(solution)/shard_map/ppermute | solution.py:36
  328.6 8.2 %collective-permute-start.54 = (f32[256,256]{1,0:T(8,128)S(1)}, f32[256,256]{1,0:T(8,128)S(1)}, u32[]{:S(2)}, u32[]{:S(2)}) collective-permute-start(f32[256,256]{1,0:T(8,128)S(1)} %add.428), channel_id=1, source_target_pairs={{0,128},{128,0},{1,129},{129,1},{2,130},{130,2},{3,131},{131,3},{4... | collective-permute-start | bytes 786440 | tf_op jit(solution)/shard_map/ppermute | solution.py:36
Sparse Core Ops, SparseCore 0:
  15.5 44.0 all-gather.1
  210.2 98.0 reduce-scatter.1

commit v3 on v1

--- a/solution.py
+++ b/solution.py
@@ -18,6 +18,7 @@
 ROW_AXES = ("yh", "x", "c")
 COL_AXES = ("z", "yl")
 ALL_AXES = ROW_AXES + COL_AXES
+TOTAL_ORDER = ("c", "yl", "yh", "x", "z")
 
 
 def normalize(matrix):
@@ -27,8 +28,8 @@
     )
 
 
-def butterfly_sum(x, sizes):
-    for axis in ALL_AXES:
+def butterfly_sum(x, axes, sizes):
+    for axis in axes:
         n = sizes[axis]
         k = 1
         while k < n:
@@ -145,7 +146,9 @@
     mass_ratio = local_rows * row_devices / local_cands
     col_index = lax.axis_index("z") * sizes["yl"] + lax.axis_index("yl")
     own_start = col_index * local_cands
-    gathered = lax.all_gather(normalize(cand_rows), COL_AXES, axis=0, tiled=True)
+    gathered = lax.all_gather(
+        lax.all_gather(normalize(cand_rows), "yl", axis=0, tiled=True), "z", axis=0, tiled=True
+    )
     cn_blocks = gathered.reshape(block_count, BLOCK, feature_count)
     xn = normalize(data_rows)
     mass_col = data_mass.reshape(local_rows, 1)
@@ -153,17 +156,17 @@
     scale_blocks = jnp.ones((block_count, BLOCK), jnp.float32)
     for sweep_index in range(ITERS - 1):
         _, part_total = sweep(xn, cn_blocks, scale_blocks, mass_col, links)
-        whole_total = butterfly_sum(part_total, sizes)
+        whole_total = butterfly_sum(part_total, TOTAL_ORDER, sizes)
         scale_blocks = mass_ratio * cand_mass.reshape(block_count, BLOCK) / whole_total
     ds_col, part_total, partial_sums = sweep(
         xn, cn_blocks, scale_blocks, mass_col, links, rows=data_rows
     )
-    whole_total = butterfly_sum(part_total, sizes).reshape(-1)
+    whole_total = butterfly_sum(part_total, TOTAL_ORDER, sizes).reshape(-1)
     own_total = lax.dynamic_slice_in_dim(whole_total, own_start, local_cands)
     own_scale = mass_ratio * lax.dynamic_slice_in_dim(cand_mass, own_start, local_cands) / own_total
     flat_sums = partial_sums.reshape(cand_total, feature_count)
     share_rows = lax.psum_scatter(flat_sums, COL_AXES, scatter_dimension=0, tiled=True)
-    own_sums = lax.psum(share_rows, ROW_AXES)
+    own_sums = butterfly_sum(share_rows, ("c", "x", "yh"), sizes)
     new_support = own_sums / own_total[:, None]
     return (ds_col.reshape(local_rows), own_scale, new_support)
 

time: 448 us -> 331 us (0.74); the launches traced: 440 us -> 329 us
  waiting for transfers between devices: 355 us -> 221 us
  starting transfers between devices: 25.1 us -> 41.8 us
  blocking collectives: 0 us -> 6.02 us
    psum x1 -> x0, waiting for transfers between devices: 137 us -> none  [on_device(): own_sums = lax.psum(share_rows, ROW_AXES)]
    reduce_scatter x1, waiting for transfers between devices: 64.9 us -> 98.8 us  [on_device(): lax.psum_scatter(flat_sums, COL_AXES, scatter_dimension=0, tiled=True)]
    all_gather x1, waiting for transfers between devices: 74.9 us -> 42.6 us  [on_device(): lax.all_gather(lax.all_gather(normalize(cand_rows), 'yl', axis=0, tiled=T...]
    ppermute x24 -> x28, starting transfers between devices: 25 us -> 41.7 us  [butterfly_sum(): x = x + lax.ppermute(x, axis, [(j, j ^ k) for j in range(n)])]
    all_gather x0 -> x1, blocking collectives: none -> 6.02 us  [on_device(): lax.all_gather(normalize(cand_rows), 'yl', axis=0, tiled=True)]
    ppermute x24 -> x28, waiting for transfers between devices: 77.5 us -> 79.1 us  [butterfly_sum(): x = x + lax.ppermute(x, axis, [(j, j ^ k) for j in range(n)])]
  transfers between devices with their start and end apart: 27 -> 30, of which waited for: 26 -> 28; matrix products, arithmetic and copies ran while one was open for 1% -> 1% of each run, Pallas kernels for 0% -> 0%
where the time goes in v3:
time: 331 us; the launch traced here: 329 us
  waiting for transfers between devices  221 us (67%)
  starting transfers between devices  41.8 us (13%)
  Pallas kernels  37.4 us (11%)
  between operations  14.2 us (4%)
  other arithmetic  6.14 us (2%)
  blocking collectives  6.02 us (2%)
    reduce_scatter x1, waiting for transfers between devices, on_device(): lax.psum_scatter(flat_sums, COL_AXES, scatter_dimension=0, tiled=True)  98.8 us
    ppermute x28, waiting for transfers between devices, butterfly_sum(): x = x + lax.ppermute(x, axis, [(j, j ^ k) for j in range(n)])  79.1 us
    all_gather x1, waiting for transfers between devices, on_device(): lax.all_gather(lax.all_gather(normalize(cand_rows), 'yl', axis=0, tiled=T...  42.6 us
    ppermute x28, starting transfers between devices, butterfly_sum(): x = x + lax.ppermute(x, axis, [(j, j ^ k) for j in range(n)])  41.7 us
    pallas_call x3, Pallas kernels, sweep(): pl.pallas_call(functools.partial(sweep_body, nbr, inv_width, inv_count, b...  37.4 us
  transfers between devices with their start and end apart: 30, of which 28 were waited for; matrix products, arithmetic and copies ran while one was open for 1% of the time, Pallas kernels for 0%

profile of v3, /device:TPU:4, one launch (start us, length us, event | category | flops | bytes accessed | tf_op | source)
XLA Modules:
  0.0 328.6 jit_solution(11557683874704927295)
XLA Ops:
  7.2 1.1 fusion.2
  8.3 1.0 fusion.3
  9.3 6.0 %all_gather.6 = bf16[512,256]{1,0:T(8,128)(2,1)} all-gather(bf16[256,256]{1,0:T(8,128)(2,1)S(1)} %fusion.3), channel_id=1, replica_groups=mesh['yh'=2,'x'=4,'c'=2,'z'=8,'yl'=2] {'yl'}, dimensions={0}, use_global_device_ids=true | all-gather | bytes 393216 | tf_op jit(solution)/shard_map/all_gather | solution.py:150
  15.4 1.0 reshape.47.mass_ref
  16.4 0.3 fusion
  16.7 0.3 fusion.1.xn_ref
  17.0 42.6 %all-gather.2.cloned.1.call-done = bf16[4096,256]{1,0:T(8,128)(2,1)} async-done(((bf16[512,256]{1,0:T(8,128)(2,1)}), bf16[4096,256]{1,0:T(8,128)(2,1)}) %all-gather.2.cloned.1.call-update) | async-done | bytes 2097168 | tf_op jit(solution)/shard_map/all_gather | solution.py:149
  59.6 1.6 copy-done.1
  61.2 10.4 %shard_map.76 = (f32[1536,1]{1,0:T(8,128)}, f32[32,128]{1,0:T(8,128)S(1)}) custom-call(s32[12,16]{1,0:T(8,128)S(1)} %copy-done.2, bf16[1536,256]{1,0:T(8,128)(2,1)S(1)} %fusion.1.xn_ref, bf16[32,128,256]{2,1,0:T(8,128)(2,1)S(1)} %bitcast.7, f32[32,128]{1,0:T(8,128)S(1)} %broadcast_in_dim.2.scale_ref, f32[1536,1]{1,0:T(8,128)S(1)} %reshape.47.mass_ref), custom_call_target="tpu_custom_call" | custom-call | flops 1610612736 | bytes 2883584 | tf_op jit(solution)/shard_map/pallas_call | solution.py:117
  71.6 1.2 collective-permute-done
  72.8 1.5 collective-permute-start.1
  74.3 2.3 collective-permute-done.1
  76.5 3.0 collective-permute-start.2
  79.5 2.2 collective-permute-done.2
  81.8 1.2 collective-permute-start.3
  83.0 2.6 collective-permute-done.3
  85.6 0.5 collective-permute-start.4
  86.1 4.8 %collective-permute-done.4 = f32[32,128]{1,0:T(8,128)S(1)} collective-permute-done((f32[32,128]{1,0:T(8,128)S(1)}, f32[32,128]{1,0:T(8,128)S(1)}, u32[]{:S(2)}, u32[]{:S(2)}) %collective-permute-start.4) | collective-permute-done | bytes 16416 | tf_op jit(solution)/shard_map/ppermute | solution.py:36
  90.9 1.2 collective-permute-start.5
  92.1 2.5 collective-permute-done.5
  94.6 1.2 collective-permute-start.6
  95.8 3.4 %collective-permute-done.6 = f32[32,128]{1,0:T(8,128)S(1)} collective-permute-done((f32[32,128]{1,0:T(8,128)S(1)}, f32[32,128]{1,0:T(8,128)S(1)}, u32[]{:S(2)}, u32[]{:S(2)}) %collective-permute-start.6) | collective-permute-done | bytes 16416 | tf_op jit(solution)/shard_map/ppermute | solution.py:36
  99.3 3.0 collective-permute-start.7
  102.2 4.7 %collective-permute-done.7 = f32[32,128]{1,0:T(8,128)S(1)} collective-permute-done((f32[32,128]{1,0:T(8,128)S(1)}, f32[32,128]{1,0:T(8,128)S(1)}, u32[]{:S(2)}, u32[]{:S(2)}) %collective-permute-start.7) | collective-permute-done | bytes 16416 | tf_op jit(solution)/shard_map/ppermute | solution.py:36
  106.9 10.4 %shard_map.77 = (f32[1536,1]{1,0:T(8,128)}, f32[32,128]{1,0:T(8,128)S(1)}) custom-call(s32[12,16]{1,0:T(8,128)S(1)} %copy-done.2, bf16[1536,256]{1,0:T(8,128)(2,1)S(1)} %fusion.1.xn_ref, bf16[32,128,256]{2,1,0:T(8,128)(2,1)S(1)} %bitcast.8, f32[32,128]{1,0:T(8,128)S(1)} %bitcast_divide_fusion.1.scale_ref, f32[1536,1]{1,0:T(8,128)S(1)} %reshape.47.mass_ref), custom_call_target="tpu_custom_call" | custom-call | flops 1610612736 | bytes 2883584 | tf_op jit(solution)/shard_map/pallas_call | solution.py:117
  117.3 1.2 collective-permute-done.8
  118.5 1.5 collective-permute-start.9
  120.0 2.3 collective-permute-done.9
  122.3 3.0 collective-permute-start.10
  125.3 2.2 collective-permute-done.10
  127.5 1.1 collective-permute-start.11
  128.6 2.8 collective-permute-done.11
  131.4 0.3 collective-permute-start.12
  131.7 4.9 %collective-permute-done.12 = f32[32,128]{1,0:T(8,128)S(1)} collective-permute-done((f32[32,128]{1,0:T(8,128)S(1)}, f32[32,128]{1,0:T(8,128)S(1)}, u32[]{:S(2)}, u32[]{:S(2)}) %collective-permute-start.12) | collective-permute-done | bytes 16416 | tf_op jit(solution)/shard_map/ppermute | solution.py:36
  136.7 1.1 collective-permute-start.13
  137.8 2.6 collective-permute-done.13
  140.4 1.2 collective-permute-start.14
  141.7 3.4 %collective-permute-done.14 = f32[32,128]{1,0:T(8,128)S(1)} collective-permute-done((f32[32,128]{1,0:T(8,128)S(1)}, f32[32,128]{1,0:T(8,128)S(1)}, u32[]{:S(2)}, u32[]{:S(2)}) %collective-permute-start.14) | collective-permute-done | bytes 16416 | tf_op jit(solution)/shard_map/ppermute | solution.py:36
  145.1 3.0 collective-permute-start.15
  148.1 4.7 %collective-permute-done.15 = f32[32,128]{1,0:T(8,128)S(1)} collective-permute-done((f32[32,128]{1,0:T(8,128)S(1)}, f32[32,128]{1,0:T(8,128)S(1)}, u32[]{:S(2)}, u32[]{:S(2)}) %collective-permute-start.15) | collective-permute-done | bytes 16416 | tf_op jit(solution)/shard_map/ppermute | solution.py:36
  152.7 16.5 %shard_map.78 = (f32[1536,1]{1,0:T(8,128)S(1)}, f32[32,128]{1,0:T(8,128)S(1)}, f32[32,128,256]{2,1,0:T(8,128)}) custom-call(s32[12,16]{1,0:T(8,128)S(1)} %copy-done.2, bf16[1536,256]{1,0:T(8,128)(2,1)S(1)} %fusion.1.xn_ref, bf16[32,128,256]{2,1,0:T(8,128)(2,1)S(1)} %bitcast.9, f32[32,128]{1,0:T(8,128)S(1)} %bitcast_divide_fusion.scale_ref, ...), custom_call_target="tpu_custom_call" | custom-call | flops 3221225472 | bytes 7864320 | tf_op jit(solution)/shard_map/pallas_call | solution.py:117
  169.3 98.8 %reduce-scatter.2.cloned.1.call-done = f32[256,256]{1,0:T(8,128)} async-done(((f32[4096,256]{1,0:T(8,128)}), f32[256,256]{1,0:T(8,128)}) %reduce-scatter.2.cloned.1.call-update) | async-done | bytes 262160 | tf_op jit(solution)/shard_map/reduce_scatter | solution.py:168
  268.1 1.7 collective-permute-done.24
  269.9 1.0 add.145
  270.8 1.3 collective-permute-start.25
  272.1 7.2 %collective-permute-done.25 = f32[256,256]{1,0:T(8,128)S(1)} collective-permute-done((f32[256,256]{1,0:T(8,128)S(1)}, f32[256,256]{1,0:T(8,128)S(1)}, u32[]{:S(2)}, u32[]{:S(2)}) %collective-permute-start.25) | collective-permute-done | bytes 262176 | tf_op jit(solution)/shard_map/ppermute | solution.py:36
  279.3 0.4 collective-permute-start.26
  279.7 1.2 collective-permute-done.16
  281.1 3.5 %collective-permute-done.17 = f32[32,128]{1,0:T(8,128)S(1)} collective-permute-done((f32[32,128]{1,0:T(8,128)S(1)}, f32[32,128]{1,0:T(8,128)S(1)}, u32[]{:S(2)}, u32[]{:S(2)}) %collective-permute-start.17) | collective-permute-done | bytes 16416 | tf_op jit(solution)/shard_map/ppermute | solution.py:36
  284.6 3.0 collective-permute-start.18
  287.6 2.3 collective-permute-done.18
  289.9 2.3 collective-permute-start.19
  292.2 1.7 collective-permute-done.19
  293.9 2.9 collective-permute-start.20
  296.9 2.3 collective-permute-done.20
  299.4 3.5 %collective-permute-done.21 = f32[32,128]{1,0:T(8,128)S(1)} collective-permute-done((f32[32,128]{1,0:T(8,128)S(1)}, f32[32,128]{1,0:T(8,128)S(1)}, u32[]{:S(2)}, u32[]{:S(2)}) %collective-permute-start.21) | collective-permute-done | bytes 16416 | tf_op jit(solution)/shard_map/ppermute | solution.py:36
  302.9 1.7 collective-permute-start.22
  304.7 2.9 collective-permute-done.22
  307.6 4.5 %collective-permute-start.23 = (f32[32,128]{1,0:T(8,128)S(1)}, f32[32,128]{1,0:T(8,128)S(1)}, u32[]{:S(2)}, u32[]{:S(2)}) collective-permute-start(f32[32,128]{1,0:T(8,128)S(1)} %add.143), channel_id=1, source_target_pairs={{0,8},{2,10},{4,12},{6,14},{8,0},{10,2},{12,4},{14,6},{1,9},{3,11}... | collective-permute-start | bytes 49160 | tf_op jit(solution)/shard_map/ppermute | solution.py:36
  312.1 0.9 reduce
  313.0 2.3 collective-permute-start.27
  315.3 0.6 multiply_divide_fusion
  316.0 5.0 %collective-permute-done.27 = f32[256,256]{1,0:T(8,128)S(1)} collective-permute-done((f32[256,256]{1,0:T(8,128)S(1)}, f32[256,256]{1,0:T(8,128)S(1)}, u32[]{:S(2)}, u32[]{:S(2)}) %collective-permute-start.27) | collective-permute-done | bytes 262176 | tf_op jit(solution)/shard_map/ppermute | solution.py:36
  321.0 0.8 add_divide_fusion
  (48 shorter events, 0.8 us)
Async XLA Ops:
  7.2 9.2 %copy-start = (bf16[1536,256]{1,0:T(8,128)(2,1)S(1)}, bf16[1536,256]{1,0:T(8,128)(2,1)}, u32[]{:S(2)}) copy-start(bf16[1536,256]{1,0:T(8,128)(2,1)} %rest_0_.1) | copy-start | bytes 2359300
  7.2 52.4 %all-gather.2.cloned.1.call-start = ((), (), s32[]{:S(2)}) async-start(), calls=%async_computation.1 | async-start | bytes 2359296 | tf_op jit(solution)/shard_map/all_gather | solution.py:149
  15.4 44.2 %copy-start.2 = (s32[12,16]{1,0:T(8,128)S(1)}, s32[12,16]{1,0:T(8,128)}, u32[]{:S(2)}) copy-start(s32[12,16]{1,0:T(8,128)} %links_ref.5) | copy-start | bytes 2308
  15.4 252.7 %reduce-scatter.2.cloned.1.call-start = ((), (), s32[]{:S(2)}) async-start(), calls=%async_computation.2 | async-start | bytes 4456448 | tf_op jit(solution)/shard_map/reduce_scatter | solution.py:168
  59.6 1.6 copy-start.1
  61.2 45.7 %copy-start.3 = (f32[4096]{0:T(1024)S(1)}, f32[4096]{0:T(1024)}, u32[]{:S(2)}) copy-start(f32[4096]{0:T(1024)} %param.9) | copy-start | bytes 49156
  71.6 1.2 collective-permute-start
  72.8 3.7 %collective-permute-start.1 = (f32[32,128]{1,0:T(8,128)S(1)}, f32[32,128]{1,0:T(8,128)S(1)}, u32[]{:S(2)}, u32[]{:S(2)}) collective-permute-start(f32[32,128]{1,0:T(8,128)S(1)} %add.119), channel_id=1, source_target_pairs={{0,1},{1,0},{2,3},{3,2},{4,5},{5,4},{6,7},{7,6},{8,9},{9,8},{10,11... | collective-permute-start | bytes 49160 | tf_op jit(solution)/shard_map/ppermute | solution.py:36
  76.5 5.2 %collective-permute-start.2 = (f32[32,128]{1,0:T(8,128)S(1)}, f32[32,128]{1,0:T(8,128)S(1)}, u32[]{:S(2)}, u32[]{:S(2)}) collective-permute-start(f32[32,128]{1,0:T(8,128)S(1)} %add.120), channel_id=1, source_target_pairs={{0,128},{128,0},{1,129},{129,1},{2,130},{130,2},{3,131},{131,3},{4... | collective-permute-start | bytes 49160 | tf_op jit(solution)/shard_map/ppermute | solution.py:36
  81.8 3.8 %collective-permute-start.3 = (f32[32,128]{1,0:T(8,128)S(1)}, f32[32,128]{1,0:T(8,128)S(1)}, u32[]{:S(2)}, u32[]{:S(2)}) collective-permute-start(f32[32,128]{1,0:T(8,128)S(1)} %add.121), channel_id=1, source_target_pairs={{0,32},{32,0},{64,96},{96,64},{1,33},{33,1},{65,97},{97,65},{2,34}... | collective-permute-start | bytes 49160 | tf_op jit(solution)/shard_map/ppermute | solution.py:36
  85.6 5.2 %collective-permute-start.4 = (f32[32,128]{1,0:T(8,128)S(1)}, f32[32,128]{1,0:T(8,128)S(1)}, u32[]{:S(2)}, u32[]{:S(2)}) collective-permute-start(f32[32,128]{1,0:T(8,128)S(1)} %add.122), channel_id=1, source_target_pairs={{0,64},{32,96},{64,0},{96,32},{1,65},{33,97},{65,1},{97,33},{2,66}... | collective-permute-start | bytes 49160 | tf_op jit(solution)/shard_map/ppermute | solution.py:36
  90.9 3.7 %collective-permute-start.5 = (f32[32,128]{1,0:T(8,128)S(1)}, f32[32,128]{1,0:T(8,128)S(1)}, u32[]{:S(2)}, u32[]{:S(2)}) collective-permute-start(f32[32,128]{1,0:T(8,128)S(1)} %add.123), channel_id=1, source_target_pairs={{0,2},{2,0},{4,6},{6,4},{8,10},{10,8},{12,14},{14,12},{1,3},{3,1},... | collective-permute-start | bytes 49160 | tf_op jit(solution)/shard_map/ppermute | solution.py:36
  94.6 4.6 %collective-permute-start.6 = (f32[32,128]{1,0:T(8,128)S(1)}, f32[32,128]{1,0:T(8,128)S(1)}, u32[]{:S(2)}, u32[]{:S(2)}) collective-permute-start(f32[32,128]{1,0:T(8,128)S(1)} %add.124), channel_id=1, source_target_pairs={{0,4},{2,6},{4,0},{6,2},{8,12},{10,14},{12,8},{14,10},{1,5},{3,7},... | collective-permute-start | bytes 49160 | tf_op jit(solution)/shard_map/ppermute | solution.py:36
  99.3 7.6 %collective-permute-start.7 = (f32[32,128]{1,0:T(8,128)S(1)}, f32[32,128]{1,0:T(8,128)S(1)}, u32[]{:S(2)}, u32[]{:S(2)}) collective-permute-start(f32[32,128]{1,0:T(8,128)S(1)} %add.125), channel_id=1, source_target_pairs={{0,8},{2,10},{4,12},{6,14},{8,0},{10,2},{12,4},{14,6},{1,9},{3,11}... | collective-permute-start | bytes 49160 | tf_op jit(solution)/shard_map/ppermute | solution.py:36
  117.3 1.2 collective-permute-start.8
  118.5 3.7 %collective-permute-start.9 = (f32[32,128]{1,0:T(8,128)S(1)}, f32[32,128]{1,0:T(8,128)S(1)}, u32[]{:S(2)}, u32[]{:S(2)}) collective-permute-start(f32[32,128]{1,0:T(8,128)S(1)} %add.127), channel_id=1, source_target_pairs={{0,1},{1,0},{2,3},{3,2},{4,5},{5,4},{6,7},{7,6},{8,9},{9,8},{10,11... | collective-permute-start | bytes 49160 | tf_op jit(solution)/shard_map/ppermute | solution.py:36
  122.3 5.2 %collective-permute-start.10 = (f32[32,128]{1,0:T(8,128)S(1)}, f32[32,128]{1,0:T(8,128)S(1)}, u32[]{:S(2)}, u32[]{:S(2)}) collective-permute-start(f32[32,128]{1,0:T(8,128)S(1)} %add.128), channel_id=1, source_target_pairs={{0,128},{128,0},{1,129},{129,1},{2,130},{130,2},{3,131},{131,3},{4... | collective-permute-start | bytes 49160 | tf_op jit(solution)/shard_map/ppermute | solution.py:36
  127.5 3.9 %collective-permute-start.11 = (f32[32,128]{1,0:T(8,128)S(1)}, f32[32,128]{1,0:T(8,128)S(1)}, u32[]{:S(2)}, u32[]{:S(2)}) collective-permute-start(f32[32,128]{1,0:T(8,128)S(1)} %add.129), channel_id=1, source_target_pairs={{0,32},{32,0},{64,96},{96,64},{1,33},{33,1},{65,97},{97,65},{2,34}... | collective-permute-start | bytes 49160 | tf_op jit(solution)/shard_map/ppermute | solution.py:36
  131.4 5.2 %collective-permute-start.12 = (f32[32,128]{1,0:T(8,128)S(1)}, f32[32,128]{1,0:T(8,128)S(1)}, u32[]{:S(2)}, u32[]{:S(2)}) collective-permute-start(f32[32,128]{1,0:T(8,128)S(1)} %add.130), channel_id=1, source_target_pairs={{0,64},{32,96},{64,0},{96,32},{1,65},{33,97},{65,1},{97,33},{2,66}... | collective-permute-start | bytes 49160 | tf_op jit(solution)/shard_map/ppermute | solution.py:36
  136.7 3.7 %collective-permute-start.13 = (f32[32,128]{1,0:T(8,128)S(1)}, f32[32,128]{1,0:T(8,128)S(1)}, u32[]{:S(2)}, u32[]{:S(2)}) collective-permute-start(f32[32,128]{1,0:T(8,128)S(1)} %add.131), channel_id=1, source_target_pairs={{0,2},{2,0},{4,6},{6,4},{8,10},{10,8},{12,14},{14,12},{1,3},{3,1},... | collective-permute-start | bytes 49160 | tf_op jit(solution)/shard_map/ppermute | solution.py:36
  140.4 4.6 %collective-permute-start.14 = (f32[32,128]{1,0:T(8,128)S(1)}, f32[32,128]{1,0:T(8,128)S(1)}, u32[]{:S(2)}, u32[]{:S(2)}) collective-permute-start(f32[32,128]{1,0:T(8,128)S(1)} %add.132), channel_id=1, source_target_pairs={{0,4},{2,6},{4,0},{6,2},{8,12},{10,14},{12,8},{14,10},{1,5},{3,7},... | collective-permute-start | bytes 49160 | tf_op jit(solution)/shard_map/ppermute | solution.py:36
  145.1 7.6 %collective-permute-start.15 = (f32[32,128]{1,0:T(8,128)S(1)}, f32[32,128]{1,0:T(8,128)S(1)}, u32[]{:S(2)}, u32[]{:S(2)}) collective-permute-start(f32[32,128]{1,0:T(8,128)S(1)} %add.133), channel_id=1, source_target_pairs={{0,8},{2,10},{4,12},{6,14},{8,0},{10,2},{12,4},{14,6},{1,9},{3,11}... | collective-permute-start | bytes 49160 | tf_op jit(solution)/shard_map/ppermute | solution.py:36
  268.1 1.7 collective-permute-start.24
  270.8 8.4 %collective-permute-start.25 = (f32[256,256]{1,0:T(8,128)S(1)}, f32[256,256]{1,0:T(8,128)S(1)}, u32[]{:S(2)}, u32[]{:S(2)}) collective-permute-start(f32[256,256]{1,0:T(8,128)S(1)} %add.145), channel_id=1, source_target_pairs={{0,32},{32,0},{64,96},{96,64},{1,33},{33,1},{65,97},{97,65},{2,34}... | collective-permute-start | bytes 786440 | tf_op jit(solution)/shard_map/ppermute | solution.py:36
  279.3 33.7 %collective-permute-start.26 = (f32[256,256]{1,0:T(8,128)S(1)}, f32[256,256]{1,0:T(8,128)S(1)}, u32[]{:S(2)}, u32[]{:S(2)}) collective-permute-start(f32[256,256]{1,0:T(8,128)S(1)} %add.146), channel_id=1, source_target_pairs={{0,64},{32,96},{64,0},{96,32},{1,65},{33,97},{65,1},{97,33},{2,66}... | collective-permute-start | bytes 786440 | tf_op jit(solution)/shard_map/ppermute | solution.py:36
  279.7 1.2 collective-permute-start.16
  280.9 3.7 %collective-permute-start.17 = (f32[32,128]{1,0:T(8,128)S(1)}, f32[32,128]{1,0:T(8,128)S(1)}, u32[]{:S(2)}, u32[]{:S(2)}) collective-permute-start(f32[32,128]{1,0:T(8,128)S(1)} %add.137), channel_id=1, source_target_pairs={{0,1},{1,0},{2,3},{3,2},{4,5},{5,4},{6,7},{7,6},{8,9},{9,8},{10,11... | collective-permute-start | bytes 49160 | tf_op jit(solution)/shard_map/ppermute | solution.py:36
  284.6 5.2 %collective-permute-start.18 = (f32[32,128]{1,0:T(8,128)S(1)}, f32[32,128]{1,0:T(8,128)S(1)}, u32[]{:S(2)}, u32[]{:S(2)}) collective-permute-start(f32[32,128]{1,0:T(8,128)S(1)} %add.138), channel_id=1, source_target_pairs={{0,128},{128,0},{1,129},{129,1},{2,130},{130,2},{3,131},{131,3},{4... | collective-permute-start | bytes 49160 | tf_op jit(solution)/shard_map/ppermute | solution.py:36
  289.9 4.1 %collective-permute-start.19 = (f32[32,128]{1,0:T(8,128)S(1)}, f32[32,128]{1,0:T(8,128)S(1)}, u32[]{:S(2)}, u32[]{:S(2)}) collective-permute-start(f32[32,128]{1,0:T(8,128)S(1)} %add.139), channel_id=1, source_target_pairs={{0,32},{32,0},{64,96},{96,64},{1,33},{33,1},{65,97},{97,65},{2,34}... | collective-permute-start | bytes 49160 | tf_op jit(solution)/shard_map/ppermute | solution.py:36
  293.9 5.2 %collective-permute-start.20 = (f32[32,128]{1,0:T(8,128)S(1)}, f32[32,128]{1,0:T(8,128)S(1)}, u32[]{:S(2)}, u32[]{:S(2)}) collective-permute-start(f32[32,128]{1,0:T(8,128)S(1)} %add.140), channel_id=1, source_target_pairs={{0,64},{32,96},{64,0},{96,32},{1,65},{33,97},{65,1},{97,33},{2,66}... | collective-permute-start | bytes 49160 | tf_op jit(solution)/shard_map/ppermute | solution.py:36
  299.2 3.7 %collective-permute-start.21 = (f32[32,128]{1,0:T(8,128)S(1)}, f32[32,128]{1,0:T(8,128)S(1)}, u32[]{:S(2)}, u32[]{:S(2)}) collective-permute-start(f32[32,128]{1,0:T(8,128)S(1)} %add.141), channel_id=1, source_target_pairs={{0,2},{2,0},{4,6},{6,4},{8,10},{10,8},{12,14},{14,12},{1,3},{3,1},... | collective-permute-start | bytes 49160 | tf_op jit(solution)/shard_map/ppermute | solution.py:36
  302.9 4.6 %collective-permute-start.22 = (f32[32,128]{1,0:T(8,128)S(1)}, f32[32,128]{1,0:T(8,128)S(1)}, u32[]{:S(2)}, u32[]{:S(2)}) collective-permute-start(f32[32,128]{1,0:T(8,128)S(1)} %add.142), channel_id=1, source_target_pairs={{0,4},{2,6},{4,0},{6,2},{8,12},{10,14},{12,8},{14,10},{1,5},{3,7},... | collective-permute-start | bytes 49160 | tf_op jit(solution)/shard_map/ppermute | solution.py:36
  307.6 7.7 %collective-permute-start.23 = (f32[32,128]{1,0:T(8,128)S(1)}, f32[32,128]{1,0:T(8,128)S(1)}, u32[]{:S(2)}, u32[]{:S(2)}) collective-permute-start(f32[32,128]{1,0:T(8,128)S(1)} %add.143), channel_id=1, source_target_pairs={{0,8},{2,10},{4,12},{6,14},{8,0},{10,2},{12,4},{14,6},{1,9},{3,11}... | collective-permute-start | bytes 49160 | tf_op jit(solution)/shard_map/ppermute | solution.py:36
  313.0 8.0 %collective-permute-start.27 = (f32[256,256]{1,0:T(8,128)S(1)}, f32[256,256]{1,0:T(8,128)S(1)}, u32[]{:S(2)}, u32[]{:S(2)}) collective-permute-start(f32[256,256]{1,0:T(8,128)S(1)} %add.147), channel_id=1, source_target_pairs={{0,128},{128,0},{1,129},{129,1},{2,130},{130,2},{3,131},{131,3},{4... | collective-permute-start | bytes 786440 | tf_op jit(solution)/shard_map/ppermute | solution.py:36
Sparse Core Ops, SparseCore 0:
  15.5 44.0 all-gather.1
  169.4 98.6 reduce-scatter.1

commit v4 on v3

--- a/solution.py
+++ b/solution.py
@@ -161,12 +161,16 @@
     ds_col, part_total, partial_sums = sweep(
         xn, cn_blocks, scale_blocks, mass_col, links, rows=data_rows
     )
-    whole_total = butterfly_sum(part_total, TOTAL_ORDER, sizes).reshape(-1)
-    own_total = lax.dynamic_slice_in_dim(whole_total, own_start, local_cands)
+    pad = 8
+    totals = jnp.pad(part_total.reshape(col_devices, 1, local_cands), ((0, 0), (0, pad - 1), (0, 0)))
+    packed = jnp.concatenate(
+        [partial_sums.reshape(col_devices, local_cands, feature_count), totals], axis=1
+    ).reshape(col_devices * (local_cands + pad), feature_count)
+    joined = lax.psum_scatter(packed, COL_AXES, scatter_dimension=0, tiled=True)
+    joined = butterfly_sum(joined, ("c", "x", "yh"), sizes)
+    own_sums = joined[:local_cands]
+    own_total = joined[local_cands]
     own_scale = mass_ratio * lax.dynamic_slice_in_dim(cand_mass, own_start, local_cands) / own_total
-    flat_sums = partial_sums.reshape(cand_total, feature_count)
-    share_rows = lax.psum_scatter(flat_sums, COL_AXES, scatter_dimension=0, tiled=True)
-    own_sums = butterfly_sum(share_rows, ("c", "x", "yh"), sizes)
     new_support = own_sums / own_total[:, None]
     return (ds_col.reshape(local_rows), own_scale, new_support)
 

time: 331 us -> 313 us (0.946)
  starting transfers between devices: 41.8 us -> 27 us
  waiting for transfers between devices: 221 us -> 212 us
  other arithmetic: 6.14 us -> 13 us
    ppermute x28 -> x20, starting transfers between devices: 41.7 us -> 26.9 us  [butterfly_sum(): x = x + lax.ppermute(x, axis, [(j, j ^ k) for j in range(n)])]
    ppermute x28 -> x20, waiting for transfers between devices: 79.1 us -> 70.8 us  [butterfly_sum(): x = x + lax.ppermute(x, axis, [(j, j ^ k) for j in range(n)])]
    concatenate x0 -> x1, other arithmetic: none -> 4.61 us  [on_device(): jnp.concatenate([partial_sums.reshape(col_devices, local_cands, feature_c...]
  transfers between devices with their start and end apart: 30 -> 22, of which waited for: 28 -> 22; matrix products, arithmetic and copies ran while one was open for 1% -> 1% of each run, Pallas kernels for 0% -> 0%
where the time goes in v4:
time: 313 us
  waiting for transfers between devices  212 us (68%)
  Pallas kernels  37.4 us (12%)
  starting transfers between devices  27 us (9%)
  between operations  14.2 us (5%)
  other arithmetic  13 us (4%)
  blocking collectives  6.02 us (2%)
    reduce_scatter x1, waiting for transfers between devices, on_device(): joined = lax.psum_scatter(packed, COL_AXES, scatter_dimension=0, tiled=True)  101 us
    ppermute x20, waiting for transfers between devices, butterfly_sum(): x = x + lax.ppermute(x, axis, [(j, j ^ k) for j in range(n)])  70.8 us
    all_gather x1, waiting for transfers between devices, on_device(): lax.all_gather(lax.all_gather(normalize(cand_rows), 'yl', axis=0, tiled=T...  40.3 us
    pallas_call x3, Pallas kernels, sweep(): pl.pallas_call(functools.partial(sweep_body, nbr, inv_width, inv_count, b...  37.4 us
    ppermute x20, starting transfers between devices, butterfly_sum(): x = x + lax.ppermute(x, axis, [(j, j ^ k) for j in range(n)])  26.9 us
  transfers between devices with their start and end apart: 22, of which 22 were waited for; matrix products, arithmetic and copies ran while one was open for 1% of the time, Pallas kernels for 0%

profile of v4, /device:TPU:4, one launch (start us, length us, event | category | flops | bytes accessed | tf_op | source)
XLA Modules:
  0.0 312.5 jit_solution(5357122376525225976)
XLA Ops:
  7.2 0.0 copy-start.2
  7.2 0.0 all-gather.2.cloned.1.call-start
  7.2 1.0 fusion.2
  8.3 1.0 fusion.3
  9.3 6.0 %all_gather.6 = bf16[512,256]{1,0:T(8,128)(2,1)} all-gather(bf16[256,256]{1,0:T(8,128)(2,1)S(1)} %fusion.3), channel_id=1, replica_groups=mesh['yh'=2,'x'=4,'c'=2,'z'=8,'yl'=2] {'yl'}, dimensions={0}, use_global_device_ids=true | all-gather | bytes 393216 | tf_op jit(solution)/shard_map/all_gather | solution.py:150
  15.3 0.0 all-gather.2.cloned.1.call-update
  15.3 0.0 reduce-scatter.2.cloned.1.call-start
  15.4 1.0 reshape.51.mass_ref
  16.3 0.0 copy-start.3
  16.3 1.4 fusion
  17.8 1.4 fusion.1.xn_ref
  19.2 40.3 %all-gather.2.cloned.1.call-done = bf16[4096,256]{1,0:T(8,128)(2,1)} async-done(((bf16[512,256]{1,0:T(8,128)(2,1)}), bf16[4096,256]{1,0:T(8,128)(2,1)}) %all-gather.2.cloned.1.call-update) | async-done | bytes 2097168 | tf_op jit(solution)/shard_map/all_gather | solution.py:149
  59.5 0.0 copy-done.2
  59.5 1.6 copy-done.1
  61.1 10.4 %shard_map.76 = (f32[1536,1]{1,0:T(8,128)}, f32[32,128]{1,0:T(8,128)S(1)}) custom-call(s32[12,16]{1,0:T(8,128)S(1)} %copy-done.2, bf16[1536,256]{1,0:T(8,128)(2,1)S(1)} %fusion.1.xn_ref, bf16[32,128,256]{2,1,0:T(8,128)(2,1)S(1)} %bitcast.9, f32[32,128]{1,0:T(8,128)S(1)} %broadcast_in_dim.2.scale_ref, f32[1536,1]{1,0:T(8,128)S(1)} %reshape.51.mass_ref), custom_call_target="tpu_custom_call" | custom-call | flops 1610612736 | bytes 2883584 | tf_op jit(solution)/shard_map/pallas_call | solution.py:117
  71.5 0.0 collective-permute-start
  71.5 1.2 collective-permute-done
  72.7 1.5 collective-permute-start.1
  74.2 2.3 collective-permute-done.1
  76.4 3.0 collective-permute-start.2
  79.4 2.2 collective-permute-done.2
  81.7 1.2 collective-permute-start.3
  82.8 2.6 collective-permute-done.3
  85.5 0.5 collective-permute-start.4
  86.0 4.8 %collective-permute-done.4 = f32[32,128]{1,0:T(8,128)S(1)} collective-permute-done((f32[32,128]{1,0:T(8,128)S(1)}, f32[32,128]{1,0:T(8,128)S(1)}, u32[]{:S(2)}, u32[]{:S(2)}) %collective-permute-start.4) | collective-permute-done | bytes 16416 | tf_op jit(solution)/shard_map/ppermute | solution.py:36
  90.7 1.2 collective-permute-start.5
  92.0 2.5 collective-permute-done.5
  94.5 1.2 collective-permute-start.6
  95.7 3.4 %collective-permute-done.6 = f32[32,128]{1,0:T(8,128)S(1)} collective-permute-done((f32[32,128]{1,0:T(8,128)S(1)}, f32[32,128]{1,0:T(8,128)S(1)}, u32[]{:S(2)}, u32[]{:S(2)}) %collective-permute-start.6) | collective-permute-done | bytes 16416 | tf_op jit(solution)/shard_map/ppermute | solution.py:36
  99.1 3.0 collective-permute-start.7
  102.1 4.7 %collective-permute-done.7 = f32[32,128]{1,0:T(8,128)S(1)} collective-permute-done((f32[32,128]{1,0:T(8,128)S(1)}, f32[32,128]{1,0:T(8,128)S(1)}, u32[]{:S(2)}, u32[]{:S(2)}) %collective-permute-start.7) | collective-permute-done | bytes 16416 | tf_op jit(solution)/shard_map/ppermute | solution.py:36
  106.8 10.4 %shard_map.77 = (f32[1536,1]{1,0:T(8,128)}, f32[32,128]{1,0:T(8,128)S(1)}) custom-call(s32[12,16]{1,0:T(8,128)S(1)} %copy-done.2, bf16[1536,256]{1,0:T(8,128)(2,1)S(1)} %fusion.1.xn_ref, bf16[32,128,256]{2,1,0:T(8,128)(2,1)S(1)} %bitcast.10, f32[32,128]{1,0:T(8,128)S(1)} %bitcast_divide_fusion.1.scale_ref, f32[1536,1]{1,0:T(8,128)S(1)} %reshape.51.mass_ref), custom_call_target="tpu_custom_call" | custom-call | flops 1610612736 | bytes 2883584 | tf_op jit(solution)/shard_map/pallas_call | solution.py:117
  117.2 0.0 collective-permute-start.8
  117.2 1.2 collective-permute-done.8
  118.4 1.5 collective-permute-start.9
  119.9 2.3 collective-permute-done.9
  122.1 3.0 collective-permute-start.10
  125.1 2.2 collective-permute-done.10
  127.4 1.1 collective-permute-start.11
  128.5 2.8 collective-permute-done.11
  131.3 0.3 collective-permute-start.12
  131.6 4.9 %collective-permute-done.12 = f32[32,128]{1,0:T(8,128)S(1)} collective-permute-done((f32[32,128]{1,0:T(8,128)S(1)}, f32[32,128]{1,0:T(8,128)S(1)}, u32[]{:S(2)}, u32[]{:S(2)}) %collective-permute-start.12) | collective-permute-done | bytes 16416 | tf_op jit(solution)/shard_map/ppermute | solution.py:36
  136.5 1.1 collective-permute-start.13
  137.7 2.6 collective-permute-done.13
  140.3 1.3 collective-permute-start.14
  141.5 3.4 %collective-permute-done.14 = f32[32,128]{1,0:T(8,128)S(1)} collective-permute-done((f32[32,128]{1,0:T(8,128)S(1)}, f32[32,128]{1,0:T(8,128)S(1)}, u32[]{:S(2)}, u32[]{:S(2)}) %collective-permute-start.14) | collective-permute-done | bytes 16416 | tf_op jit(solution)/shard_map/ppermute | solution.py:36
  144.9 3.0 collective-permute-start.15
  147.9 4.7 %collective-permute-done.15 = f32[32,128]{1,0:T(8,128)S(1)} collective-permute-done((f32[32,128]{1,0:T(8,128)S(1)}, f32[32,128]{1,0:T(8,128)S(1)}, u32[]{:S(2)}, u32[]{:S(2)}) %collective-permute-start.15) | collective-permute-done | bytes 16416 | tf_op jit(solution)/shard_map/ppermute | solution.py:36
  152.6 16.6 %shard_map.78 = (f32[1536,1]{1,0:T(8,128)S(1)}, f32[32,128]{1,0:T(8,128)S(1)}, f32[32,128,256]{2,1,0:T(8,128)}) custom-call(s32[12,16]{1,0:T(8,128)S(1)} %copy-done.2, bf16[1536,256]{1,0:T(8,128)(2,1)S(1)} %fusion.1.xn_ref, bf16[32,128,256]{2,1,0:T(8,128)(2,1)S(1)} %bitcast.11, f32[32,128]{1,0:T(8,128)S(1)} %bitcast_divide_fusion.scale_ref, ...), custom_call_target="tpu_custom_call" | custom-call | flops 3221225472 | bytes 7864320 | tf_op jit(solution)/shard_map/pallas_call | solution.py:117
  169.2 4.6 %select_maximum_fusion = f32[16,264,256]{2,1,0:T(8,128)} fusion(f32[16,1,256]{2,1,0:T(1,128)S(1)} %bitcast.8, f32[16,256,256]{2,1,0:T(8,128)} %bitcast.13), kind=kLoop, calls=%fused_computation | loop fusion | flops 3244032 | bytes 8536064 | tf_op jit(solution)/shard_map/concatenate | solution.py:166
  173.8 0.0 reduce-scatter.2.cloned.1.call-update
  173.8 101.2 %reduce-scatter.2.cloned.1.call-done = f32[264,256]{1,0:T(8,128)} async-done(((f32[4224,256]{1,0:T(8,128)}), f32[264,256]{1,0:T(8,128)}) %reduce-scatter.2.cloned.1.call-update) | async-done | bytes 270352 | tf_op jit(solution)/shard_map/reduce_scatter | solution.py:169
  275.1 0.0 collective-permute-start.16
  275.1 1.8 collective-permute-done.16
  276.8 1.0 add.114
  277.8 0.5 collective-permute-start.17
  278.4 8.1 %collective-permute-done.17 = f32[264,256]{1,0:T(8,128)S(1)} collective-permute-done((f32[264,256]{1,0:T(8,128)S(1)}, f32[264,256]{1,0:T(8,128)S(1)}, u32[]{:S(2)}, u32[]{:S(2)}) %collective-permute-start.17) | collective-permute-done | bytes 270368 | tf_op jit(solution)/shard_map/ppermute | solution.py:36
  286.5 0.6 collective-permute-start.18
  287.1 8.7 %collective-permute-done.18 = f32[264,256]{1,0:T(8,128)S(1)} collective-permute-done((f32[264,256]{1,0:T(8,128)S(1)}, f32[264,256]{1,0:T(8,128)S(1)}, u32[]{:S(2)}, u32[]{:S(2)}) %collective-permute-start.18) | collective-permute-done | bytes 270368 | tf_op jit(solution)/shard_map/ppermute | solution.py:36
  295.8 2.9 collective-permute-start.19
  298.7 0.9 reduce
  299.6 4.6 %collective-permute-done.19 = f32[264,256]{1,0:T(8,128)S(1)} collective-permute-done((f32[264,256]{1,0:T(8,128)S(1)}, f32[264,256]{1,0:T(8,128)S(1)}, u32[]{:S(2)}, u32[]{:S(2)}) %collective-permute-start.19) | collective-permute-done | bytes 270368 | tf_op jit(solution)/shard_map/ppermute | solution.py:36
  304.2 0.8 slice_divide_fusion
  305.0 0.6 multiply_divide_fusion
  (27 shorter events, 0.2 us)
Async XLA Ops:
  7.2 52.4 %copy-start.2 = (s32[12,16]{1,0:T(8,128)S(1)}, s32[12,16]{1,0:T(8,128)}, u32[]{:S(2)}) copy-start(s32[12,16]{1,0:T(8,128)} %links_ref.5) | copy-start | bytes 2308
  7.2 52.3 %all-gather.2.cloned.1.call-start = ((), (), s32[]{:S(2)}) async-start(), calls=%async_computation.1 | async-start | bytes 2359296 | tf_op jit(solution)/shard_map/all_gather | solution.py:149
  15.3 259.8 %reduce-scatter.2.cloned.1.call-start = ((), (), s32[]{:S(2)}) async-start(), calls=%async_computation.2 | async-start | bytes 4595712 | tf_op jit(solution)/shard_map/reduce_scatter | solution.py:169
  16.3 90.5 %copy-start.3 = (f32[4096]{0:T(1024)S(1)}, f32[4096]{0:T(1024)}, u32[]{:S(2)}) copy-start(f32[4096]{0:T(1024)} %param.9) | copy-start | bytes 49156
  59.5 1.6 copy-start.1
  71.5 81.1 %copy-start = (bf16[1536,256]{1,0:T(8,128)(2,1)S(1)}, bf16[1536,256]{1,0:T(8,128)(2,1)}, u32[]{:S(2)}) copy-start(bf16[1536,256]{1,0:T(8,128)(2,1)} %rest_0_.1) | copy-start | bytes 2359300
  71.5 1.2 collective-permute-start
  72.7 3.7 %collective-permute-start.1 = (f32[32,128]{1,0:T(8,128)S(1)}, f32[32,128]{1,0:T(8,128)S(1)}, u32[]{:S(2)}, u32[]{:S(2)}) collective-permute-start(f32[32,128]{1,0:T(8,128)S(1)} %add.96), channel_id=1, source_target_pairs={{0,1},{1,0},{2,3},{3,2},{4,5},{5,4},{6,7},{7,6},{8,9},{9,8},{10,11... | collective-permute-start | bytes 49160 | tf_op jit(solution)/shard_map/ppermute | solution.py:36
  76.4 5.2 %collective-permute-start.2 = (f32[32,128]{1,0:T(8,128)S(1)}, f32[32,128]{1,0:T(8,128)S(1)}, u32[]{:S(2)}, u32[]{:S(2)}) collective-permute-start(f32[32,128]{1,0:T(8,128)S(1)} %add.97), channel_id=1, source_target_pairs={{0,128},{128,0},{1,129},{129,1},{2,130},{130,2},{3,131},{131,3},{4... | collective-permute-start | bytes 49160 | tf_op jit(solution)/shard_map/ppermute | solution.py:36
  81.7 3.8 %collective-permute-start.3 = (f32[32,128]{1,0:T(8,128)S(1)}, f32[32,128]{1,0:T(8,128)S(1)}, u32[]{:S(2)}, u32[]{:S(2)}) collective-permute-start(f32[32,128]{1,0:T(8,128)S(1)} %add.98), channel_id=1, source_target_pairs={{0,32},{32,0},{64,96},{96,64},{1,33},{33,1},{65,97},{97,65},{2,34}... | collective-permute-start | bytes 49160 | tf_op jit(solution)/shard_map/ppermute | solution.py:36
  85.5 5.2 %collective-permute-start.4 = (f32[32,128]{1,0:T(8,128)S(1)}, f32[32,128]{1,0:T(8,128)S(1)}, u32[]{:S(2)}, u32[]{:S(2)}) collective-permute-start(f32[32,128]{1,0:T(8,128)S(1)} %add.99), channel_id=1, source_target_pairs={{0,64},{32,96},{64,0},{96,32},{1,65},{33,97},{65,1},{97,33},{2,66}... | collective-permute-start | bytes 49160 | tf_op jit(solution)/shard_map/ppermute | solution.py:36
  90.7 3.7 %collective-permute-start.5 = (f32[32,128]{1,0:T(8,128)S(1)}, f32[32,128]{1,0:T(8,128)S(1)}, u32[]{:S(2)}, u32[]{:S(2)}) collective-permute-start(f32[32,128]{1,0:T(8,128)S(1)} %add.100), channel_id=1, source_target_pairs={{0,2},{2,0},{4,6},{6,4},{8,10},{10,8},{12,14},{14,12},{1,3},{3,1},... | collective-permute-start | bytes 49160 | tf_op jit(solution)/shard_map/ppermute | solution.py:36
  94.5 4.6 %collective-permute-start.6 = (f32[32,128]{1,0:T(8,128)S(1)}, f32[32,128]{1,0:T(8,128)S(1)}, u32[]{:S(2)}, u32[]{:S(2)}) collective-permute-start(f32[32,128]{1,0:T(8,128)S(1)} %add.101), channel_id=1, source_target_pairs={{0,4},{2,6},{4,0},{6,2},{8,12},{10,14},{12,8},{14,10},{1,5},{3,7},... | collective-permute-start | bytes 49160 | tf_op jit(solution)/shard_map/ppermute | solution.py:36
  99.1 7.6 %collective-permute-start.7 = (f32[32,128]{1,0:T(8,128)S(1)}, f32[32,128]{1,0:T(8,128)S(1)}, u32[]{:S(2)}, u32[]{:S(2)}) collective-permute-start(f32[32,128]{1,0:T(8,128)S(1)} %add.102), channel_id=1, source_target_pairs={{0,8},{2,10},{4,12},{6,14},{8,0},{10,2},{12,4},{14,6},{1,9},{3,11}... | collective-permute-start | bytes 49160 | tf_op jit(solution)/shard_map/ppermute | solution.py:36
  117.2 1.2 collective-permute-start.8
  118.4 3.7 %collective-permute-start.9 = (f32[32,128]{1,0:T(8,128)S(1)}, f32[32,128]{1,0:T(8,128)S(1)}, u32[]{:S(2)}, u32[]{:S(2)}) collective-permute-start(f32[32,128]{1,0:T(8,128)S(1)} %add.104), channel_id=1, source_target_pairs={{0,1},{1,0},{2,3},{3,2},{4,5},{5,4},{6,7},{7,6},{8,9},{9,8},{10,11... | collective-permute-start | bytes 49160 | tf_op jit(solution)/shard_map/ppermute | solution.py:36
  122.1 5.2 %collective-permute-start.10 = (f32[32,128]{1,0:T(8,128)S(1)}, f32[32,128]{1,0:T(8,128)S(1)}, u32[]{:S(2)}, u32[]{:S(2)}) collective-permute-start(f32[32,128]{1,0:T(8,128)S(1)} %add.105), channel_id=1, source_target_pairs={{0,128},{128,0},{1,129},{129,1},{2,130},{130,2},{3,131},{131,3},{4... | collective-permute-start | bytes 49160 | tf_op jit(solution)/shard_map/ppermute | solution.py:36
  127.4 3.9 %collective-permute-start.11 = (f32[32,128]{1,0:T(8,128)S(1)}, f32[32,128]{1,0:T(8,128)S(1)}, u32[]{:S(2)}, u32[]{:S(2)}) collective-permute-start(f32[32,128]{1,0:T(8,128)S(1)} %add.106), channel_id=1, source_target_pairs={{0,32},{32,0},{64,96},{96,64},{1,33},{33,1},{65,97},{97,65},{2,34}... | collective-permute-start | bytes 49160 | tf_op jit(solution)/shard_map/ppermute | solution.py:36
  131.3 5.2 %collective-permute-start.12 = (f32[32,128]{1,0:T(8,128)S(1)}, f32[32,128]{1,0:T(8,128)S(1)}, u32[]{:S(2)}, u32[]{:S(2)}) collective-permute-start(f32[32,128]{1,0:T(8,128)S(1)} %add.107), channel_id=1, source_target_pairs={{0,64},{32,96},{64,0},{96,32},{1,65},{33,97},{65,1},{97,33},{2,66}... | collective-permute-start | bytes 49160 | tf_op jit(solution)/shard_map/ppermute | solution.py:36
  136.5 3.7 %collective-permute-start.13 = (f32[32,128]{1,0:T(8,128)S(1)}, f32[32,128]{1,0:T(8,128)S(1)}, u32[]{:S(2)}, u32[]{:S(2)}) collective-permute-start(f32[32,128]{1,0:T(8,128)S(1)} %add.108), channel_id=1, source_target_pairs={{0,2},{2,0},{4,6},{6,4},{8,10},{10,8},{12,14},{14,12},{1,3},{3,1},... | collective-permute-start | bytes 49160 | tf_op jit(solution)/shard_map/ppermute | solution.py:36
  140.3 4.6 %collective-permute-start.14 = (f32[32,128]{1,0:T(8,128)S(1)}, f32[32,128]{1,0:T(8,128)S(1)}, u32[]{:S(2)}, u32[]{:S(2)}) collective-permute-start(f32[32,128]{1,0:T(8,128)S(1)} %add.109), channel_id=1, source_target_pairs={{0,4},{2,6},{4,0},{6,2},{8,12},{10,14},{12,8},{14,10},{1,5},{3,7},... | collective-permute-start | bytes 49160 | tf_op jit(solution)/shard_map/ppermute | solution.py:36
  144.9 7.6 %collective-permute-start.15 = (f32[32,128]{1,0:T(8,128)S(1)}, f32[32,128]{1,0:T(8,128)S(1)}, u32[]{:S(2)}, u32[]{:S(2)}) collective-permute-start(f32[32,128]{1,0:T(8,128)S(1)} %add.110), channel_id=1, source_target_pairs={{0,8},{2,10},{4,12},{6,14},{8,0},{10,2},{12,4},{14,6},{1,9},{3,11}... | collective-permute-start | bytes 49160 | tf_op jit(solution)/shard_map/ppermute | solution.py:36
  275.1 1.8 collective-permute-start.16
  277.8 8.6 %collective-permute-start.17 = (f32[264,256]{1,0:T(8,128)S(1)}, f32[264,256]{1,0:T(8,128)S(1)}, u32[]{:S(2)}, u32[]{:S(2)}) collective-permute-start(f32[264,256]{1,0:T(8,128)S(1)} %add.114), channel_id=1, source_target_pairs={{0,32},{32,0},{64,96},{96,64},{1,33},{33,1},{65,97},{97,65},{2,34}... | collective-permute-start | bytes 811016 | tf_op jit(solution)/shard_map/ppermute | solution.py:36
  286.5 9.3 %collective-permute-start.18 = (f32[264,256]{1,0:T(8,128)S(1)}, f32[264,256]{1,0:T(8,128)S(1)}, u32[]{:S(2)}, u32[]{:S(2)}) collective-permute-start(f32[264,256]{1,0:T(8,128)S(1)} %add.115), channel_id=1, source_target_pairs={{0,64},{32,96},{64,0},{96,32},{1,65},{33,97},{65,1},{97,33},{2,66}... | collective-permute-start | bytes 811016 | tf_op jit(solution)/shard_map/ppermute | solution.py:36
  295.8 8.4 %collective-permute-start.19 = (f32[264,256]{1,0:T(8,128)S(1)}, f32[264,256]{1,0:T(8,128)S(1)}, u32[]{:S(2)}, u32[]{:S(2)}) collective-permute-start(f32[264,256]{1,0:T(8,128)S(1)} %add.116), channel_id=1, source_target_pairs={{0,128},{128,0},{1,129},{129,1},{2,130},{130,2},{3,131},{131,3},{4... | collective-permute-start | bytes 811016 | tf_op jit(solution)/shard_map/ppermute | solution.py:36
Sparse Core Ops, SparseCore 0:
  15.4 44.0 all-gather.1
  174.0 101.0 reduce-scatter.1

commit v5 on v4

--- a/solution.py
+++ b/solution.py
@@ -14,6 +14,7 @@
 
 EPS = 0.05
 OFFSET = 1.0
+PAD = 8
 
 ROW_AXES = ("yh", "x", "c")
 COL_AXES = ("z", "yl")
@@ -49,16 +50,17 @@
 def sweep_body(nbr, inv_width, inv_count, bary, links_ref, xn_ref, cn_ref, scale_ref, mass_ref,
                *rest):
     if bary:
-        rows_ref, ds_ref, ct_ref, ws_ref, kbuf = rest
+        rows_ref, ds_ref, ws_ref, kbuf = rest
     else:
         ds_ref, ct_ref, kbuf = rest
     b = pl.program_id(0)
 
     @pl.when(b == 0)
     def _():
-        ct_ref[...] = jnp.zeros_like(ct_ref)
         if bary:
             ws_ref[...] = jnp.zeros_like(ws_ref)
+        else:
+            ct_ref[...] = jnp.zeros_like(ct_ref)
 
     xn = xn_ref[...]
     acc = jnp.zeros((BLOCK, BLOCK), jnp.float32)
@@ -76,12 +78,16 @@
         blk = links_ref[b, s]
         k = kbuf[s]
         part = jnp.sum(k * ds, axis=0, keepdims=True)
-        ct_ref[pl.ds(blk, 1), :] += part
         if bary:
+            q = blk // 2
+            half = pl.multiple_of((blk % 2) * BLOCK, BLOCK)
+            ws_ref[q, pl.ds(2 * BLOCK, 1), pl.ds(half, BLOCK)] += part
             w = (k * ds).astype(jnp.bfloat16)
-            ws_ref[blk] += lax.dot_general(
+            ws_ref[q, pl.ds(half, BLOCK), :] += lax.dot_general(
                 w, rows, (((0,), (0,)), ((), ())), preferred_element_type=jnp.float32
             )
+        else:
+            ct_ref[pl.ds(blk, 1), :] += part
 
 
 def sweep(xn, cn_blocks, scale_blocks, mass_col, links, rows=None):
@@ -97,22 +103,19 @@
         pl.BlockSpec((block_count, BLOCK), lambda b, L: (0, 0)),
         pl.BlockSpec((BLOCK, 1), lambda b, L: (b, 0)),
     ]
-    out_specs = [
-        pl.BlockSpec((BLOCK, 1), lambda b, L: (b, 0)),
-        pl.BlockSpec((block_count, BLOCK), lambda b, L: (0, 0)),
-    ]
-    out_shape = [
-        jax.ShapeDtypeStruct((local_rows, 1), jnp.float32),
-        jax.ShapeDtypeStruct((block_count, BLOCK), jnp.float32),
-    ]
+    out_specs = [pl.BlockSpec((BLOCK, 1), lambda b, L: (b, 0))]
+    out_shape = [jax.ShapeDtypeStruct((local_rows, 1), jnp.float32)]
+    packed_rows = 2 * BLOCK + PAD
     args = [links, xn, cn_blocks, scale_blocks, mass_col]
     if bary:
         in_specs.append(pl.BlockSpec((BLOCK, feature_count), lambda b, L: (b, 0)))
-        out_specs.append(
-            pl.BlockSpec((block_count, BLOCK, feature_count), lambda b, L: (0, 0, 0))
-        )
-        out_shape.append(jax.ShapeDtypeStruct((block_count, BLOCK, feature_count), jnp.float32))
+        packed = (block_count // 2, packed_rows, feature_count)
+        out_specs.append(pl.BlockSpec(packed, lambda b, L: (0, 0, 0)))
+        out_shape.append(jax.ShapeDtypeStruct(packed, jnp.float32))
         args.append(rows)
+    else:
+        out_specs.append(pl.BlockSpec((block_count, BLOCK), lambda b, L: (0, 0)))
+        out_shape.append(jax.ShapeDtypeStruct((block_count, BLOCK), jnp.float32))
     flops = 2 * local_rows * nbr * BLOCK * feature_count * (2 if bary else 1)
     return pl.pallas_call(
         functools.partial(sweep_body, nbr, inv_width, inv_count, bary),
@@ -158,15 +161,8 @@
         _, part_total = sweep(xn, cn_blocks, scale_blocks, mass_col, links)
         whole_total = butterfly_sum(part_total, TOTAL_ORDER, sizes)
         scale_blocks = mass_ratio * cand_mass.reshape(block_count, BLOCK) / whole_total
-    ds_col, part_total, partial_sums = sweep(
-        xn, cn_blocks, scale_blocks, mass_col, links, rows=data_rows
-    )
-    pad = 8
-    totals = jnp.pad(part_total.reshape(col_devices, 1, local_cands), ((0, 0), (0, pad - 1), (0, 0)))
-    packed = jnp.concatenate(
-        [partial_sums.reshape(col_devices, local_cands, feature_count), totals], axis=1
-    ).reshape(col_devices * (local_cands + pad), feature_count)
-    joined = lax.psum_scatter(packed, COL_AXES, scatter_dimension=0, tiled=True)
+    ds_col, packed = sweep(xn, cn_blocks, scale_blocks, mass_col, links, rows=data_rows)
+    joined = lax.psum_scatter(packed.reshape(-1, feature_count), COL_AXES, scatter_dimension=0, tiled=True)
     joined = butterfly_sum(joined, ("c", "x", "yh"), sizes)
     own_sums = joined[:local_cands]
     own_total = joined[local_cands]

time: 313 us -> 308 us (0.984)
  other arithmetic: 13 us -> 6.14 us
    concatenate x1 -> x0, other arithmetic: 4.61 us -> none  [on_device(): jnp.concatenate([partial_sums.reshape(col_devices, local_cands, feature_c...]
where the time goes in v5:
time: 308 us
  waiting for transfers between devices  212 us (69%)
  Pallas kernels  37.3 us (12%)
  starting transfers between devices  29.4 us (10%)
  between operations  14.2 us (5%)
  other arithmetic  6.14 us (2%)
  blocking collectives  6.02 us (2%)
    reduce_scatter x1, waiting for transfers between devices, on_device(): lax.psum_scatter(packed.reshape(-1, feature_count), COL_AXES, scatter_dim...  101 us
    ppermute x20, waiting for transfers between devices, butterfly_sum(): x = x + lax.ppermute(x, axis, [(j, j ^ k) for j in range(n)])  68.8 us
    all_gather x1, waiting for transfers between devices, on_device(): lax.all_gather(lax.all_gather(normalize(cand_rows), 'yl', axis=0, tiled=T...  42.6 us
    pallas_call x3, Pallas kernels, sweep(): pl.pallas_call(functools.partial(sweep_body, nbr, inv_width, inv_count, b...  37.3 us
    ppermute x20, starting transfers between devices, butterfly_sum(): x = x + lax.ppermute(x, axis, [(j, j ^ k) for j in range(n)])  29.3 us
  transfers between devices with their start and end apart: 22, of which 22 were waited for; matrix products, arithmetic and copies ran while one was open for 1% of the time, Pallas kernels for 0%

profile of v5, /device:TPU:4, one launch (start us, length us, event | category | flops | bytes accessed | tf_op | source)
XLA Modules:
  0.0 307.6 jit_solution(14355429747727210726)
XLA Ops:
  7.2 0.0 copy-start
  7.2 0.0 all-gather.2.cloned.1.call-start
  7.2 1.1 fusion.2
  8.3 1.0 fusion.3
  9.3 6.0 %all_gather.6 = bf16[512,256]{1,0:T(8,128)(2,1)} all-gather(bf16[256,256]{1,0:T(8,128)(2,1)S(1)} %fusion.3), channel_id=1, replica_groups=mesh['yh'=2,'x'=4,'c'=2,'z'=8,'yl'=2] {'yl'}, dimensions={0}, use_global_device_ids=true | all-gather | bytes 393216 | tf_op jit(solution)/shard_map/all_gather | solution.py:153
  15.4 0.0 all-gather.2.cloned.1.call-update
  15.4 0.0 copy-start.2
  15.4 0.0 reduce-scatter.2.cloned.1.call-start
  15.4 1.0 reshape.43.mass_ref
  16.4 0.0 copy-done
  16.4 0.3 fusion
  16.7 0.3 fusion.1.xn_ref
  17.0 42.6 %all-gather.2.cloned.1.call-done = bf16[4096,256]{1,0:T(8,128)(2,1)} async-done(((bf16[512,256]{1,0:T(8,128)(2,1)}), bf16[4096,256]{1,0:T(8,128)(2,1)}) %all-gather.2.cloned.1.call-update) | async-done | bytes 2097168 | tf_op jit(solution)/shard_map/all_gather | solution.py:152
  59.6 0.0 copy-done.2
  59.6 1.6 copy-done.1
  61.2 10.4 %shard_map.76 = (f32[1536,1]{1,0:T(8,128)}, f32[32,128]{1,0:T(8,128)S(1)}) custom-call(s32[12,16]{1,0:T(8,128)S(1)} %copy-done.2, bf16[1536,256]{1,0:T(8,128)(2,1)S(1)} %fusion.1.xn_ref, bf16[32,128,256]{2,1,0:T(8,128)(2,1)S(1)} %bitcast.6, f32[32,128]{1,0:T(8,128)S(1)} %broadcast_in_dim.2.scale_ref, f32[1536,1]{1,0:T(8,128)S(1)} %reshape.43.mass_ref), custom_call_target="tpu_custom_call" | custom-call | flops 1610612736 | bytes 2883584 | tf_op jit(solution)/shard_map/pallas_call | solution.py:120
  71.6 0.0 collective-permute-start
  71.6 1.2 collective-permute-done
  72.8 1.5 collective-permute-start.1
  74.3 2.3 collective-permute-done.1
  76.5 3.0 collective-permute-start.2
  79.5 2.2 collective-permute-done.2
  81.8 1.2 collective-permute-start.3
  83.0 2.6 collective-permute-done.3
  85.6 0.5 collective-permute-start.4
  86.1 4.8 %collective-permute-done.4 = f32[32,128]{1,0:T(8,128)S(1)} collective-permute-done((f32[32,128]{1,0:T(8,128)S(1)}, f32[32,128]{1,0:T(8,128)S(1)}, u32[]{:S(2)}, u32[]{:S(2)}) %collective-permute-start.4) | collective-permute-done | bytes 16416 | tf_op jit(solution)/shard_map/ppermute | solution.py:37
  90.9 1.2 collective-permute-start.5
  92.1 2.5 collective-permute-done.5
  94.6 1.2 collective-permute-start.6
  95.8 3.4 %collective-permute-done.6 = f32[32,128]{1,0:T(8,128)S(1)} collective-permute-done((f32[32,128]{1,0:T(8,128)S(1)}, f32[32,128]{1,0:T(8,128)S(1)}, u32[]{:S(2)}, u32[]{:S(2)}) %collective-permute-start.6) | collective-permute-done | bytes 16416 | tf_op jit(solution)/shard_map/ppermute | solution.py:37
  99.2 3.0 collective-permute-start.7
  102.2 4.7 %collective-permute-done.7 = f32[32,128]{1,0:T(8,128)S(1)} collective-permute-done((f32[32,128]{1,0:T(8,128)S(1)}, f32[32,128]{1,0:T(8,128)S(1)}, u32[]{:S(2)}, u32[]{:S(2)}) %collective-permute-start.7) | collective-permute-done | bytes 16416 | tf_op jit(solution)/shard_map/ppermute | solution.py:37
  106.9 10.4 %shard_map.77 = (f32[1536,1]{1,0:T(8,128)}, f32[32,128]{1,0:T(8,128)S(1)}) custom-call(s32[12,16]{1,0:T(8,128)S(1)} %copy-done.2, bf16[1536,256]{1,0:T(8,128)(2,1)S(1)} %fusion.1.xn_ref, bf16[32,128,256]{2,1,0:T(8,128)(2,1)S(1)} %bitcast.7, f32[32,128]{1,0:T(8,128)S(1)} %bitcast_divide_fusion.1.scale_ref, f32[1536,1]{1,0:T(8,128)S(1)} %reshape.43.mass_ref), custom_call_target="tpu_custom_call" | custom-call | flops 1610612736 | bytes 2883584 | tf_op jit(solution)/shard_map/pallas_call | solution.py:120
  117.3 0.0 collective-permute-start.8
  117.3 1.2 collective-permute-done.8
  118.5 1.5 collective-permute-start.9
  120.0 2.3 collective-permute-done.9
  122.3 3.0 collective-permute-start.10
  125.3 2.2 collective-permute-done.10
  127.5 1.1 collective-permute-start.11
  128.6 2.8 collective-permute-done.11
  131.4 0.3 collective-permute-start.12
  131.7 4.9 %collective-permute-done.12 = f32[32,128]{1,0:T(8,128)S(1)} collective-permute-done((f32[32,128]{1,0:T(8,128)S(1)}, f32[32,128]{1,0:T(8,128)S(1)}, u32[]{:S(2)}, u32[]{:S(2)}) %collective-permute-start.12) | collective-permute-done | bytes 16416 | tf_op jit(solution)/shard_map/ppermute | solution.py:37
  136.7 1.1 collective-permute-start.13
  137.8 2.6 collective-permute-done.13
  140.4 1.3 collective-permute-start.14
  141.7 3.4 %collective-permute-done.14 = f32[32,128]{1,0:T(8,128)S(1)} collective-permute-done((f32[32,128]{1,0:T(8,128)S(1)}, f32[32,128]{1,0:T(8,128)S(1)}, u32[]{:S(2)}, u32[]{:S(2)}) %collective-permute-start.14) | collective-permute-done | bytes 16416 | tf_op jit(solution)/shard_map/ppermute | solution.py:37
  145.1 3.0 collective-permute-start.15
  148.0 4.7 %collective-permute-done.15 = f32[32,128]{1,0:T(8,128)S(1)} collective-permute-done((f32[32,128]{1,0:T(8,128)S(1)}, f32[32,128]{1,0:T(8,128)S(1)}, u32[]{:S(2)}, u32[]{:S(2)}) %collective-permute-start.15) | collective-permute-done | bytes 16416 | tf_op jit(solution)/shard_map/ppermute | solution.py:37
  152.7 16.5 %shard_map.78 = (f32[1536,1]{1,0:T(8,128)S(1)}, f32[16,264,256]{2,1,0:T(8,128)}) custom-call(s32[12,16]{1,0:T(8,128)S(1)} %copy-done.2, bf16[1536,256]{1,0:T(8,128)(2,1)S(1)} %fusion.1.xn_ref, bf16[32,128,256]{2,1,0:T(8,128)(2,1)S(1)} %bitcast.8, f32[32,128]{1,0:T(8,128)S(1)} %bitcast_divide_fusion.scale_ref, f32[1536,1]{1,0:T(8,128)S(1)} %reshape.43.mass_ref, ...), custom_call_target="tpu_custom_call" | custom-call | flops 3221225472 | bytes 7864320 | tf_op jit(solution)/shard_map/pallas_call | solution.py:120
  169.2 0.0 reduce-scatter.2.cloned.1.call-update
  169.2 100.5 %reduce-scatter.2.cloned.1.call-done = f32[264,256]{1,0:T(8,128)} async-done(((f32[4224,256]{1,0:T(8,128)}), f32[264,256]{1,0:T(8,128)}) %reduce-scatter.2.cloned.1.call-update) | async-done | bytes 270352 | tf_op jit(solution)/shard_map/reduce_scatter | solution.py:165
  269.8 0.0 collective-permute-start.16
  269.8 1.8 collective-permute-done.16
  271.5 1.0 add.112
  272.5 2.0 collective-permute-start.17
  274.5 6.8 %collective-permute-done.17 = f32[264,256]{1,0:T(8,128)S(1)} collective-permute-done((f32[264,256]{1,0:T(8,128)S(1)}, f32[264,256]{1,0:T(8,128)S(1)}, u32[]{:S(2)}, u32[]{:S(2)}) %collective-permute-start.17) | collective-permute-done | bytes 270368 | tf_op jit(solution)/shard_map/ppermute | solution.py:37
  281.3 1.2 collective-permute-start.18
  282.5 8.2 %collective-permute-done.18 = f32[264,256]{1,0:T(8,128)S(1)} collective-permute-done((f32[264,256]{1,0:T(8,128)S(1)}, f32[264,256]{1,0:T(8,128)S(1)}, u32[]{:S(2)}, u32[]{:S(2)}) %collective-permute-start.18) | collective-permute-done | bytes 270368 | tf_op jit(solution)/shard_map/ppermute | solution.py:37
  290.8 3.4 %collective-permute-start.19 = (f32[264,256]{1,0:T(8,128)S(1)}, f32[264,256]{1,0:T(8,128)S(1)}, u32[]{:S(2)}, u32[]{:S(2)}) collective-permute-start(f32[264,256]{1,0:T(8,128)S(1)} %add.114), channel_id=1, source_target_pairs={{0,128},{128,0},{1,129},{129,1},{2,130},{130,2},{3,131},{131,3},{4... | collective-permute-start | bytes 811016 | tf_op jit(solution)/shard_map/ppermute | solution.py:37
  294.1 0.9 reduce
  295.0 4.3 %collective-permute-done.19 = f32[264,256]{1,0:T(8,128)S(1)} collective-permute-done((f32[264,256]{1,0:T(8,128)S(1)}, f32[264,256]{1,0:T(8,128)S(1)}, u32[]{:S(2)}, u32[]{:S(2)}) %collective-permute-start.19) | collective-permute-done | bytes 270368 | tf_op jit(solution)/shard_map/ppermute | solution.py:37
  299.3 0.8 slice_divide_fusion
  300.1 0.6 multiply_divide_fusion
  (26 shorter events, 0.2 us)
Async XLA Ops:
  7.2 9.2 %copy-start = (bf16[1536,256]{1,0:T(8,128)(2,1)S(1)}, bf16[1536,256]{1,0:T(8,128)(2,1)}, u32[]{:S(2)}) copy-start(bf16[1536,256]{1,0:T(8,128)(2,1)} %rest_0_.1) | copy-start | bytes 2359300
  7.2 52.4 %all-gather.2.cloned.1.call-start = ((), (), s32[]{:S(2)}) async-start(), calls=%async_computation.1 | async-start | bytes 2359296 | tf_op jit(solution)/shard_map/all_gather | solution.py:152
  15.4 44.2 %copy-start.2 = (s32[12,16]{1,0:T(8,128)S(1)}, s32[12,16]{1,0:T(8,128)}, u32[]{:S(2)}) copy-start(s32[12,16]{1,0:T(8,128)} %links_ref.5) | copy-start | bytes 2308
  15.4 254.4 %reduce-scatter.2.cloned.1.call-start = ((), (), s32[]{:S(2)}) async-start(), calls=%async_computation.2 | async-start | bytes 4595712 | tf_op jit(solution)/shard_map/reduce_scatter | solution.py:165
  59.6 1.6 copy-start.1
  61.2 45.7 %copy-start.3 = (f32[4096]{0:T(1024)S(1)}, f32[4096]{0:T(1024)}, u32[]{:S(2)}) copy-start(f32[4096]{0:T(1024)} %param.9) | copy-start | bytes 49156
  71.6 1.2 collective-permute-start
  72.8 3.7 %collective-permute-start.1 = (f32[32,128]{1,0:T(8,128)S(1)}, f32[32,128]{1,0:T(8,128)S(1)}, u32[]{:S(2)}, u32[]{:S(2)}) collective-permute-start(f32[32,128]{1,0:T(8,128)S(1)} %add.94), channel_id=1, source_target_pairs={{0,1},{1,0},{2,3},{3,2},{4,5},{5,4},{6,7},{7,6},{8,9},{9,8},{10,11... | collective-permute-start | bytes 49160 | tf_op jit(solution)/shard_map/ppermute | solution.py:37
  76.5 5.2 %collective-permute-start.2 = (f32[32,128]{1,0:T(8,128)S(1)}, f32[32,128]{1,0:T(8,128)S(1)}, u32[]{:S(2)}, u32[]{:S(2)}) collective-permute-start(f32[32,128]{1,0:T(8,128)S(1)} %add.95), channel_id=1, source_target_pairs={{0,128},{128,0},{1,129},{129,1},{2,130},{130,2},{3,131},{131,3},{4... | collective-permute-start | bytes 49160 | tf_op jit(solution)/shard_map/ppermute | solution.py:37
  81.8 3.8 %collective-permute-start.3 = (f32[32,128]{1,0:T(8,128)S(1)}, f32[32,128]{1,0:T(8,128)S(1)}, u32[]{:S(2)}, u32[]{:S(2)}) collective-permute-start(f32[32,128]{1,0:T(8,128)S(1)} %add.96), channel_id=1, source_target_pairs={{0,32},{32,0},{64,96},{96,64},{1,33},{33,1},{65,97},{97,65},{2,34}... | collective-permute-start | bytes 49160 | tf_op jit(solution)/shard_map/ppermute | solution.py:37
  85.6 5.2 %collective-permute-start.4 = (f32[32,128]{1,0:T(8,128)S(1)}, f32[32,128]{1,0:T(8,128)S(1)}, u32[]{:S(2)}, u32[]{:S(2)}) collective-permute-start(f32[32,128]{1,0:T(8,128)S(1)} %add.97), channel_id=1, source_target_pairs={{0,64},{32,96},{64,0},{96,32},{1,65},{33,97},{65,1},{97,33},{2,66}... | collective-permute-start | bytes 49160 | tf_op jit(solution)/shard_map/ppermute | solution.py:37
  90.9 3.7 %collective-permute-start.5 = (f32[32,128]{1,0:T(8,128)S(1)}, f32[32,128]{1,0:T(8,128)S(1)}, u32[]{:S(2)}, u32[]{:S(2)}) collective-permute-start(f32[32,128]{1,0:T(8,128)S(1)} %add.98), channel_id=1, source_target_pairs={{0,2},{2,0},{4,6},{6,4},{8,10},{10,8},{12,14},{14,12},{1,3},{3,1},... | collective-permute-start | bytes 49160 | tf_op jit(solution)/shard_map/ppermute | solution.py:37
  94.6 4.6 %collective-permute-start.6 = (f32[32,128]{1,0:T(8,128)S(1)}, f32[32,128]{1,0:T(8,128)S(1)}, u32[]{:S(2)}, u32[]{:S(2)}) collective-permute-start(f32[32,128]{1,0:T(8,128)S(1)} %add.99), channel_id=1, source_target_pairs={{0,4},{2,6},{4,0},{6,2},{8,12},{10,14},{12,8},{14,10},{1,5},{3,7},... | collective-permute-start | bytes 49160 | tf_op jit(solution)/shard_map/ppermute | solution.py:37
  99.2 7.6 %collective-permute-start.7 = (f32[32,128]{1,0:T(8,128)S(1)}, f32[32,128]{1,0:T(8,128)S(1)}, u32[]{:S(2)}, u32[]{:S(2)}) collective-permute-start(f32[32,128]{1,0:T(8,128)S(1)} %add.100), channel_id=1, source_target_pairs={{0,8},{2,10},{4,12},{6,14},{8,0},{10,2},{12,4},{14,6},{1,9},{3,11}... | collective-permute-start | bytes 49160 | tf_op jit(solution)/shard_map/ppermute | solution.py:37
  117.3 1.2 collective-permute-start.8
  118.5 3.7 %collective-permute-start.9 = (f32[32,128]{1,0:T(8,128)S(1)}, f32[32,128]{1,0:T(8,128)S(1)}, u32[]{:S(2)}, u32[]{:S(2)}) collective-permute-start(f32[32,128]{1,0:T(8,128)S(1)} %add.102), channel_id=1, source_target_pairs={{0,1},{1,0},{2,3},{3,2},{4,5},{5,4},{6,7},{7,6},{8,9},{9,8},{10,11... | collective-permute-start | bytes 49160 | tf_op jit(solution)/shard_map/ppermute | solution.py:37
  122.3 5.2 %collective-permute-start.10 = (f32[32,128]{1,0:T(8,128)S(1)}, f32[32,128]{1,0:T(8,128)S(1)}, u32[]{:S(2)}, u32[]{:S(2)}) collective-permute-start(f32[32,128]{1,0:T(8,128)S(1)} %add.103), channel_id=1, source_target_pairs={{0,128},{128,0},{1,129},{129,1},{2,130},{130,2},{3,131},{131,3},{4... | collective-permute-start | bytes 49160 | tf_op jit(solution)/shard_map/ppermute | solution.py:37
  127.5 3.9 %collective-permute-start.11 = (f32[32,128]{1,0:T(8,128)S(1)}, f32[32,128]{1,0:T(8,128)S(1)}, u32[]{:S(2)}, u32[]{:S(2)}) collective-permute-start(f32[32,128]{1,0:T(8,128)S(1)} %add.104), channel_id=1, source_target_pairs={{0,32},{32,0},{64,96},{96,64},{1,33},{33,1},{65,97},{97,65},{2,34}... | collective-permute-start | bytes 49160 | tf_op jit(solution)/shard_map/ppermute | solution.py:37
  131.4 5.2 %collective-permute-start.12 = (f32[32,128]{1,0:T(8,128)S(1)}, f32[32,128]{1,0:T(8,128)S(1)}, u32[]{:S(2)}, u32[]{:S(2)}) collective-permute-start(f32[32,128]{1,0:T(8,128)S(1)} %add.105), channel_id=1, source_target_pairs={{0,64},{32,96},{64,0},{96,32},{1,65},{33,97},{65,1},{97,33},{2,66}... | collective-permute-start | bytes 49160 | tf_op jit(solution)/shard_map/ppermute | solution.py:37
  136.7 3.7 %collective-permute-start.13 = (f32[32,128]{1,0:T(8,128)S(1)}, f32[32,128]{1,0:T(8,128)S(1)}, u32[]{:S(2)}, u32[]{:S(2)}) collective-permute-start(f32[32,128]{1,0:T(8,128)S(1)} %add.106), channel_id=1, source_target_pairs={{0,2},{2,0},{4,6},{6,4},{8,10},{10,8},{12,14},{14,12},{1,3},{3,1},... | collective-permute-start | bytes 49160 | tf_op jit(solution)/shard_map/ppermute | solution.py:37
  140.4 4.6 %collective-permute-start.14 = (f32[32,128]{1,0:T(8,128)S(1)}, f32[32,128]{1,0:T(8,128)S(1)}, u32[]{:S(2)}, u32[]{:S(2)}) collective-permute-start(f32[32,128]{1,0:T(8,128)S(1)} %add.107), channel_id=1, source_target_pairs={{0,4},{2,6},{4,0},{6,2},{8,12},{10,14},{12,8},{14,10},{1,5},{3,7},... | collective-permute-start | bytes 49160 | tf_op jit(solution)/shard_map/ppermute | solution.py:37
  145.1 7.6 %collective-permute-start.15 = (f32[32,128]{1,0:T(8,128)S(1)}, f32[32,128]{1,0:T(8,128)S(1)}, u32[]{:S(2)}, u32[]{:S(2)}) collective-permute-start(f32[32,128]{1,0:T(8,128)S(1)} %add.108), channel_id=1, source_target_pairs={{0,8},{2,10},{4,12},{6,14},{8,0},{10,2},{12,4},{14,6},{1,9},{3,11}... | collective-permute-start | bytes 49160 | tf_op jit(solution)/shard_map/ppermute | solution.py:37
  269.8 1.8 collective-permute-start.16
  272.5 8.7 %collective-permute-start.17 = (f32[264,256]{1,0:T(8,128)S(1)}, f32[264,256]{1,0:T(8,128)S(1)}, u32[]{:S(2)}, u32[]{:S(2)}) collective-permute-start(f32[264,256]{1,0:T(8,128)S(1)} %add.112), channel_id=1, source_target_pairs={{0,32},{32,0},{64,96},{96,64},{1,33},{33,1},{65,97},{97,65},{2,34}... | collective-permute-start | bytes 811016 | tf_op jit(solution)/shard_map/ppermute | solution.py:37
  281.3 9.4 %collective-permute-start.18 = (f32[264,256]{1,0:T(8,128)S(1)}, f32[264,256]{1,0:T(8,128)S(1)}, u32[]{:S(2)}, u32[]{:S(2)}) collective-permute-start(f32[264,256]{1,0:T(8,128)S(1)} %add.113), channel_id=1, source_target_pairs={{0,64},{32,96},{64,0},{96,32},{1,65},{33,97},{65,1},{97,33},{2,66}... | collective-permute-start | bytes 811016 | tf_op jit(solution)/shard_map/ppermute | solution.py:37
  290.8 8.5 %collective-permute-start.19 = (f32[264,256]{1,0:T(8,128)S(1)}, f32[264,256]{1,0:T(8,128)S(1)}, u32[]{:S(2)}, u32[]{:S(2)}) collective-permute-start(f32[264,256]{1,0:T(8,128)S(1)} %add.114), channel_id=1, source_target_pairs={{0,128},{128,0},{1,129},{129,1},{2,130},{130,2},{3,131},{131,3},{4... | collective-permute-start | bytes 811016 | tf_op jit(solution)/shard_map/ppermute | solution.py:37
Sparse Core Ops, SparseCore 0:
  15.5 44.0 all-gather.1
  169.4 100.3 reduce-scatter.1

commit v6 on v5

--- a/solution.py
+++ b/solution.py
@@ -47,12 +47,13 @@
     return jnp.exp(scores * inv_width - OFFSET) * inv_count
 
 
-def sweep_body(nbr, inv_width, inv_count, bary, links_ref, xn_ref, cn_ref, scale_ref, mass_ref,
-               *rest):
-    if bary:
-        rows_ref, ds_ref, ws_ref, kbuf = rest
+def sweep_body(nbr, inv_width, inv_count, bary, first, links_ref, *refs):
+    if first:
+        xn_ref, cn_ref, scale_ref, mass_ref, ds_ref, ct_ref, kbuf = refs
+    elif bary:
+        kbuf, scale_ref, mass_ref, rows_ref, ds_ref, ws_ref = refs
     else:
-        ds_ref, ct_ref, kbuf = rest
+        kbuf, scale_ref, mass_ref, ds_ref, ct_ref = refs
     b = pl.program_id(0)
 
     @pl.when(b == 0)
@@ -62,12 +63,16 @@
         else:
             ct_ref[...] = jnp.zeros_like(ct_ref)
 
-    xn = xn_ref[...]
     acc = jnp.zeros((BLOCK, BLOCK), jnp.float32)
+    if first:
+        xn = xn_ref[...]
     for s in range(nbr):
         blk = links_ref[b, s]
-        k = _kernel_slot(xn, cn_ref, blk, inv_width, inv_count)
-        kbuf[s] = k
+        if first:
+            k = _kernel_slot(xn, cn_ref, blk, inv_width, inv_count)
+            kbuf[s] = k
+        else:
+            k = kbuf[s]
         acc = acc + k * scale_ref[pl.ds(blk, 1), :]
     row_total = jnp.sum(acc, axis=1, keepdims=True)
     ds = mass_ref[...] / row_total
@@ -90,41 +95,58 @@
             ct_ref[pl.ds(blk, 1), :] += part
 
 
-def sweep(xn, cn_blocks, scale_blocks, mass_col, links, rows=None):
-    local_rows, feature_count = xn.shape
-    block_count = cn_blocks.shape[0]
+def sweep(links, scale_blocks, mass_col, xn=None, cn_blocks=None, kern=None, rows=None):
     local_blocks, nbr = links.shape
+    local_rows = local_blocks * BLOCK
+    block_count = scale_blocks.shape[0]
+    feature_count = 256 if rows is None else rows.shape[1]
+    first = kern is None
     bary = rows is not None
-    inv_width = 1.0 / (feature_count * EPS)
-    inv_count = 1.0 / (nbr * BLOCK)
-    in_specs = [
-        pl.BlockSpec((BLOCK, feature_count), lambda b, L: (b, 0)),
-        pl.BlockSpec((block_count, BLOCK, feature_count), lambda b, L: (0, 0, 0)),
+    k_spec = pl.BlockSpec((nbr, BLOCK, BLOCK), lambda b, L: (b, 0, 0))
+    k_shape = jax.ShapeDtypeStruct((local_blocks * nbr, BLOCK, BLOCK), jnp.float32)
+    small = [
         pl.BlockSpec((block_count, BLOCK), lambda b, L: (0, 0)),
         pl.BlockSpec((BLOCK, 1), lambda b, L: (b, 0)),
     ]
     out_specs = [pl.BlockSpec((BLOCK, 1), lambda b, L: (b, 0))]
     out_shape = [jax.ShapeDtypeStruct((local_rows, 1), jnp.float32)]
-    packed_rows = 2 * BLOCK + PAD
-    args = [links, xn, cn_blocks, scale_blocks, mass_col]
-    if bary:
-        in_specs.append(pl.BlockSpec((BLOCK, feature_count), lambda b, L: (b, 0)))
+    ct_spec = pl.BlockSpec((block_count, BLOCK), lambda b, L: (0, 0))
+    ct_shape = jax.ShapeDtypeStruct((block_count, BLOCK), jnp.float32)
+    flops = 6 * local_rows * nbr * BLOCK
+    transcendentals = 0
+    if first:
+        feature_count = xn.shape[1]
+        in_specs = [
+            pl.BlockSpec((BLOCK, feature_count), lambda b, L: (b, 0)),
+            pl.BlockSpec((block_count, BLOCK, feature_count), lambda b, L: (0, 0, 0)),
+        ] + small
+        args = [links, xn, cn_blocks, scale_blocks, mass_col]
+        out_specs += [ct_spec, k_spec]
+        out_shape += [ct_shape, k_shape]
+        flops += 2 * local_rows * nbr * BLOCK * feature_count
+        transcendentals = local_rows * nbr * BLOCK
+    elif bary:
+        packed_rows = 2 * BLOCK + PAD
         packed = (block_count // 2, packed_rows, feature_count)
+        in_specs = [k_spec] + small + [pl.BlockSpec((BLOCK, feature_count), lambda b, L: (b, 0))]
+        args = [links, kern, scale_blocks, mass_col, rows]
         out_specs.append(pl.BlockSpec(packed, lambda b, L: (0, 0, 0)))
         out_shape.append(jax.ShapeDtypeStruct(packed, jnp.float32))
-        args.append(rows)
+        flops += 2 * local_rows * nbr * BLOCK * feature_count
     else:
-        out_specs.append(pl.BlockSpec((block_count, BLOCK), lambda b, L: (0, 0)))
-        out_shape.append(jax.ShapeDtypeStruct((block_count, BLOCK), jnp.float32))
-    flops = 2 * local_rows * nbr * BLOCK * feature_count * (2 if bary else 1)
+        in_specs = [k_spec] + small
+        args = [links, kern, scale_blocks, mass_col]
+        out_specs.append(ct_spec)
+        out_shape.append(ct_shape)
+    inv_width = 1.0 / (feature_count * EPS)
+    inv_count = 1.0 / (nbr * BLOCK)
     return pl.pallas_call(
-        functools.partial(sweep_body, nbr, inv_width, inv_count, bary),
+        functools.partial(sweep_body, nbr, inv_width, inv_count, bary, first),
         grid_spec=pltpu.PrefetchScalarGridSpec(
             num_scalar_prefetch=1,
             grid=(local_blocks,),
             in_specs=in_specs,
             out_specs=out_specs,
-            scratch_shapes=[pltpu.VMEM((nbr, BLOCK, BLOCK), jnp.float32)],
         ),
         out_shape=out_shape,
         compiler_params=pltpu.CompilerParams(
@@ -132,9 +154,8 @@
         ),
         cost_estimate=pl.CostEstimate(
             flops=flops,
-            transcendentals=local_rows * nbr * BLOCK,
-            bytes_accessed=block_count * BLOCK * feature_count * (2 + (4 if bary else 0))
-            + local_rows * feature_count * (4 if bary else 2),
+            transcendentals=transcendentals,
+            bytes_accessed=local_rows * nbr * BLOCK * 4 + block_count * BLOCK * feature_count * 4,
         ),
     )(*args)
 
@@ -157,11 +178,15 @@
     mass_col = data_mass.reshape(local_rows, 1)
     links = block_links.astype(jnp.int32)
     scale_blocks = jnp.ones((block_count, BLOCK), jnp.float32)
+    kern = None
     for sweep_index in range(ITERS - 1):
-        _, part_total = sweep(xn, cn_blocks, scale_blocks, mass_col, links)
+        if kern is None:
+            _, part_total, kern = sweep(links, scale_blocks, mass_col, xn=xn, cn_blocks=cn_blocks)
+        else:
+            _, part_total = sweep(links, scale_blocks, mass_col, kern=kern)
         whole_total = butterfly_sum(part_total, TOTAL_ORDER, sizes)
         scale_blocks = mass_ratio * cand_mass.reshape(block_count, BLOCK) / whole_total
-    ds_col, packed = sweep(xn, cn_blocks, scale_blocks, mass_col, links, rows=data_rows)
+    ds_col, packed = sweep(links, scale_blocks, mass_col, kern=kern, rows=data_rows)
     joined = lax.psum_scatter(packed.reshape(-1, feature_count), COL_AXES, scatter_dimension=0, tiled=True)
     joined = butterfly_sum(joined, ("c", "x", "yh"), sizes)
     own_sums = joined[:local_cands]

time: 308 us -> 310 us (level)
  no operation moved by 1% of the time
where the time goes in v6:
time: 310 us; the launch traced here: 309 us
  waiting for transfers between devices  212 us (68%)
  Pallas kernels  38.9 us (13%)
  starting transfers between devices  29.5 us (10%)
  between operations  14.2 us (5%)
  other arithmetic  6.14 us (2%)
  blocking collectives  6.02 us (2%)
    reduce_scatter x1, waiting for transfers between devices, on_device(): lax.psum_scatter(packed.reshape(-1, feature_count), COL_AXES, scatter_dim...  101 us
    ppermute x20, waiting for transfers between devices, butterfly_sum(): x = x + lax.ppermute(x, axis, [(j, j ^ k) for j in range(n)])  68.7 us
    all_gather x1, waiting for transfers between devices, on_device(): lax.all_gather(lax.all_gather(normalize(cand_rows), 'yl', axis=0, tiled=T...  42.6 us
    pallas_call x3, Pallas kernels, sweep(): pl.pallas_call(functools.partial(sweep_body, nbr, inv_width, inv_count, b...  38.9 us
    ppermute x20, starting transfers between devices, butterfly_sum(): x = x + lax.ppermute(x, axis, [(j, j ^ k) for j in range(n)])  29.4 us
  transfers between devices with their start and end apart: 22, of which 22 were waited for; matrix products, arithmetic and copies ran while one was open for 1% of the time, Pallas kernels for 0%

profile of v6, /device:TPU:4, one launch (start us, length us, event | category | flops | bytes accessed | tf_op | source)
XLA Modules:
  0.0 309.2 jit_solution(1327737502261341136)
XLA Ops:
  7.2 0.0 copy-start
  7.2 0.0 all-gather.2.cloned.1.call-start
  7.2 1.1 fusion.2
  8.3 1.0 fusion.3
  9.3 6.0 %all_gather.6 = bf16[512,256]{1,0:T(8,128)(2,1)} all-gather(bf16[256,256]{1,0:T(8,128)(2,1)S(1)} %fusion.3), channel_id=1, replica_groups=mesh['yh'=2,'x'=4,'c'=2,'z'=8,'yl'=2] {'yl'}, dimensions={0}, use_global_device_ids=true | all-gather | bytes 393216 | tf_op jit(solution)/shard_map/all_gather | solution.py:174
  15.4 0.0 all-gather.2.cloned.1.call-update
  15.4 0.0 copy-start.1
  15.4 0.0 reduce-scatter.2.cloned.1.call-start
  15.4 1.0 reshape.43.refs_3_.refs_2_
  16.4 0.0 copy-done
  16.4 0.3 fusion
  16.7 0.3 fusion.1.refs_0_
  17.0 42.6 %all-gather.2.cloned.1.call-done = bf16[4096,256]{1,0:T(8,128)(2,1)} async-done(((bf16[512,256]{1,0:T(8,128)(2,1)}), bf16[4096,256]{1,0:T(8,128)(2,1)}) %all-gather.2.cloned.1.call-update) | async-done | bytes 2097168 | tf_op jit(solution)/shard_map/all_gather | solution.py:173
  59.6 0.0 copy-done.1
  59.6 1.6 copy-done.2
  61.2 11.5 %shard_map.76 = (f32[1536,1]{1,0:T(8,128)}, f32[32,128]{1,0:T(8,128)S(1)}, f32[192,128,128]{2,1,0:T(8,128)}) custom-call(s32[12,16]{1,0:T(8,128)S(1)} %copy-done.1, bf16[1536,256]{1,0:T(8,128)(2,1)S(1)} %fusion.1.refs_0_, bf16[32,128,256]{2,1,0:T(8,128)(2,1)S(1)} %bitcast.6, f32[32,128]{1,0:T(8,128)S(1)} %broadcast_in_dim.2.refs_2_, ...), custom_call_target="tpu_custom_call" | custom-call | flops 1629487104 | bytes 16777216 | tf_op jit(solution)/shard_map/pallas_call | solution.py:143
  72.7 0.0 collective-permute-start
  72.7 1.2 collective-permute-done
  73.9 1.5 collective-permute-start.1
  75.4 2.3 collective-permute-done.1
  77.7 3.0 collective-permute-start.2
  80.7 2.2 collective-permute-done.2
  82.9 1.2 collective-permute-start.3
  84.1 2.7 collective-permute-done.3
  86.7 0.5 collective-permute-start.4
  87.2 4.8 %collective-permute-done.4 = f32[32,128]{1,0:T(8,128)S(1)} collective-permute-done((f32[32,128]{1,0:T(8,128)S(1)}, f32[32,128]{1,0:T(8,128)S(1)}, u32[]{:S(2)}, u32[]{:S(2)}) %collective-permute-start.4) | collective-permute-done | bytes 16416 | tf_op jit(solution)/shard_map/ppermute | solution.py:37
  92.0 1.2 collective-permute-start.5
  93.2 2.5 collective-permute-done.5
  95.7 1.2 collective-permute-start.6
  97.0 3.4 %collective-permute-done.6 = f32[32,128]{1,0:T(8,128)S(1)} collective-permute-done((f32[32,128]{1,0:T(8,128)S(1)}, f32[32,128]{1,0:T(8,128)S(1)}, u32[]{:S(2)}, u32[]{:S(2)}) %collective-permute-start.6) | collective-permute-done | bytes 16416 | tf_op jit(solution)/shard_map/ppermute | solution.py:37
  100.4 3.0 collective-permute-start.7
  103.4 4.7 %collective-permute-done.7 = f32[32,128]{1,0:T(8,128)S(1)} collective-permute-done((f32[32,128]{1,0:T(8,128)S(1)}, f32[32,128]{1,0:T(8,128)S(1)}, u32[]{:S(2)}, u32[]{:S(2)}) %collective-permute-start.7) | collective-permute-done | bytes 16416 | tf_op jit(solution)/shard_map/ppermute | solution.py:37
  108.0 11.4 %shard_map.77 = (f32[1536,1]{1,0:T(8,128)}, f32[32,128]{1,0:T(8,128)S(1)}) custom-call(s32[12,16]{1,0:T(8,128)S(1)} %copy-done.1, f32[192,128,128]{2,1,0:T(8,128)} %get-tuple-element.8.refs_0_, f32[32,128]{1,0:T(8,128)S(1)} %bitcast_divide_fusion.1.refs_1_, f32[1536,1]{1,0:T(8,128)S(1)} %reshape.43.refs_3_.refs_2_), custom_call_target="tpu_custom_call" | custom-call | flops 18874368 | bytes 16777216 | tf_op jit(solution)/shard_map/pallas_call | solution.py:143
  119.4 0.0 collective-permute-start.8
  119.4 1.2 collective-permute-done.8
  120.6 1.5 collective-permute-start.9
  122.1 2.2 collective-permute-done.9
  124.4 3.0 collective-permute-start.10
  127.4 2.2 collective-permute-done.10
  129.6 1.1 collective-permute-start.11
  130.7 2.8 collective-permute-done.11
  133.5 0.3 collective-permute-start.12
  133.8 4.9 %collective-permute-done.12 = f32[32,128]{1,0:T(8,128)S(1)} collective-permute-done((f32[32,128]{1,0:T(8,128)S(1)}, f32[32,128]{1,0:T(8,128)S(1)}, u32[]{:S(2)}, u32[]{:S(2)}) %collective-permute-start.12) | collective-permute-done | bytes 16416 | tf_op jit(solution)/shard_map/ppermute | solution.py:37
  138.8 1.1 collective-permute-start.13
  139.9 2.6 collective-permute-done.13
  142.5 1.3 collective-permute-start.14
  143.8 3.4 %collective-permute-done.14 = f32[32,128]{1,0:T(8,128)S(1)} collective-permute-done((f32[32,128]{1,0:T(8,128)S(1)}, f32[32,128]{1,0:T(8,128)S(1)}, u32[]{:S(2)}, u32[]{:S(2)}) %collective-permute-start.14) | collective-permute-done | bytes 16416 | tf_op jit(solution)/shard_map/ppermute | solution.py:37
  147.2 3.0 collective-permute-start.15
  150.2 4.6 %collective-permute-done.15 = f32[32,128]{1,0:T(8,128)S(1)} collective-permute-done((f32[32,128]{1,0:T(8,128)S(1)}, f32[32,128]{1,0:T(8,128)S(1)}, u32[]{:S(2)}, u32[]{:S(2)}) %collective-permute-start.15) | collective-permute-done | bytes 16416 | tf_op jit(solution)/shard_map/ppermute | solution.py:37
  154.8 16.0 %shard_map.78 = (f32[1536,1]{1,0:T(8,128)S(1)}, f32[16,264,256]{2,1,0:T(8,128)}) custom-call(s32[12,16]{1,0:T(8,128)S(1)} %copy-done.1, f32[192,128,128]{2,1,0:T(8,128)} %get-tuple-element.8.refs_0_, f32[32,128]{1,0:T(8,128)S(1)} %bitcast_divide_fusion.refs_1_, f32[1536,1]{1,0:T(8,128)S(1)} %reshape.43.refs_3_.refs_2_, bf16[1536,256]{1,0:T(8,128)(2,1)S(1)} %copy-done), custom_call_target="tpu_custom_call" | custom-call | flops 1629487104 | bytes 16777216 | tf_op jit(solution)/shard_map/pallas_call | solution.py:143
  170.8 0.0 reduce-scatter.2.cloned.1.call-update
  170.8 100.6 %reduce-scatter.2.cloned.1.call-done = f32[264,256]{1,0:T(8,128)} async-done(((f32[4224,256]{1,0:T(8,128)}), f32[264,256]{1,0:T(8,128)}) %reduce-scatter.2.cloned.1.call-update) | async-done | bytes 270352 | tf_op jit(solution)/shard_map/reduce_scatter | solution.py:190
  271.4 0.0 collective-permute-start.16
  271.4 1.8 collective-permute-done.16
  273.1 1.0 add.112
  274.1 1.9 collective-permute-start.17
  276.1 6.8 %collective-permute-done.17 = f32[264,256]{1,0:T(8,128)S(1)} collective-permute-done((f32[264,256]{1,0:T(8,128)S(1)}, f32[264,256]{1,0:T(8,128)S(1)}, u32[]{:S(2)}, u32[]{:S(2)}) %collective-permute-start.17) | collective-permute-done | bytes 270368 | tf_op jit(solution)/shard_map/ppermute | solution.py:37
  282.9 1.2 collective-permute-start.18
  284.1 8.2 %collective-permute-done.18 = f32[264,256]{1,0:T(8,128)S(1)} collective-permute-done((f32[264,256]{1,0:T(8,128)S(1)}, f32[264,256]{1,0:T(8,128)S(1)}, u32[]{:S(2)}, u32[]{:S(2)}) %collective-permute-start.18) | collective-permute-done | bytes 270368 | tf_op jit(solution)/shard_map/ppermute | solution.py:37
  292.4 3.4 %collective-permute-start.19 = (f32[264,256]{1,0:T(8,128)S(1)}, f32[264,256]{1,0:T(8,128)S(1)}, u32[]{:S(2)}, u32[]{:S(2)}) collective-permute-start(f32[264,256]{1,0:T(8,128)S(1)} %add.114), channel_id=1, source_target_pairs={{0,128},{128,0},{1,129},{129,1},{2,130},{130,2},{3,131},{131,3},{4... | collective-permute-start | bytes 811016 | tf_op jit(solution)/shard_map/ppermute | solution.py:37
  295.7 0.9 reduce
  296.6 4.2 %collective-permute-done.19 = f32[264,256]{1,0:T(8,128)S(1)} collective-permute-done((f32[264,256]{1,0:T(8,128)S(1)}, f32[264,256]{1,0:T(8,128)S(1)}, u32[]{:S(2)}, u32[]{:S(2)}) %collective-permute-start.19) | collective-permute-done | bytes 270368 | tf_op jit(solution)/shard_map/ppermute | solution.py:37
  300.9 0.8 slice_divide_fusion
  301.7 0.6 multiply_divide_fusion
  (26 shorter events, 0.2 us)
Async XLA Ops:
  7.2 9.2 %copy-start = (bf16[1536,256]{1,0:T(8,128)(2,1)S(1)}, bf16[1536,256]{1,0:T(8,128)(2,1)}, u32[]{:S(2)}) copy-start(bf16[1536,256]{1,0:T(8,128)(2,1)} %refs_3_.1) | copy-start | bytes 2359300
  7.2 52.4 %all-gather.2.cloned.1.call-start = ((), (), s32[]{:S(2)}) async-start(), calls=%async_computation.1 | async-start | bytes 2359296 | tf_op jit(solution)/shard_map/all_gather | solution.py:173
  15.4 44.2 %copy-start.1 = (s32[12,16]{1,0:T(8,128)S(1)}, s32[12,16]{1,0:T(8,128)}, u32[]{:S(2)}) copy-start(s32[12,16]{1,0:T(8,128)} %links_ref.5) | copy-start | bytes 2308
  15.4 256.0 %reduce-scatter.2.cloned.1.call-start = ((), (), s32[]{:S(2)}) async-start(), calls=%async_computation.2 | async-start | bytes 4595712 | tf_op jit(solution)/shard_map/reduce_scatter | solution.py:190
  59.6 1.6 copy-start.2
  61.2 46.8 %copy-start.3 = (f32[4096]{0:T(1024)S(1)}, f32[4096]{0:T(1024)}, u32[]{:S(2)}) copy-start(f32[4096]{0:T(1024)} %param.9) | copy-start | bytes 49156
  72.7 1.2 collective-permute-start
  73.9 3.7 %collective-permute-start.1 = (f32[32,128]{1,0:T(8,128)S(1)}, f32[32,128]{1,0:T(8,128)S(1)}, u32[]{:S(2)}, u32[]{:S(2)}) collective-permute-start(f32[32,128]{1,0:T(8,128)S(1)} %add.94), channel_id=1, source_target_pairs={{0,1},{1,0},{2,3},{3,2},{4,5},{5,4},{6,7},{7,6},{8,9},{9,8},{10,11... | collective-permute-start | bytes 49160 | tf_op jit(solution)/shard_map/ppermute | solution.py:37
  77.7 5.2 %collective-permute-start.2 = (f32[32,128]{1,0:T(8,128)S(1)}, f32[32,128]{1,0:T(8,128)S(1)}, u32[]{:S(2)}, u32[]{:S(2)}) collective-permute-start(f32[32,128]{1,0:T(8,128)S(1)} %add.95), channel_id=1, source_target_pairs={{0,128},{128,0},{1,129},{129,1},{2,130},{130,2},{3,131},{131,3},{4... | collective-permute-start | bytes 49160 | tf_op jit(solution)/shard_map/ppermute | solution.py:37
  82.9 3.8 %collective-permute-start.3 = (f32[32,128]{1,0:T(8,128)S(1)}, f32[32,128]{1,0:T(8,128)S(1)}, u32[]{:S(2)}, u32[]{:S(2)}) collective-permute-start(f32[32,128]{1,0:T(8,128)S(1)} %add.96), channel_id=1, source_target_pairs={{0,32},{32,0},{64,96},{96,64},{1,33},{33,1},{65,97},{97,65},{2,34}... | collective-permute-start | bytes 49160 | tf_op jit(solution)/shard_map/ppermute | solution.py:37
  86.7 5.2 %collective-permute-start.4 = (f32[32,128]{1,0:T(8,128)S(1)}, f32[32,128]{1,0:T(8,128)S(1)}, u32[]{:S(2)}, u32[]{:S(2)}) collective-permute-start(f32[32,128]{1,0:T(8,128)S(1)} %add.97), channel_id=1, source_target_pairs={{0,64},{32,96},{64,0},{96,32},{1,65},{33,97},{65,1},{97,33},{2,66}... | collective-permute-start | bytes 49160 | tf_op jit(solution)/shard_map/ppermute | solution.py:37
  92.0 3.7 %collective-permute-start.5 = (f32[32,128]{1,0:T(8,128)S(1)}, f32[32,128]{1,0:T(8,128)S(1)}, u32[]{:S(2)}, u32[]{:S(2)}) collective-permute-start(f32[32,128]{1,0:T(8,128)S(1)} %add.98), channel_id=1, source_target_pairs={{0,2},{2,0},{4,6},{6,4},{8,10},{10,8},{12,14},{14,12},{1,3},{3,1},... | collective-permute-start | bytes 49160 | tf_op jit(solution)/shard_map/ppermute | solution.py:37
  95.7 4.6 %collective-permute-start.6 = (f32[32,128]{1,0:T(8,128)S(1)}, f32[32,128]{1,0:T(8,128)S(1)}, u32[]{:S(2)}, u32[]{:S(2)}) collective-permute-start(f32[32,128]{1,0:T(8,128)S(1)} %add.99), channel_id=1, source_target_pairs={{0,4},{2,6},{4,0},{6,2},{8,12},{10,14},{12,8},{14,10},{1,5},{3,7},... | collective-permute-start | bytes 49160 | tf_op jit(solution)/shard_map/ppermute | solution.py:37
  100.4 7.6 %collective-permute-start.7 = (f32[32,128]{1,0:T(8,128)S(1)}, f32[32,128]{1,0:T(8,128)S(1)}, u32[]{:S(2)}, u32[]{:S(2)}) collective-permute-start(f32[32,128]{1,0:T(8,128)S(1)} %add.100), channel_id=1, source_target_pairs={{0,8},{2,10},{4,12},{6,14},{8,0},{10,2},{12,4},{14,6},{1,9},{3,11}... | collective-permute-start | bytes 49160 | tf_op jit(solution)/shard_map/ppermute | solution.py:37
  119.4 1.2 collective-permute-start.8
  120.6 3.7 %collective-permute-start.9 = (f32[32,128]{1,0:T(8,128)S(1)}, f32[32,128]{1,0:T(8,128)S(1)}, u32[]{:S(2)}, u32[]{:S(2)}) collective-permute-start(f32[32,128]{1,0:T(8,128)S(1)} %add.102), channel_id=1, source_target_pairs={{0,1},{1,0},{2,3},{3,2},{4,5},{5,4},{6,7},{7,6},{8,9},{9,8},{10,11... | collective-permute-start | bytes 49160 | tf_op jit(solution)/shard_map/ppermute | solution.py:37
  124.4 5.2 %collective-permute-start.10 = (f32[32,128]{1,0:T(8,128)S(1)}, f32[32,128]{1,0:T(8,128)S(1)}, u32[]{:S(2)}, u32[]{:S(2)}) collective-permute-start(f32[32,128]{1,0:T(8,128)S(1)} %add.103), channel_id=1, source_target_pairs={{0,128},{128,0},{1,129},{129,1},{2,130},{130,2},{3,131},{131,3},{4... | collective-permute-start | bytes 49160 | tf_op jit(solution)/shard_map/ppermute | solution.py:37
  129.6 3.9 %collective-permute-start.11 = (f32[32,128]{1,0:T(8,128)S(1)}, f32[32,128]{1,0:T(8,128)S(1)}, u32[]{:S(2)}, u32[]{:S(2)}) collective-permute-start(f32[32,128]{1,0:T(8,128)S(1)} %add.104), channel_id=1, source_target_pairs={{0,32},{32,0},{64,96},{96,64},{1,33},{33,1},{65,97},{97,65},{2,34}... | collective-permute-start | bytes 49160 | tf_op jit(solution)/shard_map/ppermute | solution.py:37
  133.5 5.2 %collective-permute-start.12 = (f32[32,128]{1,0:T(8,128)S(1)}, f32[32,128]{1,0:T(8,128)S(1)}, u32[]{:S(2)}, u32[]{:S(2)}) collective-permute-start(f32[32,128]{1,0:T(8,128)S(1)} %add.105), channel_id=1, source_target_pairs={{0,64},{32,96},{64,0},{96,32},{1,65},{33,97},{65,1},{97,33},{2,66}... | collective-permute-start | bytes 49160 | tf_op jit(solution)/shard_map/ppermute | solution.py:37
  138.8 3.7 %collective-permute-start.13 = (f32[32,128]{1,0:T(8,128)S(1)}, f32[32,128]{1,0:T(8,128)S(1)}, u32[]{:S(2)}, u32[]{:S(2)}) collective-permute-start(f32[32,128]{1,0:T(8,128)S(1)} %add.106), channel_id=1, source_target_pairs={{0,2},{2,0},{4,6},{6,4},{8,10},{10,8},{12,14},{14,12},{1,3},{3,1},... | collective-permute-start | bytes 49160 | tf_op jit(solution)/shard_map/ppermute | solution.py:37
  142.5 4.6 %collective-permute-start.14 = (f32[32,128]{1,0:T(8,128)S(1)}, f32[32,128]{1,0:T(8,128)S(1)}, u32[]{:S(2)}, u32[]{:S(2)}) collective-permute-start(f32[32,128]{1,0:T(8,128)S(1)} %add.107), channel_id=1, source_target_pairs={{0,4},{2,6},{4,0},{6,2},{8,12},{10,14},{12,8},{14,10},{1,5},{3,7},... | collective-permute-start | bytes 49160 | tf_op jit(solution)/shard_map/ppermute | solution.py:37
  147.2 7.6 %collective-permute-start.15 = (f32[32,128]{1,0:T(8,128)S(1)}, f32[32,128]{1,0:T(8,128)S(1)}, u32[]{:S(2)}, u32[]{:S(2)}) collective-permute-start(f32[32,128]{1,0:T(8,128)S(1)} %add.108), channel_id=1, source_target_pairs={{0,8},{2,10},{4,12},{6,14},{8,0},{10,2},{12,4},{14,6},{1,9},{3,11}... | collective-permute-start | bytes 49160 | tf_op jit(solution)/shard_map/ppermute | solution.py:37
  271.4 1.8 collective-permute-start.16
  274.1 8.7 %collective-permute-start.17 = (f32[264,256]{1,0:T(8,128)S(1)}, f32[264,256]{1,0:T(8,128)S(1)}, u32[]{:S(2)}, u32[]{:S(2)}) collective-permute-start(f32[264,256]{1,0:T(8,128)S(1)} %add.112), channel_id=1, source_target_pairs={{0,32},{32,0},{64,96},{96,64},{1,33},{33,1},{65,97},{97,65},{2,34}... | collective-permute-start | bytes 811016 | tf_op jit(solution)/shard_map/ppermute | solution.py:37
  282.9 9.4 %collective-permute-start.18 = (f32[264,256]{1,0:T(8,128)S(1)}, f32[264,256]{1,0:T(8,128)S(1)}, u32[]{:S(2)}, u32[]{:S(2)}) collective-permute-start(f32[264,256]{1,0:T(8,128)S(1)} %add.113), channel_id=1, source_target_pairs={{0,64},{32,96},{64,0},{96,32},{1,65},{33,97},{65,1},{97,33},{2,66}... | collective-permute-start | bytes 811016 | tf_op jit(solution)/shard_map/ppermute | solution.py:37
  292.4 8.5 %collective-permute-start.19 = (f32[264,256]{1,0:T(8,128)S(1)}, f32[264,256]{1,0:T(8,128)S(1)}, u32[]{:S(2)}, u32[]{:S(2)}) collective-permute-start(f32[264,256]{1,0:T(8,128)S(1)} %add.114), channel_id=1, source_target_pairs={{0,128},{128,0},{1,129},{129,1},{2,130},{130,2},{3,131},{131,3},{4... | collective-permute-start | bytes 811016 | tf_op jit(solution)/shard_map/ppermute | solution.py:37
Sparse Core Ops, SparseCore 0:
  15.5 44.0 all-gather.1
  170.9 100.4 reduce-scatter.1

commit v7 on v5

--- a/solution.py
+++ b/solution.py
@@ -79,11 +79,11 @@
         k = kbuf[s]
         part = jnp.sum(k * ds, axis=0, keepdims=True)
         if bary:
-            q = blk // 2
-            half = pl.multiple_of((blk % 2) * BLOCK, BLOCK)
-            ws_ref[q, pl.ds(2 * BLOCK, 1), pl.ds(half, BLOCK)] += part
+            half_count = ws_ref.shape[0] // 2
+            slot = (blk % 2) * half_count + blk // 2
+            ws_ref[slot, pl.ds(BLOCK, 1), pl.ds(0, BLOCK)] += part
             w = (k * ds).astype(jnp.bfloat16)
-            ws_ref[q, pl.ds(half, BLOCK), :] += lax.dot_general(
+            ws_ref[slot, pl.ds(0, BLOCK), :] += lax.dot_general(
                 w, rows, (((0,), (0,)), ((), ())), preferred_element_type=jnp.float32
             )
         else:
@@ -105,11 +105,11 @@
     ]
     out_specs = [pl.BlockSpec((BLOCK, 1), lambda b, L: (b, 0))]
     out_shape = [jax.ShapeDtypeStruct((local_rows, 1), jnp.float32)]
-    packed_rows = 2 * BLOCK + PAD
+    packed_rows = BLOCK + PAD
     args = [links, xn, cn_blocks, scale_blocks, mass_col]
     if bary:
         in_specs.append(pl.BlockSpec((BLOCK, feature_count), lambda b, L: (b, 0)))
-        packed = (block_count // 2, packed_rows, feature_count)
+        packed = (block_count, packed_rows, feature_count)
         out_specs.append(pl.BlockSpec(packed, lambda b, L: (0, 0, 0)))
         out_shape.append(jax.ShapeDtypeStruct(packed, jnp.float32))
         args.append(rows)
@@ -162,10 +162,16 @@
         whole_total = butterfly_sum(part_total, TOTAL_ORDER, sizes)
         scale_blocks = mass_ratio * cand_mass.reshape(block_count, BLOCK) / whole_total
     ds_col, packed = sweep(xn, cn_blocks, scale_blocks, mass_col, links, rows=data_rows)
-    joined = lax.psum_scatter(packed.reshape(-1, feature_count), COL_AXES, scatter_dimension=0, tiled=True)
-    joined = butterfly_sum(joined, ("c", "x", "yh"), sizes)
-    own_sums = joined[:local_cands]
-    own_total = joined[local_cands]
+    joined = lax.psum_scatter(
+        packed.reshape(-1, feature_count), ("c",) + COL_AXES, scatter_dimension=0, tiled=True
+    )
+    joined = butterfly_sum(joined, ("x", "yh"), sizes)
+    other = lax.ppermute(joined, "c", [(0, 1), (1, 0)])
+    first_core = lax.axis_index("c") == 0
+    low = jnp.where(first_core, joined, other)
+    high = jnp.where(first_core, other, joined)
+    own_sums = jnp.concatenate([low[:BLOCK], high[:BLOCK]], axis=0)
+    own_total = jnp.concatenate([low[BLOCK, :BLOCK], high[BLOCK, :BLOCK]], axis=0)
     own_scale = mass_ratio * lax.dynamic_slice_in_dim(cand_mass, own_start, local_cands) / own_total
     new_support = own_sums / own_total[:, None]
     return (ds_col.reshape(local_rows), own_scale, new_support)

time: 308 us -> 337 us (1.094)
  waiting for transfers between devices: 212 us -> 240 us
    reduce_scatter x1, waiting for transfers between devices: 101 us -> 136 us  [on_device(): lax.psum_scatter(packed.reshape(-1, feature_count), ('c',) + COL_AXES, sc...]
    ppermute x20 -> x19, waiting for transfers between devices: 68.8 us -> 60.6 us  [butterfly_sum(): x = x + lax.ppermute(x, axis, [(j, j ^ k) for j in range(n)])]
    ppermute x20 -> x19, starting transfers between devices: 29.3 us -> 28.8 us  [butterfly_sum(): x = x + lax.ppermute(x, axis, [(j, j ^ k) for j in range(n)])]
where the time goes in v7:
time: 337 us; the launch traced here: 335 us
  waiting for transfers between devices  240 us (71%)
  Pallas kernels  37.5 us (11%)
  starting transfers between devices  28.9 us (9%)
  between operations  14.2 us (4%)
  other arithmetic  6.05 us (2%)
  blocking collectives  6.02 us (2%)
    reduce_scatter x1, waiting for transfers between devices, on_device(): lax.psum_scatter(packed.reshape(-1, feature_count), ('c',) + COL_AXES, sc...  136 us
    ppermute x19, waiting for transfers between devices, butterfly_sum(): x = x + lax.ppermute(x, axis, [(j, j ^ k) for j in range(n)])  60.6 us
    all_gather x1, waiting for transfers between devices, on_device(): lax.all_gather(lax.all_gather(normalize(cand_rows), 'yl', axis=0, tiled=T...  42.6 us
    pallas_call x3, Pallas kernels, sweep(): pl.pallas_call(functools.partial(sweep_body, nbr, inv_width, inv_count, b...  37.5 us
    ppermute x19, starting transfers between devices, butterfly_sum(): x = x + lax.ppermute(x, axis, [(j, j ^ k) for j in range(n)])  28.8 us
  transfers between devices with their start and end apart: 22, of which 22 were waited for; matrix products, arithmetic and copies ran while one was open for 1% of the time, Pallas kernels for 0%

profile of v7, /device:TPU:4, one launch (start us, length us, event | category | flops | bytes accessed | tf_op | source)
XLA Modules:
  0.0 334.9 jit_solution(7587502639766603904)
XLA Ops:
  7.2 0.0 copy-start
  7.2 0.0 all-gather.2.cloned.1.call-start
  7.2 1.1 fusion.2
  8.3 1.0 fusion.3
  9.3 6.0 %all_gather.6 = bf16[512,256]{1,0:T(8,128)(2,1)} all-gather(bf16[256,256]{1,0:T(8,128)(2,1)S(1)} %fusion.3), channel_id=1, replica_groups=mesh['yh'=2,'x'=4,'c'=2,'z'=8,'yl'=2] {'yl'}, dimensions={0}, use_global_device_ids=true | all-gather | bytes 393216 | tf_op jit(solution)/shard_map/all_gather | solution.py:153
  15.4 0.0 all-gather.2.cloned.1.call-update
  15.4 0.0 copy-start.2
  15.4 0.0 reduce-scatter.2.cloned.1.call-start
  15.4 1.0 reshape.43.mass_ref
  16.4 0.0 copy-done
  16.4 0.3 fusion
  16.7 0.3 fusion.1.xn_ref
  17.0 42.6 %all-gather.2.cloned.1.call-done = bf16[4096,256]{1,0:T(8,128)(2,1)} async-done(((bf16[512,256]{1,0:T(8,128)(2,1)}), bf16[4096,256]{1,0:T(8,128)(2,1)}) %all-gather.2.cloned.1.call-update) | async-done | bytes 2097168 | tf_op jit(solution)/shard_map/all_gather | solution.py:152
  59.6 0.0 copy-done.2
  59.6 1.6 copy-done.1
  61.2 10.4 %shard_map.76 = (f32[1536,1]{1,0:T(8,128)}, f32[32,128]{1,0:T(8,128)S(1)}) custom-call(s32[12,16]{1,0:T(8,128)S(1)} %copy-done.2, bf16[1536,256]{1,0:T(8,128)(2,1)S(1)} %fusion.1.xn_ref, bf16[32,128,256]{2,1,0:T(8,128)(2,1)S(1)} %bitcast.9, f32[32,128]{1,0:T(8,128)S(1)} %broadcast_in_dim.2.scale_ref, f32[1536,1]{1,0:T(8,128)S(1)} %reshape.43.mass_ref), custom_call_target="tpu_custom_call" | custom-call | flops 1610612736 | bytes 2883584 | tf_op jit(solution)/shard_map/pallas_call | solution.py:120
  71.6 0.0 collective-permute-start
  71.6 1.2 collective-permute-done
  72.8 1.5 collective-permute-start.1
  74.3 2.3 collective-permute-done.1
  76.5 3.0 collective-permute-start.2
  79.5 2.2 collective-permute-done.2
  81.8 1.2 collective-permute-start.3
  83.0 2.6 collective-permute-done.3
  85.6 0.5 collective-permute-start.4
  86.1 4.8 %collective-permute-done.4 = f32[32,128]{1,0:T(8,128)S(1)} collective-permute-done((f32[32,128]{1,0:T(8,128)S(1)}, f32[32,128]{1,0:T(8,128)S(1)}, u32[]{:S(2)}, u32[]{:S(2)}) %collective-permute-start.4) | collective-permute-done | bytes 16416 | tf_op jit(solution)/shard_map/ppermute | solution.py:37
  90.9 1.2 collective-permute-start.5
  92.1 2.5 collective-permute-done.5
  94.6 1.2 collective-permute-start.6
  95.8 3.4 %collective-permute-done.6 = f32[32,128]{1,0:T(8,128)S(1)} collective-permute-done((f32[32,128]{1,0:T(8,128)S(1)}, f32[32,128]{1,0:T(8,128)S(1)}, u32[]{:S(2)}, u32[]{:S(2)}) %collective-permute-start.6) | collective-permute-done | bytes 16416 | tf_op jit(solution)/shard_map/ppermute | solution.py:37
  99.2 3.0 collective-permute-start.7
  102.2 4.7 %collective-permute-done.7 = f32[32,128]{1,0:T(8,128)S(1)} collective-permute-done((f32[32,128]{1,0:T(8,128)S(1)}, f32[32,128]{1,0:T(8,128)S(1)}, u32[]{:S(2)}, u32[]{:S(2)}) %collective-permute-start.7) | collective-permute-done | bytes 16416 | tf_op jit(solution)/shard_map/ppermute | solution.py:37
  106.9 10.4 %shard_map.77 = (f32[1536,1]{1,0:T(8,128)}, f32[32,128]{1,0:T(8,128)S(1)}) custom-call(s32[12,16]{1,0:T(8,128)S(1)} %copy-done.2, bf16[1536,256]{1,0:T(8,128)(2,1)S(1)} %fusion.1.xn_ref, bf16[32,128,256]{2,1,0:T(8,128)(2,1)S(1)} %bitcast.10, f32[32,128]{1,0:T(8,128)S(1)} %bitcast_divide_fusion.1.scale_ref, f32[1536,1]{1,0:T(8,128)S(1)} %reshape.43.mass_ref), custom_call_target="tpu_custom_call" | custom-call | flops 1610612736 | bytes 2883584 | tf_op jit(solution)/shard_map/pallas_call | solution.py:120
  117.3 0.0 collective-permute-start.8
  117.3 1.2 collective-permute-done.8
  118.5 1.5 collective-permute-start.9
  120.0 2.3 collective-permute-done.9
  122.3 3.0 collective-permute-start.10
  125.3 2.2 collective-permute-done.10
  127.5 1.1 collective-permute-start.11
  128.6 2.8 collective-permute-done.11
  131.4 0.3 collective-permute-start.12
  131.7 5.0 %collective-permute-done.12 = f32[32,128]{1,0:T(8,128)S(1)} collective-permute-done((f32[32,128]{1,0:T(8,128)S(1)}, f32[32,128]{1,0:T(8,128)S(1)}, u32[]{:S(2)}, u32[]{:S(2)}) %collective-permute-start.12) | collective-permute-done | bytes 16416 | tf_op jit(solution)/shard_map/ppermute | solution.py:37
  136.7 1.1 collective-permute-start.13
  137.8 2.6 collective-permute-done.13
  140.4 1.2 collective-permute-start.14
  141.7 3.4 %collective-permute-done.14 = f32[32,128]{1,0:T(8,128)S(1)} collective-permute-done((f32[32,128]{1,0:T(8,128)S(1)}, f32[32,128]{1,0:T(8,128)S(1)}, u32[]{:S(2)}, u32[]{:S(2)}) %collective-permute-start.14) | collective-permute-done | bytes 16416 | tf_op jit(solution)/shard_map/ppermute | solution.py:37
  145.1 3.0 collective-permute-start.15
  148.0 4.7 %collective-permute-done.15 = f32[32,128]{1,0:T(8,128)S(1)} collective-permute-done((f32[32,128]{1,0:T(8,128)S(1)}, f32[32,128]{1,0:T(8,128)S(1)}, u32[]{:S(2)}, u32[]{:S(2)}) %collective-permute-start.15) | collective-permute-done | bytes 16416 | tf_op jit(solution)/shard_map/ppermute | solution.py:37
  152.7 16.7 %shard_map.78 = (f32[1536,1]{1,0:T(8,128)S(1)}, f32[32,136,256]{2,1,0:T(8,128)}) custom-call(s32[12,16]{1,0:T(8,128)S(1)} %copy-done.2, bf16[1536,256]{1,0:T(8,128)(2,1)S(1)} %fusion.1.xn_ref, bf16[32,128,256]{2,1,0:T(8,128)(2,1)S(1)} %bitcast.11, f32[32,128]{1,0:T(8,128)S(1)} %bitcast_divide_fusion.scale_ref, f32[1536,1]{1,0:T(8,128)S(1)} %reshape.43.mass_ref, ...), custom_call_target="tpu_custom_call" | custom-call | flops 3221225472 | bytes 7864320 | tf_op jit(solution)/shard_map/pallas_call | solution.py:120
  169.4 0.0 reduce-scatter.2.cloned.1.call-update
  169.4 135.9 %reduce-scatter.2.cloned.1.call-done = f32[136,256]{1,0:T(8,128)} async-done(((f32[4352,256]{1,0:T(8,128)}), f32[136,256]{1,0:T(8,128)}) %reduce-scatter.2.cloned.1.call-update) | async-done | bytes 139280 | tf_op jit(solution)/shard_map/reduce_scatter | solution.py:165
  305.4 0.9 collective-permute-start.16
  306.2 4.4 %collective-permute-done.16 = f32[136,256]{1,0:T(8,128)S(1)} collective-permute-done((f32[136,256]{1,0:T(8,128)}, f32[136,256]{1,0:T(8,128)S(1)}, u32[]{:S(2)}, u32[]{:S(2)}) %collective-permute-start.16) | collective-permute-done | bytes 139296 | tf_op jit(solution)/shard_map/ppermute | solution.py:37
  310.6 0.9 add.109
  311.6 1.3 collective-permute-start.17
  312.9 5.3 %collective-permute-done.17 = f32[136,256]{1,0:T(8,128)S(1)} collective-permute-done((f32[136,256]{1,0:T(8,128)S(1)}, f32[136,256]{1,0:T(8,128)S(1)}, u32[]{:S(2)}, u32[]{:S(2)}) %collective-permute-start.17) | collective-permute-done | bytes 139296 | tf_op jit(solution)/shard_map/ppermute | solution.py:37
  318.2 3.8 %collective-permute-start.18 = (f32[136,256]{1,0:T(8,128)S(1)}, f32[136,256]{1,0:T(8,128)S(1)}, u32[]{:S(2)}, u32[]{:S(2)}) collective-permute-start(f32[136,256]{1,0:T(8,128)S(1)} %add.110), channel_id=1, source_target_pairs={{0,128},{128,0},{1,129},{129,1},{2,130},{130,2},{3,131},{131,3},{4... | collective-permute-start | bytes 417800 | tf_op jit(solution)/shard_map/ppermute | solution.py:37
  322.0 3.0 collective-permute-done.18
  325.1 0.1 collective-permute-start.19
  325.2 0.9 reduce
  326.1 0.5 collective-permute-done.19
  326.6 0.6 pad_maximum_fusion
  327.3 0.8 maximum_divide_fusion
  (28 shorter events, 0.2 us)
Async XLA Ops:
  7.2 9.2 %copy-start = (bf16[1536,256]{1,0:T(8,128)(2,1)S(1)}, bf16[1536,256]{1,0:T(8,128)(2,1)}, u32[]{:S(2)}) copy-start(bf16[1536,256]{1,0:T(8,128)(2,1)} %rest_0_.1) | copy-start | bytes 2359300
  7.2 52.4 %all-gather.2.cloned.1.call-start = ((), (), s32[]{:S(2)}) async-start(), calls=%async_computation.1 | async-start | bytes 2359296 | tf_op jit(solution)/shard_map/all_gather | solution.py:152
  15.4 44.2 %copy-start.2 = (s32[12,16]{1,0:T(8,128)S(1)}, s32[12,16]{1,0:T(8,128)}, u32[]{:S(2)}) copy-start(s32[12,16]{1,0:T(8,128)} %links_ref.5) | copy-start | bytes 2308
  15.4 290.0 %reduce-scatter.2.cloned.1.call-start = ((), (), s32[]{:S(2)}) async-start(), calls=%async_computation.2 | async-start | bytes 4595712 | tf_op jit(solution)/shard_map/reduce_scatter | solution.py:165
  59.6 1.6 copy-start.1
  61.2 45.7 %copy-start.3 = (f32[4096]{0:T(1024)S(1)}, f32[4096]{0:T(1024)}, u32[]{:S(2)}) copy-start(f32[4096]{0:T(1024)} %param.9) | copy-start | bytes 49156
  71.6 1.2 collective-permute-start
  72.8 3.7 %collective-permute-start.1 = (f32[32,128]{1,0:T(8,128)S(1)}, f32[32,128]{1,0:T(8,128)S(1)}, u32[]{:S(2)}, u32[]{:S(2)}) collective-permute-start(f32[32,128]{1,0:T(8,128)S(1)} %add.91), channel_id=1, source_target_pairs={{0,1},{1,0},{2,3},{3,2},{4,5},{5,4},{6,7},{7,6},{8,9},{9,8},{10,11... | collective-permute-start | bytes 49160 | tf_op jit(solution)/shard_map/ppermute | solution.py:37
  76.5 5.2 %collective-permute-start.2 = (f32[32,128]{1,0:T(8,128)S(1)}, f32[32,128]{1,0:T(8,128)S(1)}, u32[]{:S(2)}, u32[]{:S(2)}) collective-permute-start(f32[32,128]{1,0:T(8,128)S(1)} %add.92), channel_id=1, source_target_pairs={{0,128},{128,0},{1,129},{129,1},{2,130},{130,2},{3,131},{131,3},{4... | collective-permute-start | bytes 49160 | tf_op jit(solution)/shard_map/ppermute | solution.py:37
  81.8 3.8 %collective-permute-start.3 = (f32[32,128]{1,0:T(8,128)S(1)}, f32[32,128]{1,0:T(8,128)S(1)}, u32[]{:S(2)}, u32[]{:S(2)}) collective-permute-start(f32[32,128]{1,0:T(8,128)S(1)} %add.93), channel_id=1, source_target_pairs={{0,32},{32,0},{64,96},{96,64},{1,33},{33,1},{65,97},{97,65},{2,34}... | collective-permute-start | bytes 49160 | tf_op jit(solution)/shard_map/ppermute | solution.py:37
  85.6 5.2 %collective-permute-start.4 = (f32[32,128]{1,0:T(8,128)S(1)}, f32[32,128]{1,0:T(8,128)S(1)}, u32[]{:S(2)}, u32[]{:S(2)}) collective-permute-start(f32[32,128]{1,0:T(8,128)S(1)} %add.94), channel_id=1, source_target_pairs={{0,64},{32,96},{64,0},{96,32},{1,65},{33,97},{65,1},{97,33},{2,66}... | collective-permute-start | bytes 49160 | tf_op jit(solution)/shard_map/ppermute | solution.py:37
  90.9 3.7 %collective-permute-start.5 = (f32[32,128]{1,0:T(8,128)S(1)}, f32[32,128]{1,0:T(8,128)S(1)}, u32[]{:S(2)}, u32[]{:S(2)}) collective-permute-start(f32[32,128]{1,0:T(8,128)S(1)} %add.95), channel_id=1, source_target_pairs={{0,2},{2,0},{4,6},{6,4},{8,10},{10,8},{12,14},{14,12},{1,3},{3,1},... | collective-permute-start | bytes 49160 | tf_op jit(solution)/shard_map/ppermute | solution.py:37
  94.6 4.6 %collective-permute-start.6 = (f32[32,128]{1,0:T(8,128)S(1)}, f32[32,128]{1,0:T(8,128)S(1)}, u32[]{:S(2)}, u32[]{:S(2)}) collective-permute-start(f32[32,128]{1,0:T(8,128)S(1)} %add.96), channel_id=1, source_target_pairs={{0,4},{2,6},{4,0},{6,2},{8,12},{10,14},{12,8},{14,10},{1,5},{3,7},... | collective-permute-start | bytes 49160 | tf_op jit(solution)/shard_map/ppermute | solution.py:37
  99.2 7.6 %collective-permute-start.7 = (f32[32,128]{1,0:T(8,128)S(1)}, f32[32,128]{1,0:T(8,128)S(1)}, u32[]{:S(2)}, u32[]{:S(2)}) collective-permute-start(f32[32,128]{1,0:T(8,128)S(1)} %add.97), channel_id=1, source_target_pairs={{0,8},{2,10},{4,12},{6,14},{8,0},{10,2},{12,4},{14,6},{1,9},{3,11}... | collective-permute-start | bytes 49160 | tf_op jit(solution)/shard_map/ppermute | solution.py:37
  117.3 1.2 collective-permute-start.8
  118.5 3.7 %collective-permute-start.9 = (f32[32,128]{1,0:T(8,128)S(1)}, f32[32,128]{1,0:T(8,128)S(1)}, u32[]{:S(2)}, u32[]{:S(2)}) collective-permute-start(f32[32,128]{1,0:T(8,128)S(1)} %add.99), channel_id=1, source_target_pairs={{0,1},{1,0},{2,3},{3,2},{4,5},{5,4},{6,7},{7,6},{8,9},{9,8},{10,11... | collective-permute-start | bytes 49160 | tf_op jit(solution)/shard_map/ppermute | solution.py:37
  122.3 5.2 %collective-permute-start.10 = (f32[32,128]{1,0:T(8,128)S(1)}, f32[32,128]{1,0:T(8,128)S(1)}, u32[]{:S(2)}, u32[]{:S(2)}) collective-permute-start(f32[32,128]{1,0:T(8,128)S(1)} %add.100), channel_id=1, source_target_pairs={{0,128},{128,0},{1,129},{129,1},{2,130},{130,2},{3,131},{131,3},{4... | collective-permute-start | bytes 49160 | tf_op jit(solution)/shard_map/ppermute | solution.py:37
  127.5 3.9 %collective-permute-start.11 = (f32[32,128]{1,0:T(8,128)S(1)}, f32[32,128]{1,0:T(8,128)S(1)}, u32[]{:S(2)}, u32[]{:S(2)}) collective-permute-start(f32[32,128]{1,0:T(8,128)S(1)} %add.101), channel_id=1, source_target_pairs={{0,32},{32,0},{64,96},{96,64},{1,33},{33,1},{65,97},{97,65},{2,34}... | collective-permute-start | bytes 49160 | tf_op jit(solution)/shard_map/ppermute | solution.py:37
  131.4 5.2 %collective-permute-start.12 = (f32[32,128]{1,0:T(8,128)S(1)}, f32[32,128]{1,0:T(8,128)S(1)}, u32[]{:S(2)}, u32[]{:S(2)}) collective-permute-start(f32[32,128]{1,0:T(8,128)S(1)} %add.102), channel_id=1, source_target_pairs={{0,64},{32,96},{64,0},{96,32},{1,65},{33,97},{65,1},{97,33},{2,66}... | collective-permute-start | bytes 49160 | tf_op jit(solution)/shard_map/ppermute | solution.py:37
  136.7 3.7 %collective-permute-start.13 = (f32[32,128]{1,0:T(8,128)S(1)}, f32[32,128]{1,0:T(8,128)S(1)}, u32[]{:S(2)}, u32[]{:S(2)}) collective-permute-start(f32[32,128]{1,0:T(8,128)S(1)} %add.103), channel_id=1, source_target_pairs={{0,2},{2,0},{4,6},{6,4},{8,10},{10,8},{12,14},{14,12},{1,3},{3,1},... | collective-permute-start | bytes 49160 | tf_op jit(solution)/shard_map/ppermute | solution.py:37
  140.4 4.6 %collective-permute-start.14 = (f32[32,128]{1,0:T(8,128)S(1)}, f32[32,128]{1,0:T(8,128)S(1)}, u32[]{:S(2)}, u32[]{:S(2)}) collective-permute-start(f32[32,128]{1,0:T(8,128)S(1)} %add.104), channel_id=1, source_target_pairs={{0,4},{2,6},{4,0},{6,2},{8,12},{10,14},{12,8},{14,10},{1,5},{3,7},... | collective-permute-start | bytes 49160 | tf_op jit(solution)/shard_map/ppermute | solution.py:37
  145.1 7.6 %collective-permute-start.15 = (f32[32,128]{1,0:T(8,128)S(1)}, f32[32,128]{1,0:T(8,128)S(1)}, u32[]{:S(2)}, u32[]{:S(2)}) collective-permute-start(f32[32,128]{1,0:T(8,128)S(1)} %add.105), channel_id=1, source_target_pairs={{0,8},{2,10},{4,12},{6,14},{8,0},{10,2},{12,4},{14,6},{1,9},{3,11}... | collective-permute-start | bytes 49160 | tf_op jit(solution)/shard_map/ppermute | solution.py:37
  305.4 5.3 %collective-permute-start.16 = (f32[136,256]{1,0:T(8,128)}, f32[136,256]{1,0:T(8,128)S(1)}, u32[]{:S(2)}, u32[]{:S(2)}) collective-permute-start(f32[136,256]{1,0:T(8,128)} %reduce-scatter.2.cloned.1.call-done), channel_id=1, source_target_pairs={{0,32},{32,0},{64,96},{96,64},{1,33},{33,1},{65,97},{97,65},{2,34}... | collective-permute-start | bytes 417800 | tf_op jit(solution)/shard_map/ppermute | solution.py:37
  311.6 6.6 %collective-permute-start.17 = (f32[136,256]{1,0:T(8,128)S(1)}, f32[136,256]{1,0:T(8,128)S(1)}, u32[]{:S(2)}, u32[]{:S(2)}) collective-permute-start(f32[136,256]{1,0:T(8,128)S(1)} %add.109), channel_id=1, source_target_pairs={{0,64},{32,96},{64,0},{96,32},{1,65},{33,97},{65,1},{97,33},{2,66}... | collective-permute-start | bytes 417800 | tf_op jit(solution)/shard_map/ppermute | solution.py:37
  318.2 6.9 %collective-permute-start.18 = (f32[136,256]{1,0:T(8,128)S(1)}, f32[136,256]{1,0:T(8,128)S(1)}, u32[]{:S(2)}, u32[]{:S(2)}) collective-permute-start(f32[136,256]{1,0:T(8,128)S(1)} %add.110), channel_id=1, source_target_pairs={{0,128},{128,0},{1,129},{129,1},{2,130},{130,2},{3,131},{131,3},{4... | collective-permute-start | bytes 417800 | tf_op jit(solution)/shard_map/ppermute | solution.py:37
  325.1 1.4 collective-permute-start.19
Sparse Core Ops, SparseCore 0:
  15.5 44.0 all-gather.1
  169.5 135.7 reduce-scatter.1

commit v8 on v5

--- a/solution.py
+++ b/solution.py
@@ -1,4 +1,5 @@
 import functools
+import math
 
 import jax
 import jax.numpy as jnp
@@ -44,7 +45,8 @@
     scores = lax.dot_general(
         xn, cand, (((1,), (1,)), ((), ())), preferred_element_type=jnp.float32
     )
-    return jnp.exp(scores * inv_width - OFFSET) * inv_count
+    log2e = 1.0 / math.log(2.0)
+    return jnp.exp2(scores * (inv_width * log2e) + (math.log2(inv_count) - OFFSET * log2e))
 
 
 def sweep_body(nbr, inv_width, inv_count, bary, links_ref, xn_ref, cn_ref, scale_ref, mass_ref,

time: 308 us -> 307 us (level)
  no operation moved by 1% of the time
where the time goes in v8:
time: 307 us
  waiting for transfers between devices  215 us (70%)
  Pallas kernels  36.6 us (12%)
  starting transfers between devices  27 us (9%)
  between operations  14.2 us (5%)
  other arithmetic  6.14 us (2%)
  blocking collectives  6.02 us (2%)
    reduce_scatter x1, waiting for transfers between devices, on_device(): lax.psum_scatter(packed.reshape(-1, feature_count), COL_AXES, scatter_dim...  101 us
    ppermute x20, waiting for transfers between devices, butterfly_sum(): x = x + lax.ppermute(x, axis, [(j, j ^ k) for j in range(n)])  70.8 us
    all_gather x1, waiting for transfers between devices, on_device(): lax.all_gather(lax.all_gather(normalize(cand_rows), 'yl', axis=0, tiled=T...  42.6 us
    pallas_call x3, Pallas kernels, sweep(): pl.pallas_call(functools.partial(sweep_body, nbr, inv_width, inv_count, b...  36.6 us
    ppermute x20, starting transfers between devices, butterfly_sum(): x = x + lax.ppermute(x, axis, [(j, j ^ k) for j in range(n)])  26.9 us
  transfers between devices with their start and end apart: 22, of which 22 were waited for; matrix products, arithmetic and copies ran while one was open for 1% of the time, Pallas kernels for 0%

profile of v8, /device:TPU:4, one launch (start us, length us, event | category | flops | bytes accessed | tf_op | source)
XLA Modules:
  0.0 307.2 jit_solution(3787454390032238778)
XLA Ops:
  7.2 0.0 copy-start
  7.2 0.0 all-gather.2.cloned.1.call-start
  7.2 1.1 fusion.2
  8.3 1.0 fusion.3
  9.3 6.0 %all_gather.6 = bf16[512,256]{1,0:T(8,128)(2,1)} all-gather(bf16[256,256]{1,0:T(8,128)(2,1)S(1)} %fusion.3), channel_id=1, replica_groups=mesh['yh'=2,'x'=4,'c'=2,'z'=8,'yl'=2] {'yl'}, dimensions={0}, use_global_device_ids=true | all-gather | bytes 393216 | tf_op jit(solution)/shard_map/all_gather | solution.py:155
  15.4 0.0 all-gather.2.cloned.1.call-update
  15.4 0.0 copy-start.2
  15.4 0.0 reduce-scatter.2.cloned.1.call-start
  15.4 1.0 reshape.43.mass_ref
  16.4 0.0 copy-done
  16.4 0.3 fusion
  16.7 0.3 fusion.1.xn_ref
  17.0 42.6 %all-gather.2.cloned.1.call-done = bf16[4096,256]{1,0:T(8,128)(2,1)} async-done(((bf16[512,256]{1,0:T(8,128)(2,1)}), bf16[4096,256]{1,0:T(8,128)(2,1)}) %all-gather.2.cloned.1.call-update) | async-done | bytes 2097168 | tf_op jit(solution)/shard_map/all_gather | solution.py:154
  59.6 0.0 copy-done.2
  59.6 1.6 copy-done.1
  61.2 10.1 %shard_map.76 = (f32[1536,1]{1,0:T(8,128)}, f32[32,128]{1,0:T(8,128)S(1)}) custom-call(s32[12,16]{1,0:T(8,128)S(1)} %copy-done.2, bf16[1536,256]{1,0:T(8,128)(2,1)S(1)} %fusion.1.xn_ref, bf16[32,128,256]{2,1,0:T(8,128)(2,1)S(1)} %bitcast.6, f32[32,128]{1,0:T(8,128)S(1)} %broadcast_in_dim.2.scale_ref, f32[1536,1]{1,0:T(8,128)S(1)} %reshape.43.mass_ref), custom_call_target="tpu_custom_call" | custom-call | flops 1610612736 | bytes 2883584 | tf_op jit(solution)/shard_map/pallas_call | solution.py:122
  71.3 0.0 collective-permute-start
  71.3 1.2 collective-permute-done
  72.4 1.5 collective-permute-start.1
  73.9 2.3 collective-permute-done.1
  76.2 3.0 collective-permute-start.2
  79.2 2.2 collective-permute-done.2
  81.4 1.2 collective-permute-start.3
  82.6 2.6 collective-permute-done.3
  85.3 0.5 collective-permute-start.4
  85.7 4.8 %collective-permute-done.4 = f32[32,128]{1,0:T(8,128)S(1)} collective-permute-done((f32[32,128]{1,0:T(8,128)S(1)}, f32[32,128]{1,0:T(8,128)S(1)}, u32[]{:S(2)}, u32[]{:S(2)}) %collective-permute-start.4) | collective-permute-done | bytes 16416 | tf_op jit(solution)/shard_map/ppermute | solution.py:38
  90.5 1.2 collective-permute-start.5
  91.7 2.5 collective-permute-done.5
  94.3 1.2 collective-permute-start.6
  95.5 3.4 %collective-permute-done.6 = f32[32,128]{1,0:T(8,128)S(1)} collective-permute-done((f32[32,128]{1,0:T(8,128)S(1)}, f32[32,128]{1,0:T(8,128)S(1)}, u32[]{:S(2)}, u32[]{:S(2)}) %collective-permute-start.6) | collective-permute-done | bytes 16416 | tf_op jit(solution)/shard_map/ppermute | solution.py:38
  98.9 3.0 collective-permute-start.7
  101.9 4.7 %collective-permute-done.7 = f32[32,128]{1,0:T(8,128)S(1)} collective-permute-done((f32[32,128]{1,0:T(8,128)S(1)}, f32[32,128]{1,0:T(8,128)S(1)}, u32[]{:S(2)}, u32[]{:S(2)}) %collective-permute-start.7) | collective-permute-done | bytes 16416 | tf_op jit(solution)/shard_map/ppermute | solution.py:38
  106.6 10.1 %shard_map.77 = (f32[1536,1]{1,0:T(8,128)}, f32[32,128]{1,0:T(8,128)S(1)}) custom-call(s32[12,16]{1,0:T(8,128)S(1)} %copy-done.2, bf16[1536,256]{1,0:T(8,128)(2,1)S(1)} %fusion.1.xn_ref, bf16[32,128,256]{2,1,0:T(8,128)(2,1)S(1)} %bitcast.7, f32[32,128]{1,0:T(8,128)S(1)} %bitcast_divide_fusion.1.scale_ref, f32[1536,1]{1,0:T(8,128)S(1)} %reshape.43.mass_ref), custom_call_target="tpu_custom_call" | custom-call | flops 1610612736 | bytes 2883584 | tf_op jit(solution)/shard_map/pallas_call | solution.py:122
  116.7 0.0 collective-permute-start.8
  116.7 1.2 collective-permute-done.8
  117.8 1.5 collective-permute-start.9
  119.3 2.3 collective-permute-done.9
  121.6 3.0 collective-permute-start.10
  124.6 2.2 collective-permute-done.10
  126.8 1.1 collective-permute-start.11
  127.9 2.8 collective-permute-done.11
  130.7 0.3 collective-permute-start.12
  131.1 4.9 %collective-permute-done.12 = f32[32,128]{1,0:T(8,128)S(1)} collective-permute-done((f32[32,128]{1,0:T(8,128)S(1)}, f32[32,128]{1,0:T(8,128)S(1)}, u32[]{:S(2)}, u32[]{:S(2)}) %collective-permute-start.12) | collective-permute-done | bytes 16416 | tf_op jit(solution)/shard_map/ppermute | solution.py:38
  136.0 1.1 collective-permute-start.13
  137.1 2.6 collective-permute-done.13
  139.7 1.2 collective-permute-start.14
  141.0 3.4 %collective-permute-done.14 = f32[32,128]{1,0:T(8,128)S(1)} collective-permute-done((f32[32,128]{1,0:T(8,128)S(1)}, f32[32,128]{1,0:T(8,128)S(1)}, u32[]{:S(2)}, u32[]{:S(2)}) %collective-permute-start.14) | collective-permute-done | bytes 16416 | tf_op jit(solution)/shard_map/ppermute | solution.py:38
  144.4 3.0 collective-permute-start.15
  147.4 4.6 %collective-permute-done.15 = f32[32,128]{1,0:T(8,128)S(1)} collective-permute-done((f32[32,128]{1,0:T(8,128)S(1)}, f32[32,128]{1,0:T(8,128)S(1)}, u32[]{:S(2)}, u32[]{:S(2)}) %collective-permute-start.15) | collective-permute-done | bytes 16416 | tf_op jit(solution)/shard_map/ppermute | solution.py:38
  152.0 16.4 %shard_map.78 = (f32[1536,1]{1,0:T(8,128)S(1)}, f32[16,264,256]{2,1,0:T(8,128)}) custom-call(s32[12,16]{1,0:T(8,128)S(1)} %copy-done.2, bf16[1536,256]{1,0:T(8,128)(2,1)S(1)} %fusion.1.xn_ref, bf16[32,128,256]{2,1,0:T(8,128)(2,1)S(1)} %bitcast.8, f32[32,128]{1,0:T(8,128)S(1)} %bitcast_divide_fusion.scale_ref, f32[1536,1]{1,0:T(8,128)S(1)} %reshape.43.mass_ref, ...), custom_call_target="tpu_custom_call" | custom-call | flops 3221225472 | bytes 7864320 | tf_op jit(solution)/shard_map/pallas_call | solution.py:122
  168.4 0.0 reduce-scatter.2.cloned.1.call-update
  168.5 101.3 %reduce-scatter.2.cloned.1.call-done = f32[264,256]{1,0:T(8,128)} async-done(((f32[4224,256]{1,0:T(8,128)}), f32[264,256]{1,0:T(8,128)}) %reduce-scatter.2.cloned.1.call-update) | async-done | bytes 270352 | tf_op jit(solution)/shard_map/reduce_scatter | solution.py:167
  269.7 0.0 collective-permute-start.16
  269.7 1.8 collective-permute-done.16
  271.5 1.0 add.112
  272.5 0.5 collective-permute-start.17
  273.0 8.1 %collective-permute-done.17 = f32[264,256]{1,0:T(8,128)S(1)} collective-permute-done((f32[264,256]{1,0:T(8,128)S(1)}, f32[264,256]{1,0:T(8,128)S(1)}, u32[]{:S(2)}, u32[]{:S(2)}) %collective-permute-start.17) | collective-permute-done | bytes 270368 | tf_op jit(solution)/shard_map/ppermute | solution.py:38
  281.1 0.6 collective-permute-start.18
  281.8 8.7 %collective-permute-done.18 = f32[264,256]{1,0:T(8,128)S(1)} collective-permute-done((f32[264,256]{1,0:T(8,128)S(1)}, f32[264,256]{1,0:T(8,128)S(1)}, u32[]{:S(2)}, u32[]{:S(2)}) %collective-permute-start.18) | collective-permute-done | bytes 270368 | tf_op jit(solution)/shard_map/ppermute | solution.py:38
  290.5 2.9 collective-permute-start.19
  293.4 0.9 reduce
  294.2 4.6 %collective-permute-done.19 = f32[264,256]{1,0:T(8,128)S(1)} collective-permute-done((f32[264,256]{1,0:T(8,128)S(1)}, f32[264,256]{1,0:T(8,128)S(1)}, u32[]{:S(2)}, u32[]{:S(2)}) %collective-permute-start.19) | collective-permute-done | bytes 270368 | tf_op jit(solution)/shard_map/ppermute | solution.py:38
  298.9 0.8 slice_divide_fusion
  299.7 0.6 multiply_divide_fusion
  (26 shorter events, 0.2 us)
Async XLA Ops:
  7.2 9.2 %copy-start = (bf16[1536,256]{1,0:T(8,128)(2,1)S(1)}, bf16[1536,256]{1,0:T(8,128)(2,1)}, u32[]{:S(2)}) copy-start(bf16[1536,256]{1,0:T(8,128)(2,1)} %rest_0_.1) | copy-start | bytes 2359300
  7.2 52.4 %all-gather.2.cloned.1.call-start = ((), (), s32[]{:S(2)}) async-start(), calls=%async_computation.1 | async-start | bytes 2359296 | tf_op jit(solution)/shard_map/all_gather | solution.py:154
  15.4 44.2 %copy-start.2 = (s32[12,16]{1,0:T(8,128)S(1)}, s32[12,16]{1,0:T(8,128)}, u32[]{:S(2)}) copy-start(s32[12,16]{1,0:T(8,128)} %links_ref.5) | copy-start | bytes 2308
  15.4 254.3 %reduce-scatter.2.cloned.1.call-start = ((), (), s32[]{:S(2)}) async-start(), calls=%async_computation.2 | async-start | bytes 4595712 | tf_op jit(solution)/shard_map/reduce_scatter | solution.py:167
  59.6 1.6 copy-start.1
  61.2 45.4 %copy-start.3 = (f32[4096]{0:T(1024)S(1)}, f32[4096]{0:T(1024)}, u32[]{:S(2)}) copy-start(f32[4096]{0:T(1024)} %param.9) | copy-start | bytes 49156
  71.3 1.2 collective-permute-start
  72.4 3.7 %collective-permute-start.1 = (f32[32,128]{1,0:T(8,128)S(1)}, f32[32,128]{1,0:T(8,128)S(1)}, u32[]{:S(2)}, u32[]{:S(2)}) collective-permute-start(f32[32,128]{1,0:T(8,128)S(1)} %add.94), channel_id=1, source_target_pairs={{0,1},{1,0},{2,3},{3,2},{4,5},{5,4},{6,7},{7,6},{8,9},{9,8},{10,11... | collective-permute-start | bytes 49160 | tf_op jit(solution)/shard_map/ppermute | solution.py:38
  76.2 5.2 %collective-permute-start.2 = (f32[32,128]{1,0:T(8,128)S(1)}, f32[32,128]{1,0:T(8,128)S(1)}, u32[]{:S(2)}, u32[]{:S(2)}) collective-permute-start(f32[32,128]{1,0:T(8,128)S(1)} %add.95), channel_id=1, source_target_pairs={{0,128},{128,0},{1,129},{129,1},{2,130},{130,2},{3,131},{131,3},{4... | collective-permute-start | bytes 49160 | tf_op jit(solution)/shard_map/ppermute | solution.py:38
  81.4 3.8 %collective-permute-start.3 = (f32[32,128]{1,0:T(8,128)S(1)}, f32[32,128]{1,0:T(8,128)S(1)}, u32[]{:S(2)}, u32[]{:S(2)}) collective-permute-start(f32[32,128]{1,0:T(8,128)S(1)} %add.96), channel_id=1, source_target_pairs={{0,32},{32,0},{64,96},{96,64},{1,33},{33,1},{65,97},{97,65},{2,34}... | collective-permute-start | bytes 49160 | tf_op jit(solution)/shard_map/ppermute | solution.py:38
  85.3 5.2 %collective-permute-start.4 = (f32[32,128]{1,0:T(8,128)S(1)}, f32[32,128]{1,0:T(8,128)S(1)}, u32[]{:S(2)}, u32[]{:S(2)}) collective-permute-start(f32[32,128]{1,0:T(8,128)S(1)} %add.97), channel_id=1, source_target_pairs={{0,64},{32,96},{64,0},{96,32},{1,65},{33,97},{65,1},{97,33},{2,66}... | collective-permute-start | bytes 49160 | tf_op jit(solution)/shard_map/ppermute | solution.py:38
  90.5 3.7 %collective-permute-start.5 = (f32[32,128]{1,0:T(8,128)S(1)}, f32[32,128]{1,0:T(8,128)S(1)}, u32[]{:S(2)}, u32[]{:S(2)}) collective-permute-start(f32[32,128]{1,0:T(8,128)S(1)} %add.98), channel_id=1, source_target_pairs={{0,2},{2,0},{4,6},{6,4},{8,10},{10,8},{12,14},{14,12},{1,3},{3,1},... | collective-permute-start | bytes 49160 | tf_op jit(solution)/shard_map/ppermute | solution.py:38
  94.3 4.6 %collective-permute-start.6 = (f32[32,128]{1,0:T(8,128)S(1)}, f32[32,128]{1,0:T(8,128)S(1)}, u32[]{:S(2)}, u32[]{:S(2)}) collective-permute-start(f32[32,128]{1,0:T(8,128)S(1)} %add.99), channel_id=1, source_target_pairs={{0,4},{2,6},{4,0},{6,2},{8,12},{10,14},{12,8},{14,10},{1,5},{3,7},... | collective-permute-start | bytes 49160 | tf_op jit(solution)/shard_map/ppermute | solution.py:38
  98.9 7.6 %collective-permute-start.7 = (f32[32,128]{1,0:T(8,128)S(1)}, f32[32,128]{1,0:T(8,128)S(1)}, u32[]{:S(2)}, u32[]{:S(2)}) collective-permute-start(f32[32,128]{1,0:T(8,128)S(1)} %add.100), channel_id=1, source_target_pairs={{0,8},{2,10},{4,12},{6,14},{8,0},{10,2},{12,4},{14,6},{1,9},{3,11}... | collective-permute-start | bytes 49160 | tf_op jit(solution)/shard_map/ppermute | solution.py:38
  116.7 1.2 collective-permute-start.8
  117.8 3.7 %collective-permute-start.9 = (f32[32,128]{1,0:T(8,128)S(1)}, f32[32,128]{1,0:T(8,128)S(1)}, u32[]{:S(2)}, u32[]{:S(2)}) collective-permute-start(f32[32,128]{1,0:T(8,128)S(1)} %add.102), channel_id=1, source_target_pairs={{0,1},{1,0},{2,3},{3,2},{4,5},{5,4},{6,7},{7,6},{8,9},{9,8},{10,11... | collective-permute-start | bytes 49160 | tf_op jit(solution)/shard_map/ppermute | solution.py:38
  121.6 5.2 %collective-permute-start.10 = (f32[32,128]{1,0:T(8,128)S(1)}, f32[32,128]{1,0:T(8,128)S(1)}, u32[]{:S(2)}, u32[]{:S(2)}) collective-permute-start(f32[32,128]{1,0:T(8,128)S(1)} %add.103), channel_id=1, source_target_pairs={{0,128},{128,0},{1,129},{129,1},{2,130},{130,2},{3,131},{131,3},{4... | collective-permute-start | bytes 49160 | tf_op jit(solution)/shard_map/ppermute | solution.py:38
  126.8 3.9 %collective-permute-start.11 = (f32[32,128]{1,0:T(8,128)S(1)}, f32[32,128]{1,0:T(8,128)S(1)}, u32[]{:S(2)}, u32[]{:S(2)}) collective-permute-start(f32[32,128]{1,0:T(8,128)S(1)} %add.104), channel_id=1, source_target_pairs={{0,32},{32,0},{64,96},{96,64},{1,33},{33,1},{65,97},{97,65},{2,34}... | collective-permute-start | bytes 49160 | tf_op jit(solution)/shard_map/ppermute | solution.py:38
  130.7 5.2 %collective-permute-start.12 = (f32[32,128]{1,0:T(8,128)S(1)}, f32[32,128]{1,0:T(8,128)S(1)}, u32[]{:S(2)}, u32[]{:S(2)}) collective-permute-start(f32[32,128]{1,0:T(8,128)S(1)} %add.105), channel_id=1, source_target_pairs={{0,64},{32,96},{64,0},{96,32},{1,65},{33,97},{65,1},{97,33},{2,66}... | collective-permute-start | bytes 49160 | tf_op jit(solution)/shard_map/ppermute | solution.py:38
  136.0 3.7 %collective-permute-start.13 = (f32[32,128]{1,0:T(8,128)S(1)}, f32[32,128]{1,0:T(8,128)S(1)}, u32[]{:S(2)}, u32[]{:S(2)}) collective-permute-start(f32[32,128]{1,0:T(8,128)S(1)} %add.106), channel_id=1, source_target_pairs={{0,2},{2,0},{4,6},{6,4},{8,10},{10,8},{12,14},{14,12},{1,3},{3,1},... | collective-permute-start | bytes 49160 | tf_op jit(solution)/shard_map/ppermute | solution.py:38
  139.7 4.6 %collective-permute-start.14 = (f32[32,128]{1,0:T(8,128)S(1)}, f32[32,128]{1,0:T(8,128)S(1)}, u32[]{:S(2)}, u32[]{:S(2)}) collective-permute-start(f32[32,128]{1,0:T(8,128)S(1)} %add.107), channel_id=1, source_target_pairs={{0,4},{2,6},{4,0},{6,2},{8,12},{10,14},{12,8},{14,10},{1,5},{3,7},... | collective-permute-start | bytes 49160 | tf_op jit(solution)/shard_map/ppermute | solution.py:38
  144.4 7.6 %collective-permute-start.15 = (f32[32,128]{1,0:T(8,128)S(1)}, f32[32,128]{1,0:T(8,128)S(1)}, u32[]{:S(2)}, u32[]{:S(2)}) collective-permute-start(f32[32,128]{1,0:T(8,128)S(1)} %add.108), channel_id=1, source_target_pairs={{0,8},{2,10},{4,12},{6,14},{8,0},{10,2},{12,4},{14,6},{1,9},{3,11}... | collective-permute-start | bytes 49160 | tf_op jit(solution)/shard_map/ppermute | solution.py:38
  269.7 1.8 collective-permute-start.16
  272.5 8.6 %collective-permute-start.17 = (f32[264,256]{1,0:T(8,128)S(1)}, f32[264,256]{1,0:T(8,128)S(1)}, u32[]{:S(2)}, u32[]{:S(2)}) collective-permute-start(f32[264,256]{1,0:T(8,128)S(1)} %add.112), channel_id=1, source_target_pairs={{0,32},{32,0},{64,96},{96,64},{1,33},{33,1},{65,97},{97,65},{2,34}... | collective-permute-start | bytes 811016 | tf_op jit(solution)/shard_map/ppermute | solution.py:38
  281.1 9.3 %collective-permute-start.18 = (f32[264,256]{1,0:T(8,128)S(1)}, f32[264,256]{1,0:T(8,128)S(1)}, u32[]{:S(2)}, u32[]{:S(2)}) collective-permute-start(f32[264,256]{1,0:T(8,128)S(1)} %add.113), channel_id=1, source_target_pairs={{0,64},{32,96},{64,0},{96,32},{1,65},{33,97},{65,1},{97,33},{2,66}... | collective-permute-start | bytes 811016 | tf_op jit(solution)/shard_map/ppermute | solution.py:38
  290.5 8.4 %collective-permute-start.19 = (f32[264,256]{1,0:T(8,128)S(1)}, f32[264,256]{1,0:T(8,128)S(1)}, u32[]{:S(2)}, u32[]{:S(2)}) collective-permute-start(f32[264,256]{1,0:T(8,128)S(1)} %add.114), channel_id=1, source_target_pairs={{0,128},{128,0},{1,129},{129,1},{2,130},{130,2},{3,131},{131,3},{4... | collective-permute-start | bytes 811016 | tf_op jit(solution)/shard_map/ppermute | solution.py:38
Sparse Core Ops, SparseCore 0:
  15.5 44.0 all-gather.1
  168.6 101.0 reduce-scatter.1

commit v9 on v8

--- a/solution.py
+++ b/solution.py
@@ -16,6 +16,7 @@
 EPS = 0.05
 OFFSET = 1.0
 PAD = 8
+SUB = 4
 
 ROW_AXES = ("yh", "x", "c")
 COL_AXES = ("z", "yl")
@@ -64,32 +65,35 @@
         else:
             ct_ref[...] = jnp.zeros_like(ct_ref)
 
-    xn = xn_ref[...]
-    acc = jnp.zeros((BLOCK, BLOCK), jnp.float32)
-    for s in range(nbr):
-        blk = links_ref[b, s]
-        k = _kernel_slot(xn, cn_ref, blk, inv_width, inv_count)
-        kbuf[s] = k
-        acc = acc + k * scale_ref[pl.ds(blk, 1), :]
-    row_total = jnp.sum(acc, axis=1, keepdims=True)
-    ds = mass_ref[...] / row_total
-    ds_ref[...] = ds
-    if bary:
-        rows = rows_ref[...]
-    for s in range(nbr):
-        blk = links_ref[b, s]
-        k = kbuf[s]
-        part = jnp.sum(k * ds, axis=0, keepdims=True)
+    for u in range(SUB):
+        step = b * SUB + u
+        lo = u * BLOCK
+        xn = xn_ref[pl.ds(lo, BLOCK), :]
+        acc = jnp.zeros((BLOCK, BLOCK), jnp.float32)
+        for s in range(nbr):
+            blk = links_ref[step, s]
+            k = _kernel_slot(xn, cn_ref, blk, inv_width, inv_count)
+            kbuf[u, s] = k
+            acc = acc + k * scale_ref[pl.ds(blk, 1), :]
+        row_total = jnp.sum(acc, axis=1, keepdims=True)
+        ds = mass_ref[pl.ds(lo, BLOCK), :] / row_total
+        ds_ref[pl.ds(lo, BLOCK), :] = ds
         if bary:
-            q = blk // 2
-            half = pl.multiple_of((blk % 2) * BLOCK, BLOCK)
-            ws_ref[q, pl.ds(2 * BLOCK, 1), pl.ds(half, BLOCK)] += part
-            w = (k * ds).astype(jnp.bfloat16)
-            ws_ref[q, pl.ds(half, BLOCK), :] += lax.dot_general(
-                w, rows, (((0,), (0,)), ((), ())), preferred_element_type=jnp.float32
-            )
-        else:
-            ct_ref[pl.ds(blk, 1), :] += part
+            rows = rows_ref[pl.ds(lo, BLOCK), :]
+        for s in range(nbr):
+            blk = links_ref[step, s]
+            k = kbuf[u, s]
+            part = jnp.sum(k * ds, axis=0, keepdims=True)
+            if bary:
+                q = blk // 2
+                half = pl.multiple_of((blk % 2) * BLOCK, BLOCK)
+                ws_ref[q, pl.ds(2 * BLOCK, 1), pl.ds(half, BLOCK)] += part
+                w = (k * ds).astype(jnp.bfloat16)
+                ws_ref[q, pl.ds(half, BLOCK), :] += lax.dot_general(
+                    w, rows, (((0,), (0,)), ((), ())), preferred_element_type=jnp.float32
+                )
+            else:
+                ct_ref[pl.ds(blk, 1), :] += part
 
 
 def sweep(xn, cn_blocks, scale_blocks, mass_col, links, rows=None):
@@ -100,17 +104,17 @@
     inv_width = 1.0 / (feature_count * EPS)
     inv_count = 1.0 / (nbr * BLOCK)
     in_specs = [
-        pl.BlockSpec((BLOCK, feature_count), lambda b, L: (b, 0)),
+        pl.BlockSpec((SUB * BLOCK, feature_count), lambda b, L: (b, 0)),
         pl.BlockSpec((block_count, BLOCK, feature_count), lambda b, L: (0, 0, 0)),
         pl.BlockSpec((block_count, BLOCK), lambda b, L: (0, 0)),
-        pl.BlockSpec((BLOCK, 1), lambda b, L: (b, 0)),
+        pl.BlockSpec((SUB * BLOCK, 1), lambda b, L: (b, 0)),
     ]
-    out_specs = [pl.BlockSpec((BLOCK, 1), lambda b, L: (b, 0))]
+    out_specs = [pl.BlockSpec((SUB * BLOCK, 1), lambda b, L: (b, 0))]
     out_shape = [jax.ShapeDtypeStruct((local_rows, 1), jnp.float32)]
     packed_rows = 2 * BLOCK + PAD
     args = [links, xn, cn_blocks, scale_blocks, mass_col]
     if bary:
-        in_specs.append(pl.BlockSpec((BLOCK, feature_count), lambda b, L: (b, 0)))
+        in_specs.append(pl.BlockSpec((SUB * BLOCK, feature_count), lambda b, L: (b, 0)))
         packed = (block_count // 2, packed_rows, feature_count)
         out_specs.append(pl.BlockSpec(packed, lambda b, L: (0, 0, 0)))
         out_shape.append(jax.ShapeDtypeStruct(packed, jnp.float32))
@@ -123,10 +127,10 @@
         functools.partial(sweep_body, nbr, inv_width, inv_count, bary),
         grid_spec=pltpu.PrefetchScalarGridSpec(
             num_scalar_prefetch=1,
-            grid=(local_blocks,),
+            grid=(local_blocks // SUB,),
             in_specs=in_specs,
             out_specs=out_specs,
-            scratch_shapes=[pltpu.VMEM((nbr, BLOCK, BLOCK), jnp.float32)],
+            scratch_shapes=[pltpu.VMEM((SUB, nbr, BLOCK, BLOCK), jnp.float32)],
         ),
         out_shape=out_shape,
         compiler_params=pltpu.CompilerParams(

time: 307 us -> 299 us (0.974)
  Pallas kernels: 36.6 us -> 28.6 us
    pallas_call x3, Pallas kernels: 36.6 us -> 28.6 us  [sweep(): pl.pallas_call(functools.partial(sweep_body, nbr, inv_width, inv_count, b...]
where the time goes in v9:
time: 299 us
  waiting for transfers between devices  214 us (72%)
  Pallas kernels  28.6 us (10%)
  starting transfers between devices  27.6 us (9%)
  between operations  14.2 us (5%)
  other arithmetic  6.14 us (2%)
  blocking collectives  6.02 us (2%)
    reduce_scatter x1, waiting for transfers between devices, on_device(): lax.psum_scatter(packed.reshape(-1, feature_count), COL_AXES, scatter_dim...  101 us
    ppermute x20, waiting for transfers between devices, butterfly_sum(): x = x + lax.ppermute(x, axis, [(j, j ^ k) for j in range(n)])  70.2 us
    all_gather x1, waiting for transfers between devices, on_device(): lax.all_gather(lax.all_gather(normalize(cand_rows), 'yl', axis=0, tiled=T...  42.6 us
    pallas_call x3, Pallas kernels, sweep(): pl.pallas_call(functools.partial(sweep_body, nbr, inv_width, inv_count, b...  28.6 us
    ppermute x20, starting transfers between devices, butterfly_sum(): x = x + lax.ppermute(x, axis, [(j, j ^ k) for j in range(n)])  27.5 us
    all_gather x1, blocking collectives, on_device(): lax.all_gather(normalize(cand_rows), 'yl', axis=0, tiled=True)  6.02 us
  transfers between devices with their start and end apart: 22, of which 22 were waited for; matrix products, arithmetic and copies ran while one was open for 1% of the time, Pallas kernels for 0%

profile of v9, /device:TPU:4, one launch (start us, length us, event | category | flops | bytes accessed | tf_op | source)
XLA Modules:
  0.0 299.2 jit_solution(9958343047363212761)
XLA Ops:
  7.2 0.0 copy-start
  7.2 0.0 all-gather.2.cloned.1.call-start
  7.2 1.1 fusion.2
  8.3 1.0 fusion.3
  9.3 6.0 %all_gather.6 = bf16[512,256]{1,0:T(8,128)(2,1)} all-gather(bf16[256,256]{1,0:T(8,128)(2,1)S(1)} %fusion.3), channel_id=1, replica_groups=mesh['yh'=2,'x'=4,'c'=2,'z'=8,'yl'=2] {'yl'}, dimensions={0}, use_global_device_ids=true | all-gather | bytes 393216 | tf_op jit(solution)/shard_map/all_gather | solution.py:159
  15.4 0.0 all-gather.2.cloned.1.call-update
  15.4 0.0 copy-start.2
  15.4 0.0 reduce-scatter.2.cloned.1.call-start
  15.4 1.0 reshape.43.mass_ref
  16.4 0.0 copy-done
  16.4 0.3 fusion
  16.7 0.3 fusion.1.xn_ref
  17.0 42.6 %all-gather.2.cloned.1.call-done = bf16[4096,256]{1,0:T(8,128)(2,1)} async-done(((bf16[512,256]{1,0:T(8,128)(2,1)}), bf16[4096,256]{1,0:T(8,128)(2,1)}) %all-gather.2.cloned.1.call-update) | async-done | bytes 2097168 | tf_op jit(solution)/shard_map/all_gather | solution.py:158
  59.6 0.0 copy-done.2
  59.6 1.6 copy-done.1
  61.2 6.7 %shard_map.76 = (f32[1536,1]{1,0:T(8,128)}, f32[32,128]{1,0:T(8,128)S(1)}) custom-call(s32[12,16]{1,0:T(8,128)S(1)} %copy-done.2, bf16[1536,256]{1,0:T(8,128)(2,1)S(1)} %fusion.1.xn_ref, bf16[32,128,256]{2,1,0:T(8,128)(2,1)S(1)} %bitcast.6, f32[32,128]{1,0:T(8,128)S(1)} %broadcast_in_dim.2.scale_ref, f32[1536,1]{1,0:T(8,128)S(1)} %reshape.43.mass_ref), custom_call_target="tpu_custom_call" | custom-call | flops 1610612736 | bytes 2883584 | tf_op jit(solution)/shard_map/pallas_call | solution.py:126
  67.9 0.0 collective-permute-start
  67.9 1.2 collective-permute-done
  69.1 1.5 collective-permute-start.1
  70.6 2.2 collective-permute-done.1
  72.8 3.0 %collective-permute-start.2 = (f32[32,128]{1,0:T(8,128)S(1)}, f32[32,128]{1,0:T(8,128)S(1)}, u32[]{:S(2)}, u32[]{:S(2)}) collective-permute-start(f32[32,128]{1,0:T(8,128)S(1)} %add.95), channel_id=1, source_target_pairs={{0,128},{128,0},{1,129},{129,1},{2,130},{130,2},{3,131},{131,3},{4... | collective-permute-start | bytes 49160 | tf_op jit(solution)/shard_map/ppermute | solution.py:39
  75.8 2.2 collective-permute-done.2
  78.0 1.2 collective-permute-start.3
  79.2 2.6 collective-permute-done.3
  81.9 0.5 collective-permute-start.4
  82.4 4.8 %collective-permute-done.4 = f32[32,128]{1,0:T(8,128)S(1)} collective-permute-done((f32[32,128]{1,0:T(8,128)S(1)}, f32[32,128]{1,0:T(8,128)S(1)}, u32[]{:S(2)}, u32[]{:S(2)}) %collective-permute-start.4) | collective-permute-done | bytes 16416 | tf_op jit(solution)/shard_map/ppermute | solution.py:39
  87.1 1.2 collective-permute-start.5
  88.3 2.5 collective-permute-done.5
  90.9 1.3 collective-permute-start.6
  92.2 3.3 %collective-permute-done.6 = f32[32,128]{1,0:T(8,128)S(1)} collective-permute-done((f32[32,128]{1,0:T(8,128)S(1)}, f32[32,128]{1,0:T(8,128)S(1)}, u32[]{:S(2)}, u32[]{:S(2)}) %collective-permute-start.6) | collective-permute-done | bytes 16416 | tf_op jit(solution)/shard_map/ppermute | solution.py:39
  95.5 3.0 %collective-permute-start.7 = (f32[32,128]{1,0:T(8,128)S(1)}, f32[32,128]{1,0:T(8,128)S(1)}, u32[]{:S(2)}, u32[]{:S(2)}) collective-permute-start(f32[32,128]{1,0:T(8,128)S(1)} %add.100), channel_id=1, source_target_pairs={{0,8},{2,10},{4,12},{6,14},{8,0},{10,2},{12,4},{14,6},{1,9},{3,11}... | collective-permute-start | bytes 49160 | tf_op jit(solution)/shard_map/ppermute | solution.py:39
  98.5 4.6 %collective-permute-done.7 = f32[32,128]{1,0:T(8,128)S(1)} collective-permute-done((f32[32,128]{1,0:T(8,128)S(1)}, f32[32,128]{1,0:T(8,128)S(1)}, u32[]{:S(2)}, u32[]{:S(2)}) %collective-permute-start.7) | collective-permute-done | bytes 16416 | tf_op jit(solution)/shard_map/ppermute | solution.py:39
  103.2 6.7 %shard_map.77 = (f32[1536,1]{1,0:T(8,128)}, f32[32,128]{1,0:T(8,128)S(1)}) custom-call(s32[12,16]{1,0:T(8,128)S(1)} %copy-done.2, bf16[1536,256]{1,0:T(8,128)(2,1)S(1)} %fusion.1.xn_ref, bf16[32,128,256]{2,1,0:T(8,128)(2,1)S(1)} %bitcast.7, f32[32,128]{1,0:T(8,128)S(1)} %bitcast_divide_fusion.1.scale_ref, f32[1536,1]{1,0:T(8,128)S(1)} %reshape.43.mass_ref), custom_call_target="tpu_custom_call" | custom-call | flops 1610612736 | bytes 2883584 | tf_op jit(solution)/shard_map/pallas_call | solution.py:126
  109.9 0.0 collective-permute-start.8
  109.9 1.2 collective-permute-done.8
  111.0 1.5 collective-permute-start.9
  112.6 2.2 collective-permute-done.9
  114.8 3.1 %collective-permute-start.10 = (f32[32,128]{1,0:T(8,128)S(1)}, f32[32,128]{1,0:T(8,128)S(1)}, u32[]{:S(2)}, u32[]{:S(2)}) collective-permute-start(f32[32,128]{1,0:T(8,128)S(1)} %add.103), channel_id=1, source_target_pairs={{0,128},{128,0},{1,129},{129,1},{2,130},{130,2},{3,131},{131,3},{4... | collective-permute-start | bytes 49160 | tf_op jit(solution)/shard_map/ppermute | solution.py:39
  117.9 2.2 collective-permute-done.10
  120.0 1.1 collective-permute-start.11
  121.1 2.8 collective-permute-done.11
  123.9 0.4 collective-permute-start.12
  124.3 4.9 %collective-permute-done.12 = f32[32,128]{1,0:T(8,128)S(1)} collective-permute-done((f32[32,128]{1,0:T(8,128)S(1)}, f32[32,128]{1,0:T(8,128)S(1)}, u32[]{:S(2)}, u32[]{:S(2)}) %collective-permute-start.12) | collective-permute-done | bytes 16416 | tf_op jit(solution)/shard_map/ppermute | solution.py:39
  129.2 1.2 collective-permute-start.13
  130.3 2.6 collective-permute-done.13
  132.9 1.3 collective-permute-start.14
  134.2 3.3 %collective-permute-done.14 = f32[32,128]{1,0:T(8,128)S(1)} collective-permute-done((f32[32,128]{1,0:T(8,128)S(1)}, f32[32,128]{1,0:T(8,128)S(1)}, u32[]{:S(2)}, u32[]{:S(2)}) %collective-permute-start.14) | collective-permute-done | bytes 16416 | tf_op jit(solution)/shard_map/ppermute | solution.py:39
  137.6 3.0 %collective-permute-start.15 = (f32[32,128]{1,0:T(8,128)S(1)}, f32[32,128]{1,0:T(8,128)S(1)}, u32[]{:S(2)}, u32[]{:S(2)}) collective-permute-start(f32[32,128]{1,0:T(8,128)S(1)} %add.108), channel_id=1, source_target_pairs={{0,8},{2,10},{4,12},{6,14},{8,0},{10,2},{12,4},{14,6},{1,9},{3,11}... | collective-permute-start | bytes 49160 | tf_op jit(solution)/shard_map/ppermute | solution.py:39
  140.6 4.6 %collective-permute-done.15 = f32[32,128]{1,0:T(8,128)S(1)} collective-permute-done((f32[32,128]{1,0:T(8,128)S(1)}, f32[32,128]{1,0:T(8,128)S(1)}, u32[]{:S(2)}, u32[]{:S(2)}) %collective-permute-start.15) | collective-permute-done | bytes 16416 | tf_op jit(solution)/shard_map/ppermute | solution.py:39
  145.2 15.2 %shard_map.78 = (f32[1536,1]{1,0:T(8,128)S(1)}, f32[16,264,256]{2,1,0:T(8,128)}) custom-call(s32[12,16]{1,0:T(8,128)S(1)} %copy-done.2, bf16[1536,256]{1,0:T(8,128)(2,1)S(1)} %fusion.1.xn_ref, bf16[32,128,256]{2,1,0:T(8,128)(2,1)S(1)} %bitcast.8, f32[32,128]{1,0:T(8,128)S(1)} %bitcast_divide_fusion.scale_ref, f32[1536,1]{1,0:T(8,128)S(1)} %reshape.43.mass_ref, ...), custom_call_target="tpu_custom_call" | custom-call | flops 3221225472 | bytes 7864320 | tf_op jit(solution)/shard_map/pallas_call | solution.py:126
  160.4 0.0 reduce-scatter.2.cloned.1.call-update
  160.4 101.3 %reduce-scatter.2.cloned.1.call-done = f32[264,256]{1,0:T(8,128)} async-done(((f32[4224,256]{1,0:T(8,128)}), f32[264,256]{1,0:T(8,128)}) %reduce-scatter.2.cloned.1.call-update) | async-done | bytes 270352 | tf_op jit(solution)/shard_map/reduce_scatter | solution.py:171
  261.7 0.0 collective-permute-start.16
  261.7 1.8 collective-permute-done.16
  263.5 1.0 add.112
  264.5 0.6 collective-permute-start.17
  265.0 8.0 %collective-permute-done.17 = f32[264,256]{1,0:T(8,128)S(1)} collective-permute-done((f32[264,256]{1,0:T(8,128)S(1)}, f32[264,256]{1,0:T(8,128)S(1)}, u32[]{:S(2)}, u32[]{:S(2)}) %collective-permute-start.17) | collective-permute-done | bytes 270368 | tf_op jit(solution)/shard_map/ppermute | solution.py:39
  273.1 0.6 collective-permute-start.18
  273.7 8.7 %collective-permute-done.18 = f32[264,256]{1,0:T(8,128)S(1)} collective-permute-done((f32[264,256]{1,0:T(8,128)S(1)}, f32[264,256]{1,0:T(8,128)S(1)}, u32[]{:S(2)}, u32[]{:S(2)}) %collective-permute-start.18) | collective-permute-done | bytes 270368 | tf_op jit(solution)/shard_map/ppermute | solution.py:39
  282.5 2.9 collective-permute-start.19
  285.4 0.9 reduce
  286.3 4.5 %collective-permute-done.19 = f32[264,256]{1,0:T(8,128)S(1)} collective-permute-done((f32[264,256]{1,0:T(8,128)S(1)}, f32[264,256]{1,0:T(8,128)S(1)}, u32[]{:S(2)}, u32[]{:S(2)}) %collective-permute-start.19) | collective-permute-done | bytes 270368 | tf_op jit(solution)/shard_map/ppermute | solution.py:39
  290.9 0.8 slice_divide_fusion
  291.7 0.6 multiply_divide_fusion
  (26 shorter events, 0.2 us)
Async XLA Ops:
  7.2 9.2 %copy-start = (bf16[1536,256]{1,0:T(8,128)(2,1)S(1)}, bf16[1536,256]{1,0:T(8,128)(2,1)}, u32[]{:S(2)}) copy-start(bf16[1536,256]{1,0:T(8,128)(2,1)} %rest_0_.1) | copy-start | bytes 2359300
  7.2 52.4 %all-gather.2.cloned.1.call-start = ((), (), s32[]{:S(2)}) async-start(), calls=%async_computation.1 | async-start | bytes 2359296 | tf_op jit(solution)/shard_map/all_gather | solution.py:158
  15.4 44.2 %copy-start.2 = (s32[12,16]{1,0:T(8,128)S(1)}, s32[12,16]{1,0:T(8,128)}, u32[]{:S(2)}) copy-start(s32[12,16]{1,0:T(8,128)} %links_ref.5) | copy-start | bytes 2308
  15.4 246.3 %reduce-scatter.2.cloned.1.call-start = ((), (), s32[]{:S(2)}) async-start(), calls=%async_computation.2 | async-start | bytes 4595712 | tf_op jit(solution)/shard_map/reduce_scatter | solution.py:171
  59.6 1.6 copy-start.1
  61.2 42.0 %copy-start.3 = (f32[4096]{0:T(1024)S(1)}, f32[4096]{0:T(1024)}, u32[]{:S(2)}) copy-start(f32[4096]{0:T(1024)} %param.9) | copy-start | bytes 49156
  67.9 1.2 collective-permute-start
  69.1 3.7 %collective-permute-start.1 = (f32[32,128]{1,0:T(8,128)S(1)}, f32[32,128]{1,0:T(8,128)S(1)}, u32[]{:S(2)}, u32[]{:S(2)}) collective-permute-start(f32[32,128]{1,0:T(8,128)S(1)} %add.94), channel_id=1, source_target_pairs={{0,1},{1,0},{2,3},{3,2},{4,5},{5,4},{6,7},{7,6},{8,9},{9,8},{10,11... | collective-permute-start | bytes 49160 | tf_op jit(solution)/shard_map/ppermute | solution.py:39
  72.8 5.2 %collective-permute-start.2 = (f32[32,128]{1,0:T(8,128)S(1)}, f32[32,128]{1,0:T(8,128)S(1)}, u32[]{:S(2)}, u32[]{:S(2)}) collective-permute-start(f32[32,128]{1,0:T(8,128)S(1)} %add.95), channel_id=1, source_target_pairs={{0,128},{128,0},{1,129},{129,1},{2,130},{130,2},{3,131},{131,3},{4... | collective-permute-start | bytes 49160 | tf_op jit(solution)/shard_map/ppermute | solution.py:39
  78.0 3.8 %collective-permute-start.3 = (f32[32,128]{1,0:T(8,128)S(1)}, f32[32,128]{1,0:T(8,128)S(1)}, u32[]{:S(2)}, u32[]{:S(2)}) collective-permute-start(f32[32,128]{1,0:T(8,128)S(1)} %add.96), channel_id=1, source_target_pairs={{0,32},{32,0},{64,96},{96,64},{1,33},{33,1},{65,97},{97,65},{2,34}... | collective-permute-start | bytes 49160 | tf_op jit(solution)/shard_map/ppermute | solution.py:39
  81.9 5.2 %collective-permute-start.4 = (f32[32,128]{1,0:T(8,128)S(1)}, f32[32,128]{1,0:T(8,128)S(1)}, u32[]{:S(2)}, u32[]{:S(2)}) collective-permute-start(f32[32,128]{1,0:T(8,128)S(1)} %add.97), channel_id=1, source_target_pairs={{0,64},{32,96},{64,0},{96,32},{1,65},{33,97},{65,1},{97,33},{2,66}... | collective-permute-start | bytes 49160 | tf_op jit(solution)/shard_map/ppermute | solution.py:39
  87.1 3.7 %collective-permute-start.5 = (f32[32,128]{1,0:T(8,128)S(1)}, f32[32,128]{1,0:T(8,128)S(1)}, u32[]{:S(2)}, u32[]{:S(2)}) collective-permute-start(f32[32,128]{1,0:T(8,128)S(1)} %add.98), channel_id=1, source_target_pairs={{0,2},{2,0},{4,6},{6,4},{8,10},{10,8},{12,14},{14,12},{1,3},{3,1},... | collective-permute-start | bytes 49160 | tf_op jit(solution)/shard_map/ppermute | solution.py:39
  90.9 4.6 %collective-permute-start.6 = (f32[32,128]{1,0:T(8,128)S(1)}, f32[32,128]{1,0:T(8,128)S(1)}, u32[]{:S(2)}, u32[]{:S(2)}) collective-permute-start(f32[32,128]{1,0:T(8,128)S(1)} %add.99), channel_id=1, source_target_pairs={{0,4},{2,6},{4,0},{6,2},{8,12},{10,14},{12,8},{14,10},{1,5},{3,7},... | collective-permute-start | bytes 49160 | tf_op jit(solution)/shard_map/ppermute | solution.py:39
  95.5 7.6 %collective-permute-start.7 = (f32[32,128]{1,0:T(8,128)S(1)}, f32[32,128]{1,0:T(8,128)S(1)}, u32[]{:S(2)}, u32[]{:S(2)}) collective-permute-start(f32[32,128]{1,0:T(8,128)S(1)} %add.100), channel_id=1, source_target_pairs={{0,8},{2,10},{4,12},{6,14},{8,0},{10,2},{12,4},{14,6},{1,9},{3,11}... | collective-permute-start | bytes 49160 | tf_op jit(solution)/shard_map/ppermute | solution.py:39
  109.9 1.2 collective-permute-start.8
  111.0 3.7 %collective-permute-start.9 = (f32[32,128]{1,0:T(8,128)S(1)}, f32[32,128]{1,0:T(8,128)S(1)}, u32[]{:S(2)}, u32[]{:S(2)}) collective-permute-start(f32[32,128]{1,0:T(8,128)S(1)} %add.102), channel_id=1, source_target_pairs={{0,1},{1,0},{2,3},{3,2},{4,5},{5,4},{6,7},{7,6},{8,9},{9,8},{10,11... | collective-permute-start | bytes 49160 | tf_op jit(solution)/shard_map/ppermute | solution.py:39
  114.8 5.2 %collective-permute-start.10 = (f32[32,128]{1,0:T(8,128)S(1)}, f32[32,128]{1,0:T(8,128)S(1)}, u32[]{:S(2)}, u32[]{:S(2)}) collective-permute-start(f32[32,128]{1,0:T(8,128)S(1)} %add.103), channel_id=1, source_target_pairs={{0,128},{128,0},{1,129},{129,1},{2,130},{130,2},{3,131},{131,3},{4... | collective-permute-start | bytes 49160 | tf_op jit(solution)/shard_map/ppermute | solution.py:39
  120.0 3.9 %collective-permute-start.11 = (f32[32,128]{1,0:T(8,128)S(1)}, f32[32,128]{1,0:T(8,128)S(1)}, u32[]{:S(2)}, u32[]{:S(2)}) collective-permute-start(f32[32,128]{1,0:T(8,128)S(1)} %add.104), channel_id=1, source_target_pairs={{0,32},{32,0},{64,96},{96,64},{1,33},{33,1},{65,97},{97,65},{2,34}... | collective-permute-start | bytes 49160 | tf_op jit(solution)/shard_map/ppermute | solution.py:39
  123.9 5.2 %collective-permute-start.12 = (f32[32,128]{1,0:T(8,128)S(1)}, f32[32,128]{1,0:T(8,128)S(1)}, u32[]{:S(2)}, u32[]{:S(2)}) collective-permute-start(f32[32,128]{1,0:T(8,128)S(1)} %add.105), channel_id=1, source_target_pairs={{0,64},{32,96},{64,0},{96,32},{1,65},{33,97},{65,1},{97,33},{2,66}... | collective-permute-start | bytes 49160 | tf_op jit(solution)/shard_map/ppermute | solution.py:39
  129.2 3.7 %collective-permute-start.13 = (f32[32,128]{1,0:T(8,128)S(1)}, f32[32,128]{1,0:T(8,128)S(1)}, u32[]{:S(2)}, u32[]{:S(2)}) collective-permute-start(f32[32,128]{1,0:T(8,128)S(1)} %add.106), channel_id=1, source_target_pairs={{0,2},{2,0},{4,6},{6,4},{8,10},{10,8},{12,14},{14,12},{1,3},{3,1},... | collective-permute-start | bytes 49160 | tf_op jit(solution)/shard_map/ppermute | solution.py:39
  132.9 4.6 %collective-permute-start.14 = (f32[32,128]{1,0:T(8,128)S(1)}, f32[32,128]{1,0:T(8,128)S(1)}, u32[]{:S(2)}, u32[]{:S(2)}) collective-permute-start(f32[32,128]{1,0:T(8,128)S(1)} %add.107), channel_id=1, source_target_pairs={{0,4},{2,6},{4,0},{6,2},{8,12},{10,14},{12,8},{14,10},{1,5},{3,7},... | collective-permute-start | bytes 49160 | tf_op jit(solution)/shard_map/ppermute | solution.py:39
  137.6 7.6 %collective-permute-start.15 = (f32[32,128]{1,0:T(8,128)S(1)}, f32[32,128]{1,0:T(8,128)S(1)}, u32[]{:S(2)}, u32[]{:S(2)}) collective-permute-start(f32[32,128]{1,0:T(8,128)S(1)} %add.108), channel_id=1, source_target_pairs={{0,8},{2,10},{4,12},{6,14},{8,0},{10,2},{12,4},{14,6},{1,9},{3,11}... | collective-permute-start | bytes 49160 | tf_op jit(solution)/shard_map/ppermute | solution.py:39
  261.7 1.8 collective-permute-start.16
  264.5 8.6 %collective-permute-start.17 = (f32[264,256]{1,0:T(8,128)S(1)}, f32[264,256]{1,0:T(8,128)S(1)}, u32[]{:S(2)}, u32[]{:S(2)}) collective-permute-start(f32[264,256]{1,0:T(8,128)S(1)} %add.112), channel_id=1, source_target_pairs={{0,32},{32,0},{64,96},{96,64},{1,33},{33,1},{65,97},{97,65},{2,34}... | collective-permute-start | bytes 811016 | tf_op jit(solution)/shard_map/ppermute | solution.py:39
  273.1 9.3 %collective-permute-start.18 = (f32[264,256]{1,0:T(8,128)S(1)}, f32[264,256]{1,0:T(8,128)S(1)}, u32[]{:S(2)}, u32[]{:S(2)}) collective-permute-start(f32[264,256]{1,0:T(8,128)S(1)} %add.113), channel_id=1, source_target_pairs={{0,64},{32,96},{64,0},{96,32},{1,65},{33,97},{65,1},{97,33},{2,66}... | collective-permute-start | bytes 811016 | tf_op jit(solution)/shard_map/ppermute | solution.py:39
  282.5 8.4 %collective-permute-start.19 = (f32[264,256]{1,0:T(8,128)S(1)}, f32[264,256]{1,0:T(8,128)S(1)}, u32[]{:S(2)}, u32[]{:S(2)}) collective-permute-start(f32[264,256]{1,0:T(8,128)S(1)} %add.114), channel_id=1, source_target_pairs={{0,128},{128,0},{1,129},{129,1},{2,130},{130,2},{3,131},{131,3},{4... | collective-permute-start | bytes 811016 | tf_op jit(solution)/shard_map/ppermute | solution.py:39
Sparse Core Ops, SparseCore 0:
  15.5 44.0 all-gather.1
  160.6 101.1 reduce-scatter.1

commit v10 on v9

--- a/solution.py
+++ b/solution.py
@@ -155,9 +155,13 @@
     mass_ratio = local_rows * row_devices / local_cands
     col_index = lax.axis_index("z") * sizes["yl"] + lax.axis_index("yl")
     own_start = col_index * local_cands
-    gathered = lax.all_gather(
-        lax.all_gather(normalize(cand_rows), "yl", axis=0, tiled=True), "z", axis=0, tiled=True
-    )
+    own_cn = normalize(cand_rows)
+    pair_cn = lax.ppermute(own_cn, "yl", [(0, 1), (1, 0)])
+    first_lo = lax.axis_index("yl") == 0
+    slab = jnp.concatenate(
+        [jnp.where(first_lo, own_cn, pair_cn), jnp.where(first_lo, pair_cn, own_cn)], axis=0
+    )
+    gathered = lax.all_gather(slab, "z", axis=0, tiled=True)
     cn_blocks = gathered.reshape(block_count, BLOCK, feature_count)
     xn = normalize(data_rows)
     mass_col = data_mass.reshape(local_rows, 1)
@@ -169,9 +173,17 @@
         scale_blocks = mass_ratio * cand_mass.reshape(block_count, BLOCK) / whole_total
     ds_col, packed = sweep(xn, cn_blocks, scale_blocks, mass_col, links, rows=data_rows)
     joined = lax.psum_scatter(packed.reshape(-1, feature_count), COL_AXES, scatter_dimension=0, tiled=True)
-    joined = butterfly_sum(joined, ("c", "x", "yh"), sizes)
-    own_sums = joined[:local_cands]
-    own_total = joined[local_cands]
+    first_core = lax.axis_index("c") == 0
+    sums_a, sums_b, totals = joined[:BLOCK], joined[BLOCK:2 * BLOCK], joined[2 * BLOCK:]
+    keep = jnp.concatenate([jnp.where(first_core, sums_a, sums_b), totals], axis=0)
+    give = jnp.concatenate([jnp.where(first_core, sums_b, sums_a), totals], axis=0)
+    mine = keep + lax.ppermute(give, "c", [(0, 1), (1, 0)])
+    mine = butterfly_sum(mine, ("x", "yh"), sizes)
+    other = lax.ppermute(mine, "c", [(0, 1), (1, 0)])
+    low = jnp.where(first_core, mine, other)
+    high = jnp.where(first_core, other, mine)
+    own_sums = jnp.concatenate([low[:BLOCK], high[:BLOCK]], axis=0)
+    own_total = low[BLOCK]
     own_scale = mass_ratio * lax.dynamic_slice_in_dim(cand_mass, own_start, local_cands) / own_total
     new_support = own_sums / own_total[:, None]
     return (ds_col.reshape(local_rows), own_scale, new_support)

time: 299 us -> 296 us (0.990)
  blocking collectives: 6.02 us -> 0 us
  waiting for transfers between devices: 214 us -> 210 us
  starting transfers between devices: 27.6 us -> 31 us
    ppermute x20 -> x19, waiting for transfers between devices: 70.2 us -> 60.7 us  [butterfly_sum(): x = x + lax.ppermute(x, axis, [(j, j ^ k) for j in range(n)])]
    all_gather x1 -> x0, blocking collectives: 6.02 us -> none  [on_device(): lax.all_gather(normalize(cand_rows), 'yl', axis=0, tiled=True)]
    ppermute x0 -> x3, waiting for transfers between devices: none -> 5.47 us  [the longest x1 3.66 us: on_device(): pair_cn = lax.ppermute(own_cn, 'yl', [(0, 1), (1, 0)])]
    ppermute x20 -> x19, starting transfers between devices: 27.5 us -> 29.1 us  [butterfly_sum(): x = x + lax.ppermute(x, axis, [(j, j ^ k) for j in range(n)])]
  transfers between devices with their start and end apart: 22 -> 24, of which waited for: 22 -> 24; matrix products, arithmetic and copies ran while one was open for 1% -> 1% of each run, Pallas kernels for 0% -> 0%
where the time goes in v10:
time: 296 us; the launch traced here: 294 us
  waiting for transfers between devices  210 us (71%)
  starting transfers between devices  31 us (10%)
  Pallas kernels  28.6 us (10%)
  between operations  14.2 us (5%)
  other arithmetic  7.92 us (3%)
    reduce_scatter x1, waiting for transfers between devices, on_device(): lax.psum_scatter(packed.reshape(-1, feature_count), COL_AXES, scatter_dim...  101 us
    ppermute x19, waiting for transfers between devices, butterfly_sum(): x = x + lax.ppermute(x, axis, [(j, j ^ k) for j in range(n)])  60.7 us
    all_gather x1, waiting for transfers between devices, on_device(): gathered = lax.all_gather(slab, 'z', axis=0, tiled=True)  43.3 us
    ppermute x19, starting transfers between devices, butterfly_sum(): x = x + lax.ppermute(x, axis, [(j, j ^ k) for j in range(n)])  29.1 us
    pallas_call x3, Pallas kernels, sweep(): pl.pallas_call(functools.partial(sweep_body, nbr, inv_width, inv_count, b...  28.6 us
  transfers between devices with their start and end apart: 24, of which 24 were waited for; matrix products, arithmetic and copies ran while one was open for 1% of the time, Pallas kernels for 0%

profile of v10, /device:TPU:4, one launch (start us, length us, event | category | flops | bytes accessed | tf_op | source)
XLA Modules:
  0.0 294.3 jit_solution(2755965077981907349)
XLA Ops:
  7.2 0.0 all-gather.2.cloned.1.call-start
  7.2 1.1 fusion.2
  8.3 1.0 fusion.3
  9.3 1.7 collective-permute-start
  11.0 3.7 %collective-permute-done = bf16[256,256]{1,0:T(8,128)(2,1)S(1)} collective-permute-done((bf16[256,256]{1,0:T(8,128)(2,1)S(1)}, bf16[256,256]{1,0:T(8,128)(2,1)S(1)}, u32[]{:S(2)}, u32[]{:S(2)}) %collective-permute-start) | collective-permute-done | bytes 131104 | tf_op jit(solution)/shard_map/ppermute | solution.py:159
  14.7 1.0 broadcast_select_fusion.1
  15.7 0.7 pad_maximum_fusion
  16.4 0.0 all-gather.2.cloned.1.call-update
  16.5 0.0 reduce-scatter.2.cloned.1.call-start
  16.5 0.3 reshape.43.mass_ref
  16.8 0.3 fusion
  17.1 0.3 fusion.1.xn_ref
  17.4 43.3 %all-gather.2.cloned.1.call-done = bf16[4096,256]{1,0:T(8,128)(2,1)} async-done(((bf16[512,256]{1,0:T(8,128)(2,1)}), bf16[4096,256]{1,0:T(8,128)(2,1)}) %all-gather.2.cloned.1.call-update) | async-done | bytes 2097168 | tf_op jit(solution)/shard_map/all_gather | solution.py:164
  60.7 1.6 copy-done.1
  62.2 6.7 %shard_map.76 = (f32[1536,1]{1,0:T(8,128)}, f32[32,128]{1,0:T(8,128)S(1)}) custom-call(s32[12,16]{1,0:T(8,128)S(1)} %copy-done.2, bf16[1536,256]{1,0:T(8,128)(2,1)S(1)} %fusion.1.xn_ref, bf16[32,128,256]{2,1,0:T(8,128)(2,1)S(1)} %bitcast.6, f32[32,128]{1,0:T(8,128)S(1)} %broadcast_in_dim.2.scale_ref, f32[1536,1]{1,0:T(8,128)S(1)} %reshape.43.mass_ref), custom_call_target="tpu_custom_call" | custom-call | flops 1610612736 | bytes 2883584 | tf_op jit(solution)/shard_map/pallas_call | solution.py:126
  68.9 1.2 collective-permute-done.1
  70.1 1.5 collective-permute-start.2
  71.6 2.3 collective-permute-done.2
  73.9 3.0 %collective-permute-start.3 = (f32[32,128]{1,0:T(8,128)S(1)}, f32[32,128]{1,0:T(8,128)S(1)}, u32[]{:S(2)}, u32[]{:S(2)}) collective-permute-start(f32[32,128]{1,0:T(8,128)S(1)} %add.95), channel_id=1, source_target_pairs={{0,128},{128,0},{1,129},{129,1},{2,130},{130,2},{3,131},{131,3},{4... | collective-permute-start | bytes 49160 | tf_op jit(solution)/shard_map/ppermute | solution.py:39
  76.9 2.2 collective-permute-done.3
  79.1 1.2 collective-permute-start.4
  80.3 2.7 collective-permute-done.4
  83.0 0.5 collective-permute-start.5
  83.4 4.8 %collective-permute-done.5 = f32[32,128]{1,0:T(8,128)S(1)} collective-permute-done((f32[32,128]{1,0:T(8,128)S(1)}, f32[32,128]{1,0:T(8,128)S(1)}, u32[]{:S(2)}, u32[]{:S(2)}) %collective-permute-start.5) | collective-permute-done | bytes 16416 | tf_op jit(solution)/shard_map/ppermute | solution.py:39
  88.2 1.2 collective-permute-start.6
  89.4 2.5 collective-permute-done.6
  91.9 1.3 collective-permute-start.7
  93.2 3.4 %collective-permute-done.7 = f32[32,128]{1,0:T(8,128)S(1)} collective-permute-done((f32[32,128]{1,0:T(8,128)S(1)}, f32[32,128]{1,0:T(8,128)S(1)}, u32[]{:S(2)}, u32[]{:S(2)}) %collective-permute-start.7) | collective-permute-done | bytes 16416 | tf_op jit(solution)/shard_map/ppermute | solution.py:39
  96.6 3.0 %collective-permute-start.8 = (f32[32,128]{1,0:T(8,128)S(1)}, f32[32,128]{1,0:T(8,128)S(1)}, u32[]{:S(2)}, u32[]{:S(2)}) collective-permute-start(f32[32,128]{1,0:T(8,128)S(1)} %add.100), channel_id=1, source_target_pairs={{0,8},{2,10},{4,12},{6,14},{8,0},{10,2},{12,4},{14,6},{1,9},{3,11}... | collective-permute-start | bytes 49160 | tf_op jit(solution)/shard_map/ppermute | solution.py:39
  99.6 4.7 %collective-permute-done.8 = f32[32,128]{1,0:T(8,128)S(1)} collective-permute-done((f32[32,128]{1,0:T(8,128)S(1)}, f32[32,128]{1,0:T(8,128)S(1)}, u32[]{:S(2)}, u32[]{:S(2)}) %collective-permute-start.8) | collective-permute-done | bytes 16416 | tf_op jit(solution)/shard_map/ppermute | solution.py:39
  104.2 6.7 %shard_map.77 = (f32[1536,1]{1,0:T(8,128)}, f32[32,128]{1,0:T(8,128)S(1)}) custom-call(s32[12,16]{1,0:T(8,128)S(1)} %copy-done.2, bf16[1536,256]{1,0:T(8,128)(2,1)S(1)} %fusion.1.xn_ref, bf16[32,128,256]{2,1,0:T(8,128)(2,1)S(1)} %bitcast.7, f32[32,128]{1,0:T(8,128)S(1)} %bitcast_divide_fusion.1.scale_ref, f32[1536,1]{1,0:T(8,128)S(1)} %reshape.43.mass_ref), custom_call_target="tpu_custom_call" | custom-call | flops 1610612736 | bytes 2883584 | tf_op jit(solution)/shard_map/pallas_call | solution.py:126
  110.9 1.2 collective-permute-done.9
  112.1 1.5 collective-permute-start.10
  113.6 2.3 collective-permute-done.10
  115.9 3.0 %collective-permute-start.11 = (f32[32,128]{1,0:T(8,128)S(1)}, f32[32,128]{1,0:T(8,128)S(1)}, u32[]{:S(2)}, u32[]{:S(2)}) collective-permute-start(f32[32,128]{1,0:T(8,128)S(1)} %add.103), channel_id=1, source_target_pairs={{0,128},{128,0},{1,129},{129,1},{2,130},{130,2},{3,131},{131,3},{4... | collective-permute-start | bytes 49160 | tf_op jit(solution)/shard_map/ppermute | solution.py:39
  118.9 2.2 collective-permute-done.11
  121.1 1.1 collective-permute-start.12
  122.2 2.8 collective-permute-done.12
  125.0 0.3 collective-permute-start.13
  125.3 4.9 %collective-permute-done.13 = f32[32,128]{1,0:T(8,128)S(1)} collective-permute-done((f32[32,128]{1,0:T(8,128)S(1)}, f32[32,128]{1,0:T(8,128)S(1)}, u32[]{:S(2)}, u32[]{:S(2)}) %collective-permute-start.13) | collective-permute-done | bytes 16416 | tf_op jit(solution)/shard_map/ppermute | solution.py:39
  130.3 1.2 collective-permute-start.14
  131.4 2.6 collective-permute-done.14
  134.0 1.3 collective-permute-start.15
  135.3 3.4 %collective-permute-done.15 = f32[32,128]{1,0:T(8,128)S(1)} collective-permute-done((f32[32,128]{1,0:T(8,128)S(1)}, f32[32,128]{1,0:T(8,128)S(1)}, u32[]{:S(2)}, u32[]{:S(2)}) %collective-permute-start.15) | collective-permute-done | bytes 16416 | tf_op jit(solution)/shard_map/ppermute | solution.py:39
  138.7 3.0 %collective-permute-start.16 = (f32[32,128]{1,0:T(8,128)S(1)}, f32[32,128]{1,0:T(8,128)S(1)}, u32[]{:S(2)}, u32[]{:S(2)}) collective-permute-start(f32[32,128]{1,0:T(8,128)S(1)} %add.108), channel_id=1, source_target_pairs={{0,8},{2,10},{4,12},{6,14},{8,0},{10,2},{12,4},{14,6},{1,9},{3,11}... | collective-permute-start | bytes 49160 | tf_op jit(solution)/shard_map/ppermute | solution.py:39
  141.6 4.7 %collective-permute-done.16 = f32[32,128]{1,0:T(8,128)S(1)} collective-permute-done((f32[32,128]{1,0:T(8,128)S(1)}, f32[32,128]{1,0:T(8,128)S(1)}, u32[]{:S(2)}, u32[]{:S(2)}) %collective-permute-start.16) | collective-permute-done | bytes 16416 | tf_op jit(solution)/shard_map/ppermute | solution.py:39
  146.3 15.2 %shard_map.78 = (f32[1536,1]{1,0:T(8,128)S(1)}, f32[16,264,256]{2,1,0:T(8,128)}) custom-call(s32[12,16]{1,0:T(8,128)S(1)} %copy-done.2, bf16[1536,256]{1,0:T(8,128)(2,1)S(1)} %fusion.1.xn_ref, bf16[32,128,256]{2,1,0:T(8,128)(2,1)S(1)} %bitcast.8, f32[32,128]{1,0:T(8,128)S(1)} %bitcast_divide_fusion.scale_ref, f32[1536,1]{1,0:T(8,128)S(1)} %reshape.43.mass_ref, ...), custom_call_target="tpu_custom_call" | custom-call | flops 3221225472 | bytes 7864320 | tf_op jit(solution)/shard_map/pallas_call | solution.py:126
  161.5 0.0 reduce-scatter.2.cloned.1.call-update
  161.6 100.6 %reduce-scatter.2.cloned.1.call-done = f32[264,256]{1,0:T(8,128)} async-done(((f32[4224,256]{1,0:T(8,128)}), f32[264,256]{1,0:T(8,128)}) %reduce-scatter.2.cloned.1.call-update) | async-done | bytes 270352 | tf_op jit(solution)/shard_map/reduce_scatter | solution.py:175
  262.1 0.7 slice.26
  262.8 1.0 slice_select_fusion.2
  263.8 0.1 collective-permute-start.17
  263.9 1.3 collective-permute-done.17
  265.3 1.3 collective-permute-start.18
  266.6 4.5 %collective-permute-done.18 = f32[136,256]{1,0:T(8,128)S(1)} collective-permute-done((f32[136,256]{1,0:T(8,128)S(1)}, f32[136,256]{1,0:T(8,128)S(1)}, u32[]{:S(2)}, u32[]{:S(2)}) %collective-permute-start.18) | collective-permute-done | bytes 139296 | tf_op jit(solution)/shard_map/ppermute | solution.py:39
  271.1 1.3 collective-permute-start.19
  272.5 5.3 %collective-permute-done.19 = f32[136,256]{1,0:T(8,128)S(1)} collective-permute-done((f32[136,256]{1,0:T(8,128)S(1)}, f32[136,256]{1,0:T(8,128)S(1)}, u32[]{:S(2)}, u32[]{:S(2)}) %collective-permute-start.19) | collective-permute-done | bytes 139296 | tf_op jit(solution)/shard_map/ppermute | solution.py:39
  277.8 3.7 %collective-permute-start.20 = (f32[136,256]{1,0:T(8,128)S(1)}, f32[136,256]{1,0:T(8,128)S(1)}, u32[]{:S(2)}, u32[]{:S(2)}) collective-permute-start(f32[136,256]{1,0:T(8,128)S(1)} %add.114), channel_id=1, source_target_pairs={{0,128},{128,0},{1,129},{129,1},{2,130},{130,2},{3,131},{131,3},{4... | collective-permute-start | bytes 417800 | tf_op jit(solution)/shard_map/ppermute | solution.py:39
  281.4 3.0 %collective-permute-done.20 = f32[136,256]{1,0:T(8,128)S(1)} collective-permute-done((f32[136,256]{1,0:T(8,128)S(1)}, f32[136,256]{1,0:T(8,128)S(1)}, u32[]{:S(2)}, u32[]{:S(2)}) %collective-permute-start.20) | collective-permute-done | bytes 139296 | tf_op jit(solution)/shard_map/ppermute | solution.py:39
  284.5 0.1 collective-permute-start.21
  284.6 0.9 reduce
  285.5 0.5 collective-permute-done.21
  286.0 0.6 multiply_divide_fusion
  286.7 0.8 maximum_divide_fusion
  (39 shorter events, 0.3 us)
Async XLA Ops:
  7.2 9.4 %copy-start.4 = (f32[1536]{0:T(1024)S(1)}, f32[1536]{0:T(1024)}, u32[]{:S(2)}) copy-start(f32[1536]{0:T(1024)} %param.6) | copy-start | bytes 18436
  7.2 9.6 %copy-start = (bf16[1536,256]{1,0:T(8,128)(2,1)S(1)}, bf16[1536,256]{1,0:T(8,128)(2,1)}, u32[]{:S(2)}) copy-start(bf16[1536,256]{1,0:T(8,128)(2,1)} %rest_0_.1) | copy-start | bytes 2359300
  7.2 53.5 %all-gather.2.cloned.1.call-start = ((), (), s32[]{:S(2)}) async-start(), calls=%async_computation.1 | async-start | bytes 2359296 | tf_op jit(solution)/shard_map/all_gather | solution.py:164
  9.3 5.3 %collective-permute-start = (bf16[256,256]{1,0:T(8,128)(2,1)S(1)}, bf16[256,256]{1,0:T(8,128)(2,1)S(1)}, u32[]{:S(2)}, u32[]{:S(2)}) collective-permute-start(bf16[256,256]{1,0:T(8,128)(2,1)S(1)} %fusion.3), channel_id=1, source_target_pairs={{0,1},{1,0},{2,3},{3,2},{4,5},{5,4},{6,7},{7,6},{8,9},{9,8},{10,11... | collective-permute-start | bytes 393224 | tf_op jit(solution)/shard_map/ppermute | solution.py:159
  16.4 44.2 %copy-start.2 = (s32[12,16]{1,0:T(8,128)S(1)}, s32[12,16]{1,0:T(8,128)}, u32[]{:S(2)}) copy-start(s32[12,16]{1,0:T(8,128)} %links_ref.5) | copy-start | bytes 2308
  16.5 245.7 %reduce-scatter.2.cloned.1.call-start = ((), (), s32[]{:S(2)}) async-start(), calls=%async_computation.2 | async-start | bytes 4595712 | tf_op jit(solution)/shard_map/reduce_scatter | solution.py:175
  60.7 1.6 copy-start.1
  62.2 42.0 %copy-start.3 = (f32[4096]{0:T(1024)S(1)}, f32[4096]{0:T(1024)}, u32[]{:S(2)}) copy-start(f32[4096]{0:T(1024)} %param.9) | copy-start | bytes 49156
  68.9 1.2 collective-permute-start.1
  70.1 3.7 %collective-permute-start.2 = (f32[32,128]{1,0:T(8,128)S(1)}, f32[32,128]{1,0:T(8,128)S(1)}, u32[]{:S(2)}, u32[]{:S(2)}) collective-permute-start(f32[32,128]{1,0:T(8,128)S(1)} %add.94), channel_id=1, source_target_pairs={{0,1},{1,0},{2,3},{3,2},{4,5},{5,4},{6,7},{7,6},{8,9},{9,8},{10,11... | collective-permute-start | bytes 49160 | tf_op jit(solution)/shard_map/ppermute | solution.py:39
  73.9 5.2 %collective-permute-start.3 = (f32[32,128]{1,0:T(8,128)S(1)}, f32[32,128]{1,0:T(8,128)S(1)}, u32[]{:S(2)}, u32[]{:S(2)}) collective-permute-start(f32[32,128]{1,0:T(8,128)S(1)} %add.95), channel_id=1, source_target_pairs={{0,128},{128,0},{1,129},{129,1},{2,130},{130,2},{3,131},{131,3},{4... | collective-permute-start | bytes 49160 | tf_op jit(solution)/shard_map/ppermute | solution.py:39
  79.1 3.8 %collective-permute-start.4 = (f32[32,128]{1,0:T(8,128)S(1)}, f32[32,128]{1,0:T(8,128)S(1)}, u32[]{:S(2)}, u32[]{:S(2)}) collective-permute-start(f32[32,128]{1,0:T(8,128)S(1)} %add.96), channel_id=1, source_target_pairs={{0,32},{32,0},{64,96},{96,64},{1,33},{33,1},{65,97},{97,65},{2,34}... | collective-permute-start | bytes 49160 | tf_op jit(solution)/shard_map/ppermute | solution.py:39
  83.0 5.2 %collective-permute-start.5 = (f32[32,128]{1,0:T(8,128)S(1)}, f32[32,128]{1,0:T(8,128)S(1)}, u32[]{:S(2)}, u32[]{:S(2)}) collective-permute-start(f32[32,128]{1,0:T(8,128)S(1)} %add.97), channel_id=1, source_target_pairs={{0,64},{32,96},{64,0},{96,32},{1,65},{33,97},{65,1},{97,33},{2,66}... | collective-permute-start | bytes 49160 | tf_op jit(solution)/shard_map/ppermute | solution.py:39
  88.2 3.7 %collective-permute-start.6 = (f32[32,128]{1,0:T(8,128)S(1)}, f32[32,128]{1,0:T(8,128)S(1)}, u32[]{:S(2)}, u32[]{:S(2)}) collective-permute-start(f32[32,128]{1,0:T(8,128)S(1)} %add.98), channel_id=1, source_target_pairs={{0,2},{2,0},{4,6},{6,4},{8,10},{10,8},{12,14},{14,12},{1,3},{3,1},... | collective-permute-start | bytes 49160 | tf_op jit(solution)/shard_map/ppermute | solution.py:39
  91.9 4.6 %collective-permute-start.7 = (f32[32,128]{1,0:T(8,128)S(1)}, f32[32,128]{1,0:T(8,128)S(1)}, u32[]{:S(2)}, u32[]{:S(2)}) collective-permute-start(f32[32,128]{1,0:T(8,128)S(1)} %add.99), channel_id=1, source_target_pairs={{0,4},{2,6},{4,0},{6,2},{8,12},{10,14},{12,8},{14,10},{1,5},{3,7},... | collective-permute-start | bytes 49160 | tf_op jit(solution)/shard_map/ppermute | solution.py:39
  96.6 7.6 %collective-permute-start.8 = (f32[32,128]{1,0:T(8,128)S(1)}, f32[32,128]{1,0:T(8,128)S(1)}, u32[]{:S(2)}, u32[]{:S(2)}) collective-permute-start(f32[32,128]{1,0:T(8,128)S(1)} %add.100), channel_id=1, source_target_pairs={{0,8},{2,10},{4,12},{6,14},{8,0},{10,2},{12,4},{14,6},{1,9},{3,11}... | collective-permute-start | bytes 49160 | tf_op jit(solution)/shard_map/ppermute | solution.py:39
  110.9 1.2 collective-permute-start.9
  112.1 3.7 %collective-permute-start.10 = (f32[32,128]{1,0:T(8,128)S(1)}, f32[32,128]{1,0:T(8,128)S(1)}, u32[]{:S(2)}, u32[]{:S(2)}) collective-permute-start(f32[32,128]{1,0:T(8,128)S(1)} %add.102), channel_id=1, source_target_pairs={{0,1},{1,0},{2,3},{3,2},{4,5},{5,4},{6,7},{7,6},{8,9},{9,8},{10,11... | collective-permute-start | bytes 49160 | tf_op jit(solution)/shard_map/ppermute | solution.py:39
  115.9 5.2 %collective-permute-start.11 = (f32[32,128]{1,0:T(8,128)S(1)}, f32[32,128]{1,0:T(8,128)S(1)}, u32[]{:S(2)}, u32[]{:S(2)}) collective-permute-start(f32[32,128]{1,0:T(8,128)S(1)} %add.103), channel_id=1, source_target_pairs={{0,128},{128,0},{1,129},{129,1},{2,130},{130,2},{3,131},{131,3},{4... | collective-permute-start | bytes 49160 | tf_op jit(solution)/shard_map/ppermute | solution.py:39
  121.1 3.9 %collective-permute-start.12 = (f32[32,128]{1,0:T(8,128)S(1)}, f32[32,128]{1,0:T(8,128)S(1)}, u32[]{:S(2)}, u32[]{:S(2)}) collective-permute-start(f32[32,128]{1,0:T(8,128)S(1)} %add.104), channel_id=1, source_target_pairs={{0,32},{32,0},{64,96},{96,64},{1,33},{33,1},{65,97},{97,65},{2,34}... | collective-permute-start | bytes 49160 | tf_op jit(solution)/shard_map/ppermute | solution.py:39
  125.0 5.2 %collective-permute-start.13 = (f32[32,128]{1,0:T(8,128)S(1)}, f32[32,128]{1,0:T(8,128)S(1)}, u32[]{:S(2)}, u32[]{:S(2)}) collective-permute-start(f32[32,128]{1,0:T(8,128)S(1)} %add.105), channel_id=1, source_target_pairs={{0,64},{32,96},{64,0},{96,32},{1,65},{33,97},{65,1},{97,33},{2,66}... | collective-permute-start | bytes 49160 | tf_op jit(solution)/shard_map/ppermute | solution.py:39
  130.3 3.7 %collective-permute-start.14 = (f32[32,128]{1,0:T(8,128)S(1)}, f32[32,128]{1,0:T(8,128)S(1)}, u32[]{:S(2)}, u32[]{:S(2)}) collective-permute-start(f32[32,128]{1,0:T(8,128)S(1)} %add.106), channel_id=1, source_target_pairs={{0,2},{2,0},{4,6},{6,4},{8,10},{10,8},{12,14},{14,12},{1,3},{3,1},... | collective-permute-start | bytes 49160 | tf_op jit(solution)/shard_map/ppermute | solution.py:39
  134.0 4.6 %collective-permute-start.15 = (f32[32,128]{1,0:T(8,128)S(1)}, f32[32,128]{1,0:T(8,128)S(1)}, u32[]{:S(2)}, u32[]{:S(2)}) collective-permute-start(f32[32,128]{1,0:T(8,128)S(1)} %add.107), channel_id=1, source_target_pairs={{0,4},{2,6},{4,0},{6,2},{8,12},{10,14},{12,8},{14,10},{1,5},{3,7},... | collective-permute-start | bytes 49160 | tf_op jit(solution)/shard_map/ppermute | solution.py:39
  138.7 7.6 %collective-permute-start.16 = (f32[32,128]{1,0:T(8,128)S(1)}, f32[32,128]{1,0:T(8,128)S(1)}, u32[]{:S(2)}, u32[]{:S(2)}) collective-permute-start(f32[32,128]{1,0:T(8,128)S(1)} %add.108), channel_id=1, source_target_pairs={{0,8},{2,10},{4,12},{6,14},{8,0},{10,2},{12,4},{14,6},{1,9},{3,11}... | collective-permute-start | bytes 49160 | tf_op jit(solution)/shard_map/ppermute | solution.py:39
  263.8 1.4 collective-permute-start.17
  265.3 5.8 %collective-permute-start.18 = (f32[136,256]{1,0:T(8,128)S(1)}, f32[136,256]{1,0:T(8,128)S(1)}, u32[]{:S(2)}, u32[]{:S(2)}) collective-permute-start(f32[136,256]{1,0:T(8,128)S(1)} %fusion.4), channel_id=1, source_target_pairs={{0,32},{32,0},{64,96},{96,64},{1,33},{33,1},{65,97},{97,65},{2,34}... | collective-permute-start | bytes 417800 | tf_op jit(solution)/shard_map/ppermute | solution.py:39
  271.1 6.6 %collective-permute-start.19 = (f32[136,256]{1,0:T(8,128)S(1)}, f32[136,256]{1,0:T(8,128)S(1)}, u32[]{:S(2)}, u32[]{:S(2)}) collective-permute-start(f32[136,256]{1,0:T(8,128)S(1)} %add.113), channel_id=1, source_target_pairs={{0,64},{32,96},{64,0},{96,32},{1,65},{33,97},{65,1},{97,33},{2,66}... | collective-permute-start | bytes 417800 | tf_op jit(solution)/shard_map/ppermute | solution.py:39
  277.8 6.7 %collective-permute-start.20 = (f32[136,256]{1,0:T(8,128)S(1)}, f32[136,256]{1,0:T(8,128)S(1)}, u32[]{:S(2)}, u32[]{:S(2)}) collective-permute-start(f32[136,256]{1,0:T(8,128)S(1)} %add.114), channel_id=1, source_target_pairs={{0,128},{128,0},{1,129},{129,1},{2,130},{130,2},{3,131},{131,3},{4... | collective-permute-start | bytes 417800 | tf_op jit(solution)/shard_map/ppermute | solution.py:39
  284.5 1.4 collective-permute-start.21
Sparse Core Ops, SparseCore 0:
  16.6 44.0 all-gather.1
  161.7 100.4 reduce-scatter.1

commit v11 on v10

--- a/solution.py
+++ b/solution.py
@@ -172,7 +172,12 @@
         whole_total = butterfly_sum(part_total, TOTAL_ORDER, sizes)
         scale_blocks = mass_ratio * cand_mass.reshape(block_count, BLOCK) / whole_total
     ds_col, packed = sweep(xn, cn_blocks, scale_blocks, mass_col, links, rows=data_rows)
-    joined = lax.psum_scatter(packed.reshape(-1, feature_count), COL_AXES, scatter_dimension=0, tiled=True)
+    pair = lax.psum_scatter(packed.reshape(-1, feature_count), "z", scatter_dimension=0, tiled=True)
+    part_rows = pair.shape[0] // 2
+    first_lo = lax.axis_index("yl") == 0
+    keep = jnp.where(first_lo, pair[:part_rows], pair[part_rows:])
+    give = jnp.where(first_lo, pair[part_rows:], pair[:part_rows])
+    joined = keep + lax.ppermute(give, "yl", [(0, 1), (1, 0)])
     first_core = lax.axis_index("c") == 0
     sums_a, sums_b, totals = joined[:BLOCK], joined[BLOCK:2 * BLOCK], joined[2 * BLOCK:]
     keep = jnp.concatenate([jnp.where(first_core, sums_a, sums_b), totals], axis=0)

time: 296 us -> 259 us (0.88)
  waiting for transfers between devices: 210 us -> 173 us
    reduce_scatter x1, waiting for transfers between devices: 101 us -> 55.2 us  [on_device(): lax.psum_scatter(packed.reshape(-1, feature_count), 'z', scatter_dimensio...]
    ppermute x0 -> x1, waiting for transfers between devices: none -> 6.8 us  [on_device(): joined = keep + lax.ppermute(give, 'yl', [(0, 1), (1, 0)])]
  transfers between devices with their start and end apart: 24 -> 25, of which waited for: 24 -> 25; matrix products, arithmetic and copies ran while one was open for 1% -> 1% of each run, Pallas kernels for 0% -> 0%
where the time goes in v11:
time: 259 us; the launch traced here: 258 us
  waiting for transfers between devices  173 us (67%)
  starting transfers between devices  31.2 us (12%)
  Pallas kernels  28.6 us (11%)
  between operations  14.3 us (6%)
  other arithmetic  9.14 us (4%)
    ppermute x19, waiting for transfers between devices, butterfly_sum(): x = x + lax.ppermute(x, axis, [(j, j ^ k) for j in range(n)])  62 us
    reduce_scatter x1, waiting for transfers between devices, on_device(): lax.psum_scatter(packed.reshape(-1, feature_count), 'z', scatter_dimensio...  55.2 us
    all_gather x1, waiting for transfers between devices, on_device(): gathered = lax.all_gather(slab, 'z', axis=0, tiled=True)  43.3 us
    pallas_call x3, Pallas kernels, sweep(): pl.pallas_call(functools.partial(sweep_body, nbr, inv_width, inv_count, b...  28.6 us
    ppermute x19, starting transfers between devices, butterfly_sum(): x = x + lax.ppermute(x, axis, [(j, j ^ k) for j in range(n)])  27.7 us
    ppermute x1, waiting for transfers between devices, on_device(): joined = keep + lax.ppermute(give, 'yl', [(0, 1), (1, 0)])  6.8 us
  transfers between devices with their start and end apart: 25, of which 25 were waited for; matrix products, arithmetic and copies ran while one was open for 1% of the time, Pallas kernels for 0%

profile of v11, /device:TPU:4, one launch (start us, length us, event | category | flops | bytes accessed | tf_op | source)
XLA Modules:
  0.0 257.8 jit_solution(14013322605375762054)
XLA Ops:
  7.2 0.0 all-gather.2.cloned.1.call-start
  7.2 1.1 fusion.2
  8.3 1.0 fusion.3
  9.3 1.7 collective-permute-start
  11.0 3.7 %collective-permute-done = bf16[256,256]{1,0:T(8,128)(2,1)S(1)} collective-permute-done((bf16[256,256]{1,0:T(8,128)(2,1)S(1)}, bf16[256,256]{1,0:T(8,128)(2,1)S(1)}, u32[]{:S(2)}, u32[]{:S(2)}) %collective-permute-start) | collective-permute-done | bytes 131104 | tf_op jit(solution)/shard_map/ppermute | solution.py:159
  14.7 1.0 broadcast_select_fusion.1
  15.7 0.7 pad_maximum_fusion
  16.5 0.0 reduce-scatter.2.cloned.1.call-start
  16.5 0.3 reshape.43.mass_ref
  16.8 0.3 fusion
  17.1 0.3 fusion.1.xn_ref
  17.4 43.3 %all-gather.2.cloned.1.call-done = bf16[4096,256]{1,0:T(8,128)(2,1)} async-done(((bf16[512,256]{1,0:T(8,128)(2,1)}), bf16[4096,256]{1,0:T(8,128)(2,1)}) %all-gather.2.cloned.1.call-update) | async-done | bytes 2097168 | tf_op jit(solution)/shard_map/all_gather | solution.py:164
  60.7 1.6 copy-done.1
  62.2 6.7 %shard_map.76 = (f32[1536,1]{1,0:T(8,128)}, f32[32,128]{1,0:T(8,128)S(1)}) custom-call(s32[12,16]{1,0:T(8,128)S(1)} %copy-done.2, bf16[1536,256]{1,0:T(8,128)(2,1)S(1)} %fusion.1.xn_ref, bf16[32,128,256]{2,1,0:T(8,128)(2,1)S(1)} %bitcast.6, f32[32,128]{1,0:T(8,128)S(1)} %broadcast_in_dim.2.scale_ref, f32[1536,1]{1,0:T(8,128)S(1)} %reshape.43.mass_ref), custom_call_target="tpu_custom_call" | custom-call | flops 1610612736 | bytes 2883584 | tf_op jit(solution)/shard_map/pallas_call | solution.py:126
  69.0 1.2 collective-permute-done.1
  70.1 1.5 collective-permute-start.2
  71.6 2.3 collective-permute-done.2
  73.9 3.0 %collective-permute-start.3 = (f32[32,128]{1,0:T(8,128)S(1)}, f32[32,128]{1,0:T(8,128)S(1)}, u32[]{:S(2)}, u32[]{:S(2)}) collective-permute-start(f32[32,128]{1,0:T(8,128)S(1)} %add.98), channel_id=1, source_target_pairs={{0,128},{128,0},{1,129},{129,1},{2,130},{130,2},{3,131},{131,3},{4... | collective-permute-start | bytes 49160 | tf_op jit(solution)/shard_map/ppermute | solution.py:39
  76.9 2.2 collective-permute-done.3
  79.1 1.2 collective-permute-start.4
  80.3 2.7 %collective-permute-done.4 = f32[32,128]{1,0:T(8,128)S(1)} collective-permute-done((f32[32,128]{1,0:T(8,128)S(1)}, f32[32,128]{1,0:T(8,128)S(1)}, u32[]{:S(2)}, u32[]{:S(2)}) %collective-permute-start.4) | collective-permute-done | bytes 16416 | tf_op jit(solution)/shard_map/ppermute | solution.py:39
  83.0 0.4 collective-permute-start.5
  83.4 4.8 %collective-permute-done.5 = f32[32,128]{1,0:T(8,128)S(1)} collective-permute-done((f32[32,128]{1,0:T(8,128)S(1)}, f32[32,128]{1,0:T(8,128)S(1)}, u32[]{:S(2)}, u32[]{:S(2)}) %collective-permute-start.5) | collective-permute-done | bytes 16416 | tf_op jit(solution)/shard_map/ppermute | solution.py:39
  88.2 1.2 collective-permute-start.6
  89.4 2.6 collective-permute-done.6
  92.0 1.2 collective-permute-start.7
  93.2 3.4 %collective-permute-done.7 = f32[32,128]{1,0:T(8,128)S(1)} collective-permute-done((f32[32,128]{1,0:T(8,128)S(1)}, f32[32,128]{1,0:T(8,128)S(1)}, u32[]{:S(2)}, u32[]{:S(2)}) %collective-permute-start.7) | collective-permute-done | bytes 16416 | tf_op jit(solution)/shard_map/ppermute | solution.py:39
  96.6 3.0 %collective-permute-start.8 = (f32[32,128]{1,0:T(8,128)S(1)}, f32[32,128]{1,0:T(8,128)S(1)}, u32[]{:S(2)}, u32[]{:S(2)}) collective-permute-start(f32[32,128]{1,0:T(8,128)S(1)} %add.103), channel_id=1, source_target_pairs={{0,8},{2,10},{4,12},{6,14},{8,0},{10,2},{12,4},{14,6},{1,9},{3,11}... | collective-permute-start | bytes 49160 | tf_op jit(solution)/shard_map/ppermute | solution.py:39
  99.6 4.7 %collective-permute-done.8 = f32[32,128]{1,0:T(8,128)S(1)} collective-permute-done((f32[32,128]{1,0:T(8,128)S(1)}, f32[32,128]{1,0:T(8,128)S(1)}, u32[]{:S(2)}, u32[]{:S(2)}) %collective-permute-start.8) | collective-permute-done | bytes 16416 | tf_op jit(solution)/shard_map/ppermute | solution.py:39
  104.3 6.7 %shard_map.77 = (f32[1536,1]{1,0:T(8,128)}, f32[32,128]{1,0:T(8,128)S(1)}) custom-call(s32[12,16]{1,0:T(8,128)S(1)} %copy-done.2, bf16[1536,256]{1,0:T(8,128)(2,1)S(1)} %fusion.1.xn_ref, bf16[32,128,256]{2,1,0:T(8,128)(2,1)S(1)} %bitcast.7, f32[32,128]{1,0:T(8,128)S(1)} %bitcast_divide_fusion.1.scale_ref, f32[1536,1]{1,0:T(8,128)S(1)} %reshape.43.mass_ref), custom_call_target="tpu_custom_call" | custom-call | flops 1610612736 | bytes 2883584 | tf_op jit(solution)/shard_map/pallas_call | solution.py:126
  111.0 1.2 collective-permute-done.9
  112.2 1.5 collective-permute-start.10
  113.6 2.3 collective-permute-done.10
  115.9 3.1 %collective-permute-start.11 = (f32[32,128]{1,0:T(8,128)S(1)}, f32[32,128]{1,0:T(8,128)S(1)}, u32[]{:S(2)}, u32[]{:S(2)}) collective-permute-start(f32[32,128]{1,0:T(8,128)S(1)} %add.106), channel_id=1, source_target_pairs={{0,128},{128,0},{1,129},{129,1},{2,130},{130,2},{3,131},{131,3},{4... | collective-permute-start | bytes 49160 | tf_op jit(solution)/shard_map/ppermute | solution.py:39
  119.0 2.2 collective-permute-done.11
  121.2 1.1 collective-permute-start.12
  122.2 2.8 %collective-permute-done.12 = f32[32,128]{1,0:T(8,128)S(1)} collective-permute-done((f32[32,128]{1,0:T(8,128)S(1)}, f32[32,128]{1,0:T(8,128)S(1)}, u32[]{:S(2)}, u32[]{:S(2)}) %collective-permute-start.12) | collective-permute-done | bytes 16416 | tf_op jit(solution)/shard_map/ppermute | solution.py:39
  125.0 0.3 collective-permute-start.13
  125.3 4.9 %collective-permute-done.13 = f32[32,128]{1,0:T(8,128)S(1)} collective-permute-done((f32[32,128]{1,0:T(8,128)S(1)}, f32[32,128]{1,0:T(8,128)S(1)}, u32[]{:S(2)}, u32[]{:S(2)}) %collective-permute-start.13) | collective-permute-done | bytes 16416 | tf_op jit(solution)/shard_map/ppermute | solution.py:39
  130.3 1.1 collective-permute-start.14
  131.4 2.6 %collective-permute-done.14 = f32[32,128]{1,0:T(8,128)S(1)} collective-permute-done((f32[32,128]{1,0:T(8,128)S(1)}, f32[32,128]{1,0:T(8,128)S(1)}, u32[]{:S(2)}, u32[]{:S(2)}) %collective-permute-start.14) | collective-permute-done | bytes 16416 | tf_op jit(solution)/shard_map/ppermute | solution.py:39
  134.0 1.3 collective-permute-start.15
  135.3 3.4 %collective-permute-done.15 = f32[32,128]{1,0:T(8,128)S(1)} collective-permute-done((f32[32,128]{1,0:T(8,128)S(1)}, f32[32,128]{1,0:T(8,128)S(1)}, u32[]{:S(2)}, u32[]{:S(2)}) %collective-permute-start.15) | collective-permute-done | bytes 16416 | tf_op jit(solution)/shard_map/ppermute | solution.py:39
  138.7 3.0 %collective-permute-start.16 = (f32[32,128]{1,0:T(8,128)S(1)}, f32[32,128]{1,0:T(8,128)S(1)}, u32[]{:S(2)}, u32[]{:S(2)}) collective-permute-start(f32[32,128]{1,0:T(8,128)S(1)} %add.111), channel_id=1, source_target_pairs={{0,8},{2,10},{4,12},{6,14},{8,0},{10,2},{12,4},{14,6},{1,9},{3,11}... | collective-permute-start | bytes 49160 | tf_op jit(solution)/shard_map/ppermute | solution.py:39
  141.7 4.7 %collective-permute-done.16 = f32[32,128]{1,0:T(8,128)S(1)} collective-permute-done((f32[32,128]{1,0:T(8,128)S(1)}, f32[32,128]{1,0:T(8,128)S(1)}, u32[]{:S(2)}, u32[]{:S(2)}) %collective-permute-start.16) | collective-permute-done | bytes 16416 | tf_op jit(solution)/shard_map/ppermute | solution.py:39
  146.3 15.2 %shard_map.78 = (f32[1536,1]{1,0:T(8,128)S(1)}, f32[16,264,256]{2,1,0:T(8,128)}) custom-call(s32[12,16]{1,0:T(8,128)S(1)} %copy-done.2, bf16[1536,256]{1,0:T(8,128)(2,1)S(1)} %fusion.1.xn_ref, bf16[32,128,256]{2,1,0:T(8,128)(2,1)S(1)} %bitcast.8, f32[32,128]{1,0:T(8,128)S(1)} %bitcast_divide_fusion.scale_ref, f32[1536,1]{1,0:T(8,128)S(1)} %reshape.43.mass_ref, ...), custom_call_target="tpu_custom_call" | custom-call | flops 3221225472 | bytes 7864320 | tf_op jit(solution)/shard_map/pallas_call | solution.py:126
  161.5 55.2 %reduce-scatter.2.cloned.1.call-done = f32[528,256]{1,0:T(8,128)} async-done(((f32[4224,256]{1,0:T(8,128)}), f32[528,256]{1,0:T(8,128)}) %reduce-scatter.2.cloned.1.call-update) | async-done | bytes 540688 | tf_op jit(solution)/shard_map/reduce_scatter | solution.py:175
  216.7 1.1 slice_select_fusion
  217.8 1.6 collective-permute-start.17
  219.4 6.8 %collective-permute-done.17 = f32[264,256]{1,0:T(8,128)S(1)} collective-permute-done((f32[264,256]{1,0:T(8,128)S(1)}, f32[264,256]{1,0:T(8,128)S(1)}, u32[]{:S(2)}, u32[]{:S(2)}) %collective-permute-start.17) | collective-permute-done | bytes 270368 | tf_op jit(solution)/shard_map/ppermute | solution.py:180
  226.2 1.1 select_add_fusion
  227.4 0.1 collective-permute-start.18
  227.5 1.3 collective-permute-done.18
  228.8 1.2 collective-permute-start.19
  230.1 4.6 %collective-permute-done.19 = f32[136,256]{1,0:T(8,128)S(1)} collective-permute-done((f32[136,256]{1,0:T(8,128)S(1)}, f32[136,256]{1,0:T(8,128)S(1)}, u32[]{:S(2)}, u32[]{:S(2)}) %collective-permute-start.19) | collective-permute-done | bytes 139296 | tf_op jit(solution)/shard_map/ppermute | solution.py:39
  234.7 0.6 collective-permute-start.20
  235.3 6.0 %collective-permute-done.20 = f32[136,256]{1,0:T(8,128)S(1)} collective-permute-done((f32[136,256]{1,0:T(8,128)S(1)}, f32[136,256]{1,0:T(8,128)S(1)}, u32[]{:S(2)}, u32[]{:S(2)}) %collective-permute-start.20) | collective-permute-done | bytes 139296 | tf_op jit(solution)/shard_map/ppermute | solution.py:39
  241.3 3.1 %collective-permute-start.21 = (f32[136,256]{1,0:T(8,128)S(1)}, f32[136,256]{1,0:T(8,128)S(1)}, u32[]{:S(2)}, u32[]{:S(2)}) collective-permute-start(f32[136,256]{1,0:T(8,128)S(1)} %add.118), channel_id=1, source_target_pairs={{0,128},{128,0},{1,129},{129,1},{2,130},{130,2},{3,131},{131,3},{4... | collective-permute-start | bytes 417800 | tf_op jit(solution)/shard_map/ppermute | solution.py:39
  244.4 3.6 %collective-permute-done.21 = f32[136,256]{1,0:T(8,128)S(1)} collective-permute-done((f32[136,256]{1,0:T(8,128)S(1)}, f32[136,256]{1,0:T(8,128)S(1)}, u32[]{:S(2)}, u32[]{:S(2)}) %collective-permute-start.21) | collective-permute-done | bytes 139296 | tf_op jit(solution)/shard_map/ppermute | solution.py:39
  248.0 0.1 collective-permute-start.22
  248.1 0.9 reduce
  249.0 0.5 collective-permute-done.22
  249.5 0.6 multiply_divide_fusion
  250.2 0.8 maximum_divide_fusion
  (43 shorter events, 0.3 us)
Async XLA Ops:
  7.2 9.3 %copy-start.4 = (f32[1536]{0:T(1024)S(1)}, f32[1536]{0:T(1024)}, u32[]{:S(2)}) copy-start(f32[1536]{0:T(1024)} %param.6) | copy-start | bytes 18436
  7.2 9.6 %copy-start = (bf16[1536,256]{1,0:T(8,128)(2,1)S(1)}, bf16[1536,256]{1,0:T(8,128)(2,1)}, u32[]{:S(2)}) copy-start(bf16[1536,256]{1,0:T(8,128)(2,1)} %rest_0_.1) | copy-start | bytes 2359300
  7.2 53.5 %all-gather.2.cloned.1.call-start = ((), (), s32[]{:S(2)}) async-start(), calls=%async_computation.1 | async-start | bytes 2359296 | tf_op jit(solution)/shard_map/all_gather | solution.py:164
  9.3 5.3 %collective-permute-start = (bf16[256,256]{1,0:T(8,128)(2,1)S(1)}, bf16[256,256]{1,0:T(8,128)(2,1)S(1)}, u32[]{:S(2)}, u32[]{:S(2)}) collective-permute-start(bf16[256,256]{1,0:T(8,128)(2,1)S(1)} %fusion.3), channel_id=1, source_target_pairs={{0,1},{1,0},{2,3},{3,2},{4,5},{5,4},{6,7},{7,6},{8,9},{9,8},{10,11... | collective-permute-start | bytes 393224 | tf_op jit(solution)/shard_map/ppermute | solution.py:159
  16.4 44.2 %copy-start.2 = (s32[12,16]{1,0:T(8,128)S(1)}, s32[12,16]{1,0:T(8,128)}, u32[]{:S(2)}) copy-start(s32[12,16]{1,0:T(8,128)} %links_ref.5) | copy-start | bytes 2308
  16.5 200.3 %reduce-scatter.2.cloned.1.call-start = ((), (), s32[]{:S(2)}) async-start(), calls=%async_computation.2 | async-start | bytes 4866048 | tf_op jit(solution)/shard_map/reduce_scatter | solution.py:175
  60.7 1.6 copy-start.1
  62.2 42.0 %copy-start.3 = (f32[4096]{0:T(1024)S(1)}, f32[4096]{0:T(1024)}, u32[]{:S(2)}) copy-start(f32[4096]{0:T(1024)} %param.9) | copy-start | bytes 49156
  68.9 1.2 collective-permute-start.1
  70.1 3.7 %collective-permute-start.2 = (f32[32,128]{1,0:T(8,128)S(1)}, f32[32,128]{1,0:T(8,128)S(1)}, u32[]{:S(2)}, u32[]{:S(2)}) collective-permute-start(f32[32,128]{1,0:T(8,128)S(1)} %add.97), channel_id=1, source_target_pairs={{0,1},{1,0},{2,3},{3,2},{4,5},{5,4},{6,7},{7,6},{8,9},{9,8},{10,11... | collective-permute-start | bytes 49160 | tf_op jit(solution)/shard_map/ppermute | solution.py:39
  73.9 5.2 %collective-permute-start.3 = (f32[32,128]{1,0:T(8,128)S(1)}, f32[32,128]{1,0:T(8,128)S(1)}, u32[]{:S(2)}, u32[]{:S(2)}) collective-permute-start(f32[32,128]{1,0:T(8,128)S(1)} %add.98), channel_id=1, source_target_pairs={{0,128},{128,0},{1,129},{129,1},{2,130},{130,2},{3,131},{131,3},{4... | collective-permute-start | bytes 49160 | tf_op jit(solution)/shard_map/ppermute | solution.py:39
  79.1 3.8 %collective-permute-start.4 = (f32[32,128]{1,0:T(8,128)S(1)}, f32[32,128]{1,0:T(8,128)S(1)}, u32[]{:S(2)}, u32[]{:S(2)}) collective-permute-start(f32[32,128]{1,0:T(8,128)S(1)} %add.99), channel_id=1, source_target_pairs={{0,32},{32,0},{64,96},{96,64},{1,33},{33,1},{65,97},{97,65},{2,34}... | collective-permute-start | bytes 49160 | tf_op jit(solution)/shard_map/ppermute | solution.py:39
  83.0 5.2 %collective-permute-start.5 = (f32[32,128]{1,0:T(8,128)S(1)}, f32[32,128]{1,0:T(8,128)S(1)}, u32[]{:S(2)}, u32[]{:S(2)}) collective-permute-start(f32[32,128]{1,0:T(8,128)S(1)} %add.100), channel_id=1, source_target_pairs={{0,64},{32,96},{64,0},{96,32},{1,65},{33,97},{65,1},{97,33},{2,66}... | collective-permute-start | bytes 49160 | tf_op jit(solution)/shard_map/ppermute | solution.py:39
  88.2 3.7 %collective-permute-start.6 = (f32[32,128]{1,0:T(8,128)S(1)}, f32[32,128]{1,0:T(8,128)S(1)}, u32[]{:S(2)}, u32[]{:S(2)}) collective-permute-start(f32[32,128]{1,0:T(8,128)S(1)} %add.101), channel_id=1, source_target_pairs={{0,2},{2,0},{4,6},{6,4},{8,10},{10,8},{12,14},{14,12},{1,3},{3,1},... | collective-permute-start | bytes 49160 | tf_op jit(solution)/shard_map/ppermute | solution.py:39
  92.0 4.6 %collective-permute-start.7 = (f32[32,128]{1,0:T(8,128)S(1)}, f32[32,128]{1,0:T(8,128)S(1)}, u32[]{:S(2)}, u32[]{:S(2)}) collective-permute-start(f32[32,128]{1,0:T(8,128)S(1)} %add.102), channel_id=1, source_target_pairs={{0,4},{2,6},{4,0},{6,2},{8,12},{10,14},{12,8},{14,10},{1,5},{3,7},... | collective-permute-start | bytes 49160 | tf_op jit(solution)/shard_map/ppermute | solution.py:39
  96.6 7.6 %collective-permute-start.8 = (f32[32,128]{1,0:T(8,128)S(1)}, f32[32,128]{1,0:T(8,128)S(1)}, u32[]{:S(2)}, u32[]{:S(2)}) collective-permute-start(f32[32,128]{1,0:T(8,128)S(1)} %add.103), channel_id=1, source_target_pairs={{0,8},{2,10},{4,12},{6,14},{8,0},{10,2},{12,4},{14,6},{1,9},{3,11}... | collective-permute-start | bytes 49160 | tf_op jit(solution)/shard_map/ppermute | solution.py:39
  111.0 1.2 collective-permute-start.9
  112.2 3.7 %collective-permute-start.10 = (f32[32,128]{1,0:T(8,128)S(1)}, f32[32,128]{1,0:T(8,128)S(1)}, u32[]{:S(2)}, u32[]{:S(2)}) collective-permute-start(f32[32,128]{1,0:T(8,128)S(1)} %add.105), channel_id=1, source_target_pairs={{0,1},{1,0},{2,3},{3,2},{4,5},{5,4},{6,7},{7,6},{8,9},{9,8},{10,11... | collective-permute-start | bytes 49160 | tf_op jit(solution)/shard_map/ppermute | solution.py:39
  115.9 5.2 %collective-permute-start.11 = (f32[32,128]{1,0:T(8,128)S(1)}, f32[32,128]{1,0:T(8,128)S(1)}, u32[]{:S(2)}, u32[]{:S(2)}) collective-permute-start(f32[32,128]{1,0:T(8,128)S(1)} %add.106), channel_id=1, source_target_pairs={{0,128},{128,0},{1,129},{129,1},{2,130},{130,2},{3,131},{131,3},{4... | collective-permute-start | bytes 49160 | tf_op jit(solution)/shard_map/ppermute | solution.py:39
  121.2 3.9 %collective-permute-start.12 = (f32[32,128]{1,0:T(8,128)S(1)}, f32[32,128]{1,0:T(8,128)S(1)}, u32[]{:S(2)}, u32[]{:S(2)}) collective-permute-start(f32[32,128]{1,0:T(8,128)S(1)} %add.107), channel_id=1, source_target_pairs={{0,32},{32,0},{64,96},{96,64},{1,33},{33,1},{65,97},{97,65},{2,34}... | collective-permute-start | bytes 49160 | tf_op jit(solution)/shard_map/ppermute | solution.py:39
  125.0 5.2 %collective-permute-start.13 = (f32[32,128]{1,0:T(8,128)S(1)}, f32[32,128]{1,0:T(8,128)S(1)}, u32[]{:S(2)}, u32[]{:S(2)}) collective-permute-start(f32[32,128]{1,0:T(8,128)S(1)} %add.108), channel_id=1, source_target_pairs={{0,64},{32,96},{64,0},{96,32},{1,65},{33,97},{65,1},{97,33},{2,66}... | collective-permute-start | bytes 49160 | tf_op jit(solution)/shard_map/ppermute | solution.py:39
  130.3 3.7 %collective-permute-start.14 = (f32[32,128]{1,0:T(8,128)S(1)}, f32[32,128]{1,0:T(8,128)S(1)}, u32[]{:S(2)}, u32[]{:S(2)}) collective-permute-start(f32[32,128]{1,0:T(8,128)S(1)} %add.109), channel_id=1, source_target_pairs={{0,2},{2,0},{4,6},{6,4},{8,10},{10,8},{12,14},{14,12},{1,3},{3,1},... | collective-permute-start | bytes 49160 | tf_op jit(solution)/shard_map/ppermute | solution.py:39
  134.0 4.6 %collective-permute-start.15 = (f32[32,128]{1,0:T(8,128)S(1)}, f32[32,128]{1,0:T(8,128)S(1)}, u32[]{:S(2)}, u32[]{:S(2)}) collective-permute-start(f32[32,128]{1,0:T(8,128)S(1)} %add.110), channel_id=1, source_target_pairs={{0,4},{2,6},{4,0},{6,2},{8,12},{10,14},{12,8},{14,10},{1,5},{3,7},... | collective-permute-start | bytes 49160 | tf_op jit(solution)/shard_map/ppermute | solution.py:39
  138.7 7.6 %collective-permute-start.16 = (f32[32,128]{1,0:T(8,128)S(1)}, f32[32,128]{1,0:T(8,128)S(1)}, u32[]{:S(2)}, u32[]{:S(2)}) collective-permute-start(f32[32,128]{1,0:T(8,128)S(1)} %add.111), channel_id=1, source_target_pairs={{0,8},{2,10},{4,12},{6,14},{8,0},{10,2},{12,4},{14,6},{1,9},{3,11}... | collective-permute-start | bytes 49160 | tf_op jit(solution)/shard_map/ppermute | solution.py:39
  217.8 8.4 %collective-permute-start.17 = (f32[264,256]{1,0:T(8,128)S(1)}, f32[264,256]{1,0:T(8,128)S(1)}, u32[]{:S(2)}, u32[]{:S(2)}) collective-permute-start(f32[264,256]{1,0:T(8,128)S(1)} %slice_select_fusion), channel_id=1, source_target_pairs={{0,1},{1,0},{2,3},{3,2},{4,5},{5,4},{6,7},{7,6},{8,9},{9,8},{10,11... | collective-permute-start | bytes 811016 | tf_op jit(solution)/shard_map/ppermute | solution.py:180
  227.4 1.4 collective-permute-start.18
  228.8 5.8 %collective-permute-start.19 = (f32[136,256]{1,0:T(8,128)S(1)}, f32[136,256]{1,0:T(8,128)S(1)}, u32[]{:S(2)}, u32[]{:S(2)}) collective-permute-start(f32[136,256]{1,0:T(8,128)S(1)} %fusion.4), channel_id=1, source_target_pairs={{0,32},{32,0},{64,96},{96,64},{1,33},{33,1},{65,97},{97,65},{2,34}... | collective-permute-start | bytes 417800 | tf_op jit(solution)/shard_map/ppermute | solution.py:39
  234.7 6.6 %collective-permute-start.20 = (f32[136,256]{1,0:T(8,128)S(1)}, f32[136,256]{1,0:T(8,128)S(1)}, u32[]{:S(2)}, u32[]{:S(2)}) collective-permute-start(f32[136,256]{1,0:T(8,128)S(1)} %add.117), channel_id=1, source_target_pairs={{0,64},{32,96},{64,0},{96,32},{1,65},{33,97},{65,1},{97,33},{2,66}... | collective-permute-start | bytes 417800 | tf_op jit(solution)/shard_map/ppermute | solution.py:39
  241.3 6.6 %collective-permute-start.21 = (f32[136,256]{1,0:T(8,128)S(1)}, f32[136,256]{1,0:T(8,128)S(1)}, u32[]{:S(2)}, u32[]{:S(2)}) collective-permute-start(f32[136,256]{1,0:T(8,128)S(1)} %add.118), channel_id=1, source_target_pairs={{0,128},{128,0},{1,129},{129,1},{2,130},{130,2},{3,131},{131,3},{4... | collective-permute-start | bytes 417800 | tf_op jit(solution)/shard_map/ppermute | solution.py:39
  248.0 1.4 collective-permute-start.22
Sparse Core Ops, SparseCore 0:
  16.6 44.0 all-gather.1
  161.7 55.0 reduce-scatter.1

commit v12 on v11

--- a/solution.py
+++ b/solution.py
@@ -17,11 +17,12 @@
 OFFSET = 1.0
 PAD = 8
 SUB = 4
+Z_LO = 4
 
 ROW_AXES = ("yh", "x", "c")
-COL_AXES = ("z", "yl")
+COL_AXES = ("zh", "zl", "yl")
 ALL_AXES = ROW_AXES + COL_AXES
-TOTAL_ORDER = ("c", "yl", "yh", "x", "z")
+TOTAL_ORDER = ("c", "yl", "yh", "x", "zl", "zh")
 
 
 def normalize(matrix):
@@ -86,6 +87,8 @@
             part = jnp.sum(k * ds, axis=0, keepdims=True)
             if bary:
                 q = blk // 2
+                zq = q // 2
+                q = ((zq % Z_LO) * (ws_ref.shape[0] // (2 * Z_LO)) + zq // Z_LO) * 2 + q % 2
                 half = pl.multiple_of((blk % 2) * BLOCK, BLOCK)
                 ws_ref[q, pl.ds(2 * BLOCK, 1), pl.ds(half, BLOCK)] += part
                 w = (k * ds).astype(jnp.bfloat16)
@@ -149,11 +152,13 @@
     local_rows, feature_count = data_rows.shape
     local_cands = cand_rows.shape[0]
     row_devices = sizes["yh"] * sizes["x"] * sizes["c"]
-    col_devices = sizes["z"] * sizes["yl"]
+    col_devices = sizes["zh"] * sizes["zl"] * sizes["yl"]
     cand_total = local_cands * col_devices
     block_count = cand_total // BLOCK
     mass_ratio = local_rows * row_devices / local_cands
-    col_index = lax.axis_index("z") * sizes["yl"] + lax.axis_index("yl")
+    col_index = (
+        lax.axis_index("zh") * sizes["zl"] + lax.axis_index("zl")
+    ) * sizes["yl"] + lax.axis_index("yl")
     own_start = col_index * local_cands
     own_cn = normalize(cand_rows)
     pair_cn = lax.ppermute(own_cn, "yl", [(0, 1), (1, 0)])
@@ -161,7 +166,7 @@
     slab = jnp.concatenate(
         [jnp.where(first_lo, own_cn, pair_cn), jnp.where(first_lo, pair_cn, own_cn)], axis=0
     )
-    gathered = lax.all_gather(slab, "z", axis=0, tiled=True)
+    gathered = lax.all_gather(slab, ("zh", "zl"), axis=0, tiled=True)
     cn_blocks = gathered.reshape(block_count, BLOCK, feature_count)
     xn = normalize(data_rows)
     mass_col = data_mass.reshape(local_rows, 1)
@@ -172,8 +177,12 @@
         whole_total = butterfly_sum(part_total, TOTAL_ORDER, sizes)
         scale_blocks = mass_ratio * cand_mass.reshape(block_count, BLOCK) / whole_total
     ds_col, packed = sweep(xn, cn_blocks, scale_blocks, mass_col, links, rows=data_rows)
-    pair = lax.psum_scatter(packed.reshape(-1, feature_count), "z", scatter_dimension=0, tiled=True)
-    part_rows = pair.shape[0] // 2
+    quad = lax.psum_scatter(packed.reshape(-1, feature_count), "zl", scatter_dimension=0, tiled=True)
+    part_rows = quad.shape[0] // 4
+    first_hi = lax.axis_index("zh") == 0
+    keep = jnp.where(first_hi, quad[: 2 * part_rows], quad[2 * part_rows :])
+    give = jnp.where(first_hi, quad[2 * part_rows :], quad[: 2 * part_rows])
+    pair = keep + lax.ppermute(give, "zh", [(0, 1), (1, 0)])
     first_lo = lax.axis_index("yl") == 0
     keep = jnp.where(first_lo, pair[:part_rows], pair[part_rows:])
     give = jnp.where(first_lo, pair[part_rows:], pair[:part_rows])
@@ -196,7 +205,9 @@
 
 def solution(mesh):
     row_size, col_size = mesh.devices.shape
-    fine = Mesh(mesh.devices.reshape(2, row_size // 4, 2, col_size // 2, 2), ALL_AXES)
+    fine = Mesh(
+        mesh.devices.reshape(2, row_size // 4, 2, col_size // (2 * Z_LO), Z_LO, 2), ALL_AXES
+    )
     sizes = dict(fine.shape)
     placed = (
         P(ALL_AXES, None),

time: 259 us -> 315 us (1.22)
  the two profiles are of different devices: /device:TPU:4 before, /device:TPU:65 now
where the time goes in v12:
time: 315 us
  waiting for transfers between devices  205 us (65%)
  starting transfers between devices  56.1 us (18%)
  Pallas kernels  29.2 us (9%)
  between operations  14.3 us (5%)
  other arithmetic  8.51 us (3%)
    reduce_scatter x1, waiting for transfers between devices, on_device(): lax.psum_scatter(packed.reshape(-1, feature_count), 'zl', scatter_dimensi...  92.3 us
    ppermute x19, starting transfers between devices, butterfly_sum(): x = x + lax.ppermute(x, axis, [(j, j ^ k) for j in range(n)])  45.5 us
    all_gather x1, waiting for transfers between devices, on_device(): gathered = lax.all_gather(slab, ('zh', 'zl'), axis=0, tiled=True)  39.2 us
    ppermute x19, waiting for transfers between devices, butterfly_sum(): x = x + lax.ppermute(x, axis, [(j, j ^ k) for j in range(n)])  36.4 us
    pallas_call x3, Pallas kernels, sweep(): pl.pallas_call(functools.partial(sweep_body, nbr, inv_width, inv_count, b...  29.2 us
    ppermute x1, waiting for transfers between devices, on_device(): pair = keep + lax.ppermute(give, 'zh', [(0, 1), (1, 0)])  26.2 us
    ppermute x1, waiting for transfers between devices, on_device(): joined = keep + lax.ppermute(give, 'yl', [(0, 1), (1, 0)])  6.36 us
  transfers between devices with their start and end apart: 26, of which 26 were waited for; matrix products, arithmetic and copies ran while one was open for 1% of the time, Pallas kernels for 0%

profile of v12, /device:TPU:65, one launch (start us, length us, event | category | flops | bytes accessed | tf_op | source)
XLA Modules:
  0.0 314.5 jit_solution(962276026644379096)
XLA Ops:
  7.2 1.1 fusion.2
  8.3 1.0 fusion.3
  9.3 1.4 collective-permute-start
  10.7 3.1 collective-permute-done
  13.8 1.0 broadcast_select_fusion.1
  14.8 0.7 pad_maximum_fusion
  15.7 0.3 reshape.43.mass_ref
  15.9 0.3 fusion
  16.2 0.3 fusion.1.xn_ref
  16.5 39.2 %all-gather.2.cloned.1.call-done = bf16[4096,256]{1,0:T(8,128)(2,1)} async-done(((bf16[512,256]{1,0:T(8,128)(2,1)}), bf16[4096,256]{1,0:T(8,128)(2,1)}) %all-gather.2.cloned.1.call-update) | async-done | bytes 2097168 | tf_op jit(solution)/shard_map/all_gather | solution.py:169
  55.7 1.6 copy-done.1
  57.3 6.7 %shard_map.76 = (f32[1536,1]{1,0:T(8,128)}, f32[32,128]{1,0:T(8,128)S(1)}) custom-call(s32[12,16]{1,0:T(8,128)S(1)} %copy-done.2, bf16[1536,256]{1,0:T(8,128)(2,1)S(1)} %fusion.1.xn_ref, bf16[32,128,256]{2,1,0:T(8,128)(2,1)S(1)} %bitcast.6, f32[32,128]{1,0:T(8,128)S(1)} %broadcast_in_dim.2.scale_ref, f32[1536,1]{1,0:T(8,128)S(1)} %reshape.43.mass_ref), custom_call_target="tpu_custom_call" | custom-call | flops 1610612736 | bytes 2883584 | tf_op jit(solution)/shard_map/pallas_call | solution.py:129
  64.0 3.6 %collective-permute-start.1 = (f32[32,128]{1,0:T(8,128)S(1)}, f32[32,128]{1,0:T(8,128)S(1)}, u32[]{:S(2)}, u32[]{:S(2)}) collective-permute-start(f32[32,128]{1,0:T(8,128)S(1)} %get-tuple-element.7), channel_id=1, source_target_pairs={{0,16},{16,0},{1,17},{17,1},{2,18},{18,2},{3,19},{19,3},{4,20},{20... | collective-permute-start | bytes 49160 | tf_op jit(solution)/shard_map/ppermute | solution.py:40
  67.6 0.8 collective-permute-done.1
  68.5 1.2 collective-permute-start.2
  69.7 1.4 collective-permute-done.2
  71.1 2.7 collective-permute-start.3
  73.8 1.4 collective-permute-done.3
  75.2 1.2 collective-permute-start.4
  76.4 1.4 collective-permute-done.4
  77.8 2.7 collective-permute-start.5
  80.5 1.4 collective-permute-done.5
  81.9 1.8 collective-permute-start.6
  83.6 1.1 collective-permute-done.6
  84.8 1.1 collective-permute-start.7
  85.9 2.4 collective-permute-done.7
  88.3 2.7 collective-permute-start.8
  90.9 3.8 %collective-permute-done.8 = f32[32,128]{1,0:T(8,128)S(1)} collective-permute-done((f32[32,128]{1,0:T(8,128)S(1)}, f32[32,128]{1,0:T(8,128)S(1)}, u32[]{:S(2)}, u32[]{:S(2)}) %collective-permute-start.8) | collective-permute-done | bytes 16416 | tf_op jit(solution)/shard_map/ppermute | solution.py:40
  94.8 6.7 %shard_map.77 = (f32[1536,1]{1,0:T(8,128)}, f32[32,128]{1,0:T(8,128)S(1)}) custom-call(s32[12,16]{1,0:T(8,128)S(1)} %copy-done.2, bf16[1536,256]{1,0:T(8,128)(2,1)S(1)} %fusion.1.xn_ref, bf16[32,128,256]{2,1,0:T(8,128)(2,1)S(1)} %bitcast.7, f32[32,128]{1,0:T(8,128)S(1)} %bitcast_divide_fusion.1.scale_ref, f32[1536,1]{1,0:T(8,128)S(1)} %reshape.43.mass_ref), custom_call_target="tpu_custom_call" | custom-call | flops 1610612736 | bytes 2883584 | tf_op jit(solution)/shard_map/pallas_call | solution.py:129
  101.5 8.1 %collective-permute-start.9 = (f32[32,128]{1,0:T(8,128)S(1)}, f32[32,128]{1,0:T(8,128)S(1)}, u32[]{:S(2)}, u32[]{:S(2)}) collective-permute-start(f32[32,128]{1,0:T(8,128)S(1)} %get-tuple-element.8), channel_id=1, source_target_pairs={{0,16},{16,0},{1,17},{17,1},{2,18},{18,2},{3,19},{19,3},{4,20},{20... | collective-permute-start | bytes 49160 | tf_op jit(solution)/shard_map/ppermute | solution.py:40
  109.6 0.8 collective-permute-done.9
  110.4 1.2 collective-permute-start.10
  111.6 1.4 collective-permute-done.10
  113.0 2.7 collective-permute-start.11
  115.8 1.4 collective-permute-done.11
  117.1 1.2 collective-permute-start.12
  118.3 1.4 collective-permute-done.12
  119.7 2.8 collective-permute-start.13
  122.5 1.3 collective-permute-done.13
  123.8 1.7 collective-permute-start.14
  125.6 1.1 collective-permute-done.14
  126.7 1.1 collective-permute-start.15
  127.8 2.4 collective-permute-done.15
  130.2 2.8 collective-permute-start.16
  133.0 3.7 %collective-permute-done.16 = f32[32,128]{1,0:T(8,128)S(1)} collective-permute-done((f32[32,128]{1,0:T(8,128)S(1)}, f32[32,128]{1,0:T(8,128)S(1)}, u32[]{:S(2)}, u32[]{:S(2)}) %collective-permute-start.16) | collective-permute-done | bytes 16416 | tf_op jit(solution)/shard_map/ppermute | solution.py:40
  136.7 15.8 %shard_map.78 = (f32[1536,1]{1,0:T(8,128)S(1)}, f32[16,264,256]{2,1,0:T(8,128)}) custom-call(s32[12,16]{1,0:T(8,128)S(1)} %copy-done.2, bf16[1536,256]{1,0:T(8,128)(2,1)S(1)} %fusion.1.xn_ref, bf16[32,128,256]{2,1,0:T(8,128)(2,1)S(1)} %bitcast.8, f32[32,128]{1,0:T(8,128)S(1)} %bitcast_divide_fusion.scale_ref, f32[1536,1]{1,0:T(8,128)S(1)} %reshape.43.mass_ref, ...), custom_call_target="tpu_custom_call" | custom-call | flops 3221225472 | bytes 7864320 | tf_op jit(solution)/shard_map/pallas_call | solution.py:129
  152.5 92.3 %reduce-scatter.2.cloned.1.call-done = f32[1056,256]{1,0:T(8,128)} async-done(((f32[4224,256]{1,0:T(8,128)}), f32[1056,256]{1,0:T(8,128)}) %reduce-scatter.2.cloned.1.call-update) | async-done | bytes 1081360 | tf_op jit(solution)/shard_map/reduce_scatter | solution.py:180
  244.8 1.4 slice_select_fusion
  246.2 2.8 collective-permute-start.17
  249.0 26.2 %collective-permute-done.17 = f32[528,256]{1,0:T(8,128)S(1)} collective-permute-done((f32[528,256]{1,0:T(8,128)S(1)}, f32[528,256]{1,0:T(8,128)S(1)}, u32[]{:S(2)}, u32[]{:S(2)}) %collective-permute-start.17) | collective-permute-done | bytes 540704 | tf_op jit(solution)/shard_map/ppermute | solution.py:185
  275.3 1.3 collective-permute-start.18
  276.6 6.4 %collective-permute-done.18 = f32[264,256]{1,0:T(8,128)S(1)} collective-permute-done((f32[264,256]{1,0:T(8,128)S(1)}, f32[264,256]{1,0:T(8,128)S(1)}, u32[]{:S(2)}, u32[]{:S(2)}) %collective-permute-start.18) | collective-permute-done | bytes 270368 | tf_op jit(solution)/shard_map/ppermute | solution.py:189
  283.1 1.4 collective-permute-start.19
  284.5 1.0 collective-permute-done.19
  285.5 1.3 collective-permute-start.20
  286.8 3.7 %collective-permute-done.20 = f32[136,256]{1,0:T(8,128)S(1)} collective-permute-done((f32[136,256]{1,0:T(8,128)S(1)}, f32[136,256]{1,0:T(8,128)S(1)}, u32[]{:S(2)}, u32[]{:S(2)}) %collective-permute-start.20) | collective-permute-done | bytes 139296 | tf_op jit(solution)/shard_map/ppermute | solution.py:40
  290.5 2.8 collective-permute-start.21
  293.3 2.7 collective-permute-done.21
  296.1 2.8 collective-permute-start.22
  298.9 2.7 collective-permute-done.22
  301.6 3.6 %collective-permute-start.23 = (f32[136,256]{1,0:T(8,128)S(1)}, f32[136,256]{1,0:T(8,128)S(1)}, u32[]{:S(2)}, u32[]{:S(2)}) collective-permute-start(f32[136,256]{1,0:T(8,128)S(1)} %add.127), channel_id=1, source_target_pairs={{0,16},{16,0},{1,17},{17,1},{2,18},{18,2},{3,19},{19,3},{4,20},{20... | collective-permute-start | bytes 417800 | tf_op jit(solution)/shard_map/ppermute | solution.py:196
  305.2 0.9 reduce
  306.2 0.6 multiply_divide_fusion
  306.9 0.8 maximum_divide_fusion
  (49 shorter events, 0.7 us)
Async XLA Ops:
  7.2 8.5 %copy-start.5 = (f32[1536]{0:T(1024)S(1)}, f32[1536]{0:T(1024)}, u32[]{:S(2)}) copy-start(f32[1536]{0:T(1024)} %param.6) | copy-start | bytes 18436
  7.2 8.7 %copy-start = (bf16[1536,256]{1,0:T(8,128)(2,1)S(1)}, bf16[1536,256]{1,0:T(8,128)(2,1)}, u32[]{:S(2)}) copy-start(bf16[1536,256]{1,0:T(8,128)(2,1)} %rest_0_.1) | copy-start | bytes 2359300
  7.2 48.5 %all-gather.2.cloned.1.call-start = ((), (), s32[]{:S(2)}) async-start(), calls=%async_computation.1 | async-start | bytes 2359296 | tf_op jit(solution)/shard_map/all_gather | solution.py:169
  9.3 4.5 %collective-permute-start = (bf16[256,256]{1,0:T(8,128)(2,1)S(1)}, bf16[256,256]{1,0:T(8,128)(2,1)S(1)}, u32[]{:S(2)}, u32[]{:S(2)}) collective-permute-start(bf16[256,256]{1,0:T(8,128)(2,1)S(1)} %fusion.3), channel_id=1, source_target_pairs={{0,1},{1,0},{2,3},{3,2},{4,5},{5,4},{6,7},{7,6},{8,9},{9,8},{10,11... | collective-permute-start | bytes 393224 | tf_op jit(solution)/shard_map/ppermute | solution.py:164
  15.6 40.1 %copy-start.2 = (s32[12,16]{1,0:T(8,128)S(1)}, s32[12,16]{1,0:T(8,128)}, u32[]{:S(2)}) copy-start(s32[12,16]{1,0:T(8,128)} %links_ref.5) | copy-start | bytes 2308
  15.6 229.2 %reduce-scatter.2.cloned.1.call-start = ((), (), s32[]{:S(2)}) async-start(), calls=%async_computation.2 | async-start | bytes 5406720 | tf_op jit(solution)/shard_map/reduce_scatter | solution.py:180
  55.7 1.6 copy-start.1
  57.3 37.4 %copy-start.4 = (f32[4096]{0:T(1024)S(1)}, f32[4096]{0:T(1024)}, u32[]{:S(2)}) copy-start(f32[4096]{0:T(1024)} %param.9) | copy-start | bytes 49156
  64.0 4.5 %collective-permute-start.1 = (f32[32,128]{1,0:T(8,128)S(1)}, f32[32,128]{1,0:T(8,128)S(1)}, u32[]{:S(2)}, u32[]{:S(2)}) collective-permute-start(f32[32,128]{1,0:T(8,128)S(1)} %get-tuple-element.7), channel_id=1, source_target_pairs={{0,16},{16,0},{1,17},{17,1},{2,18},{18,2},{3,19},{19,3},{4,20},{20... | collective-permute-start | bytes 49160 | tf_op jit(solution)/shard_map/ppermute | solution.py:40
  68.5 2.6 collective-permute-start.2
  71.1 4.1 %collective-permute-start.3 = (f32[32,128]{1,0:T(8,128)S(1)}, f32[32,128]{1,0:T(8,128)S(1)}, u32[]{:S(2)}, u32[]{:S(2)}) collective-permute-start(f32[32,128]{1,0:T(8,128)S(1)} %add.104), channel_id=1, source_target_pairs={{0,128},{128,0},{1,129},{129,1},{2,130},{130,2},{3,131},{131,3},{4... | collective-permute-start | bytes 49160 | tf_op jit(solution)/shard_map/ppermute | solution.py:40
  75.2 2.6 collective-permute-start.4
  77.8 4.1 %collective-permute-start.5 = (f32[32,128]{1,0:T(8,128)S(1)}, f32[32,128]{1,0:T(8,128)S(1)}, u32[]{:S(2)}, u32[]{:S(2)}) collective-permute-start(f32[32,128]{1,0:T(8,128)S(1)} %add.106), channel_id=1, source_target_pairs={{0,64},{32,96},{64,0},{96,32},{1,65},{33,97},{65,1},{97,33},{2,66}... | collective-permute-start | bytes 49160 | tf_op jit(solution)/shard_map/ppermute | solution.py:40
  81.9 2.9 collective-permute-start.6
  84.8 3.5 %collective-permute-start.7 = (f32[32,128]{1,0:T(8,128)S(1)}, f32[32,128]{1,0:T(8,128)S(1)}, u32[]{:S(2)}, u32[]{:S(2)}) collective-permute-start(f32[32,128]{1,0:T(8,128)S(1)} %add.108), channel_id=1, source_target_pairs={{0,4},{2,6},{4,0},{6,2},{1,5},{3,7},{5,1},{7,3},{8,12},{10,14},{12... | collective-permute-start | bytes 49160 | tf_op jit(solution)/shard_map/ppermute | solution.py:40
  88.3 6.5 %collective-permute-start.8 = (f32[32,128]{1,0:T(8,128)S(1)}, f32[32,128]{1,0:T(8,128)S(1)}, u32[]{:S(2)}, u32[]{:S(2)}) collective-permute-start(f32[32,128]{1,0:T(8,128)S(1)} %add.109), channel_id=1, source_target_pairs={{0,8},{8,0},{1,9},{9,1},{2,10},{10,2},{3,11},{11,3},{4,12},{12,4},... | collective-permute-start | bytes 49160 | tf_op jit(solution)/shard_map/ppermute | solution.py:40
  101.5 9.0 %collective-permute-start.9 = (f32[32,128]{1,0:T(8,128)S(1)}, f32[32,128]{1,0:T(8,128)S(1)}, u32[]{:S(2)}, u32[]{:S(2)}) collective-permute-start(f32[32,128]{1,0:T(8,128)S(1)} %get-tuple-element.8), channel_id=1, source_target_pairs={{0,16},{16,0},{1,17},{17,1},{2,18},{18,2},{3,19},{19,3},{4,20},{20... | collective-permute-start | bytes 49160 | tf_op jit(solution)/shard_map/ppermute | solution.py:40
  110.4 2.6 collective-permute-start.10
  113.0 4.1 %collective-permute-start.11 = (f32[32,128]{1,0:T(8,128)S(1)}, f32[32,128]{1,0:T(8,128)S(1)}, u32[]{:S(2)}, u32[]{:S(2)}) collective-permute-start(f32[32,128]{1,0:T(8,128)S(1)} %add.112), channel_id=1, source_target_pairs={{0,128},{128,0},{1,129},{129,1},{2,130},{130,2},{3,131},{131,3},{4... | collective-permute-start | bytes 49160 | tf_op jit(solution)/shard_map/ppermute | solution.py:40
  117.1 2.6 collective-permute-start.12
  119.7 4.1 %collective-permute-start.13 = (f32[32,128]{1,0:T(8,128)S(1)}, f32[32,128]{1,0:T(8,128)S(1)}, u32[]{:S(2)}, u32[]{:S(2)}) collective-permute-start(f32[32,128]{1,0:T(8,128)S(1)} %add.114), channel_id=1, source_target_pairs={{0,64},{32,96},{64,0},{96,32},{1,65},{33,97},{65,1},{97,33},{2,66}... | collective-permute-start | bytes 49160 | tf_op jit(solution)/shard_map/ppermute | solution.py:40
  123.8 2.9 collective-permute-start.14
  126.7 3.5 %collective-permute-start.15 = (f32[32,128]{1,0:T(8,128)S(1)}, f32[32,128]{1,0:T(8,128)S(1)}, u32[]{:S(2)}, u32[]{:S(2)}) collective-permute-start(f32[32,128]{1,0:T(8,128)S(1)} %add.116), channel_id=1, source_target_pairs={{0,4},{2,6},{4,0},{6,2},{1,5},{3,7},{5,1},{7,3},{8,12},{10,14},{12... | collective-permute-start | bytes 49160 | tf_op jit(solution)/shard_map/ppermute | solution.py:40
  130.2 6.5 %collective-permute-start.16 = (f32[32,128]{1,0:T(8,128)S(1)}, f32[32,128]{1,0:T(8,128)S(1)}, u32[]{:S(2)}, u32[]{:S(2)}) collective-permute-start(f32[32,128]{1,0:T(8,128)S(1)} %add.117), channel_id=1, source_target_pairs={{0,8},{8,0},{1,9},{9,1},{2,10},{10,2},{3,11},{11,3},{4,12},{12,4},... | collective-permute-start | bytes 49160 | tf_op jit(solution)/shard_map/ppermute | solution.py:40
  244.8 30.4 %copy-start.3 = (f32[1056,256]{1,0:T(8,128)S(1)}, f32[1056,256]{1,0:T(8,128)}, u32[]{:S(2)}) copy-start(f32[1056,256]{1,0:T(8,128)} %reduce-scatter.2.cloned.1.call-done) | copy-start | bytes 3244036
  246.2 29.0 %collective-permute-start.17 = (f32[528,256]{1,0:T(8,128)S(1)}, f32[528,256]{1,0:T(8,128)S(1)}, u32[]{:S(2)}, u32[]{:S(2)}) collective-permute-start(f32[528,256]{1,0:T(8,128)S(1)} %slice_select_fusion), channel_id=1, source_target_pairs={{0,8},{8,0},{1,9},{9,1},{2,10},{10,2},{3,11},{11,3},{4,12},{12,4},... | collective-permute-start | bytes 1622024 | tf_op jit(solution)/shard_map/ppermute | solution.py:185
  275.3 7.6 %collective-permute-start.18 = (f32[264,256]{1,0:T(8,128)S(1)}, f32[264,256]{1,0:T(8,128)S(1)}, u32[]{:S(2)}, u32[]{:S(2)}) collective-permute-start(f32[264,256]{1,0:T(8,128)S(1)} %slice_select_fusion.1), channel_id=1, source_target_pairs={{0,1},{1,0},{2,3},{3,2},{4,5},{5,4},{6,7},{7,6},{8,9},{9,8},{10,11... | collective-permute-start | bytes 811016 | tf_op jit(solution)/shard_map/ppermute | solution.py:189
  283.1 2.4 collective-permute-start.19
  285.5 5.0 %collective-permute-start.20 = (f32[136,256]{1,0:T(8,128)S(1)}, f32[136,256]{1,0:T(8,128)S(1)}, u32[]{:S(2)}, u32[]{:S(2)}) collective-permute-start(f32[136,256]{1,0:T(8,128)S(1)} %fusion.4), channel_id=1, source_target_pairs={{0,32},{32,0},{64,96},{96,64},{1,33},{33,1},{65,97},{97,65},{2,34}... | collective-permute-start | bytes 417800 | tf_op jit(solution)/shard_map/ppermute | solution.py:40
  290.5 5.5 %collective-permute-start.21 = (f32[136,256]{1,0:T(8,128)S(1)}, f32[136,256]{1,0:T(8,128)S(1)}, u32[]{:S(2)}, u32[]{:S(2)}) collective-permute-start(f32[136,256]{1,0:T(8,128)S(1)} %add.125), channel_id=1, source_target_pairs={{0,64},{32,96},{64,0},{96,32},{1,65},{33,97},{65,1},{97,33},{2,66}... | collective-permute-start | bytes 417800 | tf_op jit(solution)/shard_map/ppermute | solution.py:40
  296.1 5.5 %collective-permute-start.22 = (f32[136,256]{1,0:T(8,128)S(1)}, f32[136,256]{1,0:T(8,128)S(1)}, u32[]{:S(2)}, u32[]{:S(2)}) collective-permute-start(f32[136,256]{1,0:T(8,128)S(1)} %add.126), channel_id=1, source_target_pairs={{0,128},{128,0},{1,129},{129,1},{2,130},{130,2},{3,131},{131,3},{4... | collective-permute-start | bytes 417800 | tf_op jit(solution)/shard_map/ppermute | solution.py:40
  301.6 4.6 %collective-permute-start.23 = (f32[136,256]{1,0:T(8,128)S(1)}, f32[136,256]{1,0:T(8,128)S(1)}, u32[]{:S(2)}, u32[]{:S(2)}) collective-permute-start(f32[136,256]{1,0:T(8,128)S(1)} %add.127), channel_id=1, source_target_pairs={{0,16},{16,0},{1,17},{17,1},{2,18},{18,2},{3,19},{19,3},{4,20},{20... | collective-permute-start | bytes 417800 | tf_op jit(solution)/shard_map/ppermute | solution.py:196
Sparse Core Ops, SparseCore 0:
  15.7 39.9 all-gather.1
  152.6 92.1 reduce-scatter.1

commit v13 on v10

--- a/solution.py
+++ b/solution.py
@@ -172,12 +172,23 @@
         whole_total = butterfly_sum(part_total, TOTAL_ORDER, sizes)
         scale_blocks = mass_ratio * cand_mass.reshape(block_count, BLOCK) / whole_total
     ds_col, packed = sweep(xn, cn_blocks, scale_blocks, mass_col, links, rows=data_rows)
-    joined = lax.psum_scatter(packed.reshape(-1, feature_count), COL_AXES, scatter_dimension=0, tiled=True)
+    pair = lax.psum_scatter(packed.reshape(-1, feature_count), "z", scatter_dimension=0, tiled=True)
+    part_rows = pair.shape[0] // 2
     first_core = lax.axis_index("c") == 0
-    sums_a, sums_b, totals = joined[:BLOCK], joined[BLOCK:2 * BLOCK], joined[2 * BLOCK:]
-    keep = jnp.concatenate([jnp.where(first_core, sums_a, sums_b), totals], axis=0)
-    give = jnp.concatenate([jnp.where(first_core, sums_b, sums_a), totals], axis=0)
-    mine = keep + lax.ppermute(give, "c", [(0, 1), (1, 0)])
+    keeps, gives = [], []
+    for p in range(2):
+        part = pair[p * part_rows:(p + 1) * part_rows]
+        sums_a, sums_b, totals = part[:BLOCK], part[BLOCK:2 * BLOCK], part[2 * BLOCK:]
+        keeps += [jnp.where(first_core, sums_a, sums_b), totals]
+        gives += [jnp.where(first_core, sums_b, sums_a), totals]
+    mine = jnp.concatenate(keeps, axis=0) + lax.ppermute(
+        jnp.concatenate(gives, axis=0), "c", [(0, 1), (1, 0)]
+    )
+    quarter = mine.shape[0] // 2
+    first_lo = lax.axis_index("yl") == 0
+    keep = jnp.where(first_lo, mine[:quarter], mine[quarter:])
+    give = jnp.where(first_lo, mine[quarter:], mine[:quarter])
+    mine = keep + lax.ppermute(give, "yl", [(0, 1), (1, 0)])
     mine = butterfly_sum(mine, ("x", "yh"), sizes)
     other = lax.ppermute(mine, "c", [(0, 1), (1, 0)])
     low = jnp.where(first_core, mine, other)

time: 296 us -> 256 us (0.86)
  waiting for transfers between devices: 210 us -> 169 us
    reduce_scatter x1, waiting for transfers between devices: 101 us -> 55.1 us  [on_device(): lax.psum_scatter(packed.reshape(-1, feature_count), 'z', scatter_dimensio...]
    ppermute x1 -> x2, waiting for transfers between devices: 1.35 us -> 5.78 us  [the longest x1 4.23 us: on_device(): mine = keep + lax.ppermute(give, 'yl', [(0, 1), (1, 0)])]
  transfers between devices with their start and end apart: 24 -> 25, of which waited for: 24 -> 25; matrix products, arithmetic and copies ran while one was open for 1% -> 1% of each run, Pallas kernels for 0% -> 0%
where the time goes in v13:
time: 256 us; the launch traced here: 255 us
  waiting for transfers between devices  169 us (66%)
  starting transfers between devices  31.4 us (12%)
  Pallas kernels  28.6 us (11%)
  between operations  14.3 us (6%)
  other arithmetic  8.16 us (3%)
  local copies, waits for them, and re-layouts  2.6 us (1%)
    ppermute x19, waiting for transfers between devices, butterfly_sum(): x = x + lax.ppermute(x, axis, [(j, j ^ k) for j in range(n)])  61.1 us
    reduce_scatter x1, waiting for transfers between devices, on_device(): lax.psum_scatter(packed.reshape(-1, feature_count), 'z', scatter_dimensio...  55.1 us
    all_gather x1, waiting for transfers between devices, on_device(): gathered = lax.all_gather(slab, 'z', axis=0, tiled=True)  43.3 us
    pallas_call x3, Pallas kernels, sweep(): pl.pallas_call(functools.partial(sweep_body, nbr, inv_width, inv_count, b...  28.6 us
    ppermute x19, starting transfers between devices, butterfly_sum(): x = x + lax.ppermute(x, axis, [(j, j ^ k) for j in range(n)])  27.9 us
  transfers between devices with their start and end apart: 25, of which 25 were waited for; matrix products, arithmetic and copies ran while one was open for 1% of the time, Pallas kernels for 0%

profile of v13, /device:TPU:4, one launch (start us, length us, event | category | flops | bytes accessed | tf_op | source)
XLA Modules:
  0.0 254.5 jit_solution(12375108726783082120)
XLA Ops:
  7.2 0.0 all-gather.2.cloned.1.call-start
  7.2 1.1 fusion.5
  8.3 1.0 fusion.6
  9.3 1.7 collective-permute-start
  11.0 3.7 %collective-permute-done = bf16[256,256]{1,0:T(8,128)(2,1)S(1)} collective-permute-done((bf16[256,256]{1,0:T(8,128)(2,1)S(1)}, bf16[256,256]{1,0:T(8,128)(2,1)S(1)}, u32[]{:S(2)}, u32[]{:S(2)}) %collective-permute-start) | collective-permute-done | bytes 131104 | tf_op jit(solution)/shard_map/ppermute | solution.py:159
  14.7 1.0 broadcast_select_fusion.1
  15.7 0.7 pad_maximum_fusion.4
  16.5 0.0 reduce-scatter.2.cloned.1.call-start
  16.5 0.3 reshape.43.mass_ref
  16.8 0.3 fusion
  17.1 0.3 fusion.1.xn_ref
  17.4 43.3 %all-gather.2.cloned.1.call-done = bf16[4096,256]{1,0:T(8,128)(2,1)} async-done(((bf16[512,256]{1,0:T(8,128)(2,1)}), bf16[4096,256]{1,0:T(8,128)(2,1)}) %all-gather.2.cloned.1.call-update) | async-done | bytes 2097168 | tf_op jit(solution)/shard_map/all_gather | solution.py:164
  60.7 1.6 copy-done.1
  62.2 6.7 %shard_map.76 = (f32[1536,1]{1,0:T(8,128)}, f32[32,128]{1,0:T(8,128)S(1)}) custom-call(s32[12,16]{1,0:T(8,128)S(1)} %copy-done.2, bf16[1536,256]{1,0:T(8,128)(2,1)S(1)} %fusion.1.xn_ref, bf16[32,128,256]{2,1,0:T(8,128)(2,1)S(1)} %bitcast.6, f32[32,128]{1,0:T(8,128)S(1)} %broadcast_in_dim.2.scale_ref, f32[1536,1]{1,0:T(8,128)S(1)} %reshape.43.mass_ref), custom_call_target="tpu_custom_call" | custom-call | flops 1610612736 | bytes 2883584 | tf_op jit(solution)/shard_map/pallas_call | solution.py:126
  69.0 1.2 collective-permute-done.1
  70.1 1.5 collective-permute-start.2
  71.6 2.2 collective-permute-done.2
  73.9 3.0 %collective-permute-start.3 = (f32[32,128]{1,0:T(8,128)S(1)}, f32[32,128]{1,0:T(8,128)S(1)}, u32[]{:S(2)}, u32[]{:S(2)}) collective-permute-start(f32[32,128]{1,0:T(8,128)S(1)} %add.98), channel_id=1, source_target_pairs={{0,128},{128,0},{1,129},{129,1},{2,130},{130,2},{3,131},{131,3},{4... | collective-permute-start | bytes 49160 | tf_op jit(solution)/shard_map/ppermute | solution.py:39
  76.9 2.2 collective-permute-done.3
  79.1 1.2 collective-permute-start.4
  80.3 2.6 %collective-permute-done.4 = f32[32,128]{1,0:T(8,128)S(1)} collective-permute-done((f32[32,128]{1,0:T(8,128)S(1)}, f32[32,128]{1,0:T(8,128)S(1)}, u32[]{:S(2)}, u32[]{:S(2)}) %collective-permute-start.4) | collective-permute-done | bytes 16416 | tf_op jit(solution)/shard_map/ppermute | solution.py:39
  83.0 0.5 collective-permute-start.5
  83.4 4.8 %collective-permute-done.5 = f32[32,128]{1,0:T(8,128)S(1)} collective-permute-done((f32[32,128]{1,0:T(8,128)S(1)}, f32[32,128]{1,0:T(8,128)S(1)}, u32[]{:S(2)}, u32[]{:S(2)}) %collective-permute-start.5) | collective-permute-done | bytes 16416 | tf_op jit(solution)/shard_map/ppermute | solution.py:39
  88.2 1.2 collective-permute-start.6
  89.4 2.5 collective-permute-done.6
  92.0 1.3 collective-permute-start.7
  93.2 3.4 %collective-permute-done.7 = f32[32,128]{1,0:T(8,128)S(1)} collective-permute-done((f32[32,128]{1,0:T(8,128)S(1)}, f32[32,128]{1,0:T(8,128)S(1)}, u32[]{:S(2)}, u32[]{:S(2)}) %collective-permute-start.7) | collective-permute-done | bytes 16416 | tf_op jit(solution)/shard_map/ppermute | solution.py:39
  96.6 3.0 %collective-permute-start.8 = (f32[32,128]{1,0:T(8,128)S(1)}, f32[32,128]{1,0:T(8,128)S(1)}, u32[]{:S(2)}, u32[]{:S(2)}) collective-permute-start(f32[32,128]{1,0:T(8,128)S(1)} %add.103), channel_id=1, source_target_pairs={{0,8},{2,10},{4,12},{6,14},{8,0},{10,2},{12,4},{14,6},{1,9},{3,11}... | collective-permute-start | bytes 49160 | tf_op jit(solution)/shard_map/ppermute | solution.py:39
  99.6 4.6 %collective-permute-done.8 = f32[32,128]{1,0:T(8,128)S(1)} collective-permute-done((f32[32,128]{1,0:T(8,128)S(1)}, f32[32,128]{1,0:T(8,128)S(1)}, u32[]{:S(2)}, u32[]{:S(2)}) %collective-permute-start.8) | collective-permute-done | bytes 16416 | tf_op jit(solution)/shard_map/ppermute | solution.py:39
  104.3 6.7 %shard_map.77 = (f32[1536,1]{1,0:T(8,128)}, f32[32,128]{1,0:T(8,128)S(1)}) custom-call(s32[12,16]{1,0:T(8,128)S(1)} %copy-done.2, bf16[1536,256]{1,0:T(8,128)(2,1)S(1)} %fusion.1.xn_ref, bf16[32,128,256]{2,1,0:T(8,128)(2,1)S(1)} %bitcast.7, f32[32,128]{1,0:T(8,128)S(1)} %bitcast_divide_fusion.1.scale_ref, f32[1536,1]{1,0:T(8,128)S(1)} %reshape.43.mass_ref), custom_call_target="tpu_custom_call" | custom-call | flops 1610612736 | bytes 2883584 | tf_op jit(solution)/shard_map/pallas_call | solution.py:126
  111.0 1.2 collective-permute-done.9
  112.2 1.5 collective-permute-start.10
  113.6 2.3 collective-permute-done.10
  115.9 3.0 %collective-permute-start.11 = (f32[32,128]{1,0:T(8,128)S(1)}, f32[32,128]{1,0:T(8,128)S(1)}, u32[]{:S(2)}, u32[]{:S(2)}) collective-permute-start(f32[32,128]{1,0:T(8,128)S(1)} %add.106), channel_id=1, source_target_pairs={{0,128},{128,0},{1,129},{129,1},{2,130},{130,2},{3,131},{131,3},{4... | collective-permute-start | bytes 49160 | tf_op jit(solution)/shard_map/ppermute | solution.py:39
  119.0 2.2 collective-permute-done.11
  121.2 1.1 collective-permute-start.12
  122.3 2.8 %collective-permute-done.12 = f32[32,128]{1,0:T(8,128)S(1)} collective-permute-done((f32[32,128]{1,0:T(8,128)S(1)}, f32[32,128]{1,0:T(8,128)S(1)}, u32[]{:S(2)}, u32[]{:S(2)}) %collective-permute-start.12) | collective-permute-done | bytes 16416 | tf_op jit(solution)/shard_map/ppermute | solution.py:39
  125.1 0.3 collective-permute-start.13
  125.4 4.9 %collective-permute-done.13 = f32[32,128]{1,0:T(8,128)S(1)} collective-permute-done((f32[32,128]{1,0:T(8,128)S(1)}, f32[32,128]{1,0:T(8,128)S(1)}, u32[]{:S(2)}, u32[]{:S(2)}) %collective-permute-start.13) | collective-permute-done | bytes 16416 | tf_op jit(solution)/shard_map/ppermute | solution.py:39
  130.3 1.1 collective-permute-start.14
  131.4 2.6 %collective-permute-done.14 = f32[32,128]{1,0:T(8,128)S(1)} collective-permute-done((f32[32,128]{1,0:T(8,128)S(1)}, f32[32,128]{1,0:T(8,128)S(1)}, u32[]{:S(2)}, u32[]{:S(2)}) %collective-permute-start.14) | collective-permute-done | bytes 16416 | tf_op jit(solution)/shard_map/ppermute | solution.py:39
  134.1 1.3 collective-permute-start.15
  135.3 3.4 %collective-permute-done.15 = f32[32,128]{1,0:T(8,128)S(1)} collective-permute-done((f32[32,128]{1,0:T(8,128)S(1)}, f32[32,128]{1,0:T(8,128)S(1)}, u32[]{:S(2)}, u32[]{:S(2)}) %collective-permute-start.15) | collective-permute-done | bytes 16416 | tf_op jit(solution)/shard_map/ppermute | solution.py:39
  138.7 3.0 %collective-permute-start.16 = (f32[32,128]{1,0:T(8,128)S(1)}, f32[32,128]{1,0:T(8,128)S(1)}, u32[]{:S(2)}, u32[]{:S(2)}) collective-permute-start(f32[32,128]{1,0:T(8,128)S(1)} %add.111), channel_id=1, source_target_pairs={{0,8},{2,10},{4,12},{6,14},{8,0},{10,2},{12,4},{14,6},{1,9},{3,11}... | collective-permute-start | bytes 49160 | tf_op jit(solution)/shard_map/ppermute | solution.py:39
  141.7 4.7 %collective-permute-done.16 = f32[32,128]{1,0:T(8,128)S(1)} collective-permute-done((f32[32,128]{1,0:T(8,128)S(1)}, f32[32,128]{1,0:T(8,128)S(1)}, u32[]{:S(2)}, u32[]{:S(2)}) %collective-permute-start.16) | collective-permute-done | bytes 16416 | tf_op jit(solution)/shard_map/ppermute | solution.py:39
  146.4 15.2 %shard_map.78 = (f32[1536,1]{1,0:T(8,128)S(1)}, f32[16,264,256]{2,1,0:T(8,128)}) custom-call(s32[12,16]{1,0:T(8,128)S(1)} %copy-done.2, bf16[1536,256]{1,0:T(8,128)(2,1)S(1)} %fusion.1.xn_ref, bf16[32,128,256]{2,1,0:T(8,128)(2,1)S(1)} %bitcast.8, f32[32,128]{1,0:T(8,128)S(1)} %bitcast_divide_fusion.scale_ref, f32[1536,1]{1,0:T(8,128)S(1)} %reshape.43.mass_ref, ...), custom_call_target="tpu_custom_call" | custom-call | flops 3221225472 | bytes 7864320 | tf_op jit(solution)/shard_map/pallas_call | solution.py:126
  161.6 55.1 %reduce-scatter.2.cloned.1.call-done = f32[528,256]{1,0:T(8,128)} async-done(((f32[4224,256]{1,0:T(8,128)}), f32[528,256]{1,0:T(8,128)}) %reduce-scatter.2.cloned.1.call-update) | async-done | bytes 540688 | tf_op jit(solution)/shard_map/reduce_scatter | solution.py:175
  216.7 0.7 fusion.7
  217.5 1.1 slice_select_fusion.5
  218.6 0.1 collective-permute-start.17
  218.7 1.5 collective-permute-done.17
  220.3 1.6 collective-permute-start.18
  221.9 4.2 %collective-permute-done.18 = f32[136,256]{1,0:T(8,128)S(1)} collective-permute-done((f32[136,256]{1,0:T(8,128)S(1)}, f32[136,256]{1,0:T(8,128)S(1)}, u32[]{:S(2)}, u32[]{:S(2)}) %collective-permute-start.18) | collective-permute-done | bytes 139296 | tf_op jit(solution)/shard_map/ppermute | solution.py:191
  226.2 1.3 collective-permute-start.19
  227.5 3.9 %collective-permute-done.19 = f32[136,256]{1,0:T(8,128)S(1)} collective-permute-done((f32[136,256]{1,0:T(8,128)S(1)}, f32[136,256]{1,0:T(8,128)S(1)}, u32[]{:S(2)}, u32[]{:S(2)}) %collective-permute-start.19) | collective-permute-done | bytes 139296 | tf_op jit(solution)/shard_map/ppermute | solution.py:39
  231.4 0.6 collective-permute-start.20
  232.0 6.0 %collective-permute-done.20 = f32[136,256]{1,0:T(8,128)S(1)} collective-permute-done((f32[136,256]{1,0:T(8,128)S(1)}, f32[136,256]{1,0:T(8,128)S(1)}, u32[]{:S(2)}, u32[]{:S(2)}) %collective-permute-start.20) | collective-permute-done | bytes 139296 | tf_op jit(solution)/shard_map/ppermute | solution.py:39
  238.0 3.1 %collective-permute-start.21 = (f32[136,256]{1,0:T(8,128)S(1)}, f32[136,256]{1,0:T(8,128)S(1)}, u32[]{:S(2)}, u32[]{:S(2)}) collective-permute-start(f32[136,256]{1,0:T(8,128)S(1)} %add.118), channel_id=1, source_target_pairs={{0,128},{128,0},{1,129},{129,1},{2,130},{130,2},{3,131},{131,3},{4... | collective-permute-start | bytes 417800 | tf_op jit(solution)/shard_map/ppermute | solution.py:39
  241.1 3.5 %collective-permute-done.21 = f32[136,256]{1,0:T(8,128)S(1)} collective-permute-done((f32[136,256]{1,0:T(8,128)S(1)}, f32[136,256]{1,0:T(8,128)S(1)}, u32[]{:S(2)}, u32[]{:S(2)}) %collective-permute-start.21) | collective-permute-done | bytes 139296 | tf_op jit(solution)/shard_map/ppermute | solution.py:39
  244.7 0.1 collective-permute-start.22
  244.8 0.9 reduce
  245.7 0.5 collective-permute-done.22
  246.2 0.6 multiply_divide_fusion
  246.9 0.8 maximum_divide_fusion
  (43 shorter events, 0.4 us)
Async XLA Ops:
  7.2 9.3 %copy-start.4 = (f32[1536]{0:T(1024)S(1)}, f32[1536]{0:T(1024)}, u32[]{:S(2)}) copy-start(f32[1536]{0:T(1024)} %param.6) | copy-start | bytes 18436
  7.2 9.6 %copy-start = (bf16[1536,256]{1,0:T(8,128)(2,1)S(1)}, bf16[1536,256]{1,0:T(8,128)(2,1)}, u32[]{:S(2)}) copy-start(bf16[1536,256]{1,0:T(8,128)(2,1)} %rest_0_.1) | copy-start | bytes 2359300
  7.2 53.5 %all-gather.2.cloned.1.call-start = ((), (), s32[]{:S(2)}) async-start(), calls=%async_computation.1 | async-start | bytes 2359296 | tf_op jit(solution)/shard_map/all_gather | solution.py:164
  9.3 5.3 %collective-permute-start = (bf16[256,256]{1,0:T(8,128)(2,1)S(1)}, bf16[256,256]{1,0:T(8,128)(2,1)S(1)}, u32[]{:S(2)}, u32[]{:S(2)}) collective-permute-start(bf16[256,256]{1,0:T(8,128)(2,1)S(1)} %fusion.6), channel_id=1, source_target_pairs={{0,1},{1,0},{2,3},{3,2},{4,5},{5,4},{6,7},{7,6},{8,9},{9,8},{10,11... | collective-permute-start | bytes 393224 | tf_op jit(solution)/shard_map/ppermute | solution.py:159
  16.4 44.2 %copy-start.2 = (s32[12,16]{1,0:T(8,128)S(1)}, s32[12,16]{1,0:T(8,128)}, u32[]{:S(2)}) copy-start(s32[12,16]{1,0:T(8,128)} %links_ref.5) | copy-start | bytes 2308
  16.5 200.3 %reduce-scatter.2.cloned.1.call-start = ((), (), s32[]{:S(2)}) async-start(), calls=%async_computation.2 | async-start | bytes 4866048 | tf_op jit(solution)/shard_map/reduce_scatter | solution.py:175
  60.7 1.6 copy-start.1
  62.2 42.0 %copy-start.3 = (f32[4096]{0:T(1024)S(1)}, f32[4096]{0:T(1024)}, u32[]{:S(2)}) copy-start(f32[4096]{0:T(1024)} %param.9) | copy-start | bytes 49156
  69.0 1.2 collective-permute-start.1
  70.1 3.7 %collective-permute-start.2 = (f32[32,128]{1,0:T(8,128)S(1)}, f32[32,128]{1,0:T(8,128)S(1)}, u32[]{:S(2)}, u32[]{:S(2)}) collective-permute-start(f32[32,128]{1,0:T(8,128)S(1)} %add.97), channel_id=1, source_target_pairs={{0,1},{1,0},{2,3},{3,2},{4,5},{5,4},{6,7},{7,6},{8,9},{9,8},{10,11... | collective-permute-start | bytes 49160 | tf_op jit(solution)/shard_map/ppermute | solution.py:39
  73.9 5.2 %collective-permute-start.3 = (f32[32,128]{1,0:T(8,128)S(1)}, f32[32,128]{1,0:T(8,128)S(1)}, u32[]{:S(2)}, u32[]{:S(2)}) collective-permute-start(f32[32,128]{1,0:T(8,128)S(1)} %add.98), channel_id=1, source_target_pairs={{0,128},{128,0},{1,129},{129,1},{2,130},{130,2},{3,131},{131,3},{4... | collective-permute-start | bytes 49160 | tf_op jit(solution)/shard_map/ppermute | solution.py:39
  79.1 3.8 %collective-permute-start.4 = (f32[32,128]{1,0:T(8,128)S(1)}, f32[32,128]{1,0:T(8,128)S(1)}, u32[]{:S(2)}, u32[]{:S(2)}) collective-permute-start(f32[32,128]{1,0:T(8,128)S(1)} %add.99), channel_id=1, source_target_pairs={{0,32},{32,0},{64,96},{96,64},{1,33},{33,1},{65,97},{97,65},{2,34}... | collective-permute-start | bytes 49160 | tf_op jit(solution)/shard_map/ppermute | solution.py:39
  83.0 5.2 %collective-permute-start.5 = (f32[32,128]{1,0:T(8,128)S(1)}, f32[32,128]{1,0:T(8,128)S(1)}, u32[]{:S(2)}, u32[]{:S(2)}) collective-permute-start(f32[32,128]{1,0:T(8,128)S(1)} %add.100), channel_id=1, source_target_pairs={{0,64},{32,96},{64,0},{96,32},{1,65},{33,97},{65,1},{97,33},{2,66}... | collective-permute-start | bytes 49160 | tf_op jit(solution)/shard_map/ppermute | solution.py:39
  88.2 3.7 %collective-permute-start.6 = (f32[32,128]{1,0:T(8,128)S(1)}, f32[32,128]{1,0:T(8,128)S(1)}, u32[]{:S(2)}, u32[]{:S(2)}) collective-permute-start(f32[32,128]{1,0:T(8,128)S(1)} %add.101), channel_id=1, source_target_pairs={{0,2},{2,0},{4,6},{6,4},{8,10},{10,8},{12,14},{14,12},{1,3},{3,1},... | collective-permute-start | bytes 49160 | tf_op jit(solution)/shard_map/ppermute | solution.py:39
  92.0 4.6 %collective-permute-start.7 = (f32[32,128]{1,0:T(8,128)S(1)}, f32[32,128]{1,0:T(8,128)S(1)}, u32[]{:S(2)}, u32[]{:S(2)}) collective-permute-start(f32[32,128]{1,0:T(8,128)S(1)} %add.102), channel_id=1, source_target_pairs={{0,4},{2,6},{4,0},{6,2},{8,12},{10,14},{12,8},{14,10},{1,5},{3,7},... | collective-permute-start | bytes 49160 | tf_op jit(solution)/shard_map/ppermute | solution.py:39
  96.6 7.6 %collective-permute-start.8 = (f32[32,128]{1,0:T(8,128)S(1)}, f32[32,128]{1,0:T(8,128)S(1)}, u32[]{:S(2)}, u32[]{:S(2)}) collective-permute-start(f32[32,128]{1,0:T(8,128)S(1)} %add.103), channel_id=1, source_target_pairs={{0,8},{2,10},{4,12},{6,14},{8,0},{10,2},{12,4},{14,6},{1,9},{3,11}... | collective-permute-start | bytes 49160 | tf_op jit(solution)/shard_map/ppermute | solution.py:39
  111.0 1.2 collective-permute-start.9
  112.2 3.7 %collective-permute-start.10 = (f32[32,128]{1,0:T(8,128)S(1)}, f32[32,128]{1,0:T(8,128)S(1)}, u32[]{:S(2)}, u32[]{:S(2)}) collective-permute-start(f32[32,128]{1,0:T(8,128)S(1)} %add.105), channel_id=1, source_target_pairs={{0,1},{1,0},{2,3},{3,2},{4,5},{5,4},{6,7},{7,6},{8,9},{9,8},{10,11... | collective-permute-start | bytes 49160 | tf_op jit(solution)/shard_map/ppermute | solution.py:39
  115.9 5.2 %collective-permute-start.11 = (f32[32,128]{1,0:T(8,128)S(1)}, f32[32,128]{1,0:T(8,128)S(1)}, u32[]{:S(2)}, u32[]{:S(2)}) collective-permute-start(f32[32,128]{1,0:T(8,128)S(1)} %add.106), channel_id=1, source_target_pairs={{0,128},{128,0},{1,129},{129,1},{2,130},{130,2},{3,131},{131,3},{4... | collective-permute-start | bytes 49160 | tf_op jit(solution)/shard_map/ppermute | solution.py:39
  121.2 3.9 %collective-permute-start.12 = (f32[32,128]{1,0:T(8,128)S(1)}, f32[32,128]{1,0:T(8,128)S(1)}, u32[]{:S(2)}, u32[]{:S(2)}) collective-permute-start(f32[32,128]{1,0:T(8,128)S(1)} %add.107), channel_id=1, source_target_pairs={{0,32},{32,0},{64,96},{96,64},{1,33},{33,1},{65,97},{97,65},{2,34}... | collective-permute-start | bytes 49160 | tf_op jit(solution)/shard_map/ppermute | solution.py:39
  125.1 5.2 %collective-permute-start.13 = (f32[32,128]{1,0:T(8,128)S(1)}, f32[32,128]{1,0:T(8,128)S(1)}, u32[]{:S(2)}, u32[]{:S(2)}) collective-permute-start(f32[32,128]{1,0:T(8,128)S(1)} %add.108), channel_id=1, source_target_pairs={{0,64},{32,96},{64,0},{96,32},{1,65},{33,97},{65,1},{97,33},{2,66}... | collective-permute-start | bytes 49160 | tf_op jit(solution)/shard_map/ppermute | solution.py:39
  130.3 3.7 %collective-permute-start.14 = (f32[32,128]{1,0:T(8,128)S(1)}, f32[32,128]{1,0:T(8,128)S(1)}, u32[]{:S(2)}, u32[]{:S(2)}) collective-permute-start(f32[32,128]{1,0:T(8,128)S(1)} %add.109), channel_id=1, source_target_pairs={{0,2},{2,0},{4,6},{6,4},{8,10},{10,8},{12,14},{14,12},{1,3},{3,1},... | collective-permute-start | bytes 49160 | tf_op jit(solution)/shard_map/ppermute | solution.py:39
  134.1 4.6 %collective-permute-start.15 = (f32[32,128]{1,0:T(8,128)S(1)}, f32[32,128]{1,0:T(8,128)S(1)}, u32[]{:S(2)}, u32[]{:S(2)}) collective-permute-start(f32[32,128]{1,0:T(8,128)S(1)} %add.110), channel_id=1, source_target_pairs={{0,4},{2,6},{4,0},{6,2},{8,12},{10,14},{12,8},{14,10},{1,5},{3,7},... | collective-permute-start | bytes 49160 | tf_op jit(solution)/shard_map/ppermute | solution.py:39
  138.7 7.6 %collective-permute-start.16 = (f32[32,128]{1,0:T(8,128)S(1)}, f32[32,128]{1,0:T(8,128)S(1)}, u32[]{:S(2)}, u32[]{:S(2)}) collective-permute-start(f32[32,128]{1,0:T(8,128)S(1)} %add.111), channel_id=1, source_target_pairs={{0,8},{2,10},{4,12},{6,14},{8,0},{10,2},{12,4},{14,6},{1,9},{3,11}... | collective-permute-start | bytes 49160 | tf_op jit(solution)/shard_map/ppermute | solution.py:39
  218.6 1.6 collective-permute-start.17
  220.3 5.8 %collective-permute-start.18 = (f32[136,256]{1,0:T(8,128)S(1)}, f32[136,256]{1,0:T(8,128)S(1)}, u32[]{:S(2)}, u32[]{:S(2)}) collective-permute-start(f32[136,256]{1,0:T(8,128)S(1)} %slice_select_fusion.1), channel_id=1, source_target_pairs={{0,1},{1,0},{2,3},{3,2},{4,5},{5,4},{6,7},{7,6},{8,9},{9,8},{10,11... | collective-permute-start | bytes 417800 | tf_op jit(solution)/shard_map/ppermute | solution.py:191
  226.2 5.1 %collective-permute-start.19 = (f32[136,256]{1,0:T(8,128)S(1)}, f32[136,256]{1,0:T(8,128)S(1)}, u32[]{:S(2)}, u32[]{:S(2)}) collective-permute-start(f32[136,256]{1,0:T(8,128)S(1)} %select_add_fusion), channel_id=1, source_target_pairs={{0,32},{32,0},{64,96},{96,64},{1,33},{33,1},{65,97},{97,65},{2,34}... | collective-permute-start | bytes 417800 | tf_op jit(solution)/shard_map/ppermute | solution.py:39
  231.4 6.6 %collective-permute-start.20 = (f32[136,256]{1,0:T(8,128)S(1)}, f32[136,256]{1,0:T(8,128)S(1)}, u32[]{:S(2)}, u32[]{:S(2)}) collective-permute-start(f32[136,256]{1,0:T(8,128)S(1)} %add.117), channel_id=1, source_target_pairs={{0,64},{32,96},{64,0},{96,32},{1,65},{33,97},{65,1},{97,33},{2,66}... | collective-permute-start | bytes 417800 | tf_op jit(solution)/shard_map/ppermute | solution.py:39
  238.0 6.6 %collective-permute-start.21 = (f32[136,256]{1,0:T(8,128)S(1)}, f32[136,256]{1,0:T(8,128)S(1)}, u32[]{:S(2)}, u32[]{:S(2)}) collective-permute-start(f32[136,256]{1,0:T(8,128)S(1)} %add.118), channel_id=1, source_target_pairs={{0,128},{128,0},{1,129},{129,1},{2,130},{130,2},{3,131},{131,3},{4... | collective-permute-start | bytes 417800 | tf_op jit(solution)/shard_map/ppermute | solution.py:39
  244.7 1.4 collective-permute-start.22
Sparse Core Ops, SparseCore 0:
  16.6 44.0 all-gather.1
  161.7 54.9 reduce-scatter.1

commit v14 on v13

--- a/solution.py
+++ b/solution.py
@@ -16,7 +16,7 @@
 EPS = 0.05
 OFFSET = 1.0
 PAD = 8
-SUB = 4
+SUB = 6
 
 ROW_AXES = ("yh", "x", "c")
 COL_AXES = ("z", "yl")

time: 256 us -> 255 us (level)
  no operation moved by 1% of the time
where the time goes in v14:
time: 255 us; the launch traced here: 254 us
  waiting for transfers between devices  170 us (67%)
  starting transfers between devices  31.3 us (12%)
  Pallas kernels  27.9 us (11%)
  between operations  14.3 us (6%)
  other arithmetic  8.16 us (3%)
  local copies, waits for them, and re-layouts  2.6 us (1%)
    ppermute x19, waiting for transfers between devices, butterfly_sum(): x = x + lax.ppermute(x, axis, [(j, j ^ k) for j in range(n)])  61.2 us
    reduce_scatter x1, waiting for transfers between devices, on_device(): lax.psum_scatter(packed.reshape(-1, feature_count), 'z', scatter_dimensio...  55.2 us
    all_gather x1, waiting for transfers between devices, on_device(): gathered = lax.all_gather(slab, 'z', axis=0, tiled=True)  43.3 us
    pallas_call x3, Pallas kernels, sweep(): pl.pallas_call(functools.partial(sweep_body, nbr, inv_width, inv_count, b...  27.9 us
    ppermute x19, starting transfers between devices, butterfly_sum(): x = x + lax.ppermute(x, axis, [(j, j ^ k) for j in range(n)])  27.8 us
  transfers between devices with their start and end apart: 25, of which 25 were waited for; matrix products, arithmetic and copies ran while one was open for 1% of the time, Pallas kernels for 0%

profile of v14, /device:TPU:4, one launch (start us, length us, event | category | flops | bytes accessed | tf_op | source)
XLA Modules:
  0.0 253.9 jit_solution(1116343803545934776)
XLA Ops:
  7.2 0.0 all-gather.2.cloned.1.call-start
  7.2 1.1 fusion.5
  8.3 1.0 fusion.6
  9.3 1.7 collective-permute-start
  11.0 3.7 %collective-permute-done = bf16[256,256]{1,0:T(8,128)(2,1)S(1)} collective-permute-done((bf16[256,256]{1,0:T(8,128)(2,1)S(1)}, bf16[256,256]{1,0:T(8,128)(2,1)S(1)}, u32[]{:S(2)}, u32[]{:S(2)}) %collective-permute-start) | collective-permute-done | bytes 131104 | tf_op jit(solution)/shard_map/ppermute | solution.py:159
  14.7 1.0 broadcast_select_fusion.1
  15.7 0.7 pad_maximum_fusion.4
  16.5 0.0 reduce-scatter.2.cloned.1.call-start
  16.5 0.3 reshape.43.mass_ref
  16.8 0.3 fusion
  17.1 0.3 fusion.1.xn_ref
  17.4 43.3 %all-gather.2.cloned.1.call-done = bf16[4096,256]{1,0:T(8,128)(2,1)} async-done(((bf16[512,256]{1,0:T(8,128)(2,1)}), bf16[4096,256]{1,0:T(8,128)(2,1)}) %all-gather.2.cloned.1.call-update) | async-done | bytes 2097168 | tf_op jit(solution)/shard_map/all_gather | solution.py:164
  60.7 1.6 copy-done.1
  62.2 6.4 %shard_map.76 = (f32[1536,1]{1,0:T(8,128)}, f32[32,128]{1,0:T(8,128)S(1)}) custom-call(s32[12,16]{1,0:T(8,128)S(1)} %copy-done.2, bf16[1536,256]{1,0:T(8,128)(2,1)S(1)} %fusion.1.xn_ref, bf16[32,128,256]{2,1,0:T(8,128)(2,1)S(1)} %bitcast.6, f32[32,128]{1,0:T(8,128)S(1)} %broadcast_in_dim.2.scale_ref, f32[1536,1]{1,0:T(8,128)S(1)} %reshape.43.mass_ref), custom_call_target="tpu_custom_call" | custom-call | flops 1610612736 | bytes 2883584 | tf_op jit(solution)/shard_map/pallas_call | solution.py:126
  68.7 1.2 collective-permute-done.1
  69.9 1.5 collective-permute-start.2
  71.3 2.3 collective-permute-done.2
  73.6 3.0 %collective-permute-start.3 = (f32[32,128]{1,0:T(8,128)S(1)}, f32[32,128]{1,0:T(8,128)S(1)}, u32[]{:S(2)}, u32[]{:S(2)}) collective-permute-start(f32[32,128]{1,0:T(8,128)S(1)} %add.98), channel_id=1, source_target_pairs={{0,128},{128,0},{1,129},{129,1},{2,130},{130,2},{3,131},{131,3},{4... | collective-permute-start | bytes 49160 | tf_op jit(solution)/shard_map/ppermute | solution.py:39
  76.6 2.2 collective-permute-done.3
  78.9 1.2 collective-permute-start.4
  80.0 2.7 %collective-permute-done.4 = f32[32,128]{1,0:T(8,128)S(1)} collective-permute-done((f32[32,128]{1,0:T(8,128)S(1)}, f32[32,128]{1,0:T(8,128)S(1)}, u32[]{:S(2)}, u32[]{:S(2)}) %collective-permute-start.4) | collective-permute-done | bytes 16416 | tf_op jit(solution)/shard_map/ppermute | solution.py:39
  82.7 0.4 collective-permute-start.5
  83.1 4.8 %collective-permute-done.5 = f32[32,128]{1,0:T(8,128)S(1)} collective-permute-done((f32[32,128]{1,0:T(8,128)S(1)}, f32[32,128]{1,0:T(8,128)S(1)}, u32[]{:S(2)}, u32[]{:S(2)}) %collective-permute-start.5) | collective-permute-done | bytes 16416 | tf_op jit(solution)/shard_map/ppermute | solution.py:39
  87.9 1.2 collective-permute-start.6
  89.2 2.5 collective-permute-done.6
  91.7 1.2 collective-permute-start.7
  92.9 3.4 %collective-permute-done.7 = f32[32,128]{1,0:T(8,128)S(1)} collective-permute-done((f32[32,128]{1,0:T(8,128)S(1)}, f32[32,128]{1,0:T(8,128)S(1)}, u32[]{:S(2)}, u32[]{:S(2)}) %collective-permute-start.7) | collective-permute-done | bytes 16416 | tf_op jit(solution)/shard_map/ppermute | solution.py:39
  96.3 3.0 %collective-permute-start.8 = (f32[32,128]{1,0:T(8,128)S(1)}, f32[32,128]{1,0:T(8,128)S(1)}, u32[]{:S(2)}, u32[]{:S(2)}) collective-permute-start(f32[32,128]{1,0:T(8,128)S(1)} %add.103), channel_id=1, source_target_pairs={{0,8},{2,10},{4,12},{6,14},{8,0},{10,2},{12,4},{14,6},{1,9},{3,11}... | collective-permute-start | bytes 49160 | tf_op jit(solution)/shard_map/ppermute | solution.py:39
  99.3 4.7 %collective-permute-done.8 = f32[32,128]{1,0:T(8,128)S(1)} collective-permute-done((f32[32,128]{1,0:T(8,128)S(1)}, f32[32,128]{1,0:T(8,128)S(1)}, u32[]{:S(2)}, u32[]{:S(2)}) %collective-permute-start.8) | collective-permute-done | bytes 16416 | tf_op jit(solution)/shard_map/ppermute | solution.py:39
  104.0 6.4 %shard_map.77 = (f32[1536,1]{1,0:T(8,128)}, f32[32,128]{1,0:T(8,128)S(1)}) custom-call(s32[12,16]{1,0:T(8,128)S(1)} %copy-done.2, bf16[1536,256]{1,0:T(8,128)(2,1)S(1)} %fusion.1.xn_ref, bf16[32,128,256]{2,1,0:T(8,128)(2,1)S(1)} %bitcast.7, f32[32,128]{1,0:T(8,128)S(1)} %bitcast_divide_fusion.1.scale_ref, f32[1536,1]{1,0:T(8,128)S(1)} %reshape.43.mass_ref), custom_call_target="tpu_custom_call" | custom-call | flops 1610612736 | bytes 2883584 | tf_op jit(solution)/shard_map/pallas_call | solution.py:126
  110.4 1.2 collective-permute-done.9
  111.6 1.5 collective-permute-start.10
  113.1 2.3 collective-permute-done.10
  115.4 3.1 %collective-permute-start.11 = (f32[32,128]{1,0:T(8,128)S(1)}, f32[32,128]{1,0:T(8,128)S(1)}, u32[]{:S(2)}, u32[]{:S(2)}) collective-permute-start(f32[32,128]{1,0:T(8,128)S(1)} %add.106), channel_id=1, source_target_pairs={{0,128},{128,0},{1,129},{129,1},{2,130},{130,2},{3,131},{131,3},{4... | collective-permute-start | bytes 49160 | tf_op jit(solution)/shard_map/ppermute | solution.py:39
  118.4 2.2 collective-permute-done.11
  120.6 1.1 collective-permute-start.12
  121.7 2.8 %collective-permute-done.12 = f32[32,128]{1,0:T(8,128)S(1)} collective-permute-done((f32[32,128]{1,0:T(8,128)S(1)}, f32[32,128]{1,0:T(8,128)S(1)}, u32[]{:S(2)}, u32[]{:S(2)}) %collective-permute-start.12) | collective-permute-done | bytes 16416 | tf_op jit(solution)/shard_map/ppermute | solution.py:39
  124.5 0.3 collective-permute-start.13
  124.8 5.0 %collective-permute-done.13 = f32[32,128]{1,0:T(8,128)S(1)} collective-permute-done((f32[32,128]{1,0:T(8,128)S(1)}, f32[32,128]{1,0:T(8,128)S(1)}, u32[]{:S(2)}, u32[]{:S(2)}) %collective-permute-start.13) | collective-permute-done | bytes 16416 | tf_op jit(solution)/shard_map/ppermute | solution.py:39
  129.8 1.1 collective-permute-start.14
  130.9 2.6 %collective-permute-done.14 = f32[32,128]{1,0:T(8,128)S(1)} collective-permute-done((f32[32,128]{1,0:T(8,128)S(1)}, f32[32,128]{1,0:T(8,128)S(1)}, u32[]{:S(2)}, u32[]{:S(2)}) %collective-permute-start.14) | collective-permute-done | bytes 16416 | tf_op jit(solution)/shard_map/ppermute | solution.py:39
  133.5 1.2 collective-permute-start.15
  134.7 3.4 %collective-permute-done.15 = f32[32,128]{1,0:T(8,128)S(1)} collective-permute-done((f32[32,128]{1,0:T(8,128)S(1)}, f32[32,128]{1,0:T(8,128)S(1)}, u32[]{:S(2)}, u32[]{:S(2)}) %collective-permute-start.15) | collective-permute-done | bytes 16416 | tf_op jit(solution)/shard_map/ppermute | solution.py:39
  138.1 3.0 %collective-permute-start.16 = (f32[32,128]{1,0:T(8,128)S(1)}, f32[32,128]{1,0:T(8,128)S(1)}, u32[]{:S(2)}, u32[]{:S(2)}) collective-permute-start(f32[32,128]{1,0:T(8,128)S(1)} %add.111), channel_id=1, source_target_pairs={{0,8},{2,10},{4,12},{6,14},{8,0},{10,2},{12,4},{14,6},{1,9},{3,11}... | collective-permute-start | bytes 49160 | tf_op jit(solution)/shard_map/ppermute | solution.py:39
  141.1 4.7 %collective-permute-done.16 = f32[32,128]{1,0:T(8,128)S(1)} collective-permute-done((f32[32,128]{1,0:T(8,128)S(1)}, f32[32,128]{1,0:T(8,128)S(1)}, u32[]{:S(2)}, u32[]{:S(2)}) %collective-permute-start.16) | collective-permute-done | bytes 16416 | tf_op jit(solution)/shard_map/ppermute | solution.py:39
  145.8 15.0 %shard_map.78 = (f32[1536,1]{1,0:T(8,128)S(1)}, f32[16,264,256]{2,1,0:T(8,128)}) custom-call(s32[12,16]{1,0:T(8,128)S(1)} %copy-done.2, bf16[1536,256]{1,0:T(8,128)(2,1)S(1)} %fusion.1.xn_ref, bf16[32,128,256]{2,1,0:T(8,128)(2,1)S(1)} %bitcast.8, f32[32,128]{1,0:T(8,128)S(1)} %bitcast_divide_fusion.scale_ref, f32[1536,1]{1,0:T(8,128)S(1)} %reshape.43.mass_ref, ...), custom_call_target="tpu_custom_call" | custom-call | flops 3221225472 | bytes 7864320 | tf_op jit(solution)/shard_map/pallas_call | solution.py:126
  160.9 55.2 %reduce-scatter.2.cloned.1.call-done = f32[528,256]{1,0:T(8,128)} async-done(((f32[4224,256]{1,0:T(8,128)}), f32[528,256]{1,0:T(8,128)}) %reduce-scatter.2.cloned.1.call-update) | async-done | bytes 540688 | tf_op jit(solution)/shard_map/reduce_scatter | solution.py:175
  216.1 0.7 fusion.7
  216.8 1.1 slice_select_fusion.5
  218.0 0.1 collective-permute-start.17
  218.1 1.5 collective-permute-done.17
  219.7 1.6 collective-permute-start.18
  221.3 4.2 %collective-permute-done.18 = f32[136,256]{1,0:T(8,128)S(1)} collective-permute-done((f32[136,256]{1,0:T(8,128)S(1)}, f32[136,256]{1,0:T(8,128)S(1)}, u32[]{:S(2)}, u32[]{:S(2)}) %collective-permute-start.18) | collective-permute-done | bytes 139296 | tf_op jit(solution)/shard_map/ppermute | solution.py:191
  225.5 1.3 collective-permute-start.19
  226.8 3.9 %collective-permute-done.19 = f32[136,256]{1,0:T(8,128)S(1)} collective-permute-done((f32[136,256]{1,0:T(8,128)S(1)}, f32[136,256]{1,0:T(8,128)S(1)}, u32[]{:S(2)}, u32[]{:S(2)}) %collective-permute-start.19) | collective-permute-done | bytes 139296 | tf_op jit(solution)/shard_map/ppermute | solution.py:39
  230.7 0.6 collective-permute-start.20
  231.4 6.0 %collective-permute-done.20 = f32[136,256]{1,0:T(8,128)S(1)} collective-permute-done((f32[136,256]{1,0:T(8,128)S(1)}, f32[136,256]{1,0:T(8,128)S(1)}, u32[]{:S(2)}, u32[]{:S(2)}) %collective-permute-start.20) | collective-permute-done | bytes 139296 | tf_op jit(solution)/shard_map/ppermute | solution.py:39
  237.4 3.1 %collective-permute-start.21 = (f32[136,256]{1,0:T(8,128)S(1)}, f32[136,256]{1,0:T(8,128)S(1)}, u32[]{:S(2)}, u32[]{:S(2)}) collective-permute-start(f32[136,256]{1,0:T(8,128)S(1)} %add.118), channel_id=1, source_target_pairs={{0,128},{128,0},{1,129},{129,1},{2,130},{130,2},{3,131},{131,3},{4... | collective-permute-start | bytes 417800 | tf_op jit(solution)/shard_map/ppermute | solution.py:39
  240.5 3.5 %collective-permute-done.21 = f32[136,256]{1,0:T(8,128)S(1)} collective-permute-done((f32[136,256]{1,0:T(8,128)S(1)}, f32[136,256]{1,0:T(8,128)S(1)}, u32[]{:S(2)}, u32[]{:S(2)}) %collective-permute-start.21) | collective-permute-done | bytes 139296 | tf_op jit(solution)/shard_map/ppermute | solution.py:39
  244.0 0.1 collective-permute-start.22
  244.1 0.9 reduce
  245.0 0.5 collective-permute-done.22
  245.5 0.6 multiply_divide_fusion
  246.2 0.8 maximum_divide_fusion
  (43 shorter events, 0.4 us)
Async XLA Ops:
  7.2 9.3 %copy-start.4 = (f32[1536]{0:T(1024)S(1)}, f32[1536]{0:T(1024)}, u32[]{:S(2)}) copy-start(f32[1536]{0:T(1024)} %param.6) | copy-start | bytes 18436
  7.2 9.6 %copy-start = (bf16[1536,256]{1,0:T(8,128)(2,1)S(1)}, bf16[1536,256]{1,0:T(8,128)(2,1)}, u32[]{:S(2)}) copy-start(bf16[1536,256]{1,0:T(8,128)(2,1)} %rest_0_.1) | copy-start | bytes 2359300
  7.2 53.5 %all-gather.2.cloned.1.call-start = ((), (), s32[]{:S(2)}) async-start(), calls=%async_computation.1 | async-start | bytes 2359296 | tf_op jit(solution)/shard_map/all_gather | solution.py:164
  9.3 5.3 %collective-permute-start = (bf16[256,256]{1,0:T(8,128)(2,1)S(1)}, bf16[256,256]{1,0:T(8,128)(2,1)S(1)}, u32[]{:S(2)}, u32[]{:S(2)}) collective-permute-start(bf16[256,256]{1,0:T(8,128)(2,1)S(1)} %fusion.6), channel_id=1, source_target_pairs={{0,1},{1,0},{2,3},{3,2},{4,5},{5,4},{6,7},{7,6},{8,9},{9,8},{10,11... | collective-permute-start | bytes 393224 | tf_op jit(solution)/shard_map/ppermute | solution.py:159
  16.4 44.2 %copy-start.2 = (s32[12,16]{1,0:T(8,128)S(1)}, s32[12,16]{1,0:T(8,128)}, u32[]{:S(2)}) copy-start(s32[12,16]{1,0:T(8,128)} %links_ref.5) | copy-start | bytes 2308
  16.5 199.6 %reduce-scatter.2.cloned.1.call-start = ((), (), s32[]{:S(2)}) async-start(), calls=%async_computation.2 | async-start | bytes 4866048 | tf_op jit(solution)/shard_map/reduce_scatter | solution.py:175
  60.7 1.6 copy-start.1
  62.2 41.7 %copy-start.3 = (f32[4096]{0:T(1024)S(1)}, f32[4096]{0:T(1024)}, u32[]{:S(2)}) copy-start(f32[4096]{0:T(1024)} %param.9) | copy-start | bytes 49156
  68.7 1.2 collective-permute-start.1
  69.9 3.7 %collective-permute-start.2 = (f32[32,128]{1,0:T(8,128)S(1)}, f32[32,128]{1,0:T(8,128)S(1)}, u32[]{:S(2)}, u32[]{:S(2)}) collective-permute-start(f32[32,128]{1,0:T(8,128)S(1)} %add.97), channel_id=1, source_target_pairs={{0,1},{1,0},{2,3},{3,2},{4,5},{5,4},{6,7},{7,6},{8,9},{9,8},{10,11... | collective-permute-start | bytes 49160 | tf_op jit(solution)/shard_map/ppermute | solution.py:39
  73.6 5.2 %collective-permute-start.3 = (f32[32,128]{1,0:T(8,128)S(1)}, f32[32,128]{1,0:T(8,128)S(1)}, u32[]{:S(2)}, u32[]{:S(2)}) collective-permute-start(f32[32,128]{1,0:T(8,128)S(1)} %add.98), channel_id=1, source_target_pairs={{0,128},{128,0},{1,129},{129,1},{2,130},{130,2},{3,131},{131,3},{4... | collective-permute-start | bytes 49160 | tf_op jit(solution)/shard_map/ppermute | solution.py:39
  78.9 3.8 %collective-permute-start.4 = (f32[32,128]{1,0:T(8,128)S(1)}, f32[32,128]{1,0:T(8,128)S(1)}, u32[]{:S(2)}, u32[]{:S(2)}) collective-permute-start(f32[32,128]{1,0:T(8,128)S(1)} %add.99), channel_id=1, source_target_pairs={{0,32},{32,0},{64,96},{96,64},{1,33},{33,1},{65,97},{97,65},{2,34}... | collective-permute-start | bytes 49160 | tf_op jit(solution)/shard_map/ppermute | solution.py:39
  82.7 5.2 %collective-permute-start.5 = (f32[32,128]{1,0:T(8,128)S(1)}, f32[32,128]{1,0:T(8,128)S(1)}, u32[]{:S(2)}, u32[]{:S(2)}) collective-permute-start(f32[32,128]{1,0:T(8,128)S(1)} %add.100), channel_id=1, source_target_pairs={{0,64},{32,96},{64,0},{96,32},{1,65},{33,97},{65,1},{97,33},{2,66}... | collective-permute-start | bytes 49160 | tf_op jit(solution)/shard_map/ppermute | solution.py:39
  87.9 3.7 %collective-permute-start.6 = (f32[32,128]{1,0:T(8,128)S(1)}, f32[32,128]{1,0:T(8,128)S(1)}, u32[]{:S(2)}, u32[]{:S(2)}) collective-permute-start(f32[32,128]{1,0:T(8,128)S(1)} %add.101), channel_id=1, source_target_pairs={{0,2},{2,0},{4,6},{6,4},{8,10},{10,8},{12,14},{14,12},{1,3},{3,1},... | collective-permute-start | bytes 49160 | tf_op jit(solution)/shard_map/ppermute | solution.py:39
  91.7 4.6 %collective-permute-start.7 = (f32[32,128]{1,0:T(8,128)S(1)}, f32[32,128]{1,0:T(8,128)S(1)}, u32[]{:S(2)}, u32[]{:S(2)}) collective-permute-start(f32[32,128]{1,0:T(8,128)S(1)} %add.102), channel_id=1, source_target_pairs={{0,4},{2,6},{4,0},{6,2},{8,12},{10,14},{12,8},{14,10},{1,5},{3,7},... | collective-permute-start | bytes 49160 | tf_op jit(solution)/shard_map/ppermute | solution.py:39
  96.3 7.6 %collective-permute-start.8 = (f32[32,128]{1,0:T(8,128)S(1)}, f32[32,128]{1,0:T(8,128)S(1)}, u32[]{:S(2)}, u32[]{:S(2)}) collective-permute-start(f32[32,128]{1,0:T(8,128)S(1)} %add.103), channel_id=1, source_target_pairs={{0,8},{2,10},{4,12},{6,14},{8,0},{10,2},{12,4},{14,6},{1,9},{3,11}... | collective-permute-start | bytes 49160 | tf_op jit(solution)/shard_map/ppermute | solution.py:39
  110.4 1.2 collective-permute-start.9
  111.6 3.7 %collective-permute-start.10 = (f32[32,128]{1,0:T(8,128)S(1)}, f32[32,128]{1,0:T(8,128)S(1)}, u32[]{:S(2)}, u32[]{:S(2)}) collective-permute-start(f32[32,128]{1,0:T(8,128)S(1)} %add.105), channel_id=1, source_target_pairs={{0,1},{1,0},{2,3},{3,2},{4,5},{5,4},{6,7},{7,6},{8,9},{9,8},{10,11... | collective-permute-start | bytes 49160 | tf_op jit(solution)/shard_map/ppermute | solution.py:39
  115.4 5.2 %collective-permute-start.11 = (f32[32,128]{1,0:T(8,128)S(1)}, f32[32,128]{1,0:T(8,128)S(1)}, u32[]{:S(2)}, u32[]{:S(2)}) collective-permute-start(f32[32,128]{1,0:T(8,128)S(1)} %add.106), channel_id=1, source_target_pairs={{0,128},{128,0},{1,129},{129,1},{2,130},{130,2},{3,131},{131,3},{4... | collective-permute-start | bytes 49160 | tf_op jit(solution)/shard_map/ppermute | solution.py:39
  120.6 3.9 %collective-permute-start.12 = (f32[32,128]{1,0:T(8,128)S(1)}, f32[32,128]{1,0:T(8,128)S(1)}, u32[]{:S(2)}, u32[]{:S(2)}) collective-permute-start(f32[32,128]{1,0:T(8,128)S(1)} %add.107), channel_id=1, source_target_pairs={{0,32},{32,0},{64,96},{96,64},{1,33},{33,1},{65,97},{97,65},{2,34}... | collective-permute-start | bytes 49160 | tf_op jit(solution)/shard_map/ppermute | solution.py:39
  124.5 5.2 %collective-permute-start.13 = (f32[32,128]{1,0:T(8,128)S(1)}, f32[32,128]{1,0:T(8,128)S(1)}, u32[]{:S(2)}, u32[]{:S(2)}) collective-permute-start(f32[32,128]{1,0:T(8,128)S(1)} %add.108), channel_id=1, source_target_pairs={{0,64},{32,96},{64,0},{96,32},{1,65},{33,97},{65,1},{97,33},{2,66}... | collective-permute-start | bytes 49160 | tf_op jit(solution)/shard_map/ppermute | solution.py:39
  129.8 3.7 %collective-permute-start.14 = (f32[32,128]{1,0:T(8,128)S(1)}, f32[32,128]{1,0:T(8,128)S(1)}, u32[]{:S(2)}, u32[]{:S(2)}) collective-permute-start(f32[32,128]{1,0:T(8,128)S(1)} %add.109), channel_id=1, source_target_pairs={{0,2},{2,0},{4,6},{6,4},{8,10},{10,8},{12,14},{14,12},{1,3},{3,1},... | collective-permute-start | bytes 49160 | tf_op jit(solution)/shard_map/ppermute | solution.py:39
  133.5 4.6 %collective-permute-start.15 = (f32[32,128]{1,0:T(8,128)S(1)}, f32[32,128]{1,0:T(8,128)S(1)}, u32[]{:S(2)}, u32[]{:S(2)}) collective-permute-start(f32[32,128]{1,0:T(8,128)S(1)} %add.110), channel_id=1, source_target_pairs={{0,4},{2,6},{4,0},{6,2},{8,12},{10,14},{12,8},{14,10},{1,5},{3,7},... | collective-permute-start | bytes 49160 | tf_op jit(solution)/shard_map/ppermute | solution.py:39
  138.1 7.6 %collective-permute-start.16 = (f32[32,128]{1,0:T(8,128)S(1)}, f32[32,128]{1,0:T(8,128)S(1)}, u32[]{:S(2)}, u32[]{:S(2)}) collective-permute-start(f32[32,128]{1,0:T(8,128)S(1)} %add.111), channel_id=1, source_target_pairs={{0,8},{2,10},{4,12},{6,14},{8,0},{10,2},{12,4},{14,6},{1,9},{3,11}... | collective-permute-start | bytes 49160 | tf_op jit(solution)/shard_map/ppermute | solution.py:39
  218.0 1.6 collective-permute-start.17
  219.7 5.8 %collective-permute-start.18 = (f32[136,256]{1,0:T(8,128)S(1)}, f32[136,256]{1,0:T(8,128)S(1)}, u32[]{:S(2)}, u32[]{:S(2)}) collective-permute-start(f32[136,256]{1,0:T(8,128)S(1)} %slice_select_fusion.1), channel_id=1, source_target_pairs={{0,1},{1,0},{2,3},{3,2},{4,5},{5,4},{6,7},{7,6},{8,9},{9,8},{10,11... | collective-permute-start | bytes 417800 | tf_op jit(solution)/shard_map/ppermute | solution.py:191
  225.5 5.1 %collective-permute-start.19 = (f32[136,256]{1,0:T(8,128)S(1)}, f32[136,256]{1,0:T(8,128)S(1)}, u32[]{:S(2)}, u32[]{:S(2)}) collective-permute-start(f32[136,256]{1,0:T(8,128)S(1)} %select_add_fusion), channel_id=1, source_target_pairs={{0,32},{32,0},{64,96},{96,64},{1,33},{33,1},{65,97},{97,65},{2,34}... | collective-permute-start | bytes 417800 | tf_op jit(solution)/shard_map/ppermute | solution.py:39
  230.7 6.6 %collective-permute-start.20 = (f32[136,256]{1,0:T(8,128)S(1)}, f32[136,256]{1,0:T(8,128)S(1)}, u32[]{:S(2)}, u32[]{:S(2)}) collective-permute-start(f32[136,256]{1,0:T(8,128)S(1)} %add.117), channel_id=1, source_target_pairs={{0,64},{32,96},{64,0},{96,32},{1,65},{33,97},{65,1},{97,33},{2,66}... | collective-permute-start | bytes 417800 | tf_op jit(solution)/shard_map/ppermute | solution.py:39
  237.4 6.6 %collective-permute-start.21 = (f32[136,256]{1,0:T(8,128)S(1)}, f32[136,256]{1,0:T(8,128)S(1)}, u32[]{:S(2)}, u32[]{:S(2)}) collective-permute-start(f32[136,256]{1,0:T(8,128)S(1)} %add.118), channel_id=1, source_target_pairs={{0,128},{128,0},{1,129},{129,1},{2,130},{130,2},{3,131},{131,3},{4... | collective-permute-start | bytes 417800 | tf_op jit(solution)/shard_map/ppermute | solution.py:39
  244.0 1.4 collective-permute-start.22
Sparse Core Ops, SparseCore 0:
  16.6 44.0 all-gather.1
  161.0 55.0 reduce-scatter.1
